TPU v7x, 32 devices: a whole 2x2x4 slice. The times are simulated.
32 devices in a mesh: pb: 8 (over z, y), col: 4 (over x, core).
Axes of the slice: x: 2, y: 2, z: 4, core: 2. Of those that a mesh axis runs over, the one named last changes fastest.
Arguments:
- orbitals: bfloat16 [8, 48, 4096], P('pb', None, 'col'), may hold values from -6 to 6
- screening: bfloat16 [8, 4096, 4096], P('pb', None, 'col'), may hold values from -0.0014648438 to 0.0014648438
- pairs_k: int32 [8, 4], P('pb'), may hold values from 0 to 7
Outputs:
- kernel: float32 [8, 4, 256, 1024], P('pb', None, None, 'col')
All inputs are finite; a program needn't handle non-finite values.
Results may differ from a plain program's by a relative error of at most 0.0049.
Values may be sent and summed in bfloat16 or wider, within the bound.
No kernel may reach another device: no remote copies, remote signals or barrier semaphores. Data moves between devices by JAX's collectives and lax.ppermute only.
A program may use at most 128 MiB of HBM per device.

v0:
```python
import jax
import jax.numpy as jnp
from jax import lax
from jax.sharding import PartitionSpec as P

NV = 16
NC = 32


def body(orbitals, screening, pairs_k):
    k_dev, orb_count, mu_cols = orbitals.shape
    group_count = lax.axis_size("pb")
    kpoint_count = k_dev * group_count
    group_index = lax.axis_index("pb")
    kpoint_a = pairs_k[0]
    kpoint_b = (kpoint_a - group_index) % kpoint_count
    wanted = jnp.concatenate([kpoint_a, kpoint_b])
    slot_count = wanted.shape[0]
    pair_count = slot_count // 2
    block_rows = lax.all_gather(orbitals, "pb", axis=0, tiled=True)
    indices = jnp.arange(block_rows.shape[0], dtype=jnp.int32)
    chooser = (wanted[:, None] == indices[None, :]).astype(jnp.bfloat16)
    fetched = jnp.einsum(
        "sk,kom->som", chooser, block_rows, preferred_element_type=jnp.float32
    ).astype(jnp.bfloat16)
    valence = lax.all_gather(fetched[:, :NV, :], "col", axis=2, tiled=True)
    valence_a = valence[:pair_count].astype(jnp.float32)
    valence_b = valence[pair_count:].astype(jnp.float32)
    val_pairs = (valence_a[:, :, None, :] * valence_b[:, None, :, :]).astype(jnp.bfloat16)
    val_pairs = val_pairs.reshape(pair_count * NV * NV, valence.shape[2])
    screened = jnp.dot(val_pairs, screening[0], preferred_element_type=jnp.float32).astype(
        jnp.bfloat16
    )
    screened = screened.reshape(pair_count, NV * NV, mu_cols)
    conduction = fetched[:, NV:, :].astype(jnp.float32)
    cond_pairs = (conduction[:pair_count, :, None, :] * conduction[pair_count:, None, :, :]).astype(
        jnp.bfloat16
    )
    cond_pairs = cond_pairs.reshape(pair_count, NC * NC, mu_cols)
    partial_value = jnp.einsum(
        "pan,pbn->pab", screened, cond_pairs, preferred_element_type=jnp.float32
    )
    whole_sum = lax.psum(partial_value, "col")
    column_count = whole_sum.shape[2] // lax.axis_size("col")
    result = lax.dynamic_slice_in_dim(
        whole_sum, lax.axis_index("col") * column_count, column_count, 2
    )
    return result[None]


def solution(mesh):
    placed = (P("pb", None, "col"), P("pb", None, "col"), P("pb", None))
    return jax.shard_map(
        body, mesh=mesh, in_specs=placed, out_specs=P("pb", None, None, "col"), check_vma=False
    )
```

profile of v0, /device:TPU:0, one launch (start us, length us, event | category | flops | bytes accessed | tf_op | source)
XLA Modules:
  0.0 181.1 jit_solution(12685223790277849974)
XLA Ops:
  6.5 0.0 all-gather.2.cloned.1.call-start
  6.5 34.0 %all_gather.6 = bf16[8,48,1024]{2,1,0:T(8,128)(2,1)S(1)} all-gather(bf16[1,48,1024]{2,1,0:T(8,128)(2,1)} %param.3), channel_id=1, replica_groups=mesh['pb'=8,'col'=4] {'pb'}, dimensions={0}, use_global_device_ids=true | all-gather | bytes 884736 | tf_op jit(solution)/shard_map/all_gather | solution.py:20
  40.5 0.7 and_select_fusion
  41.2 0.7 pad_add_fusion
  41.9 0.6 fusion.5
  42.5 0.4 copy.19
  42.9 0.7 slice.24
  43.6 0.0 all-gather.2.cloned.1.call-update
  43.7 0.0 all-reduce.2.cloned.1.call-start
  43.7 0.1 slice_convert_fusion
  43.8 0.1 fusion.11
  43.9 6.2 %multiply_convert_fusion = bf16[4,32,32,1024]{3,2,1,0:T(8,128)(2,1)} fusion(f32[4,32,1024]{2,1,0:T(8,128)S(1)} %get-tuple-element.6, f32[4,32,1024]{2,1,0:T(8,128)S(1)} %get-tuple-element.5), kind=kLoop, calls=%fused_computation | loop fusion | flops 8388608 | bytes 9437184 | tf_op jit(solution)/shard_map/convert_element_type | solution.py:36
  50.2 11.4 %all-gather.2.cloned.1.call-done = bf16[8,16,4096]{2,1,0:T(8,128)(2,1)} async-done(((bf16[8,16,1024]{2,1,0:T(8,128)(2,1)}), bf16[8,16,4096]{2,1,0:T(8,128)(2,1)}) %all-gather.2.cloned.1.call-update) | async-done | bytes 1048592 | tf_op jit(solution)/shard_map/all_gather | solution.py:26
  61.6 1.4 slice_convert_fusion.2
  63.0 0.0 slice-start
  63.0 5.2 %multiply_convert_fusion.1 = bf16[4,16,16,4096]{3,2,1,0:T(8,128)(2,1)} fusion(f32[4,16,4096]{2,1,0:T(8,128)S(1)} %get-tuple-element.8, f32[4,16,4096]{2,1,0:T(8,128)S(1)} %get-tuple-element.7), kind=kLoop, calls=%fused_computation.1 | loop fusion | flops 8388608 | bytes 10485760 | tf_op jit(solution)/shard_map/convert_element_type | solution.py:29
  68.2 0.0 slice-start.1
  68.2 13.8 %fusion.2 = bf16[1024,1024]{1,0:T(8,128)(2,1)S(1)} fusion(bf16[1024,4096]{1,0:T(8,128)(2,1)} %bitcast.21, bf16[1,4096,1024]{2,1,0:T(8,128)(2,1)} %param.4), kind=kOutput, calls=%fused_computation.4 | convolution fusion | flops 8590983168 | bytes 18874368 | tf_op jit(solution)/shard_map/dot_general | solution.py:31
  82.0 0.0 slice-done
  82.0 0.0 slice-done.1
  82.0 4.4 %fusion.12 = f32[4,256,1024]{2,1,0:T(8,128)} fusion(bf16[4,256,1024]{2,1,0:T(8,128)(2,1)S(1)} %bitcast.22, bf16[4,1024,1024]{2,1,0:T(8,128)(2,1)S(1)} %bitcast.20), kind=kOutput, calls=%fused_computation.21 | convolution fusion | flops 2147483648 | bytes 14680064 | tf_op jit(solution)/shard_map/pan,pbn->pab/dot_general | solution.py:40
  86.4 0.0 all-reduce.2.cloned.1.call-update
  86.4 85.6 %all-reduce.2.cloned.1.call-done = f32[4,256,1024]{2,1,0:T(8,128)} async-done(((f32[4,256,1024]{2,1,0:T(8,128)}), f32[4,256,1024]{2,1,0:T(8,128)}) %all-reduce.2.cloned.1.call-update) | async-done | bytes 4194320 | tf_op jit(solution)/shard_map/psum | solution.py:43
  172.0 2.3 %dynamic-slice_bitcast_fusion = f32[1,4,256,256]{3,2,1,0:T(8,128)} fusion(f32[4,256,1024]{2,1,0:T(8,128)} %all-reduce.2.cloned.1.call-done, s32[]{:T(128)S(6)} %select_n.11), kind=kLoop, calls=%fused_computation.6 | loop fusion | bytes 2097156 | tf_op jit(solution)/shard_map/broadcast_in_dim | solution.py:48
  (1 shorter events, 0.0 us)
Async XLA Ops:
  6.5 55.0 %all-gather.2.cloned.1.call-start = ((), (), s32[]{:S(2)}) async-start(), calls=%async_computation | async-start | bytes 1310720 | tf_op jit(solution)/shard_map/all_gather | solution.py:26
  43.7 128.3 %all-reduce.2.cloned.1.call-start = ((), (), s32[]{:S(2)}) async-start(), calls=%async_computation.1 | async-start | bytes 8388608 | tf_op jit(solution)/shard_map/psum | solution.py:43
  63.0 19.0 %slice-start = ((s8[8388608]{0:T(1024)(128)(4,1)}), s8[4194304]{0:T(1024)(128)(4,1)S(1)}, s32[]{:S(2)}) async-start(s8[8388608]{0:T(1024)(128)(4,1)} %bitcast.18), calls=%async_computation.2 | async-start | bytes 8388608
  68.2 13.8 %slice-start.1 = ((s8[8388608]{0:T(1024)(128)(4,1)}), s8[4194304]{0:T(1024)(128)(4,1)S(1)}, s32[]{:S(2)}) async-start(s8[8388608]{0:T(1024)(128)(4,1)} %bitcast.18), calls=%async_computation.3 | async-start | bytes 8388608
Sparse Core Ops, SparseCore 0:
  43.8 17.7 all-gather.1
  86.5 85.4 all-reduce.1
where the time goes:
time: 181 us
  waiting for transfers between devices  97 us (54%)
  blocking collectives  34 us (19%)
  matrix products  18.7 us (10%)
  other arithmetic  14.3 us (8%)
  between operations  13.5 us (7%)
  local copies, waits for them, and re-layouts  3.56 us (2%)
    psum x1, waiting for transfers between devices, body(): whole_sum = lax.psum(partial_value, 'col')  85.6 us
    all_gather x1, blocking collectives, body(): block_rows = lax.all_gather(orbitals, 'pb', axis=0, tiled=True)  34 us
    dot_general x1, matrix products, body(): jnp.dot(val_pairs, screening[0], preferred_element_type=jnp.float32)  13.8 us
    all_gather x1, waiting for transfers between devices, body(): valence = lax.all_gather(fetched[:, :NV, :], 'col', axis=2, tiled=True)  11.4 us
    convert_element_type x1, other arithmetic, body(): (conduction[:pair_count, :, None, :] * conduction[pair_count:, None, :, :...  6.24 us
    convert_element_type x1, other arithmetic, body(): (valence_a[:, :, None, :] * valence_b[:, None, :, :]).astype(jnp.bfloat16)  5.17 us
    dot_general x1, matrix products, body(): jnp.einsum('pan,pbn->pab', screened, cond_pairs, preferred_element_type=j...  4.36 us
  transfers between devices with their start and end apart: 2, of which 2 were waited for; matrix products, arithmetic and copies ran while one was open for 4% of the time, Pallas kernels for 0%

commit v1 on v0

v1 whole, which is shorter than its diff:
```python
import jax
import jax.numpy as jnp
from jax import lax
from jax.sharding import PartitionSpec as P

NV = 16
NC = 32


def body(orbitals, screening, pairs_k):
    k_dev, orb_count, mu_cols = orbitals.shape
    group_count = lax.axis_size("pb")
    col_count = lax.axis_size("col")
    kpoint_count = k_dev * group_count
    group_index = lax.axis_index("pb")
    kpoint_a = pairs_k[0]
    kpoint_b = (kpoint_a - group_index) % kpoint_count
    pair_count = kpoint_a.shape[0]

    valence_all = lax.all_gather(orbitals[:, :NV, :], ("pb", "col"), axis=0, tiled=True)
    valence_all = jnp.transpose(
        valence_all.reshape(kpoint_count, col_count, NV, mu_cols), (0, 2, 1, 3)
    ).reshape(kpoint_count, NV, col_count * mu_cols)
    conduction_all = lax.all_gather(orbitals[:, NV:, :], "pb", axis=0, tiled=True)

    valence_a = jnp.take(valence_all, kpoint_a, axis=0).astype(jnp.float32)
    valence_b = jnp.take(valence_all, kpoint_b, axis=0).astype(jnp.float32)
    val_pairs = (valence_a[:, :, None, :] * valence_b[:, None, :, :]).astype(jnp.bfloat16)
    val_pairs = val_pairs.reshape(pair_count * NV * NV, col_count * mu_cols)
    screened = jnp.dot(val_pairs, screening[0], preferred_element_type=jnp.float32).astype(
        jnp.bfloat16
    )
    screened = screened.reshape(pair_count, NV * NV, mu_cols)

    cond_a = jnp.take(conduction_all, kpoint_a, axis=0).astype(jnp.float32)
    cond_b = jnp.take(conduction_all, kpoint_b, axis=0).astype(jnp.float32)
    cond_pairs = (cond_a[:, :, None, :] * cond_b[:, None, :, :]).astype(jnp.bfloat16)
    cond_pairs = cond_pairs.reshape(pair_count, NC * NC, mu_cols)
    partial_value = jnp.einsum(
        "pan,pbn->pab", screened, cond_pairs, preferred_element_type=jnp.float32
    )
    result = lax.psum_scatter(partial_value, "col", scatter_dimension=2, tiled=True)
    return result[None]


def solution(mesh):
    placed = (P("pb", None, "col"), P("pb", None, "col"), P("pb", None))
    return jax.shard_map(
        body, mesh=mesh, in_specs=placed, out_specs=P("pb", None, None, "col"), check_vma=False
    )
```

time: 181 us -> 145 us (0.80)
  waiting for transfers between devices: 97 us -> 59.5 us
  local copies, waits for them, and re-layouts: 3.56 us -> 7.36 us
    psum x1 -> x0, waiting for transfers between devices: 85.6 us -> none  [body(): whole_sum = lax.psum(partial_value, 'col')]
    reduce_scatter x0 -> x1, waiting for transfers between devices: none -> 43.7 us  [body(): lax.psum_scatter(partial_value, 'col', scatter_dimension=2, tiled=True)]
    all_gather x1, waiting for transfers between devices: 11.4 us -> 15.8 us  [body(): lax.all_gather(orbitals[:, :NV, :], ('pb', 'col'), axis=0, tiled=True)]
    reshape x0 -> x2, local copies, waits for them, and re-layouts: none -> 2.85 us  [the longest x1 2.04 us: body(): valence_all.reshape(kpoint_count, col_count, NV, mu_cols)]
    gather x0 -> x4, local copies, waits for them, and re-layouts: none -> 2.29 us  [the longest x1 0.58 us: body(): valence_a = jnp.take(valence_all, kpoint_a, axis=0).astype(jnp.float32)]
    broadcast_in_dim x1 -> x0, local copies, waits for them, and re-layouts: 2.28 us -> none  [body(): return result[None]]
  transfers between devices with their start and end apart: 2 -> 2, of which waited for: 2 -> 2; matrix products, arithmetic and copies ran while one was open for 4% -> 7% of each run, Pallas kernels for 0% -> 0%
where the time goes in v1:
time: 145 us
  waiting for transfers between devices  59.5 us (41%)
  blocking collectives  33.2 us (23%)
  matrix products  18.1 us (12%)
  between operations  13.5 us (9%)
  other arithmetic  13.1 us (9%)
  local copies, waits for them, and re-layouts  7.36 us (5%)
    reduce_scatter x1, waiting for transfers between devices, body(): lax.psum_scatter(partial_value, 'col', scatter_dimension=2, tiled=True)  43.7 us
    all_gather x1, blocking collectives, body(): lax.all_gather(orbitals[:, NV:, :], 'pb', axis=0, tiled=True)  33.2 us
    all_gather x1, waiting for transfers between devices, body(): lax.all_gather(orbitals[:, :NV, :], ('pb', 'col'), axis=0, tiled=True)  15.8 us
    dot_general x1, matrix products, body(): jnp.dot(val_pairs, screening[0], preferred_element_type=jnp.float32)  13.8 us
    convert_element_type x1, other arithmetic, body(): (cond_a[:, :, None, :] * cond_b[:, None, :, :]).astype(jnp.bfloat16)  6.23 us
    convert_element_type x1, other arithmetic, body(): (valence_a[:, :, None, :] * valence_b[:, None, :, :]).astype(jnp.bfloat16)  5.18 us
    dot_general x1, matrix products, body(): jnp.einsum('pan,pbn->pab', screened, cond_pairs, preferred_element_type=j...  4.34 us
  transfers between devices with their start and end apart: 2, of which 2 were waited for; matrix products, arithmetic and copies ran while one was open for 7% of the time, Pallas kernels for 0%

profile of v1, /device:TPU:0, one launch (start us, length us, event | category | flops | bytes accessed | tf_op | source)
XLA Modules:
  0.0 144.8 jit_solution(2864001401554279524)
XLA Ops:
  6.5 0.0 all-gather.2.cloned.1.call-start
  6.5 1.4 slice.6
  7.9 0.0 all-gather.2.cloned.1.call-update
  7.9 0.0 reduce-scatter.2.cloned.1.call-start
  8.0 0.8 slice.7
  8.8 0.7 compare_and_fusion
  9.5 33.2 %all_gather.7 = bf16[8,32,1024]{2,1,0:T(8,128)(2,1)S(1)} all-gather(bf16[1,32,1024]{2,1,0:T(8,128)(2,1)S(1)} %slice.7), channel_id=1, replica_groups=mesh['pb'=8,'col'=4] {'pb'}, dimensions={0}, use_global_device_ids=true | all-gather | bytes 589824 | tf_op jit(solution)/shard_map/all_gather | solution.py:24
  42.8 0.6 gather_fusion.3
  43.3 0.7 compare_select_fusion.1
  44.0 0.6 gather_fusion.2
  44.6 0.1 select_convert_fusion.2
  44.7 6.2 %multiply_convert_fusion = bf16[4,32,32,1024]{3,2,1,0:T(8,128)(2,1)} fusion(f32[4,32,1024]{2,1,0:T(8,128)S(1)} %get-tuple-element.12, f32[4,32,1024]{2,1,0:T(8,128)S(1)} %get-tuple-element.13), kind=kLoop, calls=%fused_computation.4 | loop fusion | flops 8388608 | bytes 9437184 | tf_op jit(solution)/shard_map/convert_element_type | solution.py:37
  50.9 15.8 %all-gather.2.cloned.1.call-done = bf16[32,16,1024]{2,1,0:T(8,128)(2,1)} async-done(((bf16[1,16,1024]{2,1,0:T(8,128)(2,1)}), bf16[32,16,1024]{2,1,0:T(8,128)(2,1)}) %all-gather.2.cloned.1.call-update) | async-done | bytes 1048592 | tf_op jit(solution)/shard_map/all_gather | solution.py:20
  66.7 2.0 %copy.7 = bf16[8,4,16,1024]{3,1,2,0:T(4,128)(2,1)S(1)} copy(bf16[8,4,16,1024]{3,2,1,0:T(8,128)(2,1)} %bitcast.30) | data formatting | bytes 2097152 | tf_op jit(solution)/shard_map/reshape | solution.py:22
  68.8 0.8 reshape.42
  69.6 0.6 gather_fusion
  70.2 0.6 gather_fusion.1
  70.8 0.2 select_convert_fusion
  71.0 0.0 slice-start
  71.0 5.2 %multiply_convert_fusion.1 = bf16[4,16,16,4096]{3,2,1,0:T(8,128)(2,1)} fusion(f32[4,16,4096]{2,1,0:T(8,128)S(1)} %get-tuple-element.10, f32[4,16,4096]{2,1,0:T(8,128)S(1)} %get-tuple-element.11), kind=kLoop, calls=%fused_computation.5 | loop fusion | flops 8388608 | bytes 10485760 | tf_op jit(solution)/shard_map/convert_element_type | solution.py:28
  76.2 0.0 slice-start.1
  76.2 13.8 %fusion.2 = bf16[1024,1024]{1,0:T(8,128)(2,1)S(1)} fusion(bf16[1024,4096]{1,0:T(8,128)(2,1)} %bitcast.27, bf16[1,4096,1024]{2,1,0:T(8,128)(2,1)} %param.8), kind=kOutput, calls=%fused_computation.8 | convolution fusion | flops 8590983168 | bytes 18874368 | tf_op jit(solution)/shard_map/dot_general | solution.py:30
  90.0 0.0 slice-done
  90.0 0.0 slice-done.1
  90.0 4.3 %fusion.6 = f32[4,256,1024]{2,1,0:T(8,128)} fusion(bf16[4,256,1024]{2,1,0:T(8,128)(2,1)S(1)} %bitcast.28, bf16[4,1024,1024]{2,1,0:T(8,128)(2,1)S(1)} %bitcast.26), kind=kOutput, calls=%fused_computation.25 | convolution fusion | flops 2147483648 | bytes 14680064 | tf_op jit(solution)/shard_map/pan,pbn->pab/dot_general | solution.py:39
  94.3 0.0 reduce-scatter.2.cloned.1.call-update
  94.4 43.7 %reduce-scatter.2.cloned.1.call-done = f32[4,256,256]{2,1,0:T(8,128)} async-done(((f32[4,256,1024]{2,1,0:T(8,128)}), f32[4,256,256]{2,1,0:T(8,128)}) %reduce-scatter.2.cloned.1.call-update) | async-done | bytes 1048592 | tf_op jit(solution)/shard_map/reduce_scatter | solution.py:42
  (3 shorter events, 0.0 us)
Async XLA Ops:
  6.5 60.2 %all-gather.2.cloned.1.call-start = ((), (), s32[]{:S(2)}) async-start(), calls=%async_computation.1 | async-start | bytes 1081344 | tf_op jit(solution)/shard_map/all_gather | solution.py:20
  7.9 130.1 %reduce-scatter.2.cloned.1.call-start = ((), (), s32[]{:S(2)}) async-start(), calls=%async_computation.2 | async-start | bytes 5242880 | tf_op jit(solution)/shard_map/reduce_scatter | solution.py:42
  71.0 19.0 %slice-start = ((s8[8388608]{0:T(1024)(128)(4,1)}), s8[4194304]{0:T(1024)(128)(4,1)S(1)}, s32[]{:S(2)}) async-start(s8[8388608]{0:T(1024)(128)(4,1)} %bitcast.24), calls=%async_computation.3 | async-start | bytes 8388608
  76.2 13.8 %slice-start.1 = ((s8[8388608]{0:T(1024)(128)(4,1)}), s8[4194304]{0:T(1024)(128)(4,1)S(1)}, s32[]{:S(2)}) async-start(s8[8388608]{0:T(1024)(128)(4,1)} %bitcast.24), calls=%async_computation.4 | async-start | bytes 8388608
Sparse Core Ops, SparseCore 0:
  10.2 56.4 all-gather.1
  94.5 43.4 reduce-scatter.1

commit v2 on v1

v2 whole, which is shorter than its diff:
```python
import jax
import jax.numpy as jnp
from jax import lax
from jax.sharding import PartitionSpec as P

NV = 16
NC = 32


def swap(x, axis, bit):
    size = lax.axis_size(axis)
    return lax.ppermute(x, axis, [(i, i ^ bit) for i in range(size)])


def gather_col(mine):
    col_count = lax.axis_size("col")
    me = lax.axis_index("col")
    cur = mine[None]
    bit = col_count // 2
    while bit >= 1:
        got = swap(cur, "col", bit)
        low = (me & bit) == 0
        cur = jnp.where(low, jnp.stack([cur, got], 1), jnp.stack([got, cur], 1))
        cur = cur.reshape((-1,) + mine.shape)
        bit //= 2
    return cur


def scatter_sum_col(partial):
    col_count = lax.axis_size("col")
    me = lax.axis_index("col")
    width = partial.shape[-1] // col_count
    lead = partial.shape[:-1]
    cur = partial.reshape(lead + (col_count, width))
    bit = 1
    shift = 0
    while bit < col_count:
        parts = cur.shape[-2]
        cur = cur.reshape(lead + (parts // 2, 2, width))
        mine_bit = (me >> shift) & 1
        keep = lax.dynamic_index_in_dim(cur, mine_bit, len(lead) + 1, keepdims=False)
        send = lax.dynamic_index_in_dim(cur, 1 - mine_bit, len(lead) + 1, keepdims=False)
        cur = keep + swap(send, "col", bit)
        bit *= 2
        shift += 1
    return cur.reshape(lead + (width,))


def body(orbitals, screening, pairs_k):
    k_dev, orb_count, mu_cols = orbitals.shape
    group_count = lax.axis_size("pb")
    col_count = lax.axis_size("col")
    kpoint_count = k_dev * group_count
    group_index = lax.axis_index("pb")
    kpoint_a = pairs_k[0]
    kpoint_b = (kpoint_a - group_index) % kpoint_count
    pair_count = kpoint_a.shape[0]

    held = [orbitals]
    for s in range(1, group_count):
        held.append(
            lax.ppermute(orbitals, "pb", [(i, (i + s) % group_count) for i in range(group_count)])
        )
    held = jnp.concatenate(held, 0)

    def slot_of(k):
        return ((group_index - k // k_dev) % group_count) * k_dev + k % k_dev

    wanted = jnp.concatenate([slot_of(kpoint_a), slot_of(kpoint_b)])
    chosen = jnp.take(held, wanted, axis=0)

    valence = gather_col(chosen[:, :NV, :])
    valence = jnp.transpose(valence, (1, 2, 0, 3)).reshape(
        2 * pair_count, NV, col_count * mu_cols
    )
    valence_a = valence[:pair_count].astype(jnp.float32)
    valence_b = valence[pair_count:].astype(jnp.float32)
    val_pairs = (valence_a[:, :, None, :] * valence_b[:, None, :, :]).astype(jnp.bfloat16)
    val_pairs = val_pairs.reshape(pair_count * NV * NV, col_count * mu_cols)
    screened = jnp.dot(val_pairs, screening[0], preferred_element_type=jnp.float32).astype(
        jnp.bfloat16
    )
    screened = screened.reshape(pair_count, NV * NV, mu_cols)

    conduction = chosen[:, NV:, :].astype(jnp.float32)
    cond_pairs = (
        conduction[:pair_count, :, None, :] * conduction[pair_count:, None, :, :]
    ).astype(jnp.bfloat16)
    cond_pairs = cond_pairs.reshape(pair_count, NC * NC, mu_cols)
    partial_value = jnp.einsum(
        "pan,pbn->pab", screened, cond_pairs, preferred_element_type=jnp.float32
    )
    return scatter_sum_col(partial_value)[None]


def solution(mesh):
    placed = (P("pb", None, "col"), P("pb", None, "col"), P("pb", None))
    return jax.shard_map(
        body, mesh=mesh, in_specs=placed, out_specs=P("pb", None, None, "col"), check_vma=False
    )
```

time: 145 us -> 112 us (0.77)
  the two profiles are of different devices: /device:TPU:0 before, /device:TPU:14 now
where the time goes in v2:
time: 112 us
  waiting for transfers between devices  47.7 us (43%)
  local copies, waits for them, and re-layouts  20.2 us (18%)
  matrix products  18 us (16%)
  other arithmetic  15.3 us (14%)
  starting transfers between devices  10.4 us (9%)
    ppermute x4, waiting for transfers between devices, swap(): return lax.ppermute(x, axis, [(i, i ^ bit) for i in range(size)])  36.3 us
    dot_general x1, matrix products, body(): jnp.dot(val_pairs, screening[0], preferred_element_type=jnp.float32)  13.7 us
    ppermute x7, waiting for transfers between devices, body(): lax.ppermute(orbitals, 'pb', [(i, (i + s) % group_count) for i in range(g...  11.4 us
    ppermute x7, starting transfers between devices, body(): lax.ppermute(orbitals, 'pb', [(i, (i + s) % group_count) for i in range(g...  8.62 us
    dynamic_slice x1, local copies, waits for them, and re-layouts, scatter_sum_col(): lax.dynamic_index_in_dim(cur, mine_bit, len(lead) + 1, keepdims=False)  7.78 us
    another operation x1, local copies, waits for them, and re-layouts, scatter_sum_col(): cur = cur.reshape(lead + (parts // 2, 2, width))  6.64 us
    convert_element_type x1, other arithmetic, body(): (valence_a[:, :, None, :] * valence_b[:, None, :, :]).astype(jnp.bfloat16)  6.37 us
    dot_general x1, matrix products, body(): jnp.einsum('pan,pbn->pab', screened, cond_pairs, preferred_element_type=j...  4.36 us
  transfers between devices with their start and end apart: 11, of which 8 were waited for; matrix products, arithmetic and copies ran while one was open for 5% of the time, Pallas kernels for 0%

profile of v2, /device:TPU:14, one launch (start us, length us, event | category | flops | bytes accessed | tf_op | source)
XLA Modules:
  0.0 111.8 jit_solution(11632281185127339216)
XLA Ops:
  0.0 1.5 %collective-permute-start = (bf16[1,48,1024]{2,1,0:T(8,128)(2,1)}, bf16[1,48,1024]{2,1,0:T(8,128)(2,1)S(1)}, u32[]{:S(2)}, u32[]{:S(2)}) collective-permute-start(bf16[1,48,1024]{2,1,0:T(8,128)(2,1)} %param.3), channel_id=1, source_target_pairs={{0,4},{4,8},{8,12},{12,16},{16,20},{20,24},{24,28},{28,0},{1,5},{5... | collective-permute-start | bytes 294920 | tf_op jit(solution)/shard_map/ppermute | solution.py:62
  1.5 1.6 %collective-permute-start.1 = (bf16[1,48,1024]{2,1,0:T(8,128)(2,1)}, bf16[1,48,1024]{2,1,0:T(8,128)(2,1)S(1)}, u32[]{:S(2)}, u32[]{:S(2)}) collective-permute-start(bf16[1,48,1024]{2,1,0:T(8,128)(2,1)} %param.3), channel_id=1, source_target_pairs={{0,8},{4,12},{8,16},{12,20},{16,24},{20,28},{24,0},{28,4},{1,9},{5... | collective-permute-start | bytes 294920 | tf_op jit(solution)/shard_map/ppermute | solution.py:62
  3.1 1.2 %collective-permute-start.2 = (bf16[1,48,1024]{2,1,0:T(8,128)(2,1)}, bf16[1,48,1024]{2,1,0:T(8,128)(2,1)S(1)}, u32[]{:S(2)}, u32[]{:S(2)}) collective-permute-start(bf16[1,48,1024]{2,1,0:T(8,128)(2,1)} %param.3), channel_id=1, source_target_pairs={{0,12},{4,16},{8,20},{12,24},{16,28},{20,0},{24,4},{28,8},{1,13},{... | collective-permute-start | bytes 294920 | tf_op jit(solution)/shard_map/ppermute | solution.py:62
  4.3 1.7 %collective-permute-start.3 = (bf16[1,48,1024]{2,1,0:T(8,128)(2,1)}, bf16[1,48,1024]{2,1,0:T(8,128)(2,1)S(1)}, u32[]{:S(2)}, u32[]{:S(2)}) collective-permute-start(bf16[1,48,1024]{2,1,0:T(8,128)(2,1)} %param.3), channel_id=1, source_target_pairs={{0,16},{4,20},{8,24},{12,28},{16,0},{20,4},{24,8},{28,12},{1,17},{... | collective-permute-start | bytes 294920 | tf_op jit(solution)/shard_map/ppermute | solution.py:62
  6.0 1.3 %collective-permute-start.4 = (bf16[1,48,1024]{2,1,0:T(8,128)(2,1)}, bf16[1,48,1024]{2,1,0:T(8,128)(2,1)S(1)}, u32[]{:S(2)}, u32[]{:S(2)}) collective-permute-start(bf16[1,48,1024]{2,1,0:T(8,128)(2,1)} %param.3), channel_id=1, source_target_pairs={{0,20},{4,24},{8,28},{12,0},{16,4},{20,8},{24,12},{28,16},{1,21},{... | collective-permute-start | bytes 294920 | tf_op jit(solution)/shard_map/ppermute | solution.py:62
  7.3 0.9 constant_dynamic-update-slice_fusion.7
  8.2 0.7 and_select_fusion.2
  9.0 1.4 %collective-permute-start.5 = (bf16[1,48,1024]{2,1,0:T(8,128)(2,1)}, bf16[1,48,1024]{2,1,0:T(8,128)(2,1)S(1)}, u32[]{:S(2)}, u32[]{:S(2)}) collective-permute-start(bf16[1,48,1024]{2,1,0:T(8,128)(2,1)} %param.3), channel_id=1, source_target_pairs={{0,24},{4,28},{8,0},{12,4},{16,8},{20,12},{24,16},{28,20},{1,25},{... | collective-permute-start | bytes 294920 | tf_op jit(solution)/shard_map/ppermute | solution.py:62
  10.4 5.0 %collective-permute-done.1 = bf16[1,48,1024]{2,1,0:T(8,128)(2,1)S(1)} collective-permute-done((bf16[1,48,1024]{2,1,0:T(8,128)(2,1)}, bf16[1,48,1024]{2,1,0:T(8,128)(2,1)S(1)}, u32[]{:S(2)}, u32[]{:S(2)}) %collective-permute-start.1) | collective-permute-done | bytes 98336 | tf_op jit(solution)/shard_map/ppermute | solution.py:62
  15.4 2.1 %collective-permute-done.2 = bf16[1,48,1024]{2,1,0:T(8,128)(2,1)S(1)} collective-permute-done((bf16[1,48,1024]{2,1,0:T(8,128)(2,1)}, bf16[1,48,1024]{2,1,0:T(8,128)(2,1)S(1)}, u32[]{:S(2)}, u32[]{:S(2)}) %collective-permute-start.2) | collective-permute-done | bytes 98336 | tf_op jit(solution)/shard_map/ppermute | solution.py:62
  17.5 1.2 %collective-permute-done.3 = bf16[1,48,1024]{2,1,0:T(8,128)(2,1)S(1)} collective-permute-done((bf16[1,48,1024]{2,1,0:T(8,128)(2,1)}, bf16[1,48,1024]{2,1,0:T(8,128)(2,1)S(1)}, u32[]{:S(2)}, u32[]{:S(2)}) %collective-permute-start.3) | collective-permute-done | bytes 98336 | tf_op jit(solution)/shard_map/ppermute | solution.py:62
  18.7 1.6 %collective-permute-done.5 = bf16[1,48,1024]{2,1,0:T(8,128)(2,1)S(1)} collective-permute-done((bf16[1,48,1024]{2,1,0:T(8,128)(2,1)}, bf16[1,48,1024]{2,1,0:T(8,128)(2,1)S(1)}, u32[]{:S(2)}, u32[]{:S(2)}) %collective-permute-start.5) | collective-permute-done | bytes 98336 | tf_op jit(solution)/shard_map/ppermute | solution.py:62
  20.4 1.5 %collective-permute-done.6 = bf16[1,48,1024]{2,1,0:T(8,128)(2,1)S(1)} collective-permute-done((bf16[1,48,1024]{2,1,0:T(8,128)(2,1)}, bf16[1,48,1024]{2,1,0:T(8,128)(2,1)S(1)}, u32[]{:S(2)}, u32[]{:S(2)}) %collective-permute-start.6) | collective-permute-done | bytes 98336 | tf_op jit(solution)/shard_map/ppermute | solution.py:62
  21.9 0.6 gather_fusion
  22.8 0.6 collective-permute-start.7
  23.5 7.3 %collective-permute-done.7 = bf16[1,8,16,1024]{3,2,1,0:T(8,128)(2,1)S(1)} collective-permute-done((bf16[1,8,16,1024]{3,2,1,0:T(8,128)(2,1)S(1)}, bf16[1,8,16,1024]{3,2,1,0:T(8,128)(2,1)S(1)}, u32[]{:S(2)}, u32[]{:S(2)}) %collective-permute-start.7) | collective-permute-done | bytes 262176 | tf_op jit(solution)/shard_map/ppermute | solution.py:12
  31.0 3.0 %multiply_convert_fusion = bf16[4,32,32,1024]{3,2,1,0:T(8,128)(2,1)S(1)} fusion(f32[4,32,1024]{2,1,0:T(8,128)S(1)} %get-tuple-element.8, f32[4,32,1024]{2,1,0:T(8,128)S(1)} %get-tuple-element.7), kind=kLoop, calls=%fused_computation.1 | loop fusion | flops 8388608 | bytes 9437184 | tf_op jit(solution)/shard_map/convert_element_type | solution.py:88
  34.3 0.3 convert_bitcast_fusion.1
  34.6 1.0 copy.11
  35.7 6.4 %multiply_convert_fusion.1 = bf16[4,16,16,4096]{3,2,1,0:T(8,128)(2,1)} fusion(f32[4,16,4096]{2,1,0:T(8,128)} %bitcast.46, f32[4,16,4096]{2,1,0:T(8,128)S(1)} %bitcast.45), kind=kLoop, calls=%fused_computation.2 | loop fusion | flops 8388608 | bytes 10485760 | tf_op jit(solution)/shard_map/convert_element_type | solution.py:78
  42.0 13.7 %fusion.2 = bf16[1024,1024]{1,0:T(8,128)(2,1)S(1)} fusion(bf16[1024,4096]{1,0:T(8,128)(2,1)} %bitcast.42, bf16[1,4096,1024]{2,1,0:T(8,128)(2,1)} %param.4), kind=kOutput, calls=%fused_computation.7 | convolution fusion | flops 8590983168 | bytes 18874368 | tf_op jit(solution)/shard_map/dot_general | solution.py:80
  55.7 4.4 %fusion.11 = f32[4,256,1024]{2,1,0:T(8,128)} fusion(bf16[4,256,1024]{2,1,0:T(8,128)(2,1)S(1)} %bitcast.43, bf16[4,1024,1024]{2,1,0:T(8,128)(2,1)S(1)} %bitcast.41), kind=kOutput, calls=%fused_computation.48 | convolution fusion | flops 2147483648 | bytes 14680064 | tf_op jit(solution)/shard_map/pan,pbn->pab/dot_general | solution.py:90
  60.0 6.6 %reshape_reshape.3 = f32[4,256,2,2,256]{4,3,2,1,0:T(2,128)} reshape(f32[4,256,1024]{2,1,0:T(8,128)} %fusion.11) | data formatting | bytes 8388608 | tf_op jit(solution)/shard_map/reshape;reshape | solution.py:39
  66.7 7.8 %constant_dynamic-slice_fusion.2 = (f32[4,256,2,1,256]{4,3,2,1,0:T(1,128)S(1)}, f32[4,256,2,1,256]{4,3,2,1,0:T(1,128)S(1)}) fusion(f32[4,256,2,2,256]{4,3,2,1,0:T(2,128)} %reshape_reshape.3, s32[]{:T(128)S(6)} %select_n.156, s32[]{:T(128)S(6)} %select_n.157), kind=kLoop, calls=%fused_computation.41 | loop fusion | bytes 8388616 | tf_op jit(solution)/shard_map/jit(dynamic_index_in_dim)/dynamic_slice | solution.py:41
  74.5 1.5 %copy.14 = f32[4,256,2,1,256]{4,1,0,2,3:T(8,128)} copy(f32[4,256,2,1,256]{4,3,2,1,0:T(1,128)S(1)} %get-tuple-element.6) | data formatting | bytes 4194304 | tf_op jit(solution)/shard_map/jit(dynamic_index_in_dim)/dynamic_slice | solution.py:42
  76.0 0.5 collective-permute-start.9
  76.5 4.1 %collective-permute-done.9 = f32[4,256,2,256]{3,1,0,2:T(8,128)} collective-permute-done((f32[4,256,2,256]{3,1,0,2:T(8,128)}, f32[4,256,2,256]{3,1,0,2:T(8,128)}, u32[]{:S(2)}, u32[]{:S(2)}) %collective-permute-start.9) | collective-permute-done | bytes 2097184 | tf_op jit(solution)/shard_map/ppermute | solution.py:12
  80.6 1.9 %bitcast_add_fusion = f32[4,256,2,256]{3,1,0,2:T(8,128)S(1)} fusion(f32[4,256,2,256]{3,1,0,2:T(8,128)} %collective-permute-done.9, f32[4,256,2,1,256]{4,3,2,1,0:T(1,128)S(1)} %get-tuple-element.5), kind=kLoop, calls=%fused_computation.5 | loop fusion | flops 524288 | bytes 6291456 | tf_op jit(solution)/shard_map/add | solution.py:43
  82.5 1.3 %copy-done = f32[4,256,2,256]{3,1,0,2:T(8,128)} copy-done((f32[4,256,2,256]{3,1,0,2:T(8,128)}, f32[4,256,2,256]{3,1,0,2:T(8,128)S(1)}, u32[]{:S(2)}) %copy-start) | copy-done | bytes 2097176
  83.9 0.6 collective-permute-start.10
  84.5 24.9 %collective-permute-done.10 = f32[4,256,1,256]{3,1,0,2:T(8,128)S(1)} collective-permute-done((f32[4,256,1,256]{3,1,0,2:T(8,128)S(1)}, f32[4,256,1,256]{3,1,0,2:T(8,128)S(1)}, u32[]{:S(2)}, u32[]{:S(2)}) %collective-permute-start.10) | collective-permute-done | bytes 1048608 | tf_op jit(solution)/shard_map/ppermute | solution.py:12
  109.4 2.3 %add_bitcast_fusion = f32[1,4,256,256]{3,2,1,0:T(8,128)} fusion(f32[4,256,1,256]{3,1,0,2:T(8,128)S(1)} %collective-permute-done.10, f32[4,256,2,256]{3,1,0,2:T(8,128)} %copy-done, s32[]{:T(128)S(6)} %select_n.158), kind=kLoop, calls=%fused_computation.11 | loop fusion | flops 262144 | bytes 3145732 | tf_op jit(solution)/shard_map/broadcast_in_dim;reshape | solution.py:93
  (25 shorter events, 1.2 us)
Async XLA Ops:
  0.0 9.0 %collective-permute-start = (bf16[1,48,1024]{2,1,0:T(8,128)(2,1)}, bf16[1,48,1024]{2,1,0:T(8,128)(2,1)S(1)}, u32[]{:S(2)}, u32[]{:S(2)}) collective-permute-start(bf16[1,48,1024]{2,1,0:T(8,128)(2,1)} %param.3), channel_id=1, source_target_pairs={{0,4},{4,8},{8,12},{12,16},{16,20},{20,24},{24,28},{28,0},{1,5},{5... | collective-permute-start | bytes 294920 | tf_op jit(solution)/shard_map/ppermute | solution.py:62
  1.5 13.9 %collective-permute-start.1 = (bf16[1,48,1024]{2,1,0:T(8,128)(2,1)}, bf16[1,48,1024]{2,1,0:T(8,128)(2,1)S(1)}, u32[]{:S(2)}, u32[]{:S(2)}) collective-permute-start(bf16[1,48,1024]{2,1,0:T(8,128)(2,1)} %param.3), channel_id=1, source_target_pairs={{0,8},{4,12},{8,16},{12,20},{16,24},{20,28},{24,0},{28,4},{1,9},{5... | collective-permute-start | bytes 294920 | tf_op jit(solution)/shard_map/ppermute | solution.py:62
  3.1 14.4 %collective-permute-start.2 = (bf16[1,48,1024]{2,1,0:T(8,128)(2,1)}, bf16[1,48,1024]{2,1,0:T(8,128)(2,1)S(1)}, u32[]{:S(2)}, u32[]{:S(2)}) collective-permute-start(bf16[1,48,1024]{2,1,0:T(8,128)(2,1)} %param.3), channel_id=1, source_target_pairs={{0,12},{4,16},{8,20},{12,24},{16,28},{20,0},{24,4},{28,8},{1,13},{... | collective-permute-start | bytes 294920 | tf_op jit(solution)/shard_map/ppermute | solution.py:62
  4.3 14.4 %collective-permute-start.3 = (bf16[1,48,1024]{2,1,0:T(8,128)(2,1)}, bf16[1,48,1024]{2,1,0:T(8,128)(2,1)S(1)}, u32[]{:S(2)}, u32[]{:S(2)}) collective-permute-start(bf16[1,48,1024]{2,1,0:T(8,128)(2,1)} %param.3), channel_id=1, source_target_pairs={{0,16},{4,20},{8,24},{12,28},{16,0},{20,4},{24,8},{28,12},{1,17},{... | collective-permute-start | bytes 294920 | tf_op jit(solution)/shard_map/ppermute | solution.py:62
  6.0 12.8 %collective-permute-start.4 = (bf16[1,48,1024]{2,1,0:T(8,128)(2,1)}, bf16[1,48,1024]{2,1,0:T(8,128)(2,1)S(1)}, u32[]{:S(2)}, u32[]{:S(2)}) collective-permute-start(bf16[1,48,1024]{2,1,0:T(8,128)(2,1)} %param.3), channel_id=1, source_target_pairs={{0,20},{4,24},{8,28},{12,0},{16,4},{20,8},{24,12},{28,16},{1,21},{... | collective-permute-start | bytes 294920 | tf_op jit(solution)/shard_map/ppermute | solution.py:62
  9.0 11.3 %collective-permute-start.5 = (bf16[1,48,1024]{2,1,0:T(8,128)(2,1)}, bf16[1,48,1024]{2,1,0:T(8,128)(2,1)S(1)}, u32[]{:S(2)}, u32[]{:S(2)}) collective-permute-start(bf16[1,48,1024]{2,1,0:T(8,128)(2,1)} %param.3), channel_id=1, source_target_pairs={{0,24},{4,28},{8,0},{12,4},{16,8},{20,12},{24,16},{28,20},{1,25},{... | collective-permute-start | bytes 294920 | tf_op jit(solution)/shard_map/ppermute | solution.py:62
  15.4 6.5 %collective-permute-start.6 = (bf16[1,48,1024]{2,1,0:T(8,128)(2,1)}, bf16[1,48,1024]{2,1,0:T(8,128)(2,1)S(1)}, u32[]{:S(2)}, u32[]{:S(2)}) collective-permute-start(bf16[1,48,1024]{2,1,0:T(8,128)(2,1)} %param.3), channel_id=1, source_target_pairs={{0,28},{4,0},{8,4},{12,8},{16,12},{20,16},{24,20},{28,24},{1,29},{... | collective-permute-start | bytes 294920 | tf_op jit(solution)/shard_map/ppermute | solution.py:62
  22.8 8.0 %collective-permute-start.7 = (bf16[1,8,16,1024]{3,2,1,0:T(8,128)(2,1)S(1)}, bf16[1,8,16,1024]{3,2,1,0:T(8,128)(2,1)S(1)}, u32[]{:S(2)}, u32[]{:S(2)}) collective-permute-start(bf16[1,8,16,1024]{3,2,1,0:T(8,128)(2,1)S(1)} %get-tuple-element.12), channel_id=1, source_target_pairs={{0,2},{1,3},{2,0},{3,1},{4,6},{5,7},{6,4},{7,5},{8,10},{9,11},{10,... | collective-permute-start | bytes 786440 | tf_op jit(solution)/shard_map/ppermute | solution.py:12
  30.9 3.2 %collective-permute-start.8 = (bf16[2,8,16,1024]{3,2,1,0:T(8,128)(2,1)S(1)}, bf16[2,8,16,1024]{3,2,1,0:T(8,128)(2,1)S(1)}, u32[]{:S(2)}, u32[]{:S(2)}) collective-permute-start(bf16[2,8,16,1024]{3,2,1,0:T(8,128)(2,1)S(1)} %maximum_select_fusion.2), channel_id=1, source_target_pairs={{0,1},{1,0},{2,3},{3,2},{4,5},{5,4},{6,7},{7,6},{8,9},{9,8},{10,11... | collective-permute-start | bytes 1572872 | tf_op jit(solution)/shard_map/ppermute | solution.py:12
  76.0 4.6 %collective-permute-start.9 = (f32[4,256,2,256]{3,1,0,2:T(8,128)}, f32[4,256,2,256]{3,1,0,2:T(8,128)}, u32[]{:S(2)}, u32[]{:S(2)}) collective-permute-start(f32[4,256,2,256]{3,1,0,2:T(8,128)} %bitcast.40), channel_id=1, source_target_pairs={{0,1},{1,0},{2,3},{3,2},{4,5},{5,4},{6,7},{7,6},{8,9},{9,8},{10,11... | collective-permute-start | bytes 6291464 | tf_op jit(solution)/shard_map/ppermute | solution.py:12
  82.5 1.3 %copy-start = (f32[4,256,2,256]{3,1,0,2:T(8,128)}, f32[4,256,2,256]{3,1,0,2:T(8,128)S(1)}, u32[]{:S(2)}) copy-start(f32[4,256,2,256]{3,1,0,2:T(8,128)S(1)} %bitcast_add_fusion) | copy-start | bytes 6291460
  83.9 25.5 %collective-permute-start.10 = (f32[4,256,1,256]{3,1,0,2:T(8,128)S(1)}, f32[4,256,1,256]{3,1,0,2:T(8,128)S(1)}, u32[]{:S(2)}, u32[]{:S(2)}) collective-permute-start(f32[4,256,1,256]{3,1,0,2:T(8,128)S(1)} %constant_dynamic-slice_fusion), channel_id=1, source_target_pairs={{0,2},{1,3},{2,0},{3,1},{4,6},{5,7},{6,4},{7,5},{8,10},{9,11},{10,... | collective-permute-start | bytes 3145736 | tf_op jit(solution)/shard_map/ppermute | solution.py:12

commit v3 on v2

v3 whole, which is shorter than its diff:
```python
import jax
import jax.numpy as jnp
from jax import lax
from jax.sharding import PartitionSpec as P

NV = 16
NC = 32
PAIR_CHUNKS = 2


def swap(x, axis, bit):
    size = lax.axis_size(axis)
    return lax.ppermute(x, axis, [(i, i ^ bit) for i in range(size)])


def gather_col(mine):
    col_count = lax.axis_size("col")
    me = lax.axis_index("col")
    cur = mine[None]
    bit = col_count // 2
    while bit >= 1:
        got = swap(cur, "col", bit)
        low = (me & bit) == 0
        cur = jnp.where(low, jnp.stack([cur, got], 1), jnp.stack([got, cur], 1))
        cur = cur.reshape((-1,) + mine.shape)
        bit //= 2
    return cur


def scatter_sum_col(own_block, last_swap):
    col_count = lax.axis_size("col")
    acc = {}
    extra = None
    bit = 1
    while bit < col_count:
        deltas = [d for d in range(col_count) if d & bit and d % bit == 0]
        send = []
        for d in deltas:
            value = acc.pop(d) if d in acc else own_block(d)
            send.append(value)
        send = jnp.stack(send)
        if bit * 2 >= col_count:
            got, extra = last_swap(send, bit)
        else:
            got = swap(send, "col", bit)
        for i, d in enumerate(deltas):
            kept = d ^ bit
            base = acc.pop(kept) if kept in acc else own_block(kept)
            acc[kept] = base + got[i]
        bit *= 2
    return (acc[0] if 0 in acc else own_block(0)), extra


def screened_of(valence_a, valence_b, screening):
    chunk = valence_a.shape[0]
    valence_a = valence_a.astype(jnp.float32)
    valence_b = valence_b.astype(jnp.float32)
    val_pairs = (valence_a[:, :, None, :] * valence_b[:, None, :, :]).astype(jnp.bfloat16)
    val_pairs = val_pairs.reshape(chunk * NV * NV, valence_a.shape[2])
    screened = jnp.dot(val_pairs, screening, preferred_element_type=jnp.float32).astype(
        jnp.bfloat16
    )
    return screened.reshape(chunk, NV * NV, screening.shape[1])


def body(orbitals, screening, pairs_k):
    k_dev, orb_count, mu_cols = orbitals.shape
    group_count = lax.axis_size("pb")
    col_count = lax.axis_size("col")
    kpoint_count = k_dev * group_count
    group_index = lax.axis_index("pb")
    col_index = lax.axis_index("col")
    kpoint_a = pairs_k[0]
    kpoint_b = (kpoint_a - group_index) % kpoint_count
    pair_count = kpoint_a.shape[0]

    held = [orbitals]
    for s in range(1, group_count):
        held.append(
            lax.ppermute(orbitals, "pb", [(i, (i + s) % group_count) for i in range(group_count)])
        )
    held = jnp.concatenate(held, 0)

    def slot_of(k):
        return ((group_index - k // k_dev) % group_count) * k_dev + k % k_dev

    wanted = jnp.concatenate([slot_of(kpoint_a), slot_of(kpoint_b)])
    chosen = jnp.take(held, wanted, axis=0)

    valence = gather_col(chosen[:, :NV, :])
    valence = jnp.transpose(valence, (1, 2, 0, 3)).reshape(
        2 * pair_count, NV, col_count * mu_cols
    )
    conduction = chosen[:, NV:, :].astype(jnp.float32)
    rows_per_block = NC // col_count
    chunk = pair_count // PAIR_CHUNKS
    starts = list(range(0, pair_count, chunk))

    def valence_of(first):
        return valence[first : first + chunk], valence[pair_count + first : pair_count + first + chunk]

    results = []
    screened = screened_of(*valence_of(starts[0]), screening[0])
    for n_chunk, first in enumerate(starts):
        cond_a = conduction[first : first + chunk]
        cond_b = conduction[pair_count + first : pair_count + first + chunk]

        def own_block(delta, screened=screened, cond_a=cond_a, cond_b=cond_b):
            block = col_index ^ delta
            rows = lax.dynamic_slice_in_dim(cond_a, block * rows_per_block, rows_per_block, 1)
            cond_pairs = (rows[:, :, None, :] * cond_b[:, None, :, :]).astype(jnp.bfloat16)
            cond_pairs = cond_pairs.reshape(chunk, rows_per_block * NC, mu_cols)
            return jnp.einsum(
                "pan,pbn->pab", screened, cond_pairs, preferred_element_type=jnp.float32
            )

        def last_swap(send, bit):
            return swap(send, "col", bit), None

        summed, _ = scatter_sum_col(own_block, last_swap)
        results.append(summed)
        if n_chunk + 1 < len(starts):
            screened = screened_of(*valence_of(starts[n_chunk + 1]), screening[0])
    return jnp.concatenate(results, 0)[None]


def solution(mesh):
    placed = (P("pb", None, "col"), P("pb", None, "col"), P("pb", None))
    return jax.shard_map(
        body, mesh=mesh, in_specs=placed, out_specs=P("pb", None, None, "col"), check_vma=False
    )
```

time: 112 us -> 87.8 us (0.78)
  the two profiles are of different devices: /device:TPU:14 before, /device:TPU:16 now
where the time goes in v3:
time: 87.8 us; the launch traced here: 87.6 us
  waiting for transfers between devices  48.2 us (55%)
  starting transfers between devices  14.1 us (16%)
  matrix products  13.3 us (15%)
  other arithmetic  7.62 us (9%)
  local copies, waits for them, and re-layouts  4.11 us (5%)
    ppermute x6, waiting for transfers between devices, swap(): return lax.ppermute(x, axis, [(i, i ^ bit) for i in range(size)])  27.2 us
    ppermute x7, waiting for transfers between devices, body(): lax.ppermute(orbitals, 'pb', [(i, (i + s) % group_count) for i in range(g...  21 us
    ppermute x7, starting transfers between devices, body(): lax.ppermute(orbitals, 'pb', [(i, (i + s) % group_count) for i in range(g...  9.29 us
    dot_general x2, matrix products, screened_of(): jnp.dot(val_pairs, screening, preferred_element_type=jnp.float32)  9.01 us
    ppermute x6, starting transfers between devices, swap(): return lax.ppermute(x, axis, [(i, i ^ bit) for i in range(size)])  4.78 us
    dot_general x8, matrix products, own_block(): jnp.einsum('pan,pbn->pab', screened, cond_pairs, preferred_element_type=j...  4.25 us
    unnamed x11, local copies, waits for them, and re-layouts  3.14 us
    convert_element_type x1, other arithmetic, own_block(): (rows[:, :, None, :] * cond_b[:, None, :, :]).astype(jnp.bfloat16)  3.07 us
  transfers between devices with their start and end apart: 13, of which 7 were waited for; matrix products, arithmetic and copies ran while one was open for 9% of the time, Pallas kernels for 0%

profile of v3, /device:TPU:16, one launch (start us, length us, event | category | flops | bytes accessed | tf_op | source)
XLA Modules:
  0.0 87.6 jit_solution(9386343096257923123)
XLA Ops:
  0.5 4.4 %collective-permute-start.4 = (bf16[1,48,1024]{2,1,0:T(8,128)(2,1)}, bf16[1,48,1024]{2,1,0:T(8,128)(2,1)S(1)}, u32[]{:S(2)}, u32[]{:S(2)}) collective-permute-start(bf16[1,48,1024]{2,1,0:T(8,128)(2,1)} %param.3), channel_id=1, source_target_pairs={{0,20},{4,24},{8,28},{12,0},{16,4},{20,8},{24,12},{28,16},{1,21},{... | collective-permute-start | bytes 294920 | tf_op jit(solution)/shard_map/ppermute | solution.py:80
  4.9 2.0 %collective-permute-start.2 = (bf16[1,48,1024]{2,1,0:T(8,128)(2,1)}, bf16[1,48,1024]{2,1,0:T(8,128)(2,1)S(1)}, u32[]{:S(2)}, u32[]{:S(2)}) collective-permute-start(bf16[1,48,1024]{2,1,0:T(8,128)(2,1)} %param.3), channel_id=1, source_target_pairs={{0,12},{4,16},{8,20},{12,24},{16,28},{20,0},{24,4},{28,8},{1,13},{... | collective-permute-start | bytes 294920 | tf_op jit(solution)/shard_map/ppermute | solution.py:80
  6.9 2.4 %collective-permute-start = (bf16[1,48,1024]{2,1,0:T(8,128)(2,1)}, bf16[1,48,1024]{2,1,0:T(8,128)(2,1)S(1)}, u32[]{:S(2)}, u32[]{:S(2)}) collective-permute-start(bf16[1,48,1024]{2,1,0:T(8,128)(2,1)} %param.3), channel_id=1, source_target_pairs={{0,4},{4,8},{8,12},{12,16},{16,20},{20,24},{24,28},{28,0},{1,5},{5... | collective-permute-start | bytes 294920 | tf_op jit(solution)/shard_map/ppermute | solution.py:80
  9.3 0.9 %constant_dynamic-update-slice_fusion.7 = bf16[8,48,1024]{2,1,0:T(8,128)(2,1)S(1)} fusion(bf16[1,48,1024]{2,1,0:T(8,128)(2,1)} %param.3), kind=kLoop, calls=%fused_computation.54 | loop fusion | bytes 196608
  10.2 0.7 and_select_fusion.2
  11.1 9.2 %collective-permute-done = bf16[1,48,1024]{2,1,0:T(8,128)(2,1)S(1)} collective-permute-done((bf16[1,48,1024]{2,1,0:T(8,128)(2,1)}, bf16[1,48,1024]{2,1,0:T(8,128)(2,1)S(1)}, u32[]{:S(2)}, u32[]{:S(2)}) %collective-permute-start) | collective-permute-done | bytes 98336 | tf_op jit(solution)/shard_map/ppermute | solution.py:80
  20.3 7.0 %collective-permute-done.1 = bf16[1,48,1024]{2,1,0:T(8,128)(2,1)S(1)} collective-permute-done((bf16[1,48,1024]{2,1,0:T(8,128)(2,1)}, bf16[1,48,1024]{2,1,0:T(8,128)(2,1)S(1)}, u32[]{:S(2)}, u32[]{:S(2)}) %collective-permute-start.1) | collective-permute-done | bytes 98336 | tf_op jit(solution)/shard_map/ppermute | solution.py:80
  27.5 4.7 %collective-permute-done.6 = bf16[1,48,1024]{2,1,0:T(8,128)(2,1)S(1)} collective-permute-done((bf16[1,48,1024]{2,1,0:T(8,128)(2,1)}, bf16[1,48,1024]{2,1,0:T(8,128)(2,1)S(1)}, u32[]{:S(2)}, u32[]{:S(2)}) %collective-permute-start.6) | collective-permute-done | bytes 98336 | tf_op jit(solution)/shard_map/ppermute | solution.py:80
  32.2 0.6 gather_fusion
  33.1 1.6 %collective-permute-start.7 = (bf16[1,8,16,1024]{3,2,1,0:T(8,128)(2,1)S(1)}, bf16[1,8,16,1024]{3,2,1,0:T(8,128)(2,1)S(1)}, u32[]{:S(2)}, u32[]{:S(2)}) collective-permute-start(bf16[1,8,16,1024]{3,2,1,0:T(8,128)(2,1)S(1)} %get-tuple-element.14), channel_id=1, source_target_pairs={{0,2},{1,3},{2,0},{3,1},{4,6},{5,7},{6,4},{7,5},{8,10},{9,11},{10,... | collective-permute-start | bytes 786440 | tf_op jit(solution)/shard_map/ppermute | solution.py:13
  34.8 4.7 %collective-permute-done.7 = bf16[1,8,16,1024]{3,2,1,0:T(8,128)(2,1)S(1)} collective-permute-done((bf16[1,8,16,1024]{3,2,1,0:T(8,128)(2,1)S(1)}, bf16[1,8,16,1024]{3,2,1,0:T(8,128)(2,1)S(1)}, u32[]{:S(2)}, u32[]{:S(2)}) %collective-permute-start.7) | collective-permute-done | bytes 262176 | tf_op jit(solution)/shard_map/ppermute | solution.py:13
  39.7 3.1 %multiply_convert_fusion.2 = (bf16[2,8,32,1024]{3,2,1,0:T(8,128)(2,1)S(1)}, bf16[2,8,32,1024]{3,2,1,0:T(8,128)(2,1)S(1)}, bf16[2,8,32,1024]{3,2,1,0:T(8,128)(2,1...) fusion(f32[2,8,1024]{2,1,0:T(8,128)S(1)} %get-tuple-element.27,, ...), kind=kLoop, calls=%fused_computation.7 | loop fusion | flops 8388608 | bytes 9437184 | tf_op jit(solution)/shard_map/convert_element_type | solution.py:111
  43.5 0.7 multiply_convert_fusion.1
  44.2 0.7 slice-done
  45.0 1.4 %slice-done.1 = s8[4194304]{0:T(1024)(128)(4,1)S(1)} async-done(((s8[8388608]{0:T(1024)(128)(4,1)}), s8[4194304]{0:T(1024)(128)(4,1)S(1)}, s32[]{:S(2)}) %slice-start.1) | async-done | bytes 4194328
  46.4 4.5 %fusion.4 = bf16[512,1024]{1,0:T(8,128)(2,1)S(1)} fusion(bf16[512,4096]{1,0:T(8,128)(2,1)S(1)} %bitcast.121, bf16[1,4096,1024]{2,1,0:T(8,128)(2,1)S(1)} %bitcast.138), kind=kOutput, calls=%fused_computation.15 | convolution fusion | flops 4295491584 | bytes 13631488 | tf_op jit(solution)/shard_map/dot_general | solution.py:60
  50.9 0.7 multiply_convert_fusion
  51.6 4.5 %fusion.7 = bf16[512,1024]{1,0:T(8,128)(2,1)S(1)} fusion(bf16[512,4096]{1,0:T(8,128)(2,1)S(1)} %bitcast.122, bf16[1,4096,1024]{2,1,0:T(8,128)(2,1)S(1)} %bitcast.138), kind=kOutput, calls=%fused_computation.16 | convolution fusion | flops 4295491584 | bytes 13631488 | tf_op jit(solution)/shard_map/dot_general | solution.py:60
  56.1 0.6 convolution_bitcast_fusion.2
  56.7 0.7 convolution_bitcast_fusion.3
  57.5 0.6 collective-permute-start.9
  58.1 0.5 convolution_bitcast_fusion.1
  58.5 0.5 convolution_bitcast_fusion
  59.7 0.7 collective-permute-done.9
  60.4 0.6 fusion.15
  60.9 1.6 %collective-permute-start.10 = (f32[1,2,256,256]{3,2,1,0:T(8,128)S(1)}, f32[1,2,256,256]{3,2,1,0:T(8,128)S(1)}, u32[]{:S(2)}, u32[]{:S(2)}) collective-permute-start(f32[1,2,256,256]{3,2,1,0:T(8,128)S(1)} %fusion.15), channel_id=1, source_target_pairs={{0,2},{1,3},{2,0},{3,1},{4,6},{5,7},{6,4},{7,5},{8,10},{9,11},{10,... | collective-permute-start | bytes 1572872 | tf_op jit(solution)/shard_map/ppermute | solution.py:13
  62.5 0.5 fusion.11
  63.0 0.9 %collective-permute-start.12 = (f32[1,2,256,256]{3,2,1,0:T(8,128)S(1)}, f32[1,2,256,256]{3,2,1,0:T(8,128)S(1)}, u32[]{:S(2)}, u32[]{:S(2)}) collective-permute-start(f32[1,2,256,256]{3,2,1,0:T(8,128)S(1)} %fusion.11), channel_id=1, source_target_pairs={{0,2},{1,3},{2,0},{3,1},{4,6},{5,7},{6,4},{7,5},{8,10},{9,11},{10,... | collective-permute-start | bytes 1572872 | tf_op jit(solution)/shard_map/ppermute | solution.py:13
  63.9 0.6 fusion.24
  64.5 11.3 %collective-permute-done.10 = f32[1,2,256,256]{3,2,1,0:T(8,128)S(1)} collective-permute-done((f32[1,2,256,256]{3,2,1,0:T(8,128)S(1)}, f32[1,2,256,256]{3,2,1,0:T(8,128)S(1)}, u32[]{:S(2)}, u32[]{:S(2)}) %collective-permute-start.10) | collective-permute-done | bytes 524320 | tf_op jit(solution)/shard_map/ppermute | solution.py:13
  75.9 10.5 %collective-permute-done.12 = f32[1,2,256,256]{3,2,1,0:T(8,128)S(1)} collective-permute-done((f32[1,2,256,256]{3,2,1,0:T(8,128)S(1)}, f32[1,2,256,256]{3,2,1,0:T(8,128)S(1)}, u32[]{:S(2)}, u32[]{:S(2)}) %collective-permute-start.12) | collective-permute-done | bytes 524320 | tf_op jit(solution)/shard_map/ppermute | solution.py:13
  86.6 1.0 %maximum_bitcast_fusion = f32[1,4,256,256]{3,2,1,0:T(8,128)} fusion(f32[2,256,256]{2,1,0:T(8,128)S(1)} %fusion.13, f32[2,256,256]{2,1,0:T(8,128)S(1)} %fusion.17), kind=kLoop, calls=%fused_computation.24 | loop fusion | flops 262144 | bytes 2097152 | tf_op jit(solution)/shard_map/broadcast_in_dim | solution.py:124
  (44 shorter events, 2.9 us)
Async XLA Ops:
  0.0 27.4 %collective-permute-start.5 = (bf16[1,48,1024]{2,1,0:T(8,128)(2,1)}, bf16[1,48,1024]{2,1,0:T(8,128)(2,1)S(1)}, u32[]{:S(2)}, u32[]{:S(2)}) collective-permute-start(bf16[1,48,1024]{2,1,0:T(8,128)(2,1)} %param.3), channel_id=1, source_target_pairs={{0,24},{4,28},{8,0},{12,4},{16,8},{20,12},{24,16},{28,20},{1,25},{... | collective-permute-start | bytes 294920 | tf_op jit(solution)/shard_map/ppermute | solution.py:80
  0.5 27.0 %collective-permute-start.4 = (bf16[1,48,1024]{2,1,0:T(8,128)(2,1)}, bf16[1,48,1024]{2,1,0:T(8,128)(2,1)S(1)}, u32[]{:S(2)}, u32[]{:S(2)}) collective-permute-start(bf16[1,48,1024]{2,1,0:T(8,128)(2,1)} %param.3), channel_id=1, source_target_pairs={{0,20},{4,24},{8,28},{12,0},{16,4},{20,8},{24,12},{28,16},{1,21},{... | collective-permute-start | bytes 294920 | tf_op jit(solution)/shard_map/ppermute | solution.py:80
  4.9 22.5 %collective-permute-start.3 = (bf16[1,48,1024]{2,1,0:T(8,128)(2,1)}, bf16[1,48,1024]{2,1,0:T(8,128)(2,1)S(1)}, u32[]{:S(2)}, u32[]{:S(2)}) collective-permute-start(bf16[1,48,1024]{2,1,0:T(8,128)(2,1)} %param.3), channel_id=1, source_target_pairs={{0,16},{4,20},{8,24},{12,28},{16,0},{20,4},{24,8},{28,12},{1,17},{... | collective-permute-start | bytes 294920 | tf_op jit(solution)/shard_map/ppermute | solution.py:80
  4.9 22.5 %collective-permute-start.2 = (bf16[1,48,1024]{2,1,0:T(8,128)(2,1)}, bf16[1,48,1024]{2,1,0:T(8,128)(2,1)S(1)}, u32[]{:S(2)}, u32[]{:S(2)}) collective-permute-start(bf16[1,48,1024]{2,1,0:T(8,128)(2,1)} %param.3), channel_id=1, source_target_pairs={{0,12},{4,16},{8,20},{12,24},{16,28},{20,0},{24,4},{28,8},{1,13},{... | collective-permute-start | bytes 294920 | tf_op jit(solution)/shard_map/ppermute | solution.py:80
  6.9 13.4 %collective-permute-start = (bf16[1,48,1024]{2,1,0:T(8,128)(2,1)}, bf16[1,48,1024]{2,1,0:T(8,128)(2,1)S(1)}, u32[]{:S(2)}, u32[]{:S(2)}) collective-permute-start(bf16[1,48,1024]{2,1,0:T(8,128)(2,1)} %param.3), channel_id=1, source_target_pairs={{0,4},{4,8},{8,12},{12,16},{16,20},{20,24},{24,28},{28,0},{1,5},{5... | collective-permute-start | bytes 294920 | tf_op jit(solution)/shard_map/ppermute | solution.py:80
  20.3 7.0 %collective-permute-start.1 = (bf16[1,48,1024]{2,1,0:T(8,128)(2,1)}, bf16[1,48,1024]{2,1,0:T(8,128)(2,1)S(1)}, u32[]{:S(2)}, u32[]{:S(2)}) collective-permute-start(bf16[1,48,1024]{2,1,0:T(8,128)(2,1)} %param.3), channel_id=1, source_target_pairs={{0,8},{4,12},{8,16},{12,20},{16,24},{20,28},{24,0},{28,4},{1,9},{5... | collective-permute-start | bytes 294920 | tf_op jit(solution)/shard_map/ppermute | solution.py:80
  27.3 4.8 %collective-permute-start.6 = (bf16[1,48,1024]{2,1,0:T(8,128)(2,1)}, bf16[1,48,1024]{2,1,0:T(8,128)(2,1)S(1)}, u32[]{:S(2)}, u32[]{:S(2)}) collective-permute-start(bf16[1,48,1024]{2,1,0:T(8,128)(2,1)} %param.3), channel_id=1, source_target_pairs={{0,28},{4,0},{8,4},{12,8},{16,12},{20,16},{24,20},{28,24},{1,29},{... | collective-permute-start | bytes 294920 | tf_op jit(solution)/shard_map/ppermute | solution.py:80
  33.1 6.4 %collective-permute-start.7 = (bf16[1,8,16,1024]{3,2,1,0:T(8,128)(2,1)S(1)}, bf16[1,8,16,1024]{3,2,1,0:T(8,128)(2,1)S(1)}, u32[]{:S(2)}, u32[]{:S(2)}) collective-permute-start(bf16[1,8,16,1024]{3,2,1,0:T(8,128)(2,1)S(1)} %get-tuple-element.14), channel_id=1, source_target_pairs={{0,2},{1,3},{2,0},{3,1},{4,6},{5,7},{6,4},{7,5},{8,10},{9,11},{10,... | collective-permute-start | bytes 786440 | tf_op jit(solution)/shard_map/ppermute | solution.py:13
  39.6 3.3 %collective-permute-start.8 = (bf16[2,8,16,1024]{3,2,1,0:T(8,128)(2,1)S(1)}, bf16[2,8,16,1024]{3,2,1,0:T(8,128)(2,1)S(1)}, u32[]{:S(2)}, u32[]{:S(2)}) collective-permute-start(bf16[2,8,16,1024]{3,2,1,0:T(8,128)(2,1)S(1)} %maximum_select_fusion.2), channel_id=1, source_target_pairs={{0,1},{1,0},{2,3},{3,2},{4,5},{5,4},{6,7},{7,6},{8,9},{9,8},{10,11... | collective-permute-start | bytes 1572872 | tf_op jit(solution)/shard_map/ppermute | solution.py:13
  42.8 2.2 %slice-start = ((s8[8388608]{0:T(1024)(128)(4,1)}), s8[4194304]{0:T(1024)(128)(4,1)S(1)}, s32[]{:S(2)}) async-start(s8[8388608]{0:T(1024)(128)(4,1)} %bitcast.137), calls=%async_computation | async-start | bytes 8388608
  43.3 3.0 %slice-start.1 = ((s8[8388608]{0:T(1024)(128)(4,1)}), s8[4194304]{0:T(1024)(128)(4,1)S(1)}, s32[]{:S(2)}) async-start(s8[8388608]{0:T(1024)(128)(4,1)} %bitcast.137), calls=%async_computation.1 | async-start | bytes 8388608
  57.5 2.8 %collective-permute-start.9 = (f32[2,2,256,256]{3,2,1,0:T(8,128)S(1)}, f32[2,2,256,256]{3,2,1,0:T(8,128)S(1)}, u32[]{:S(2)}, u32[]{:S(2)}) collective-permute-start(f32[2,2,256,256]{3,2,1,0:T(8,128)S(1)} %pad_maximum_fusion), channel_id=1, source_target_pairs={{0,1},{1,0},{2,3},{3,2},{4,5},{5,4},{6,7},{7,6},{8,9},{9,8},{10,11... | collective-permute-start | bytes 3145736 | tf_op jit(solution)/shard_map/ppermute | solution.py:13
  59.1 3.4 %collective-permute-start.11 = (f32[2,2,256,256]{3,2,1,0:T(8,128)S(1)}, f32[2,2,256,256]{3,2,1,0:T(8,128)S(1)}, u32[]{:S(2)}, u32[]{:S(2)}) collective-permute-start(f32[2,2,256,256]{3,2,1,0:T(8,128)S(1)} %pad_maximum_fusion.1), channel_id=1, source_target_pairs={{0,1},{1,0},{2,3},{3,2},{4,5},{5,4},{6,7},{7,6},{8,9},{9,8},{10,11... | collective-permute-start | bytes 3145736 | tf_op jit(solution)/shard_map/ppermute | solution.py:13
  60.9 14.8 %collective-permute-start.10 = (f32[1,2,256,256]{3,2,1,0:T(8,128)S(1)}, f32[1,2,256,256]{3,2,1,0:T(8,128)S(1)}, u32[]{:S(2)}, u32[]{:S(2)}) collective-permute-start(f32[1,2,256,256]{3,2,1,0:T(8,128)S(1)} %fusion.15), channel_id=1, source_target_pairs={{0,2},{1,3},{2,0},{3,1},{4,6},{5,7},{6,4},{7,5},{8,10},{9,11},{10,... | collective-permute-start | bytes 1572872 | tf_op jit(solution)/shard_map/ppermute | solution.py:13
  63.0 23.5 %collective-permute-start.12 = (f32[1,2,256,256]{3,2,1,0:T(8,128)S(1)}, f32[1,2,256,256]{3,2,1,0:T(8,128)S(1)}, u32[]{:S(2)}, u32[]{:S(2)}) collective-permute-start(f32[1,2,256,256]{3,2,1,0:T(8,128)S(1)} %fusion.11), channel_id=1, source_target_pairs={{0,2},{1,3},{2,0},{3,1},{4,6},{5,7},{6,4},{7,5},{8,10},{9,11},{10,... | collective-permute-start | bytes 1572872 | tf_op jit(solution)/shard_map/ppermute | solution.py:13

commit v4 on v3

--- a/solution.py
+++ b/solution.py
@@ -13,13 +13,13 @@
     return lax.ppermute(x, axis, [(i, i ^ bit) for i in range(size)])
 
 
-def gather_col(mine):
-    col_count = lax.axis_size("col")
-    me = lax.axis_index("col")
+def gather_axis(mine, axis):
+    count = lax.axis_size(axis)
+    me = lax.axis_index(axis)
     cur = mine[None]
-    bit = col_count // 2
+    bit = count // 2
     while bit >= 1:
-        got = swap(cur, "col", bit)
+        got = swap(cur, axis, bit)
         low = (me & bit) == 0
         cur = jnp.where(low, jnp.stack([cur, got], 1), jnp.stack([got, cur], 1))
         cur = cur.reshape((-1,) + mine.shape)
@@ -74,20 +74,11 @@
     kpoint_b = (kpoint_a - group_index) % kpoint_count
     pair_count = kpoint_a.shape[0]
 
-    held = [orbitals]
-    for s in range(1, group_count):
-        held.append(
-            lax.ppermute(orbitals, "pb", [(i, (i + s) % group_count) for i in range(group_count)])
-        )
-    held = jnp.concatenate(held, 0)
-
-    def slot_of(k):
-        return ((group_index - k // k_dev) % group_count) * k_dev + k % k_dev
-
-    wanted = jnp.concatenate([slot_of(kpoint_a), slot_of(kpoint_b)])
+    held = gather_axis(orbitals, "pb").reshape(kpoint_count, orb_count, mu_cols)
+    wanted = jnp.concatenate([kpoint_a, kpoint_b])
     chosen = jnp.take(held, wanted, axis=0)
 
-    valence = gather_col(chosen[:, :NV, :])
+    valence = gather_axis(chosen[:, :NV, :], "col")
     valence = jnp.transpose(valence, (1, 2, 0, 3)).reshape(
         2 * pair_count, NV, col_count * mu_cols
     )

time: 87.8 us -> 82.3 us (0.937)
  the two profiles are of different devices: /device:TPU:16 before, /device:TPU:0 now
where the time goes in v4:
time: 82.3 us; the launch traced here: 81.5 us
  waiting for transfers between devices  42 us (51%)
  matrix products  13.3 us (16%)
  other arithmetic  11.8 us (14%)
  starting transfers between devices  10.9 us (13%)
  local copies, waits for them, and re-layouts  3.24 us (4%)
    ppermute x9, waiting for transfers between devices, swap(): return lax.ppermute(x, axis, [(i, i ^ bit) for i in range(size)])  42 us
    ppermute x9, starting transfers between devices, swap(): return lax.ppermute(x, axis, [(i, i ^ bit) for i in range(size)])  10.9 us
    dot_general x2, matrix products, screened_of(): jnp.dot(val_pairs, screening, preferred_element_type=jnp.float32)  9.01 us
    dot_general x8, matrix products, own_block(): jnp.einsum('pan,pbn->pab', screened, cond_pairs, preferred_element_type=j...  4.26 us
    convert_element_type x1, other arithmetic, own_block(): (rows[:, :, None, :] * cond_b[:, None, :, :]).astype(jnp.bfloat16)  3.07 us
    select_n x7, other arithmetic, gather_axis(): cur = jnp.where(low, jnp.stack([cur, got], 1), jnp.stack([got, cur], 1))  2.49 us
    unnamed x4, local copies, waits for them, and re-layouts  2.12 us
  transfers between devices with their start and end apart: 9, of which 7 were waited for; matrix products, arithmetic and copies ran while one was open for 13% of the time, Pallas kernels for 0%

profile of v4, /device:TPU:0, one launch (start us, length us, event | category | flops | bytes accessed | tf_op | source)
XLA Modules:
  0.0 81.5 jit_solution(4411839782362804619)
XLA Ops:
  0.0 4.0 %collective-permute-start = (bf16[1,1,48,1024]{3,2,0,1:T(8,128)(2,1)}, bf16[1,1,48,1024]{3,2,0,1:T(8,128)(2,1)S(1)}, u32[]{:S(2)}, u32[]{:S(2)}) collective-permute-start(bf16[1,1,48,1024]{3,2,0,1:T(8,128)(2,1)} %bitcast.156), channel_id=1, source_target_pairs={{0,16},{4,20},{8,24},{12,28},{16,0},{20,4},{24,8},{28,12},{1,17},{... | collective-permute-start | bytes 294920 | tf_op jit(solution)/shard_map/ppermute | solution.py:13
  4.0 0.7 and_select_fusion
  4.7 4.4 %collective-permute-done = bf16[1,1,48,1024]{3,2,0,1:T(8,128)(2,1)S(1)} collective-permute-done((bf16[1,1,48,1024]{3,2,0,1:T(8,128)(2,1)}, bf16[1,1,48,1024]{3,2,0,1:T(8,128)(2,1)S(1)}, u32[]{:S(2)}, u32[]{:S(2)}) %collective-permute-start) | collective-permute-done | bytes 98336 | tf_op jit(solution)/shard_map/ppermute | solution.py:13
  9.1 1.0 %maximum_select_fusion.5 = bf16[2,1,48,1024]{3,2,0,1:T(8,128)(2,1)S(1)} fusion(bf16[1,1,48,1024]{3,2,0,1:T(8,128)(2,1)S(1)} %collective-permute-done, bf16[1,1,48,1024]{3,2,0,1:T(8,128)(2,1)} %bitcast.157, pred[]{:T(512)S(6)} %eq.21), kind=kLoop, calls=%fused_computation.52 | loop fusion | flops 294912 | bytes 393217 | tf_op jit(solution)/shard_map/jit(_where)/select_n | solution.py:24
  10.1 0.9 %collective-permute-start.1 = (bf16[2,1,48,1024]{3,2,0,1:T(8,128)(2,1)S(1)}, bf16[2,1,48,1024]{3,2,0,1:T(8,128)(2,1)S(1)}, u32[]{:S(2)}, u32[]{:S(2)}) collective-permute-start(bf16[2,1,48,1024]{3,2,0,1:T(8,128)(2,1)S(1)} %maximum_select_fusion.5), channel_id=1, source_target_pairs={{0,8},{4,12},{8,0},{12,4},{16,24},{20,28},{24,16},{28,20},{1,9},{5... | collective-permute-start | bytes 589832 | tf_op jit(solution)/shard_map/ppermute | solution.py:13
  11.0 0.7 compare_and_fusion
  11.8 1.0 %fusion.18 = bf16[2,1,1,48,1024]{4,3,1,0,2:T(8,128)(2,1)S(1)} fusion(bf16[1,1,1,48,1024]{4,3,2,1,0:T(8,128)(2,1)S(1)} %bitcast.159, bf16[1,1,1,48,1024]{4,3,2,1,0:T(8,128)(2,1)} %bitcast.158, pred[]{:T(512)S(6)} %eq.21), kind=kLoop, calls=%fused_computation.50 | loop fusion | flops 294912 | bytes 393217 | tf_op jit(solution)/shard_map/jit(_where)/select_n | solution.py:24
  12.8 3.5 %collective-permute-done.1 = bf16[2,1,48,1024]{3,2,0,1:T(8,128)(2,1)S(1)} collective-permute-done((bf16[2,1,48,1024]{3,2,0,1:T(8,128)(2,1)S(1)}, bf16[2,1,48,1024]{3,2,0,1:T(8,128)(2,1)S(1)}, u32[]{:S(2)}, u32[]{:S(2)}) %collective-permute-start.1) | collective-permute-done | bytes 196640 | tf_op jit(solution)/shard_map/ppermute | solution.py:13
  16.3 1.4 %collective-permute-start.2 = (bf16[4,1,48,1024]{3,2,0,1:T(8,128)(2,1)S(1)}, bf16[4,1,48,1024]{3,2,0,1:T(8,128)(2,1)S(1)}, u32[]{:S(2)}, u32[]{:S(2)}) collective-permute-start(bf16[4,1,48,1024]{3,2,0,1:T(8,128)(2,1)S(1)} %bitcast.151), channel_id=1, source_target_pairs={{0,4},{4,0},{8,12},{12,8},{16,20},{20,16},{24,28},{28,24},{1,5},{5... | collective-permute-start | bytes 1179656 | tf_op jit(solution)/shard_map/ppermute | solution.py:13
  17.7 0.7 fusion.42
  18.4 0.7 fusion.20
  19.2 6.6 %collective-permute-done.2 = bf16[4,1,48,1024]{3,2,0,1:T(8,128)(2,1)S(1)} collective-permute-done((bf16[4,1,48,1024]{3,2,0,1:T(8,128)(2,1)S(1)}, bf16[4,1,48,1024]{3,2,0,1:T(8,128)(2,1)S(1)}, u32[]{:S(2)}, u32[]{:S(2)}) %collective-permute-start.2) | collective-permute-done | bytes 393248 | tf_op jit(solution)/shard_map/ppermute | solution.py:13
  26.0 0.6 gather_fusion
  26.9 1.5 %collective-permute-start.3 = (bf16[1,8,16,1024]{3,2,1,0:T(8,128)(2,1)S(1)}, bf16[1,8,16,1024]{3,2,1,0:T(8,128)(2,1)S(1)}, u32[]{:S(2)}, u32[]{:S(2)}) collective-permute-start(bf16[1,8,16,1024]{3,2,1,0:T(8,128)(2,1)S(1)} %get-tuple-element.14), channel_id=1, source_target_pairs={{0,2},{1,3},{2,0},{3,1},{4,6},{5,7},{6,4},{7,5},{8,10},{9,11},{10,... | collective-permute-start | bytes 786440 | tf_op jit(solution)/shard_map/ppermute | solution.py:13
  28.5 4.8 %collective-permute-done.3 = bf16[1,8,16,1024]{3,2,1,0:T(8,128)(2,1)S(1)} collective-permute-done((bf16[1,8,16,1024]{3,2,1,0:T(8,128)(2,1)S(1)}, bf16[1,8,16,1024]{3,2,1,0:T(8,128)(2,1)S(1)}, u32[]{:S(2)}, u32[]{:S(2)}) %collective-permute-start.3) | collective-permute-done | bytes 262176 | tf_op jit(solution)/shard_map/ppermute | solution.py:13
  33.5 3.1 %multiply_convert_fusion.2 = (bf16[2,8,32,1024]{3,2,1,0:T(8,128)(2,1)S(1)}, bf16[2,8,32,1024]{3,2,1,0:T(8,128)(2,1)S(1)}, bf16[2,8,32,1024]{3,2,1,0:T(8,128)(2,1...) fusion(f32[2,8,1024]{2,1,0:T(8,128)S(1)} %get-tuple-element.27,, ...), kind=kLoop, calls=%fused_computation.7 | loop fusion | flops 8388608 | bytes 9437184 | tf_op jit(solution)/shard_map/convert_element_type | solution.py:102
  37.4 0.7 multiply_convert_fusion.1
  38.2 0.7 slice-done
  38.9 1.4 %slice-done.1 = s8[4194304]{0:T(1024)(128)(4,1)S(1)} async-done(((s8[8388608]{0:T(1024)(128)(4,1)}), s8[4194304]{0:T(1024)(128)(4,1)S(1)}, s32[]{:S(2)}) %slice-start.1) | async-done | bytes 4194328
  40.3 4.5 %fusion.4 = bf16[512,1024]{1,0:T(8,128)(2,1)S(1)} fusion(bf16[512,4096]{1,0:T(8,128)(2,1)S(1)} %bitcast.137, bf16[1,4096,1024]{2,1,0:T(8,128)(2,1)S(1)} %bitcast.162), kind=kOutput, calls=%fused_computation.15 | convolution fusion | flops 4295491584 | bytes 13631488 | tf_op jit(solution)/shard_map/dot_general | solution.py:60
  44.8 0.7 multiply_convert_fusion
  45.5 4.5 %fusion.7 = bf16[512,1024]{1,0:T(8,128)(2,1)S(1)} fusion(bf16[512,4096]{1,0:T(8,128)(2,1)S(1)} %bitcast.138, bf16[1,4096,1024]{2,1,0:T(8,128)(2,1)S(1)} %bitcast.162), kind=kOutput, calls=%fused_computation.16 | convolution fusion | flops 4295491584 | bytes 13631488 | tf_op jit(solution)/shard_map/dot_general | solution.py:60
  50.0 0.7 convolution_bitcast_fusion.2
  50.8 0.6 convolution_bitcast_fusion.3
  51.4 0.6 collective-permute-start.5
  53.6 0.7 collective-permute-done.5
  54.3 0.6 fusion.15
  54.8 1.5 %collective-permute-start.6 = (f32[1,2,256,256]{3,2,1,0:T(8,128)S(1)}, f32[1,2,256,256]{3,2,1,0:T(8,128)S(1)}, u32[]{:S(2)}, u32[]{:S(2)}) collective-permute-start(f32[1,2,256,256]{3,2,1,0:T(8,128)S(1)} %fusion.15), channel_id=1, source_target_pairs={{0,2},{1,3},{2,0},{3,1},{4,6},{5,7},{6,4},{7,5},{8,10},{9,11},{10,... | collective-permute-start | bytes 1572872 | tf_op jit(solution)/shard_map/ppermute | solution.py:13
  56.8 0.9 %collective-permute-start.8 = (f32[1,2,256,256]{3,2,1,0:T(8,128)S(1)}, f32[1,2,256,256]{3,2,1,0:T(8,128)S(1)}, u32[]{:S(2)}, u32[]{:S(2)}) collective-permute-start(f32[1,2,256,256]{3,2,1,0:T(8,128)S(1)} %fusion.11), channel_id=1, source_target_pairs={{0,2},{1,3},{2,0},{3,1},{4,6},{5,7},{6,4},{7,5},{8,10},{9,11},{10,... | collective-permute-start | bytes 1572872 | tf_op jit(solution)/shard_map/ppermute | solution.py:13
  58.3 11.4 %collective-permute-done.6 = f32[1,2,256,256]{3,2,1,0:T(8,128)S(1)} collective-permute-done((f32[1,2,256,256]{3,2,1,0:T(8,128)S(1)}, f32[1,2,256,256]{3,2,1,0:T(8,128)S(1)}, u32[]{:S(2)}, u32[]{:S(2)}) %collective-permute-start.6) | collective-permute-done | bytes 524320 | tf_op jit(solution)/shard_map/ppermute | solution.py:13
  69.8 10.5 %collective-permute-done.8 = f32[1,2,256,256]{3,2,1,0:T(8,128)S(1)} collective-permute-done((f32[1,2,256,256]{3,2,1,0:T(8,128)S(1)}, f32[1,2,256,256]{3,2,1,0:T(8,128)S(1)}, u32[]{:S(2)}, u32[]{:S(2)}) %collective-permute-start.8) | collective-permute-done | bytes 524320 | tf_op jit(solution)/shard_map/ppermute | solution.py:13
  80.5 1.0 %maximum_bitcast_fusion = f32[1,4,256,256]{3,2,1,0:T(8,128)} fusion(f32[2,256,256]{2,1,0:T(8,128)S(1)} %fusion.13, f32[2,256,256]{2,1,0:T(8,128)S(1)} %fusion.17), kind=kLoop, calls=%fused_computation.24 | loop fusion | flops 262144 | bytes 2097152 | tf_op jit(solution)/shard_map/broadcast_in_dim | solution.py:115
  (35 shorter events, 4.6 us)
Async XLA Ops:
  0.0 9.1 %collective-permute-start = (bf16[1,1,48,1024]{3,2,0,1:T(8,128)(2,1)}, bf16[1,1,48,1024]{3,2,0,1:T(8,128)(2,1)S(1)}, u32[]{:S(2)}, u32[]{:S(2)}) collective-permute-start(bf16[1,1,48,1024]{3,2,0,1:T(8,128)(2,1)} %bitcast.156), channel_id=1, source_target_pairs={{0,16},{4,20},{8,24},{12,28},{16,0},{20,4},{24,8},{28,12},{1,17},{... | collective-permute-start | bytes 294920 | tf_op jit(solution)/shard_map/ppermute | solution.py:13
  10.1 6.2 %collective-permute-start.1 = (bf16[2,1,48,1024]{3,2,0,1:T(8,128)(2,1)S(1)}, bf16[2,1,48,1024]{3,2,0,1:T(8,128)(2,1)S(1)}, u32[]{:S(2)}, u32[]{:S(2)}) collective-permute-start(bf16[2,1,48,1024]{3,2,0,1:T(8,128)(2,1)S(1)} %maximum_select_fusion.5), channel_id=1, source_target_pairs={{0,8},{4,12},{8,0},{12,4},{16,24},{20,28},{24,16},{28,20},{1,9},{5... | collective-permute-start | bytes 589832 | tf_op jit(solution)/shard_map/ppermute | solution.py:13
  16.3 9.4 %collective-permute-start.2 = (bf16[4,1,48,1024]{3,2,0,1:T(8,128)(2,1)S(1)}, bf16[4,1,48,1024]{3,2,0,1:T(8,128)(2,1)S(1)}, u32[]{:S(2)}, u32[]{:S(2)}) collective-permute-start(bf16[4,1,48,1024]{3,2,0,1:T(8,128)(2,1)S(1)} %bitcast.151), channel_id=1, source_target_pairs={{0,4},{4,0},{8,12},{12,8},{16,20},{20,16},{24,28},{28,24},{1,5},{5... | collective-permute-start | bytes 1179656 | tf_op jit(solution)/shard_map/ppermute | solution.py:13
  26.9 6.4 %collective-permute-start.3 = (bf16[1,8,16,1024]{3,2,1,0:T(8,128)(2,1)S(1)}, bf16[1,8,16,1024]{3,2,1,0:T(8,128)(2,1)S(1)}, u32[]{:S(2)}, u32[]{:S(2)}) collective-permute-start(bf16[1,8,16,1024]{3,2,1,0:T(8,128)(2,1)S(1)} %get-tuple-element.14), channel_id=1, source_target_pairs={{0,2},{1,3},{2,0},{3,1},{4,6},{5,7},{6,4},{7,5},{8,10},{9,11},{10,... | collective-permute-start | bytes 786440 | tf_op jit(solution)/shard_map/ppermute | solution.py:13
  33.4 3.2 %collective-permute-start.4 = (bf16[2,8,16,1024]{3,2,1,0:T(8,128)(2,1)S(1)}, bf16[2,8,16,1024]{3,2,1,0:T(8,128)(2,1)S(1)}, u32[]{:S(2)}, u32[]{:S(2)}) collective-permute-start(bf16[2,8,16,1024]{3,2,1,0:T(8,128)(2,1)S(1)} %maximum_select_fusion.3), channel_id=1, source_target_pairs={{0,1},{1,0},{2,3},{3,2},{4,5},{5,4},{6,7},{7,6},{8,9},{9,8},{10,11... | collective-permute-start | bytes 1572872 | tf_op jit(solution)/shard_map/ppermute | solution.py:13
  36.7 2.2 %slice-start = ((s8[8388608]{0:T(1024)(128)(4,1)}), s8[4194304]{0:T(1024)(128)(4,1)S(1)}, s32[]{:S(2)}) async-start(s8[8388608]{0:T(1024)(128)(4,1)} %bitcast.161), calls=%async_computation | async-start | bytes 8388608
  37.3 3.0 %slice-start.1 = ((s8[8388608]{0:T(1024)(128)(4,1)}), s8[4194304]{0:T(1024)(128)(4,1)S(1)}, s32[]{:S(2)}) async-start(s8[8388608]{0:T(1024)(128)(4,1)} %bitcast.161), calls=%async_computation.1 | async-start | bytes 8388608
  51.4 2.8 %collective-permute-start.5 = (f32[2,2,256,256]{3,2,1,0:T(8,128)S(1)}, f32[2,2,256,256]{3,2,1,0:T(8,128)S(1)}, u32[]{:S(2)}, u32[]{:S(2)}) collective-permute-start(f32[2,2,256,256]{3,2,1,0:T(8,128)S(1)} %pad_maximum_fusion), channel_id=1, source_target_pairs={{0,1},{1,0},{2,3},{3,2},{4,5},{5,4},{6,7},{7,6},{8,9},{9,8},{10,11... | collective-permute-start | bytes 3145736 | tf_op jit(solution)/shard_map/ppermute | solution.py:13
  53.0 3.3 %collective-permute-start.7 = (f32[2,2,256,256]{3,2,1,0:T(8,128)S(1)}, f32[2,2,256,256]{3,2,1,0:T(8,128)S(1)}, u32[]{:S(2)}, u32[]{:S(2)}) collective-permute-start(f32[2,2,256,256]{3,2,1,0:T(8,128)S(1)} %pad_maximum_fusion.1), channel_id=1, source_target_pairs={{0,1},{1,0},{2,3},{3,2},{4,5},{5,4},{6,7},{7,6},{8,9},{9,8},{10,11... | collective-permute-start | bytes 3145736 | tf_op jit(solution)/shard_map/ppermute | solution.py:13
  54.8 14.8 %collective-permute-start.6 = (f32[1,2,256,256]{3,2,1,0:T(8,128)S(1)}, f32[1,2,256,256]{3,2,1,0:T(8,128)S(1)}, u32[]{:S(2)}, u32[]{:S(2)}) collective-permute-start(f32[1,2,256,256]{3,2,1,0:T(8,128)S(1)} %fusion.15), channel_id=1, source_target_pairs={{0,2},{1,3},{2,0},{3,1},{4,6},{5,7},{6,4},{7,5},{8,10},{9,11},{10,... | collective-permute-start | bytes 1572872 | tf_op jit(solution)/shard_map/ppermute | solution.py:13
  56.8 23.6 %collective-permute-start.8 = (f32[1,2,256,256]{3,2,1,0:T(8,128)S(1)}, f32[1,2,256,256]{3,2,1,0:T(8,128)S(1)}, u32[]{:S(2)}, u32[]{:S(2)}) collective-permute-start(f32[1,2,256,256]{3,2,1,0:T(8,128)S(1)} %fusion.11), channel_id=1, source_target_pairs={{0,2},{1,3},{2,0},{3,1},{4,6},{5,7},{6,4},{7,5},{8,10},{9,11},{10,... | collective-permute-start | bytes 1572872 | tf_op jit(solution)/shard_map/ppermute | solution.py:13

commit v5 on v4

--- a/solution.py
+++ b/solution.py
@@ -106,7 +106,8 @@
             )
 
         def last_swap(send, bit):
-            return swap(send, "col", bit), None
+            got = swap(send.astype(jnp.bfloat16), "col", bit)
+            return got.astype(jnp.float32), None
 
         summed, _ = scatter_sum_col(own_block, last_swap)
         results.append(summed)

time: 82.3 us -> 71 us (0.86)
  waiting for transfers between devices: 42 us -> 31.1 us
    ppermute x9, waiting for transfers between devices: 42 us -> 31.1 us  [swap(): return lax.ppermute(x, axis, [(i, i ^ bit) for i in range(size)])]
  transfers between devices with their start and end apart: 9 -> 9, of which waited for: 7 -> 7; matrix products, arithmetic and copies ran while one was open for 13% -> 14% of each run, Pallas kernels for 0% -> 0%
where the time goes in v5:
time: 71 us; the launch traced here: 70.1 us
  waiting for transfers between devices  31.1 us (44%)
  matrix products  13 us (18%)
  other arithmetic  11.7 us (16%)
  starting transfers between devices  10.7 us (15%)
  local copies, waits for them, and re-layouts  3.25 us (5%)
    ppermute x9, waiting for transfers between devices, swap(): return lax.ppermute(x, axis, [(i, i ^ bit) for i in range(size)])  31.1 us
    ppermute x9, starting transfers between devices, swap(): return lax.ppermute(x, axis, [(i, i ^ bit) for i in range(size)])  10.7 us
    dot_general x2, matrix products, screened_of(): jnp.dot(val_pairs, screening, preferred_element_type=jnp.float32)  9.1 us
    dot_general x8, matrix products, own_block(): jnp.einsum('pan,pbn->pab', screened, cond_pairs, preferred_element_type=j...  3.93 us
    convert_element_type x1, other arithmetic, own_block(): (rows[:, :, None, :] * cond_b[:, None, :, :]).astype(jnp.bfloat16)  3.09 us
    select_n x7, other arithmetic, gather_axis(): cur = jnp.where(low, jnp.stack([cur, got], 1), jnp.stack([got, cur], 1))  2.49 us
    unnamed x4, local copies, waits for them, and re-layouts  2.13 us
    convert_element_type x2, other arithmetic, screened_of(): (valence_a[:, :, None, :] * valence_b[:, None, :, :]).astype(jnp.bfloat16)  1.44 us
  transfers between devices with their start and end apart: 9, of which 7 were waited for; matrix products, arithmetic and copies ran while one was open for 14% of the time, Pallas kernels for 0%

profile of v5, /device:TPU:0, one launch (start us, length us, event | category | flops | bytes accessed | tf_op | source)
XLA Modules:
  0.0 70.1 jit_solution(6820068656036752377)
XLA Ops:
  0.0 4.0 %collective-permute-start = (bf16[1,1,48,1024]{3,2,0,1:T(8,128)(2,1)}, bf16[1,1,48,1024]{3,2,0,1:T(8,128)(2,1)S(1)}, u32[]{:S(2)}, u32[]{:S(2)}) collective-permute-start(bf16[1,1,48,1024]{3,2,0,1:T(8,128)(2,1)} %bitcast.162), channel_id=1, source_target_pairs={{0,16},{4,20},{8,24},{12,28},{16,0},{20,4},{24,8},{28,12},{1,17},{... | collective-permute-start | bytes 294920 | tf_op jit(solution)/shard_map/ppermute | solution.py:13
  4.0 0.7 and_select_fusion
  4.7 4.4 %collective-permute-done = bf16[1,1,48,1024]{3,2,0,1:T(8,128)(2,1)S(1)} collective-permute-done((bf16[1,1,48,1024]{3,2,0,1:T(8,128)(2,1)}, bf16[1,1,48,1024]{3,2,0,1:T(8,128)(2,1)S(1)}, u32[]{:S(2)}, u32[]{:S(2)}) %collective-permute-start) | collective-permute-done | bytes 98336 | tf_op jit(solution)/shard_map/ppermute | solution.py:13
  9.1 1.0 %maximum_select_fusion.5 = bf16[2,1,48,1024]{3,2,0,1:T(8,128)(2,1)S(1)} fusion(bf16[1,1,48,1024]{3,2,0,1:T(8,128)(2,1)S(1)} %collective-permute-done, bf16[1,1,48,1024]{3,2,0,1:T(8,128)(2,1)} %bitcast.163, pred[]{:T(512)S(6)} %eq.21), kind=kLoop, calls=%fused_computation.54 | loop fusion | flops 294912 | bytes 393217 | tf_op jit(solution)/shard_map/jit(_where)/select_n | solution.py:24
  10.1 0.9 %collective-permute-start.1 = (bf16[2,1,48,1024]{3,2,0,1:T(8,128)(2,1)S(1)}, bf16[2,1,48,1024]{3,2,0,1:T(8,128)(2,1)S(1)}, u32[]{:S(2)}, u32[]{:S(2)}) collective-permute-start(bf16[2,1,48,1024]{3,2,0,1:T(8,128)(2,1)S(1)} %maximum_select_fusion.5), channel_id=1, source_target_pairs={{0,8},{4,12},{8,0},{12,4},{16,24},{20,28},{24,16},{28,20},{1,9},{5... | collective-permute-start | bytes 589832 | tf_op jit(solution)/shard_map/ppermute | solution.py:13
  11.0 0.7 %compare_and_fusion = pred[8]{0:T(512)(128)(4,1)S(1)} fusion(s32[4]{0:T(128)S(1)} %and_select_fusion, s32[4]{0:T(128)} %bitcast.169), kind=kLoop, calls=%fused_computation.68 | loop fusion | flops 56 | bytes 40 | tf_op jit(solution)/shard_map/jit(_take)/and | solution.py:79
  11.8 1.0 %fusion.20 = bf16[2,1,1,48,1024]{4,3,1,0,2:T(8,128)(2,1)S(1)} fusion(bf16[1,1,1,48,1024]{4,3,2,1,0:T(8,128)(2,1)S(1)} %bitcast.165, bf16[1,1,1,48,1024]{4,3,2,1,0:T(8,128)(2,1)} %bitcast.164, pred[]{:T(512)S(6)} %eq.21), kind=kLoop, calls=%fused_computation.52 | loop fusion | flops 294912 | bytes 393217 | tf_op jit(solution)/shard_map/jit(_where)/select_n | solution.py:24
  12.8 3.5 %collective-permute-done.1 = bf16[2,1,48,1024]{3,2,0,1:T(8,128)(2,1)S(1)} collective-permute-done((bf16[2,1,48,1024]{3,2,0,1:T(8,128)(2,1)S(1)}, bf16[2,1,48,1024]{3,2,0,1:T(8,128)(2,1)S(1)}, u32[]{:S(2)}, u32[]{:S(2)}) %collective-permute-start.1) | collective-permute-done | bytes 196640 | tf_op jit(solution)/shard_map/ppermute | solution.py:13
  16.3 1.4 %collective-permute-start.2 = (bf16[4,1,48,1024]{3,2,0,1:T(8,128)(2,1)S(1)}, bf16[4,1,48,1024]{3,2,0,1:T(8,128)(2,1)S(1)}, u32[]{:S(2)}, u32[]{:S(2)}) collective-permute-start(bf16[4,1,48,1024]{3,2,0,1:T(8,128)(2,1)S(1)} %bitcast.157), channel_id=1, source_target_pairs={{0,4},{4,0},{8,12},{12,8},{16,20},{20,16},{24,28},{28,24},{1,5},{5... | collective-permute-start | bytes 1179656 | tf_op jit(solution)/shard_map/ppermute | solution.py:13
  17.7 0.7 fusion.44
  18.4 0.7 %fusion.22 = s32[8]{0:T(128)S(1)} fusion(s32[4,1]{0,1:T(1,128)S(1)} %fusion.44, s32[4,1]{0,1:T(1,128)} %bitcast.170), kind=kLoop, calls=%fused_computation.71 | loop fusion | flops 32 | bytes 64 | tf_op jit(solution)/shard_map/jit(_take)/jit(_where)/select_n | solution.py:79
  19.2 6.6 %collective-permute-done.2 = bf16[4,1,48,1024]{3,2,0,1:T(8,128)(2,1)S(1)} collective-permute-done((bf16[4,1,48,1024]{3,2,0,1:T(8,128)(2,1)S(1)}, bf16[4,1,48,1024]{3,2,0,1:T(8,128)(2,1)S(1)}, u32[]{:S(2)}, u32[]{:S(2)}) %collective-permute-start.2) | collective-permute-done | bytes 393248 | tf_op jit(solution)/shard_map/ppermute | solution.py:13
  26.0 0.6 gather_fusion
  26.9 1.5 %collective-permute-start.3 = (bf16[1,8,16,1024]{3,2,1,0:T(8,128)(2,1)S(1)}, bf16[1,8,16,1024]{3,2,1,0:T(8,128)(2,1)S(1)}, u32[]{:S(2)}, u32[]{:S(2)}) collective-permute-start(bf16[1,8,16,1024]{3,2,1,0:T(8,128)(2,1)S(1)} %get-tuple-element.14), channel_id=1, source_target_pairs={{0,2},{1,3},{2,0},{3,1},{4,6},{5,7},{6,4},{7,5},{8,10},{9,11},{10,... | collective-permute-start | bytes 786440 | tf_op jit(solution)/shard_map/ppermute | solution.py:13
  28.5 4.8 %collective-permute-done.3 = bf16[1,8,16,1024]{3,2,1,0:T(8,128)(2,1)S(1)} collective-permute-done((bf16[1,8,16,1024]{3,2,1,0:T(8,128)(2,1)S(1)}, bf16[1,8,16,1024]{3,2,1,0:T(8,128)(2,1)S(1)}, u32[]{:S(2)}, u32[]{:S(2)}) %collective-permute-start.3) | collective-permute-done | bytes 262176 | tf_op jit(solution)/shard_map/ppermute | solution.py:13
  33.5 3.1 %multiply_convert_fusion.2 = (bf16[2,8,32,1024]{3,2,1,0:T(8,128)(2,1)S(1)}, bf16[2,8,32,1024]{3,2,1,0:T(8,128)(2,1)S(1)}, bf16[2,8,32,1024]{3,2,1,0:T(8,128)(2,1...) fusion(f32[2,8,1024]{2,1,0:T(8,128)S(1)} %get-tuple-element.27,, ...), kind=kLoop, calls=%fused_computation.7 | loop fusion | flops 8388608 | bytes 9437184 | tf_op jit(solution)/shard_map/convert_element_type | solution.py:102
  37.5 0.7 %multiply_convert_fusion.1 = bf16[2,16,16,4096]{3,2,1,0:T(8,128)(2,1)S(1)} fusion(f32[2,16,4096]{2,1,0:T(8,128)S(1)} %bitcast.156, f32[2,16,4096]{2,1,0:T(8,128)S(1)} %bitcast.155), kind=kLoop, calls=%fused_computation.6 | loop fusion | flops 4194304 | bytes 5242880 | tf_op jit(solution)/shard_map/convert_element_type | solution.py:58
  38.2 0.7 slice-done
  38.9 1.4 %slice-done.1 = s8[4194304]{0:T(1024)(128)(4,1)S(1)} async-done(((s8[8388608]{0:T(1024)(128)(4,1)}), s8[4194304]{0:T(1024)(128)(4,1)S(1)}, s32[]{:S(2)}) %slice-start.1) | async-done | bytes 4194328
  40.3 4.5 %fusion.4 = bf16[512,1024]{1,0:T(8,128)(2,1)S(1)} fusion(bf16[512,4096]{1,0:T(8,128)(2,1)S(1)} %bitcast.141, bf16[1,4096,1024]{2,1,0:T(8,128)(2,1)S(1)} %bitcast.168), kind=kOutput, calls=%fused_computation.15 | convolution fusion | flops 4295491584 | bytes 13631488 | tf_op jit(solution)/shard_map/dot_general | solution.py:60
  44.9 0.7 %multiply_convert_fusion = bf16[2,16,16,4096]{3,2,1,0:T(8,128)(2,1)S(1)} fusion(f32[2,16,4096]{2,1,0:T(8,128)S(1)} %bitcast.153, f32[2,16,4096]{2,1,0:T(8,128)S(1)} %bitcast.154), kind=kLoop, calls=%fused_computation.5 | loop fusion | flops 4194304 | bytes 5242880 | tf_op jit(solution)/shard_map/convert_element_type | solution.py:58
  45.6 4.6 %fusion.7 = bf16[512,1024]{1,0:T(8,128)(2,1)S(1)} fusion(bf16[512,4096]{1,0:T(8,128)(2,1)S(1)} %bitcast.142, bf16[1,4096,1024]{2,1,0:T(8,128)(2,1)S(1)} %bitcast.168), kind=kOutput, calls=%fused_computation.16 | convolution fusion | flops 4295491584 | bytes 13631488 | tf_op jit(solution)/shard_map/dot_general | solution.py:60
  50.2 0.6 convolution_bitcast_fusion.2
  51.4 0.6 collective-permute-start.5
  53.5 0.7 collective-permute-done.5
  54.2 0.5 fusion.18
  54.7 1.5 %collective-permute-start.6 = (bf16[1,2,256,256]{3,2,1,0:T(8,128)(2,1)S(1)}, bf16[1,2,256,256]{3,2,1,0:T(8,128)(2,1)S(1)}, u32[]{:S(2)}, u32[]{:S(2)}) collective-permute-start(bf16[1,2,256,256]{3,2,1,0:T(8,128)(2,1)S(1)} %fusion.18), channel_id=1, source_target_pairs={{0,2},{1,3},{2,0},{3,1},{4,6},{5,7},{6,4},{7,5},{8,10},{9,11},{10,... | collective-permute-start | bytes 786440 | tf_op jit(solution)/shard_map/ppermute | solution.py:13
  56.7 0.5 fusion.19
  57.2 0.7 %collective-permute-start.8 = (bf16[1,2,256,256]{3,2,1,0:T(8,128)(2,1)S(1)}, bf16[1,2,256,256]{3,2,1,0:T(8,128)(2,1)S(1)}, u32[]{:S(2)}, u32[]{:S(2)}) collective-permute-start(bf16[1,2,256,256]{3,2,1,0:T(8,128)(2,1)S(1)} %fusion.19), channel_id=1, source_target_pairs={{0,2},{1,3},{2,0},{3,1},{4,6},{5,7},{6,4},{7,5},{8,10},{9,11},{10,... | collective-permute-start | bytes 786440 | tf_op jit(solution)/shard_map/ppermute | solution.py:13
  57.9 6.1 %collective-permute-done.6 = bf16[1,2,256,256]{3,2,1,0:T(8,128)(2,1)S(1)} collective-permute-done((bf16[1,2,256,256]{3,2,1,0:T(8,128)(2,1)S(1)}, bf16[1,2,256,256]{3,2,1,0:T(8,128)(2,1)S(1)}, u32[]{:S(2)}, u32[]{:S(2)}) %collective-permute-start.6) | collective-permute-done | bytes 262176 | tf_op jit(solution)/shard_map/ppermute | solution.py:13
  64.0 4.9 %collective-permute-done.8 = bf16[1,2,256,256]{3,2,1,0:T(8,128)(2,1)S(1)} collective-permute-done((bf16[1,2,256,256]{3,2,1,0:T(8,128)(2,1)S(1)}, bf16[1,2,256,256]{3,2,1,0:T(8,128)(2,1)S(1)}, u32[]{:S(2)}, u32[]{:S(2)}) %collective-permute-start.8) | collective-permute-done | bytes 262176 | tf_op jit(solution)/shard_map/ppermute | solution.py:13
  69.1 1.0 %maximum_bitcast_fusion = f32[1,4,256,256]{3,2,1,0:T(8,128)} fusion(f32[2,256,256]{2,1,0:T(8,128)S(1)} %fusion.13, f32[2,256,256]{2,1,0:T(8,128)S(1)} %fusion.17), kind=kLoop, calls=%fused_computation.24 | loop fusion | flops 262144 | bytes 2097152 | tf_op jit(solution)/shard_map/broadcast_in_dim | solution.py:116
  (35 shorter events, 4.4 us)
Async XLA Ops:
  0.0 9.1 %collective-permute-start = (bf16[1,1,48,1024]{3,2,0,1:T(8,128)(2,1)}, bf16[1,1,48,1024]{3,2,0,1:T(8,128)(2,1)S(1)}, u32[]{:S(2)}, u32[]{:S(2)}) collective-permute-start(bf16[1,1,48,1024]{3,2,0,1:T(8,128)(2,1)} %bitcast.162), channel_id=1, source_target_pairs={{0,16},{4,20},{8,24},{12,28},{16,0},{20,4},{24,8},{28,12},{1,17},{... | collective-permute-start | bytes 294920 | tf_op jit(solution)/shard_map/ppermute | solution.py:13
  10.1 6.2 %collective-permute-start.1 = (bf16[2,1,48,1024]{3,2,0,1:T(8,128)(2,1)S(1)}, bf16[2,1,48,1024]{3,2,0,1:T(8,128)(2,1)S(1)}, u32[]{:S(2)}, u32[]{:S(2)}) collective-permute-start(bf16[2,1,48,1024]{3,2,0,1:T(8,128)(2,1)S(1)} %maximum_select_fusion.5), channel_id=1, source_target_pairs={{0,8},{4,12},{8,0},{12,4},{16,24},{20,28},{24,16},{28,20},{1,9},{5... | collective-permute-start | bytes 589832 | tf_op jit(solution)/shard_map/ppermute | solution.py:13
  16.3 9.4 %collective-permute-start.2 = (bf16[4,1,48,1024]{3,2,0,1:T(8,128)(2,1)S(1)}, bf16[4,1,48,1024]{3,2,0,1:T(8,128)(2,1)S(1)}, u32[]{:S(2)}, u32[]{:S(2)}) collective-permute-start(bf16[4,1,48,1024]{3,2,0,1:T(8,128)(2,1)S(1)} %bitcast.157), channel_id=1, source_target_pairs={{0,4},{4,0},{8,12},{12,8},{16,20},{20,16},{24,28},{28,24},{1,5},{5... | collective-permute-start | bytes 1179656 | tf_op jit(solution)/shard_map/ppermute | solution.py:13
  26.9 6.4 %collective-permute-start.3 = (bf16[1,8,16,1024]{3,2,1,0:T(8,128)(2,1)S(1)}, bf16[1,8,16,1024]{3,2,1,0:T(8,128)(2,1)S(1)}, u32[]{:S(2)}, u32[]{:S(2)}) collective-permute-start(bf16[1,8,16,1024]{3,2,1,0:T(8,128)(2,1)S(1)} %get-tuple-element.14), channel_id=1, source_target_pairs={{0,2},{1,3},{2,0},{3,1},{4,6},{5,7},{6,4},{7,5},{8,10},{9,11},{10,... | collective-permute-start | bytes 786440 | tf_op jit(solution)/shard_map/ppermute | solution.py:13
  33.4 3.3 %collective-permute-start.4 = (bf16[2,8,16,1024]{3,2,1,0:T(8,128)(2,1)S(1)}, bf16[2,8,16,1024]{3,2,1,0:T(8,128)(2,1)S(1)}, u32[]{:S(2)}, u32[]{:S(2)}) collective-permute-start(bf16[2,8,16,1024]{3,2,1,0:T(8,128)(2,1)S(1)} %maximum_select_fusion.3), channel_id=1, source_target_pairs={{0,1},{1,0},{2,3},{3,2},{4,5},{5,4},{6,7},{7,6},{8,9},{9,8},{10,11... | collective-permute-start | bytes 1572872 | tf_op jit(solution)/shard_map/ppermute | solution.py:13
  36.7 2.2 %slice-start = ((s8[8388608]{0:T(1024)(128)(4,1)}), s8[4194304]{0:T(1024)(128)(4,1)S(1)}, s32[]{:S(2)}) async-start(s8[8388608]{0:T(1024)(128)(4,1)} %bitcast.167), calls=%async_computation | async-start | bytes 8388608
  37.3 3.0 %slice-start.1 = ((s8[8388608]{0:T(1024)(128)(4,1)}), s8[4194304]{0:T(1024)(128)(4,1)S(1)}, s32[]{:S(2)}) async-start(s8[8388608]{0:T(1024)(128)(4,1)} %bitcast.167), calls=%async_computation.1 | async-start | bytes 8388608
  51.4 2.8 %collective-permute-start.5 = (f32[2,2,256,256]{3,2,1,0:T(8,128)S(1)}, f32[2,2,256,256]{3,2,1,0:T(8,128)S(1)}, u32[]{:S(2)}, u32[]{:S(2)}) collective-permute-start(f32[2,2,256,256]{3,2,1,0:T(8,128)S(1)} %pad_maximum_fusion), channel_id=1, source_target_pairs={{0,1},{1,0},{2,3},{3,2},{4,5},{5,4},{6,7},{7,6},{8,9},{9,8},{10,11... | collective-permute-start | bytes 3145736 | tf_op jit(solution)/shard_map/ppermute | solution.py:13
  53.0 3.7 %collective-permute-start.7 = (f32[2,2,256,256]{3,2,1,0:T(8,128)S(1)}, f32[2,2,256,256]{3,2,1,0:T(8,128)S(1)}, u32[]{:S(2)}, u32[]{:S(2)}) collective-permute-start(f32[2,2,256,256]{3,2,1,0:T(8,128)S(1)} %pad_maximum_fusion.1), channel_id=1, source_target_pairs={{0,1},{1,0},{2,3},{3,2},{4,5},{5,4},{6,7},{7,6},{8,9},{9,8},{10,11... | collective-permute-start | bytes 3145736 | tf_op jit(solution)/shard_map/ppermute | solution.py:13
  54.7 9.2 %collective-permute-start.6 = (bf16[1,2,256,256]{3,2,1,0:T(8,128)(2,1)S(1)}, bf16[1,2,256,256]{3,2,1,0:T(8,128)(2,1)S(1)}, u32[]{:S(2)}, u32[]{:S(2)}) collective-permute-start(bf16[1,2,256,256]{3,2,1,0:T(8,128)(2,1)S(1)} %fusion.18), channel_id=1, source_target_pairs={{0,2},{1,3},{2,0},{3,1},{4,6},{5,7},{6,4},{7,5},{8,10},{9,11},{10,... | collective-permute-start | bytes 786440 | tf_op jit(solution)/shard_map/ppermute | solution.py:13
  57.2 11.8 %collective-permute-start.8 = (bf16[1,2,256,256]{3,2,1,0:T(8,128)(2,1)S(1)}, bf16[1,2,256,256]{3,2,1,0:T(8,128)(2,1)S(1)}, u32[]{:S(2)}, u32[]{:S(2)}) collective-permute-start(bf16[1,2,256,256]{3,2,1,0:T(8,128)(2,1)S(1)} %fusion.19), channel_id=1, source_target_pairs={{0,2},{1,3},{2,0},{3,1},{4,6},{5,7},{6,4},{7,5},{8,10},{9,11},{10,... | collective-permute-start | bytes 786440 | tf_op jit(solution)/shard_map/ppermute | solution.py:13

commit v6 on v4

--- a/solution.py
+++ b/solution.py
@@ -105,13 +105,20 @@
                 "pan,pbn->pab", screened, cond_pairs, preferred_element_type=jnp.float32
             )
 
-        def last_swap(send, bit):
-            return swap(send, "col", bit), None
+        following = valence_of(starts[n_chunk + 1]) if n_chunk + 1 < len(starts) else None
 
-        summed, _ = scatter_sum_col(own_block, last_swap)
+        def last_swap(send, bit, following=following):
+            send = send.astype(jnp.bfloat16)
+            if following is None:
+                return swap(send, "col", bit).astype(jnp.float32), None
+            send, following = lax.optimization_barrier((send, following))
+            got = swap(send, "col", bit)
+            screened_next = screened_of(*following, screening[0])
+            got, screened_next = lax.optimization_barrier((got, screened_next))
+            return got.astype(jnp.float32), screened_next
+
+        summed, screened = scatter_sum_col(own_block, last_swap)
         results.append(summed)
-        if n_chunk + 1 < len(starts):
-            screened = screened_of(*valence_of(starts[n_chunk + 1]), screening[0])
     return jnp.concatenate(results, 0)[None]
 
 

time: 82.3 us -> 72.7 us (0.88)
  waiting for transfers between devices: 42 us -> 32.3 us
    ppermute x9, waiting for transfers between devices: 42 us -> 32.3 us  [swap(): return lax.ppermute(x, axis, [(i, i ^ bit) for i in range(size)])]
  transfers between devices with their start and end apart: 9 -> 9, of which waited for: 7 -> 8; matrix products, arithmetic and copies ran while one was open for 13% -> 18% of each run, Pallas kernels for 0% -> 0%
where the time goes in v6:
time: 72.7 us; the launch traced here: 71.9 us
  waiting for transfers between devices  32.3 us (44%)
  matrix products  13.1 us (18%)
  other arithmetic  11.6 us (16%)
  starting transfers between devices  11.4 us (16%)
  local copies, waits for them, and re-layouts  3.26 us (4%)
    ppermute x9, waiting for transfers between devices, swap(): return lax.ppermute(x, axis, [(i, i ^ bit) for i in range(size)])  32.3 us
    ppermute x9, starting transfers between devices, swap(): return lax.ppermute(x, axis, [(i, i ^ bit) for i in range(size)])  11.4 us
    dot_general x2, matrix products, screened_of(): jnp.dot(val_pairs, screening, preferred_element_type=jnp.float32)  9.3 us
    dot_general x8, matrix products, own_block(): jnp.einsum('pan,pbn->pab', screened, cond_pairs, preferred_element_type=j...  3.75 us
    convert_element_type x1, other arithmetic, own_block(): (rows[:, :, None, :] * cond_b[:, None, :, :]).astype(jnp.bfloat16)  3.08 us
    select_n x7, other arithmetic, gather_axis(): cur = jnp.where(low, jnp.stack([cur, got], 1), jnp.stack([got, cur], 1))  2.49 us
    unnamed x4, local copies, waits for them, and re-layouts  2.19 us
  transfers between devices with their start and end apart: 9, of which 8 were waited for; matrix products, arithmetic and copies ran while one was open for 18% of the time, Pallas kernels for 0%

profile of v6, /device:TPU:0, one launch (start us, length us, event | category | flops | bytes accessed | tf_op | source)
XLA Modules:
  0.0 71.9 jit_solution(9068856549125103711)
XLA Ops:
  0.0 4.0 %collective-permute-start = (bf16[1,1,48,1024]{3,2,0,1:T(8,128)(2,1)}, bf16[1,1,48,1024]{3,2,0,1:T(8,128)(2,1)S(1)}, u32[]{:S(2)}, u32[]{:S(2)}) collective-permute-start(bf16[1,1,48,1024]{3,2,0,1:T(8,128)(2,1)} %bitcast.156), channel_id=1, source_target_pairs={{0,16},{4,20},{8,24},{12,28},{16,0},{20,4},{24,8},{28,12},{1,17},{... | collective-permute-start | bytes 294920 | tf_op jit(solution)/shard_map/ppermute | solution.py:13
  4.0 0.7 and_select_fusion
  4.7 4.4 %collective-permute-done = bf16[1,1,48,1024]{3,2,0,1:T(8,128)(2,1)S(1)} collective-permute-done((bf16[1,1,48,1024]{3,2,0,1:T(8,128)(2,1)}, bf16[1,1,48,1024]{3,2,0,1:T(8,128)(2,1)S(1)}, u32[]{:S(2)}, u32[]{:S(2)}) %collective-permute-start) | collective-permute-done | bytes 98336 | tf_op jit(solution)/shard_map/ppermute | solution.py:13
  9.1 1.0 %maximum_select_fusion.5 = bf16[2,1,48,1024]{3,2,0,1:T(8,128)(2,1)S(1)} fusion(bf16[1,1,48,1024]{3,2,0,1:T(8,128)(2,1)S(1)} %collective-permute-done, bf16[1,1,48,1024]{3,2,0,1:T(8,128)(2,1)} %bitcast.157, pred[]{:T(512)S(6)} %eq.21), kind=kLoop, calls=%fused_computation.54 | loop fusion | flops 294912 | bytes 393217 | tf_op jit(solution)/shard_map/jit(_where)/select_n | solution.py:24
  10.1 0.9 %collective-permute-start.1 = (bf16[2,1,48,1024]{3,2,0,1:T(8,128)(2,1)S(1)}, bf16[2,1,48,1024]{3,2,0,1:T(8,128)(2,1)S(1)}, u32[]{:S(2)}, u32[]{:S(2)}) collective-permute-start(bf16[2,1,48,1024]{3,2,0,1:T(8,128)(2,1)S(1)} %maximum_select_fusion.5), channel_id=1, source_target_pairs={{0,8},{4,12},{8,0},{12,4},{16,24},{20,28},{24,16},{28,20},{1,9},{5... | collective-permute-start | bytes 589832 | tf_op jit(solution)/shard_map/ppermute | solution.py:13
  11.0 0.7 %compare_and_fusion = pred[8]{0:T(512)(128)(4,1)S(1)} fusion(s32[4]{0:T(128)S(1)} %and_select_fusion, s32[4]{0:T(128)} %bitcast.163), kind=kLoop, calls=%fused_computation.68 | loop fusion | flops 56 | bytes 40 | tf_op jit(solution)/shard_map/jit(_take)/and | solution.py:79
  11.8 1.0 %fusion.18 = bf16[2,1,1,48,1024]{4,3,1,0,2:T(8,128)(2,1)S(1)} fusion(bf16[1,1,1,48,1024]{4,3,2,1,0:T(8,128)(2,1)S(1)} %bitcast.159, bf16[1,1,1,48,1024]{4,3,2,1,0:T(8,128)(2,1)} %bitcast.158, pred[]{:T(512)S(6)} %eq.21), kind=kLoop, calls=%fused_computation.52 | loop fusion | flops 294912 | bytes 393217 | tf_op jit(solution)/shard_map/jit(_where)/select_n | solution.py:24
  12.8 3.5 %collective-permute-done.1 = bf16[2,1,48,1024]{3,2,0,1:T(8,128)(2,1)S(1)} collective-permute-done((bf16[2,1,48,1024]{3,2,0,1:T(8,128)(2,1)S(1)}, bf16[2,1,48,1024]{3,2,0,1:T(8,128)(2,1)S(1)}, u32[]{:S(2)}, u32[]{:S(2)}) %collective-permute-start.1) | collective-permute-done | bytes 196640 | tf_op jit(solution)/shard_map/ppermute | solution.py:13
  16.3 1.4 %collective-permute-start.2 = (bf16[4,1,48,1024]{3,2,0,1:T(8,128)(2,1)S(1)}, bf16[4,1,48,1024]{3,2,0,1:T(8,128)(2,1)S(1)}, u32[]{:S(2)}, u32[]{:S(2)}) collective-permute-start(bf16[4,1,48,1024]{3,2,0,1:T(8,128)(2,1)S(1)} %bitcast.149), channel_id=1, source_target_pairs={{0,4},{4,0},{8,12},{12,8},{16,20},{20,16},{24,28},{28,24},{1,5},{5... | collective-permute-start | bytes 1179656 | tf_op jit(solution)/shard_map/ppermute | solution.py:13
  17.7 0.7 fusion.41
  18.4 0.7 %fusion.20 = s32[8]{0:T(128)S(1)} fusion(s32[4,1]{0,1:T(1,128)S(1)} %fusion.41, s32[4,1]{0,1:T(1,128)} %bitcast.164), kind=kLoop, calls=%fused_computation.71 | loop fusion | flops 32 | bytes 64 | tf_op jit(solution)/shard_map/jit(_take)/jit(_where)/select_n | solution.py:79
  19.2 6.6 %collective-permute-done.2 = bf16[4,1,48,1024]{3,2,0,1:T(8,128)(2,1)S(1)} collective-permute-done((bf16[4,1,48,1024]{3,2,0,1:T(8,128)(2,1)S(1)}, bf16[4,1,48,1024]{3,2,0,1:T(8,128)(2,1)S(1)}, u32[]{:S(2)}, u32[]{:S(2)}) %collective-permute-start.2) | collective-permute-done | bytes 393248 | tf_op jit(solution)/shard_map/ppermute | solution.py:13
  26.0 0.6 gather_fusion
  26.9 1.5 %collective-permute-start.3 = (bf16[1,8,16,1024]{3,2,1,0:T(8,128)(2,1)S(1)}, bf16[1,8,16,1024]{3,2,1,0:T(8,128)(2,1)S(1)}, u32[]{:S(2)}, u32[]{:S(2)}) collective-permute-start(bf16[1,8,16,1024]{3,2,1,0:T(8,128)(2,1)S(1)} %get-tuple-element.24), channel_id=1, source_target_pairs={{0,2},{1,3},{2,0},{3,1},{4,6},{5,7},{6,4},{7,5},{8,10},{9,11},{10,... | collective-permute-start | bytes 786440 | tf_op jit(solution)/shard_map/ppermute | solution.py:13
  28.5 4.8 %collective-permute-done.3 = bf16[1,8,16,1024]{3,2,1,0:T(8,128)(2,1)S(1)} collective-permute-done((bf16[1,8,16,1024]{3,2,1,0:T(8,128)(2,1)S(1)}, bf16[1,8,16,1024]{3,2,1,0:T(8,128)(2,1)S(1)}, u32[]{:S(2)}, u32[]{:S(2)}) %collective-permute-start.3) | collective-permute-done | bytes 262176 | tf_op jit(solution)/shard_map/ppermute | solution.py:13
  33.5 3.1 %multiply_convert_fusion.2 = (bf16[2,8,32,1024]{3,2,1,0:T(8,128)(2,1)S(1)}, bf16[2,8,32,1024]{3,2,1,0:T(8,128)(2,1)S(1)}, bf16[2,8,32,1024]{3,2,1,0:T(8,128)(2,1...) fusion(f32[2,8,1024]{2,1,0:T(8,128)S(1)} %get-tuple-element.37,, ...), kind=kLoop, calls=%fused_computation.7 | loop fusion | flops 8388608 | bytes 9437184 | tf_op jit(solution)/shard_map/convert_element_type | solution.py:102
  37.2 0.7 %multiply_convert_fusion.1 = bf16[2,16,16,4096]{3,2,1,0:T(8,128)(2,1)S(1)} fusion(f32[2,16,4096]{2,1,0:T(8,128)S(1)} %bitcast.147, f32[2,16,4096]{2,1,0:T(8,128)S(1)} %bitcast.148), kind=kLoop, calls=%fused_computation.6 | loop fusion | flops 4194304 | bytes 5242880 | tf_op jit(solution)/shard_map/convert_element_type | solution.py:58
  38.0 0.8 %slice-done = s8[4194304]{0:T(1024)(128)(4,1)S(1)} async-done(((s8[8388608]{0:T(1024)(128)(4,1)}), s8[4194304]{0:T(1024)(128)(4,1)S(1)}, s32[]{:S(2)}) %slice-start) | async-done | bytes 4194328
  38.8 1.4 %slice-done.1 = s8[4194304]{0:T(1024)(128)(4,1)S(1)} async-done(((s8[8388608]{0:T(1024)(128)(4,1)}), s8[4194304]{0:T(1024)(128)(4,1)S(1)}, s32[]{:S(2)}) %slice-start.1) | async-done | bytes 4194328
  40.1 4.6 %fusion.4 = bf16[512,1024]{1,0:T(8,128)(2,1)S(1)} fusion(bf16[512,4096]{1,0:T(8,128)(2,1)S(1)} %bitcast.135, bf16[1,4096,1024]{2,1,0:T(8,128)(2,1)S(1)} %bitcast.162), kind=kOutput, calls=%fused_computation.15 | convolution fusion | flops 4295491584 | bytes 13631488 | tf_op jit(solution)/shard_map/dot_general | solution.py:60
  44.7 0.5 convolution_bitcast_fusion.2
  45.8 0.6 collective-permute-start.5
  46.4 2.2 %collective-permute-done.5 = f32[2,2,256,256]{3,2,1,0:T(8,128)S(1)} collective-permute-done((f32[2,2,256,256]{3,2,1,0:T(8,128)S(1)}, f32[2,2,256,256]{3,2,1,0:T(8,128)S(1)}, u32[]{:S(2)}, u32[]{:S(2)}) %collective-permute-start.5) | collective-permute-done | bytes 1048608 | tf_op jit(solution)/shard_map/ppermute | solution.py:13
  49.1 1.5 %collective-permute-start.6 = (bf16[1,2,256,256]{3,2,1,0:T(8,128)(2,1)S(1)}, bf16[1,2,256,256]{3,2,1,0:T(8,128)(2,1)S(1)}, u32[]{:S(2)}, u32[]{:S(2)}) collective-permute-start(bf16[1,2,256,256]{3,2,1,0:T(8,128)(2,1)S(1)} %fusion.17), channel_id=1, source_target_pairs={{0,2},{1,3},{2,0},{3,1},{4,6},{5,7},{6,4},{7,5},{8,10},{9,11},{10,... | collective-permute-start | bytes 786440 | tf_op jit(solution)/shard_map/ppermute | solution.py:13
  50.6 0.7 %multiply_convert_fusion = bf16[2,16,16,4096]{3,2,1,0:T(8,128)(2,1)S(1)} fusion(f32[2,16,4096]{2,1,0:T(8,128)S(1)} %convert_element_type.150, f32[2,16,4096]{2,1,0:T(8,128)S(1)} %convert_element_type.149), kind=kLoop, calls=%fused_computation.5 | loop fusion | flops 4194304 | bytes 5242880 | tf_op jit(solution)/shard_map/convert_element_type | solution.py:58
  51.3 4.8 %fusion.7 = bf16[512,1024]{1,0:T(8,128)(2,1)S(1)} fusion(bf16[512,4096]{1,0:T(8,128)(2,1)S(1)} %bitcast.136, bf16[1,4096,1024]{2,1,0:T(8,128)(2,1)S(1)} %bitcast.162), kind=kOutput, calls=%fused_computation.16 | convolution fusion | flops 4295491584 | bytes 13631488 | tf_op jit(solution)/shard_map/dot_general | solution.py:60
  56.1 1.6 %collective-permute-done.6 = bf16[1,2,256,256]{3,2,1,0:T(8,128)(2,1)S(1)} collective-permute-done((bf16[1,2,256,256]{3,2,1,0:T(8,128)(2,1)S(1)}, bf16[1,2,256,256]{3,2,1,0:T(8,128)(2,1)S(1)}, u32[]{:S(2)}, u32[]{:S(2)}) %collective-permute-start.6) | collective-permute-done | bytes 262176 | tf_op jit(solution)/shard_map/ppermute | solution.py:13
  59.3 2.2 %collective-permute-done.7 = f32[2,2,256,256]{3,2,1,0:T(8,128)S(1)} collective-permute-done((f32[2,2,256,256]{3,2,1,0:T(8,128)S(1)}, f32[2,2,256,256]{3,2,1,0:T(8,128)S(1)}, u32[]{:S(2)}, u32[]{:S(2)}) %collective-permute-start.7) | collective-permute-done | bytes 1048608 | tf_op jit(solution)/shard_map/ppermute | solution.py:13
  62.0 1.5 %collective-permute-start.8 = (bf16[1,2,256,256]{3,2,1,0:T(8,128)(2,1)S(1)}, bf16[1,2,256,256]{3,2,1,0:T(8,128)(2,1)S(1)}, u32[]{:S(2)}, u32[]{:S(2)}) collective-permute-start(bf16[1,2,256,256]{3,2,1,0:T(8,128)(2,1)S(1)} %fusion.12), channel_id=1, source_target_pairs={{0,2},{1,3},{2,0},{3,1},{4,6},{5,7},{6,4},{7,5},{8,10},{9,11},{10,... | collective-permute-start | bytes 786440 | tf_op jit(solution)/shard_map/ppermute | solution.py:13
  63.5 6.8 %collective-permute-done.8 = bf16[1,2,256,256]{3,2,1,0:T(8,128)(2,1)S(1)} collective-permute-done((bf16[1,2,256,256]{3,2,1,0:T(8,128)(2,1)S(1)}, bf16[1,2,256,256]{3,2,1,0:T(8,128)(2,1)S(1)}, u32[]{:S(2)}, u32[]{:S(2)}) %collective-permute-start.8) | collective-permute-done | bytes 262176 | tf_op jit(solution)/shard_map/ppermute | solution.py:13
  70.4 0.5 fusion.10
  70.9 1.0 %maximum_bitcast_fusion = f32[1,4,256,256]{3,2,1,0:T(8,128)} fusion(f32[2,256,256]{2,1,0:T(8,128)S(1)} %fusion.10, f32[2,256,256]{2,1,0:T(8,128)S(1)} %fusion.16), kind=kLoop, calls=%fused_computation.29 | loop fusion | flops 262144 | bytes 2097152 | tf_op jit(solution)/shard_map/broadcast_in_dim | solution.py:122
  (36 shorter events, 4.7 us)
Async XLA Ops:
  0.0 9.1 %collective-permute-start = (bf16[1,1,48,1024]{3,2,0,1:T(8,128)(2,1)}, bf16[1,1,48,1024]{3,2,0,1:T(8,128)(2,1)S(1)}, u32[]{:S(2)}, u32[]{:S(2)}) collective-permute-start(bf16[1,1,48,1024]{3,2,0,1:T(8,128)(2,1)} %bitcast.156), channel_id=1, source_target_pairs={{0,16},{4,20},{8,24},{12,28},{16,0},{20,4},{24,8},{28,12},{1,17},{... | collective-permute-start | bytes 294920 | tf_op jit(solution)/shard_map/ppermute | solution.py:13
  10.1 6.2 %collective-permute-start.1 = (bf16[2,1,48,1024]{3,2,0,1:T(8,128)(2,1)S(1)}, bf16[2,1,48,1024]{3,2,0,1:T(8,128)(2,1)S(1)}, u32[]{:S(2)}, u32[]{:S(2)}) collective-permute-start(bf16[2,1,48,1024]{3,2,0,1:T(8,128)(2,1)S(1)} %maximum_select_fusion.5), channel_id=1, source_target_pairs={{0,8},{4,12},{8,0},{12,4},{16,24},{20,28},{24,16},{28,20},{1,9},{5... | collective-permute-start | bytes 589832 | tf_op jit(solution)/shard_map/ppermute | solution.py:13
  16.3 9.4 %collective-permute-start.2 = (bf16[4,1,48,1024]{3,2,0,1:T(8,128)(2,1)S(1)}, bf16[4,1,48,1024]{3,2,0,1:T(8,128)(2,1)S(1)}, u32[]{:S(2)}, u32[]{:S(2)}) collective-permute-start(bf16[4,1,48,1024]{3,2,0,1:T(8,128)(2,1)S(1)} %bitcast.149), channel_id=1, source_target_pairs={{0,4},{4,0},{8,12},{12,8},{16,20},{20,16},{24,28},{28,24},{1,5},{5... | collective-permute-start | bytes 1179656 | tf_op jit(solution)/shard_map/ppermute | solution.py:13
  26.9 6.4 %collective-permute-start.3 = (bf16[1,8,16,1024]{3,2,1,0:T(8,128)(2,1)S(1)}, bf16[1,8,16,1024]{3,2,1,0:T(8,128)(2,1)S(1)}, u32[]{:S(2)}, u32[]{:S(2)}) collective-permute-start(bf16[1,8,16,1024]{3,2,1,0:T(8,128)(2,1)S(1)} %get-tuple-element.24), channel_id=1, source_target_pairs={{0,2},{1,3},{2,0},{3,1},{4,6},{5,7},{6,4},{7,5},{8,10},{9,11},{10,... | collective-permute-start | bytes 786440 | tf_op jit(solution)/shard_map/ppermute | solution.py:13
  33.4 3.3 %collective-permute-start.4 = (bf16[2,8,16,1024]{3,2,1,0:T(8,128)(2,1)S(1)}, bf16[2,8,16,1024]{3,2,1,0:T(8,128)(2,1)S(1)}, u32[]{:S(2)}, u32[]{:S(2)}) collective-permute-start(bf16[2,8,16,1024]{3,2,1,0:T(8,128)(2,1)S(1)} %maximum_select_fusion.3), channel_id=1, source_target_pairs={{0,1},{1,0},{2,3},{3,2},{4,5},{5,4},{6,7},{7,6},{8,9},{9,8},{10,11... | collective-permute-start | bytes 1572872 | tf_op jit(solution)/shard_map/ppermute | solution.py:13
  36.6 2.2 %slice-start = ((s8[8388608]{0:T(1024)(128)(4,1)}), s8[4194304]{0:T(1024)(128)(4,1)S(1)}, s32[]{:S(2)}) async-start(s8[8388608]{0:T(1024)(128)(4,1)} %bitcast.161), calls=%async_computation | async-start | bytes 8388608
  37.0 3.2 %slice-start.1 = ((s8[8388608]{0:T(1024)(128)(4,1)}), s8[4194304]{0:T(1024)(128)(4,1)S(1)}, s32[]{:S(2)}) async-start(s8[8388608]{0:T(1024)(128)(4,1)} %bitcast.161), calls=%async_computation.1 | async-start | bytes 8388608
  45.8 2.8 %collective-permute-start.5 = (f32[2,2,256,256]{3,2,1,0:T(8,128)S(1)}, f32[2,2,256,256]{3,2,1,0:T(8,128)S(1)}, u32[]{:S(2)}, u32[]{:S(2)}) collective-permute-start(f32[2,2,256,256]{3,2,1,0:T(8,128)S(1)} %pad_maximum_fusion), channel_id=1, source_target_pairs={{0,1},{1,0},{2,3},{3,2},{4,5},{5,4},{6,7},{7,6},{8,9},{9,8},{10,11... | collective-permute-start | bytes 3145736 | tf_op jit(solution)/shard_map/ppermute | solution.py:13
  49.1 8.7 %collective-permute-start.6 = (bf16[1,2,256,256]{3,2,1,0:T(8,128)(2,1)S(1)}, bf16[1,2,256,256]{3,2,1,0:T(8,128)(2,1)S(1)}, u32[]{:S(2)}, u32[]{:S(2)}) collective-permute-start(bf16[1,2,256,256]{3,2,1,0:T(8,128)(2,1)S(1)} %fusion.17), channel_id=1, source_target_pairs={{0,2},{1,3},{2,0},{3,1},{4,6},{5,7},{6,4},{7,5},{8,10},{9,11},{10,... | collective-permute-start | bytes 786440 | tf_op jit(solution)/shard_map/ppermute | solution.py:13
  58.8 2.7 %collective-permute-start.7 = (f32[2,2,256,256]{3,2,1,0:T(8,128)S(1)}, f32[2,2,256,256]{3,2,1,0:T(8,128)S(1)}, u32[]{:S(2)}, u32[]{:S(2)}) collective-permute-start(f32[2,2,256,256]{3,2,1,0:T(8,128)S(1)} %pad_maximum_fusion.1), channel_id=1, source_target_pairs={{0,1},{1,0},{2,3},{3,2},{4,5},{5,4},{6,7},{7,6},{8,9},{9,8},{10,11... | collective-permute-start | bytes 3145736 | tf_op jit(solution)/shard_map/ppermute | solution.py:13
  62.0 8.4 %collective-permute-start.8 = (bf16[1,2,256,256]{3,2,1,0:T(8,128)(2,1)S(1)}, bf16[1,2,256,256]{3,2,1,0:T(8,128)(2,1)S(1)}, u32[]{:S(2)}, u32[]{:S(2)}) collective-permute-start(bf16[1,2,256,256]{3,2,1,0:T(8,128)(2,1)S(1)} %fusion.12), channel_id=1, source_target_pairs={{0,2},{1,3},{2,0},{3,1},{4,6},{5,7},{6,4},{7,5},{8,10},{9,11},{10,... | collective-permute-start | bytes 786440 | tf_op jit(solution)/shard_map/ppermute | solution.py:13

commit v7 on v5

--- a/solution.py
+++ b/solution.py
@@ -74,15 +74,17 @@
     kpoint_b = (kpoint_a - group_index) % kpoint_count
     pair_count = kpoint_a.shape[0]
 
-    held = gather_axis(orbitals, "pb").reshape(kpoint_count, orb_count, mu_cols)
     wanted = jnp.concatenate([kpoint_a, kpoint_b])
-    chosen = jnp.take(held, wanted, axis=0)
+    held_valence = gather_axis(orbitals[:, :NV, :], "pb").reshape(kpoint_count, NV, mu_cols)
+    held_conduction = gather_axis(orbitals[:, NV:, :], "pb").reshape(
+        kpoint_count, orb_count - NV, mu_cols
+    )
 
-    valence = gather_axis(chosen[:, :NV, :], "col")
+    valence = gather_axis(jnp.take(held_valence, wanted, axis=0), "col")
     valence = jnp.transpose(valence, (1, 2, 0, 3)).reshape(
         2 * pair_count, NV, col_count * mu_cols
     )
-    conduction = chosen[:, NV:, :].astype(jnp.float32)
+    conduction = jnp.take(held_conduction, wanted, axis=0).astype(jnp.float32)
     rows_per_block = NC // col_count
     chunk = pair_count // PAIR_CHUNKS
     starts = list(range(0, pair_count, chunk))

time: 71 us -> 78.7 us (1.11)
  waiting for transfers between devices: 31.1 us -> 19.1 us
  local copies, waits for them, and re-layouts: 3.25 us -> 13.3 us
  starting transfers between devices: 10.7 us -> 15.9 us
  matrix products: 13 us -> 15.7 us
  other arithmetic: 11.7 us -> 13.8 us
    ppermute x9 -> x12, waiting for transfers between devices: 31.1 us -> 19.1 us  [swap(): return lax.ppermute(x, axis, [(i, i ^ bit) for i in range(size)])]
    ppermute x9 -> x12, starting transfers between devices: 10.7 us -> 15.9 us  [swap(): return lax.ppermute(x, axis, [(i, i ^ bit) for i in range(size)])]
    convert_element_type x2, local copies, waits for them, and re-layouts: 0.09 us -> 4.44 us  [screened_of(): valence_a = valence_a.astype(jnp.float32)]
    convert_element_type x2, local copies, waits for them, and re-layouts: 0.08 us -> 4.42 us  [screened_of(): valence_b = valence_b.astype(jnp.float32)]
    dot_general x2, matrix products: 9.1 us -> 12 us  [screened_of(): jnp.dot(val_pairs, screening, preferred_element_type=jnp.float32)]
    select_n x7 -> x11, other arithmetic: 2.49 us -> 0.5 us  [gather_axis(): cur = jnp.where(low, jnp.stack([cur, got], 1), jnp.stack([got, cur], 1))]
    convert_element_type x1 -> x2, other arithmetic: 0.11 us -> 1.84 us  [the longest x1 1.71 us: screened_of(): valence_a = valence_a.astype(jnp.float32)]
    another operation x1 -> x2, local copies, waits for them, and re-layouts: 0.04 us -> 1.61 us  [gather_axis(): cur = jnp.where(low, jnp.stack([cur, got], 1), jnp.stack([got, cur], 1))]
  transfers between devices with their start and end apart: 9 -> 12, of which waited for: 7 -> 9; matrix products, arithmetic and copies ran while one was open for 14% -> 17% of each run, Pallas kernels for 0% -> 0%
where the time goes in v7:
time: 78.7 us; the launch traced here: 78.2 us
  waiting for transfers between devices  19.1 us (24%)
  starting transfers between devices  15.9 us (20%)
  matrix products  15.7 us (20%)
  other arithmetic  13.8 us (18%)
  local copies, waits for them, and re-layouts  13.3 us (17%)
    ppermute x12, waiting for transfers between devices, swap(): return lax.ppermute(x, axis, [(i, i ^ bit) for i in range(size)])  19.1 us
    ppermute x12, starting transfers between devices, swap(): return lax.ppermute(x, axis, [(i, i ^ bit) for i in range(size)])  15.9 us
    dot_general x2, matrix products, screened_of(): jnp.dot(val_pairs, screening, preferred_element_type=jnp.float32)  12 us
    convert_element_type x2, local copies, waits for them, and re-layouts, screened_of(): valence_a = valence_a.astype(jnp.float32)  4.44 us
    convert_element_type x2, local copies, waits for them, and re-layouts, screened_of(): valence_b = valence_b.astype(jnp.float32)  4.42 us
    convert_element_type x1, other arithmetic, own_block(): (rows[:, :, None, :] * cond_b[:, None, :, :]).astype(jnp.bfloat16)  4.34 us
    dot_general x8, matrix products, own_block(): jnp.einsum('pan,pbn->pab', screened, cond_pairs, preferred_element_type=j...  3.76 us
    convert_element_type x2, other arithmetic, screened_of(): (valence_a[:, :, None, :] * valence_b[:, None, :, :]).astype(jnp.bfloat16)  2.78 us
  transfers between devices with their start and end apart: 12, of which 9 were waited for; matrix products, arithmetic and copies ran while one was open for 17% of the time, Pallas kernels for 0%

profile of v7, /device:TPU:0, one launch (start us, length us, event | category | flops | bytes accessed | tf_op | source)
XLA Modules:
  0.0 78.2 jit_solution(14279391029219467287)
XLA Ops:
  0.0 0.8 slice_bitcast_fusion.7
  0.8 4.0 %collective-permute-start = (bf16[1,1,16,1024]{3,2,0,1:T(8,128)(2,1)S(1)}, bf16[1,1,16,1024]{3,2,0,1:T(8,128)(2,1)S(1)}, u32[]{:S(2)}, u32[]{:S(2)}) collective-permute-start(bf16[1,1,16,1024]{3,2,0,1:T(8,128)(2,1)S(1)} %get-tuple-element.32), channel_id=1, source_target_pairs={{0,16},{4,20},{8,24},{12,28},{16,0},{20,4},{24,8},{28,12},{1,17},{... | collective-permute-start | bytes 98312 | tf_op jit(solution)/shard_map/ppermute | solution.py:13
  4.8 0.8 %slice_bitcast_fusion.5 = (bf16[1,1,1,32,1024]{4,3,2,1,0:T(8,128)(2,1)S(1)}, bf16[1,1,32,1024]{3,2,0,1:T(8,128)(2,1)S(1)}) fusion(bf16[1,48,1024]{2,1,0:T(8,128)(2,1)} %param.3), kind=kLoop, calls=%fused_computation.62 | loop fusion | bytes 196608 | tf_op jit(solution)/shard_map/stack | solution.py:24
  5.7 0.7 fusion.46
  7.1 0.7 fusion.23
  7.8 0.7 compare_and_fusion
  8.6 2.0 %collective-permute-start.1 = (bf16[2,1,16,1024]{3,2,0,1:T(8,128)(2,1)S(1)}, bf16[2,1,16,1024]{3,2,0,1:T(8,128)(2,1)S(1)}, u32[]{:S(2)}, u32[]{:S(2)}) collective-permute-start(bf16[2,1,16,1024]{3,2,0,1:T(8,128)(2,1)S(1)} %maximum_select_fusion.8), channel_id=1, source_target_pairs={{0,8},{4,12},{8,0},{12,4},{16,24},{20,28},{24,16},{28,20},{1,9},{5... | collective-permute-start | bytes 196616 | tf_op jit(solution)/shard_map/ppermute | solution.py:13
  10.5 0.7 collective-permute-done.5
  11.2 1.3 %collective-permute-start.6 = (bf16[2,1,32,1024]{3,2,0,1:T(8,128)(2,1)S(1)}, bf16[2,1,32,1024]{3,2,0,1:T(8,128)(2,1)S(1)}, u32[]{:S(2)}, u32[]{:S(2)}) collective-permute-start(bf16[2,1,32,1024]{3,2,0,1:T(8,128)(2,1)S(1)} %maximum_select_fusion.7), channel_id=1, source_target_pairs={{0,8},{4,12},{8,0},{12,4},{16,24},{20,28},{24,16},{28,20},{1,9},{5... | collective-permute-start | bytes 393224 | tf_op jit(solution)/shard_map/ppermute | solution.py:13
  12.5 1.0 %collective-permute-done.1 = bf16[2,1,16,1024]{3,2,0,1:T(8,128)(2,1)S(1)} collective-permute-done((bf16[2,1,16,1024]{3,2,0,1:T(8,128)(2,1)S(1)}, bf16[2,1,16,1024]{3,2,0,1:T(8,128)(2,1)S(1)}, u32[]{:S(2)}, u32[]{:S(2)}) %collective-permute-start.1) | collective-permute-done | bytes 65568 | tf_op jit(solution)/shard_map/ppermute | solution.py:13
  13.6 1.9 %collective-permute-start.2 = (bf16[4,1,16,1024]{3,2,0,1:T(8,128)(2,1)S(1)}, bf16[4,1,16,1024]{3,2,0,1:T(8,128)(2,1)S(1)}, u32[]{:S(2)}, u32[]{:S(2)}) collective-permute-start(bf16[4,1,16,1024]{3,2,0,1:T(8,128)(2,1)S(1)} %bitcast.173), channel_id=1, source_target_pairs={{0,4},{4,0},{8,12},{12,8},{16,20},{20,16},{24,28},{28,24},{1,5},{5... | collective-permute-start | bytes 393224 | tf_op jit(solution)/shard_map/ppermute | solution.py:13
  15.5 0.8 collective-permute-done.6
  16.3 1.6 %collective-permute-start.7 = (bf16[4,1,32,1024]{3,2,0,1:T(8,128)(2,1)S(1)}, bf16[4,1,32,1024]{3,2,0,1:T(8,128)(2,1)S(1)}, u32[]{:S(2)}, u32[]{:S(2)}) collective-permute-start(bf16[4,1,32,1024]{3,2,0,1:T(8,128)(2,1)S(1)} %bitcast.169), channel_id=1, source_target_pairs={{0,4},{4,0},{8,12},{12,8},{16,20},{20,16},{24,28},{28,24},{1,5},{5... | collective-permute-start | bytes 786440 | tf_op jit(solution)/shard_map/ppermute | solution.py:13
  17.9 2.0 %collective-permute-done.2 = bf16[4,1,16,1024]{3,2,0,1:T(8,128)(2,1)S(1)} collective-permute-done((bf16[4,1,16,1024]{3,2,0,1:T(8,128)(2,1)S(1)}, bf16[4,1,16,1024]{3,2,0,1:T(8,128)(2,1)S(1)}, u32[]{:S(2)}, u32[]{:S(2)}) %collective-permute-start.2) | collective-permute-done | bytes 131104 | tf_op jit(solution)/shard_map/ppermute | solution.py:13
  20.7 1.9 %collective-permute-start.3 = (bf16[1,8,16,1024]{3,2,1,0:T(8,128)(2,1)S(1)}, bf16[1,8,16,1024]{3,2,1,0:T(8,128)(2,1)S(1)}, u32[]{:S(2)}, u32[]{:S(2)}) collective-permute-start(bf16[1,8,16,1024]{3,2,1,0:T(8,128)(2,1)S(1)} %bitcast_select_fusion), channel_id=1, source_target_pairs={{0,2},{1,3},{2,0},{3,1},{4,6},{5,7},{6,4},{7,5},{8,10},{9,11},{10,... | collective-permute-start | bytes 786440 | tf_op jit(solution)/shard_map/ppermute | solution.py:13
  22.7 1.1 %collective-permute-done.7 = bf16[4,1,32,1024]{3,2,0,1:T(8,128)(2,1)S(1)} collective-permute-done((bf16[4,1,32,1024]{3,2,0,1:T(8,128)(2,1)S(1)}, bf16[4,1,32,1024]{3,2,0,1:T(8,128)(2,1)S(1)}, u32[]{:S(2)}, u32[]{:S(2)}) %collective-permute-start.7) | collective-permute-done | bytes 262176 | tf_op jit(solution)/shard_map/ppermute | solution.py:13
  24.9 2.2 %collective-permute-done.3 = bf16[1,8,16,1024]{3,2,1,0:T(8,128)(2,1)S(1)} collective-permute-done((bf16[1,8,16,1024]{3,2,1,0:T(8,128)(2,1)S(1)}, bf16[1,8,16,1024]{3,2,1,0:T(8,128)(2,1)S(1)}, u32[]{:S(2)}, u32[]{:S(2)}) %collective-permute-start.3) | collective-permute-done | bytes 262176 | tf_op jit(solution)/shard_map/ppermute | solution.py:13
  27.8 4.3 %multiply_convert_fusion.2 = (bf16[2,8,32,1024]{3,2,1,0:T(8,128)(2,1)}, bf16[2,8,32,1024]{3,2,1,0:T(8,128)(2,1)}, bf16[2,8,32,1024]{3,2,1,0:T(8,128)(2,1)S(1)}, ...) fusion(f32[2,8,1024]{2,1,0:T(8,128)S(1)} %get-tuple-element.25,, ...), kind=kLoop, calls=%fused_computation.8 | loop fusion | flops 8388608 | bytes 9437184 | tf_op jit(solution)/shard_map/convert_element_type | solution.py:104
  32.4 0.8 %copy.20 = bf16[4,8,16,1024]{3,0,2,1:T(4,128)(2,1)S(1)} copy(bf16[4,8,16,1024]{3,2,1,0:T(8,128)(2,1)S(1)} %bitcast.164) | data formatting | bytes 2097152 | tf_op jit(solution)/shard_map/jit(_where)/select_n | solution.py:24
  33.2 1.7 %slice_convert_fusion.3 = (f32[2,16,4,1024]{3,2,1,0:T(4,128)}, f32[2,16,4,1024]{3,2,1,0:T(4,128)}, f32[2,16,4,1024]{3,2,1,0:T(4,128)}, f32[2,16,4,1024]{3,2,1,0:T(4,128)}) fusion(bf16[8,16,4,1024]{3,2,1,0:T(4,128)(2,1)S(1)} %bitcast.163), kind=kLoop, calls=%fused_computation.48 | loop fusion | flops 524288 | bytes 3145728 | tf_op jit(solution)/shard_map/convert_element_type | solution.py:56
  34.9 2.2 %reshape.703 = f32[2,16,4096]{2,1,0:T(8,128)} reshape(f32[2,16,4,1024]{3,2,1,0:T(4,128)} %get-tuple-element.9) | data formatting | bytes 1048576 | tf_op jit(solution)/shard_map/convert_element_type | solution.py:56
  37.1 2.2 %reshape.707 = f32[2,16,4096]{2,1,0:T(8,128)} reshape(f32[2,16,4,1024]{3,2,1,0:T(4,128)} %get-tuple-element.10) | data formatting | bytes 1048576 | tf_op jit(solution)/shard_map/convert_element_type | solution.py:57
  39.4 2.2 %reshape.706 = f32[2,16,4096]{2,1,0:T(8,128)} reshape(f32[2,16,4,1024]{3,2,1,0:T(4,128)} %get-tuple-element.11) | data formatting | bytes 1048576 | tf_op jit(solution)/shard_map/convert_element_type | solution.py:56
  41.6 2.2 %reshape.704 = f32[2,16,4096]{2,1,0:T(8,128)} reshape(f32[2,16,4,1024]{3,2,1,0:T(4,128)} %get-tuple-element.12) | data formatting | bytes 1048576 | tf_op jit(solution)/shard_map/convert_element_type | solution.py:57
  43.8 2.1 %multiply_convert_fusion.1 = bf16[2,16,16,4096]{3,2,1,0:T(8,128)(2,1)S(1)} fusion(f32[2,16,4096]{2,1,0:T(8,128)} %reshape.704, f32[2,16,4096]{2,1,0:T(8,128)} %reshape.703), kind=kLoop, calls=%fused_computation.7 | loop fusion | flops 4194304 | bytes 5242880 | tf_op jit(solution)/shard_map/convert_element_type | solution.py:58
  45.9 7.4 %fusion.4 = bf16[512,1024]{1,0:T(8,128)(2,1)S(1)} fusion(bf16[512,4096]{1,0:T(8,128)(2,1)S(1)} %bitcast.155, bf16[1,4096,1024]{2,1,0:T(8,128)(2,1)} %param.4), kind=kOutput, calls=%fused_computation.16 | convolution fusion | flops 4295491584 | bytes 13631488 | tf_op jit(solution)/shard_map/dot_general | solution.py:60
  53.3 0.7 multiply_convert_fusion
  54.1 4.6 %fusion.7 = bf16[512,1024]{1,0:T(8,128)(2,1)S(1)} fusion(bf16[512,4096]{1,0:T(8,128)(2,1)S(1)} %bitcast.156, bf16[1,4096,1024]{2,1,0:T(8,128)(2,1)S(1)} %bitcast.182), kind=kOutput, calls=%fused_computation.17 | convolution fusion | flops 4295491584 | bytes 13631488 | tf_op jit(solution)/shard_map/dot_general | solution.py:60
  62.9 1.9 %collective-permute-start.9 = (bf16[1,2,256,256]{3,2,1,0:T(8,128)(2,1)S(1)}, bf16[1,2,256,256]{3,2,1,0:T(8,128)(2,1)S(1)}, u32[]{:S(2)}, u32[]{:S(2)}) collective-permute-start(bf16[1,2,256,256]{3,2,1,0:T(8,128)(2,1)S(1)} %fusion.18), channel_id=1, source_target_pairs={{0,2},{1,3},{2,0},{3,1},{4,6},{5,7},{6,4},{7,5},{8,10},{9,11},{10,... | collective-permute-start | bytes 786440 | tf_op jit(solution)/shard_map/ppermute | solution.py:13
  66.4 5.8 %collective-permute-done.9 = bf16[1,2,256,256]{3,2,1,0:T(8,128)(2,1)S(1)} collective-permute-done((bf16[1,2,256,256]{3,2,1,0:T(8,128)(2,1)S(1)}, bf16[1,2,256,256]{3,2,1,0:T(8,128)(2,1)S(1)}, u32[]{:S(2)}, u32[]{:S(2)}) %collective-permute-start.9) | collective-permute-done | bytes 262176 | tf_op jit(solution)/shard_map/ppermute | solution.py:13
  72.2 4.9 %collective-permute-done.11 = bf16[1,2,256,256]{3,2,1,0:T(8,128)(2,1)S(1)} collective-permute-done((bf16[1,2,256,256]{3,2,1,0:T(8,128)(2,1)S(1)}, bf16[1,2,256,256]{3,2,1,0:T(8,128)(2,1)S(1)}, u32[]{:S(2)}, u32[]{:S(2)}) %collective-permute-start.11) | collective-permute-done | bytes 262176 | tf_op jit(solution)/shard_map/ppermute | solution.py:13
  77.2 1.0 %maximum_bitcast_fusion = f32[1,4,256,256]{3,2,1,0:T(8,128)} fusion(f32[2,256,256]{2,1,0:T(8,128)S(1)} %fusion.13, f32[2,256,256]{2,1,0:T(8,128)S(1)} %fusion.17), kind=kLoop, calls=%fused_computation.25 | loop fusion | flops 262144 | bytes 2097152 | tf_op jit(solution)/shard_map/broadcast_in_dim | solution.py:118
  (67 shorter events, 9.4 us)
Async XLA Ops:
  0.8 7.8 %collective-permute-start = (bf16[1,1,16,1024]{3,2,0,1:T(8,128)(2,1)S(1)}, bf16[1,1,16,1024]{3,2,0,1:T(8,128)(2,1)S(1)}, u32[]{:S(2)}, u32[]{:S(2)}) collective-permute-start(bf16[1,1,16,1024]{3,2,0,1:T(8,128)(2,1)S(1)} %get-tuple-element.32), channel_id=1, source_target_pairs={{0,16},{4,20},{8,24},{12,28},{16,0},{20,4},{24,8},{28,12},{1,17},{... | collective-permute-start | bytes 98312 | tf_op jit(solution)/shard_map/ppermute | solution.py:13
  5.7 5.6 %collective-permute-start.5 = (bf16[1,1,32,1024]{3,2,0,1:T(8,128)(2,1)S(1)}, bf16[1,1,32,1024]{3,2,0,1:T(8,128)(2,1)S(1)}, u32[]{:S(2)}, u32[]{:S(2)}) collective-permute-start(bf16[1,1,32,1024]{3,2,0,1:T(8,128)(2,1)S(1)} %get-tuple-element.30), channel_id=1, source_target_pairs={{0,16},{4,20},{8,24},{12,28},{16,0},{20,4},{24,8},{28,12},{1,17},{... | collective-permute-start | bytes 196616 | tf_op jit(solution)/shard_map/ppermute | solution.py:13
  8.6 5.0 %collective-permute-start.1 = (bf16[2,1,16,1024]{3,2,0,1:T(8,128)(2,1)S(1)}, bf16[2,1,16,1024]{3,2,0,1:T(8,128)(2,1)S(1)}, u32[]{:S(2)}, u32[]{:S(2)}) collective-permute-start(bf16[2,1,16,1024]{3,2,0,1:T(8,128)(2,1)S(1)} %maximum_select_fusion.8), channel_id=1, source_target_pairs={{0,8},{4,12},{8,0},{12,4},{16,24},{20,28},{24,16},{28,20},{1,9},{5... | collective-permute-start | bytes 196616 | tf_op jit(solution)/shard_map/ppermute | solution.py:13
  11.2 5.0 %collective-permute-start.6 = (bf16[2,1,32,1024]{3,2,0,1:T(8,128)(2,1)S(1)}, bf16[2,1,32,1024]{3,2,0,1:T(8,128)(2,1)S(1)}, u32[]{:S(2)}, u32[]{:S(2)}) collective-permute-start(bf16[2,1,32,1024]{3,2,0,1:T(8,128)(2,1)S(1)} %maximum_select_fusion.7), channel_id=1, source_target_pairs={{0,8},{4,12},{8,0},{12,4},{16,24},{20,28},{24,16},{28,20},{1,9},{5... | collective-permute-start | bytes 393224 | tf_op jit(solution)/shard_map/ppermute | solution.py:13
  13.6 6.3 %collective-permute-start.2 = (bf16[4,1,16,1024]{3,2,0,1:T(8,128)(2,1)S(1)}, bf16[4,1,16,1024]{3,2,0,1:T(8,128)(2,1)S(1)}, u32[]{:S(2)}, u32[]{:S(2)}) collective-permute-start(bf16[4,1,16,1024]{3,2,0,1:T(8,128)(2,1)S(1)} %bitcast.173), channel_id=1, source_target_pairs={{0,4},{4,0},{8,12},{12,8},{16,20},{20,16},{24,28},{28,24},{1,5},{5... | collective-permute-start | bytes 393224 | tf_op jit(solution)/shard_map/ppermute | solution.py:13
  16.3 7.5 %collective-permute-start.7 = (bf16[4,1,32,1024]{3,2,0,1:T(8,128)(2,1)S(1)}, bf16[4,1,32,1024]{3,2,0,1:T(8,128)(2,1)S(1)}, u32[]{:S(2)}, u32[]{:S(2)}) collective-permute-start(bf16[4,1,32,1024]{3,2,0,1:T(8,128)(2,1)S(1)} %bitcast.169), channel_id=1, source_target_pairs={{0,4},{4,0},{8,12},{12,8},{16,20},{20,16},{24,28},{28,24},{1,5},{5... | collective-permute-start | bytes 786440 | tf_op jit(solution)/shard_map/ppermute | solution.py:13
  20.7 6.4 %collective-permute-start.3 = (bf16[1,8,16,1024]{3,2,1,0:T(8,128)(2,1)S(1)}, bf16[1,8,16,1024]{3,2,1,0:T(8,128)(2,1)S(1)}, u32[]{:S(2)}, u32[]{:S(2)}) collective-permute-start(bf16[1,8,16,1024]{3,2,1,0:T(8,128)(2,1)S(1)} %bitcast_select_fusion), channel_id=1, source_target_pairs={{0,2},{1,3},{2,0},{3,1},{4,6},{5,7},{6,4},{7,5},{8,10},{9,11},{10,... | collective-permute-start | bytes 786440 | tf_op jit(solution)/shard_map/ppermute | solution.py:13
  27.1 0.7 copy-start.7
  27.2 5.1 %collective-permute-start.4 = (bf16[2,8,16,1024]{3,2,1,0:T(8,128)(2,1)S(1)}, bf16[2,8,16,1024]{3,2,1,0:T(8,128)(2,1)S(1)}, u32[]{:S(2)}, u32[]{:S(2)}) collective-permute-start(bf16[2,8,16,1024]{3,2,1,0:T(8,128)(2,1)S(1)} %maximum_select_fusion.2), channel_id=1, source_target_pairs={{0,1},{1,0},{2,3},{3,2},{4,5},{5,4},{6,7},{7,6},{8,9},{9,8},{10,11... | collective-permute-start | bytes 1572872 | tf_op jit(solution)/shard_map/ppermute | solution.py:13
  27.8 4.3 %copy-start.8 = (bf16[1,8,16,1024]{3,2,1,0:T(8,128)(2,1)S(1)}, bf16[1,8,16,1024]{3,2,1,0:T(8,128)(2,1)}, u32[]{:S(2)}) copy-start(bf16[1,8,16,1024]{3,2,1,0:T(8,128)(2,1)} %copy-done.7) | copy-start | bytes 786436
  43.8 10.3 %slice-start = ((s8[8388608]{0:T(1024)(128)(4,1)}), s8[4194304]{0:T(1024)(128)(4,1)S(1)}, s32[]{:S(2)}) async-start(s8[8388608]{0:T(1024)(128)(4,1)} %bitcast.181), calls=%async_computation | async-start | bytes 8388608
  45.9 7.4 %copy-start.5 = (f32[2,16,4096]{2,1,0:T(8,128)S(1)}, f32[2,16,4096]{2,1,0:T(8,128)}, u32[]{:S(2)}) copy-start(f32[2,16,4096]{2,1,0:T(8,128)} %reshape.707) | copy-start | bytes 1572868
  45.9 7.4 %copy-start.6 = (f32[2,16,4096]{2,1,0:T(8,128)S(1)}, f32[2,16,4096]{2,1,0:T(8,128)}, u32[]{:S(2)}) copy-start(f32[2,16,4096]{2,1,0:T(8,128)} %reshape.706) | copy-start | bytes 1572868
  45.9 8.2 %slice-start.1 = ((s8[8388608]{0:T(1024)(128)(4,1)}), s8[4194304]{0:T(1024)(128)(4,1)S(1)}, s32[]{:S(2)}) async-start(s8[8388608]{0:T(1024)(128)(4,1)} %bitcast.181), calls=%async_computation.1 | async-start | bytes 8388608
  54.1 4.6 %copy-start.2 = (bf16[2,8,32,1024]{3,2,1,0:T(8,128)(2,1)S(1)}, bf16[2,8,32,1024]{3,2,1,0:T(8,128)(2,1)}, u32[]{:S(2)}) copy-start(bf16[2,8,32,1024]{3,2,1,0:T(8,128)(2,1)} %get-tuple-element.34) | copy-start | bytes 3145732
  54.1 5.1 %copy-start.1 = (bf16[2,8,32,1024]{3,2,1,0:T(8,128)(2,1)S(1)}, bf16[2,8,32,1024]{3,2,1,0:T(8,128)(2,1)}, u32[]{:S(2)}) copy-start(bf16[2,8,32,1024]{3,2,1,0:T(8,128)(2,1)} %get-tuple-element.35) | copy-start | bytes 3145732
  58.7 1.2 %copy-start = (bf16[2,8,32,1024]{3,2,1,0:T(8,128)(2,1)S(1)}, bf16[2,8,32,1024]{3,2,1,0:T(8,128)(2,1)}, u32[]{:S(2)}) copy-start(bf16[2,8,32,1024]{3,2,1,0:T(8,128)(2,1)} %get-tuple-element.22) | copy-start | bytes 3145732
  59.7 2.7 %collective-permute-start.8 = (f32[2,2,256,256]{3,2,1,0:T(8,128)S(1)}, f32[2,2,256,256]{3,2,1,0:T(8,128)S(1)}, u32[]{:S(2)}, u32[]{:S(2)}) collective-permute-start(f32[2,2,256,256]{3,2,1,0:T(8,128)S(1)} %pad_maximum_fusion), channel_id=1, source_target_pairs={{0,1},{1,0},{2,3},{3,2},{4,5},{5,4},{6,7},{7,6},{8,9},{9,8},{10,11... | collective-permute-start | bytes 3145736 | tf_op jit(solution)/shard_map/ppermute | solution.py:13
  60.4 2.1 %copy-start.4 = (bf16[2,8,32,1024]{3,2,1,0:T(8,128)(2,1)S(1)}, bf16[2,8,32,1024]{3,2,1,0:T(8,128)(2,1)}, u32[]{:S(2)}) copy-start(bf16[2,8,32,1024]{3,2,1,0:T(8,128)(2,1)} %get-tuple-element.36) | copy-start | bytes 3145732
  60.9 4.4 %copy-start.3 = (bf16[2,8,32,1024]{3,2,1,0:T(8,128)(2,1)S(1)}, bf16[2,8,32,1024]{3,2,1,0:T(8,128)(2,1)}, u32[]{:S(2)}) copy-start(bf16[2,8,32,1024]{3,2,1,0:T(8,128)(2,1)} %get-tuple-element.21) | copy-start | bytes 3145732
  61.0 4.4 %collective-permute-start.10 = (f32[2,2,256,256]{3,2,1,0:T(8,128)S(1)}, f32[2,2,256,256]{3,2,1,0:T(8,128)S(1)}, u32[]{:S(2)}, u32[]{:S(2)}) collective-permute-start(f32[2,2,256,256]{3,2,1,0:T(8,128)S(1)} %pad_maximum_fusion.1), channel_id=1, source_target_pairs={{0,1},{1,0},{2,3},{3,2},{4,5},{5,4},{6,7},{7,6},{8,9},{9,8},{10,11... | collective-permute-start | bytes 3145736 | tf_op jit(solution)/shard_map/ppermute | solution.py:13
  62.9 9.2 %collective-permute-start.9 = (bf16[1,2,256,256]{3,2,1,0:T(8,128)(2,1)S(1)}, bf16[1,2,256,256]{3,2,1,0:T(8,128)(2,1)S(1)}, u32[]{:S(2)}, u32[]{:S(2)}) collective-permute-start(bf16[1,2,256,256]{3,2,1,0:T(8,128)(2,1)S(1)} %fusion.18), channel_id=1, source_target_pairs={{0,2},{1,3},{2,0},{3,1},{4,6},{5,7},{6,4},{7,5},{8,10},{9,11},{10,... | collective-permute-start | bytes 786440 | tf_op jit(solution)/shard_map/ppermute | solution.py:13
  65.8 11.3 %collective-permute-start.11 = (bf16[1,2,256,256]{3,2,1,0:T(8,128)(2,1)S(1)}, bf16[1,2,256,256]{3,2,1,0:T(8,128)(2,1)S(1)}, u32[]{:S(2)}, u32[]{:S(2)}) collective-permute-start(bf16[1,2,256,256]{3,2,1,0:T(8,128)(2,1)S(1)} %fusion.19), channel_id=1, source_target_pairs={{0,2},{1,3},{2,0},{3,1},{4,6},{5,7},{6,4},{7,5},{8,10},{9,11},{10,... | collective-permute-start | bytes 786440 | tf_op jit(solution)/shard_map/ppermute | solution.py:13

commit v8 on v7

--- a/solution.py
+++ b/solution.py
@@ -84,6 +84,7 @@
     valence = jnp.transpose(valence, (1, 2, 0, 3)).reshape(
         2 * pair_count, NV, col_count * mu_cols
     )
+    valence = lax.optimization_barrier(valence)
     conduction = jnp.take(held_conduction, wanted, axis=0).astype(jnp.float32)
     rows_per_block = NC // col_count
     chunk = pair_count // PAIR_CHUNKS

time: 78.7 us -> 72.1 us (0.916)
  local copies, waits for them, and re-layouts: 13.3 us -> 8 us
  other arithmetic: 13.8 us -> 12.2 us
    convert_element_type x4 -> x0, local copies, waits for them, and re-layouts: 8.87 us -> none  [the longest x2 4.44 us: screened_of(): valence_a = valence_a.astype(jnp.float32)]
    reshape x0 -> x1, local copies, waits for them, and re-layouts: none -> 2.61 us  [body(): jnp.transpose(valence, (1, 2, 0, 3))]
    convert_element_type x2 -> x1, other arithmetic: 2.78 us -> 1.46 us  [screened_of(): (valence_a[:, :, None, :] * valence_b[:, None, :, :]).astype(jnp.bfloat16)]
    select_n x3, local copies, waits for them, and re-layouts: 0.88 us -> 1.84 us  [gather_axis(): cur = jnp.where(low, jnp.stack([cur, got], 1), jnp.stack([got, cur], 1))]
  transfers between devices with their start and end apart: 12 -> 12, of which waited for: 9 -> 9; matrix products, arithmetic and copies ran while one was open for 17% -> 18% of each run, Pallas kernels for 0% -> 0%
where the time goes in v8:
time: 72.1 us; the launch traced here: 71.8 us
  waiting for transfers between devices  19 us (26%)
  matrix products  16.4 us (23%)
  starting transfers between devices  15.8 us (22%)
  other arithmetic  12.2 us (17%)
  local copies, waits for them, and re-layouts  8 us (11%)
    ppermute x12, waiting for transfers between devices, swap(): return lax.ppermute(x, axis, [(i, i ^ bit) for i in range(size)])  19 us
    ppermute x12, starting transfers between devices, swap(): return lax.ppermute(x, axis, [(i, i ^ bit) for i in range(size)])  15.8 us
    dot_general x2, matrix products, screened_of(): jnp.dot(val_pairs, screening, preferred_element_type=jnp.float32)  12.4 us
    convert_element_type x1, other arithmetic, own_block(): (rows[:, :, None, :] * cond_b[:, None, :, :]).astype(jnp.bfloat16)  4.37 us
    dot_general x8, matrix products, own_block(): jnp.einsum('pan,pbn->pab', screened, cond_pairs, preferred_element_type=j...  3.99 us
    reshape x1, local copies, waits for them, and re-layouts, body(): jnp.transpose(valence, (1, 2, 0, 3))  2.61 us
    select_n x3, local copies, waits for them, and re-layouts, gather_axis(): cur = jnp.where(low, jnp.stack([cur, got], 1), jnp.stack([got, cur], 1))  1.84 us
    another operation x2, local copies, waits for them, and re-layouts, gather_axis(): cur = jnp.where(low, jnp.stack([cur, got], 1), jnp.stack([got, cur], 1))  1.61 us
  transfers between devices with their start and end apart: 12, of which 9 were waited for; matrix products, arithmetic and copies ran while one was open for 18% of the time, Pallas kernels for 0%

profile of v8, /device:TPU:0, one launch (start us, length us, event | category | flops | bytes accessed | tf_op | source)
XLA Modules:
  0.0 71.8 jit_solution(6147815102519944941)
XLA Ops:
  0.0 0.8 %slice_bitcast_fusion.7 = (bf16[1,1,1,16,1024]{4,3,2,1,0:T(8,128)(2,1)S(1)}, bf16[1,1,16,1024]{3,2,0,1:T(8,128)(2,1)S(1)}) fusion(bf16[1,48,1024]{2,1,0:T(8,128)(2,1)} %param.3), kind=kLoop, calls=%fused_computation.64 | loop fusion | bytes 98304 | tf_op jit(solution)/shard_map/stack | solution.py:24
  0.8 4.0 %collective-permute-start = (bf16[1,1,16,1024]{3,2,0,1:T(8,128)(2,1)S(1)}, bf16[1,1,16,1024]{3,2,0,1:T(8,128)(2,1)S(1)}, u32[]{:S(2)}, u32[]{:S(2)}) collective-permute-start(bf16[1,1,16,1024]{3,2,0,1:T(8,128)(2,1)S(1)} %get-tuple-element.32), channel_id=1, source_target_pairs={{0,16},{4,20},{8,24},{12,28},{16,0},{20,4},{24,8},{28,12},{1,17},{... | collective-permute-start | bytes 98312 | tf_op jit(solution)/shard_map/ppermute | solution.py:13
  4.8 0.8 %slice_bitcast_fusion.5 = (bf16[1,1,1,32,1024]{4,3,2,1,0:T(8,128)(2,1)S(1)}, bf16[1,1,32,1024]{3,2,0,1:T(8,128)(2,1)S(1)}) fusion(bf16[1,48,1024]{2,1,0:T(8,128)(2,1)} %param.3), kind=kLoop, calls=%fused_computation.62 | loop fusion | bytes 196608 | tf_op jit(solution)/shard_map/stack | solution.py:24
  5.7 0.7 fusion.46
  6.4 0.7 and_select_fusion
  7.1 0.7 %fusion.23 = s32[8]{0:T(128)S(1)} fusion(s32[4,1]{0,1:T(1,128)S(1)} %fusion.46, s32[4,1]{0,1:T(1,128)} %bitcast.183), kind=kLoop, calls=%fused_computation.81 | loop fusion | flops 32 | bytes 64 | tf_op jit(solution)/shard_map/jit(_take)/jit(_where)/select_n | solution.py:83
  7.8 0.7 %compare_and_fusion = pred[8]{0:T(512)(128)(4,1)S(1)} fusion(s32[4]{0:T(128)S(1)} %and_select_fusion, s32[4]{0:T(128)} %bitcast.184), kind=kLoop, calls=%fused_computation.78 | loop fusion | flops 56 | bytes 40 | tf_op jit(solution)/shard_map/jit(_take)/and | solution.py:83
  8.6 2.0 %collective-permute-start.1 = (bf16[2,1,16,1024]{3,2,0,1:T(8,128)(2,1)S(1)}, bf16[2,1,16,1024]{3,2,0,1:T(8,128)(2,1)S(1)}, u32[]{:S(2)}, u32[]{:S(2)}) collective-permute-start(bf16[2,1,16,1024]{3,2,0,1:T(8,128)(2,1)S(1)} %maximum_select_fusion.8), channel_id=1, source_target_pairs={{0,8},{4,12},{8,0},{12,4},{16,24},{20,28},{24,16},{28,20},{1,9},{5... | collective-permute-start | bytes 196616 | tf_op jit(solution)/shard_map/ppermute | solution.py:13
  10.5 0.7 collective-permute-done.5
  11.2 1.3 %collective-permute-start.6 = (bf16[2,1,32,1024]{3,2,0,1:T(8,128)(2,1)S(1)}, bf16[2,1,32,1024]{3,2,0,1:T(8,128)(2,1)S(1)}, u32[]{:S(2)}, u32[]{:S(2)}) collective-permute-start(bf16[2,1,32,1024]{3,2,0,1:T(8,128)(2,1)S(1)} %maximum_select_fusion.7), channel_id=1, source_target_pairs={{0,8},{4,12},{8,0},{12,4},{16,24},{20,28},{24,16},{28,20},{1,9},{5... | collective-permute-start | bytes 393224 | tf_op jit(solution)/shard_map/ppermute | solution.py:13
  12.5 1.0 %collective-permute-done.1 = bf16[2,1,16,1024]{3,2,0,1:T(8,128)(2,1)S(1)} collective-permute-done((bf16[2,1,16,1024]{3,2,0,1:T(8,128)(2,1)S(1)}, bf16[2,1,16,1024]{3,2,0,1:T(8,128)(2,1)S(1)}, u32[]{:S(2)}, u32[]{:S(2)}) %collective-permute-start.1) | collective-permute-done | bytes 65568 | tf_op jit(solution)/shard_map/ppermute | solution.py:13
  13.6 1.9 %collective-permute-start.2 = (bf16[4,1,16,1024]{3,2,0,1:T(8,128)(2,1)S(1)}, bf16[4,1,16,1024]{3,2,0,1:T(8,128)(2,1)S(1)}, u32[]{:S(2)}, u32[]{:S(2)}) collective-permute-start(bf16[4,1,16,1024]{3,2,0,1:T(8,128)(2,1)S(1)} %bitcast.173), channel_id=1, source_target_pairs={{0,4},{4,0},{8,12},{12,8},{16,20},{20,16},{24,28},{28,24},{1,5},{5... | collective-permute-start | bytes 393224 | tf_op jit(solution)/shard_map/ppermute | solution.py:13
  15.5 0.8 %collective-permute-done.6 = bf16[2,1,32,1024]{3,2,0,1:T(8,128)(2,1)S(1)} collective-permute-done((bf16[2,1,32,1024]{3,2,0,1:T(8,128)(2,1)S(1)}, bf16[2,1,32,1024]{3,2,0,1:T(8,128)(2,1)S(1)}, u32[]{:S(2)}, u32[]{:S(2)}) %collective-permute-start.6) | collective-permute-done | bytes 131104 | tf_op jit(solution)/shard_map/ppermute | solution.py:13
  16.3 1.6 %collective-permute-start.7 = (bf16[4,1,32,1024]{3,2,0,1:T(8,128)(2,1)S(1)}, bf16[4,1,32,1024]{3,2,0,1:T(8,128)(2,1)S(1)}, u32[]{:S(2)}, u32[]{:S(2)}) collective-permute-start(bf16[4,1,32,1024]{3,2,0,1:T(8,128)(2,1)S(1)} %bitcast.169), channel_id=1, source_target_pairs={{0,4},{4,0},{8,12},{12,8},{16,20},{20,16},{24,28},{28,24},{1,5},{5... | collective-permute-start | bytes 786440 | tf_op jit(solution)/shard_map/ppermute | solution.py:13
  17.9 2.0 %collective-permute-done.2 = bf16[4,1,16,1024]{3,2,0,1:T(8,128)(2,1)S(1)} collective-permute-done((bf16[4,1,16,1024]{3,2,0,1:T(8,128)(2,1)S(1)}, bf16[4,1,16,1024]{3,2,0,1:T(8,128)(2,1)S(1)}, u32[]{:S(2)}, u32[]{:S(2)}) %collective-permute-start.2) | collective-permute-done | bytes 131104 | tf_op jit(solution)/shard_map/ppermute | solution.py:13
  20.0 0.6 gather_fusion
  20.7 1.9 %collective-permute-start.3 = (bf16[1,8,16,1024]{3,2,1,0:T(8,128)(2,1)S(1)}, bf16[1,8,16,1024]{3,2,1,0:T(8,128)(2,1)S(1)}, u32[]{:S(2)}, u32[]{:S(2)}) collective-permute-start(bf16[1,8,16,1024]{3,2,1,0:T(8,128)(2,1)S(1)} %bitcast_select_fusion), channel_id=1, source_target_pairs={{0,2},{1,3},{2,0},{3,1},{4,6},{5,7},{6,4},{7,5},{8,10},{9,11},{10,... | collective-permute-start | bytes 786440 | tf_op jit(solution)/shard_map/ppermute | solution.py:13
  22.7 1.1 %collective-permute-done.7 = bf16[4,1,32,1024]{3,2,0,1:T(8,128)(2,1)S(1)} collective-permute-done((bf16[4,1,32,1024]{3,2,0,1:T(8,128)(2,1)S(1)}, bf16[4,1,32,1024]{3,2,0,1:T(8,128)(2,1)S(1)}, u32[]{:S(2)}, u32[]{:S(2)}) %collective-permute-start.7) | collective-permute-done | bytes 262176 | tf_op jit(solution)/shard_map/ppermute | solution.py:13
  24.0 0.6 gather_fusion.1
  24.8 2.3 %collective-permute-done.3 = bf16[1,8,16,1024]{3,2,1,0:T(8,128)(2,1)S(1)} collective-permute-done((bf16[1,8,16,1024]{3,2,1,0:T(8,128)(2,1)S(1)}, bf16[1,8,16,1024]{3,2,1,0:T(8,128)(2,1)S(1)}, u32[]{:S(2)}, u32[]{:S(2)}) %collective-permute-start.3) | collective-permute-done | bytes 262176 | tf_op jit(solution)/shard_map/ppermute | solution.py:13
  27.8 4.4 %multiply_convert_fusion.2 = (bf16[2,8,32,1024]{3,2,1,0:T(8,128)(2,1)}, bf16[2,8,32,1024]{3,2,1,0:T(8,128)(2,1)}, bf16[2,8,32,1024]{3,2,1,0:T(8,128)(2,1)S(1)}, ...) fusion(f32[2,8,1024]{2,1,0:T(8,128)S(1)} %get-tuple-element.25,, ...), kind=kLoop, calls=%fused_computation.8 | loop fusion | flops 8388608 | bytes 9437184 | tf_op jit(solution)/shard_map/convert_element_type | solution.py:105
  32.4 1.8 %copy.20 = bf16[4,8,16,1024]{3,0,2,1:T(4,128)(2,1)} copy(bf16[4,8,16,1024]{3,2,1,0:T(8,128)(2,1)S(1)} %bitcast.161) | data formatting | bytes 2097152 | tf_op jit(solution)/shard_map/jit(_where)/select_n | solution.py:24
  34.2 2.6 %reshape.675 = bf16[8,16,4096]{2,1,0:T(8,128)(2,1)} reshape(bf16[8,16,4,1024]{3,2,1,0:T(4,128)(2,1)} %bitcast.166) | data formatting | bytes 2097152 | tf_op jit(solution)/shard_map/reshape | solution.py:84
  36.8 1.3 %slice_convert_fusion.3 = (f32[2,16,4096]{2,1,0:T(8,128)S(1)}, f32[2,16,4096]{2,1,0:T(8,128)S(1)}, f32[2,16,4096]{2,1,0:T(8,128)S(1)}, f32[2,16,4096]{2,1,0:T(8,128)S(1)}) fusion(bf16[8,16,4096]{2,1,0:T(8,128)(2,1)} %reshape.675), kind=kLoop, calls=%fused_computation.48 | loop fusion | flops 524288 | bytes 3145728 | tf_op jit(solution)/shard_map/convert_element_type | solution.py:56
  38.2 1.5 %multiply_convert_fusion = (bf16[2,16,16,4096]{3,2,1,0:T(8,128)(2,1)S(1)}, bf16[2,16,16,4096]{3,2,1,0:T(8,128)(2,1)S(1)}) fusion(f32[2,16,4096]{2,1,0:T(8,128)S(1)} %get-tuple-element.10, f32[2,16,4096]{2,1,0:T(8,128)S(1)} %get-tuple-element.11, f32[2,16,4096]{2,1,0:T(8,128)S(1)} %get-tuple-element.12, f32[2,16,4096]{2,1,0:T(8,128)S(1)} %get-tuple-element.9), kind=kLoop, calls=%fused_computation.6 | loop fusion | flops 8388608 | bytes 10485760 | tf_op jit(solution)/shard_map/convert_element_type | solution.py:58
  39.7 7.9 %fusion.7 = bf16[512,1024]{1,0:T(8,128)(2,1)S(1)} fusion(bf16[512,4096]{1,0:T(8,128)(2,1)S(1)} %bitcast.163, bf16[1,4096,1024]{2,1,0:T(8,128)(2,1)} %param.4), kind=kOutput, calls=%fused_computation.17 | convolution fusion | flops 4295491584 | bytes 13631488 | tf_op jit(solution)/shard_map/dot_general | solution.py:60
  47.6 4.5 %fusion.4 = bf16[512,1024]{1,0:T(8,128)(2,1)S(1)} fusion(bf16[512,4096]{1,0:T(8,128)(2,1)S(1)} %bitcast.162, bf16[1,4096,1024]{2,1,0:T(8,128)(2,1)S(1)} %bitcast.182), kind=kOutput, calls=%fused_computation.16 | convolution fusion | flops 4295491584 | bytes 13631488 | tf_op jit(solution)/shard_map/dot_general | solution.py:60
  56.5 1.9 %collective-permute-start.9 = (bf16[1,2,256,256]{3,2,1,0:T(8,128)(2,1)S(1)}, bf16[1,2,256,256]{3,2,1,0:T(8,128)(2,1)S(1)}, u32[]{:S(2)}, u32[]{:S(2)}) collective-permute-start(bf16[1,2,256,256]{3,2,1,0:T(8,128)(2,1)S(1)} %fusion.18), channel_id=1, source_target_pairs={{0,2},{1,3},{2,0},{3,1},{4,6},{5,7},{6,4},{7,5},{8,10},{9,11},{10,... | collective-permute-start | bytes 786440 | tf_op jit(solution)/shard_map/ppermute | solution.py:13
  58.9 0.6 fusion.19
  59.9 5.8 %collective-permute-done.9 = bf16[1,2,256,256]{3,2,1,0:T(8,128)(2,1)S(1)} collective-permute-done((bf16[1,2,256,256]{3,2,1,0:T(8,128)(2,1)S(1)}, bf16[1,2,256,256]{3,2,1,0:T(8,128)(2,1)S(1)}, u32[]{:S(2)}, u32[]{:S(2)}) %collective-permute-start.9) | collective-permute-done | bytes 262176 | tf_op jit(solution)/shard_map/ppermute | solution.py:13
  65.8 4.9 %collective-permute-done.11 = bf16[1,2,256,256]{3,2,1,0:T(8,128)(2,1)S(1)} collective-permute-done((bf16[1,2,256,256]{3,2,1,0:T(8,128)(2,1)S(1)}, bf16[1,2,256,256]{3,2,1,0:T(8,128)(2,1)S(1)}, u32[]{:S(2)}, u32[]{:S(2)}) %collective-permute-start.11) | collective-permute-done | bytes 262176 | tf_op jit(solution)/shard_map/ppermute | solution.py:13
  70.7 1.0 %maximum_bitcast_fusion = f32[1,4,256,256]{3,2,1,0:T(8,128)} fusion(f32[2,256,256]{2,1,0:T(8,128)S(1)} %fusion.13, f32[2,256,256]{2,1,0:T(8,128)S(1)} %fusion.17), kind=kLoop, calls=%fused_computation.25 | loop fusion | flops 262144 | bytes 2097152 | tf_op jit(solution)/shard_map/broadcast_in_dim | solution.py:119
  (59 shorter events, 7.1 us)
Async XLA Ops:
  0.8 7.8 %collective-permute-start = (bf16[1,1,16,1024]{3,2,0,1:T(8,128)(2,1)S(1)}, bf16[1,1,16,1024]{3,2,0,1:T(8,128)(2,1)S(1)}, u32[]{:S(2)}, u32[]{:S(2)}) collective-permute-start(bf16[1,1,16,1024]{3,2,0,1:T(8,128)(2,1)S(1)} %get-tuple-element.32), channel_id=1, source_target_pairs={{0,16},{4,20},{8,24},{12,28},{16,0},{20,4},{24,8},{28,12},{1,17},{... | collective-permute-start | bytes 98312 | tf_op jit(solution)/shard_map/ppermute | solution.py:13
  5.7 5.6 %collective-permute-start.5 = (bf16[1,1,32,1024]{3,2,0,1:T(8,128)(2,1)S(1)}, bf16[1,1,32,1024]{3,2,0,1:T(8,128)(2,1)S(1)}, u32[]{:S(2)}, u32[]{:S(2)}) collective-permute-start(bf16[1,1,32,1024]{3,2,0,1:T(8,128)(2,1)S(1)} %get-tuple-element.30), channel_id=1, source_target_pairs={{0,16},{4,20},{8,24},{12,28},{16,0},{20,4},{24,8},{28,12},{1,17},{... | collective-permute-start | bytes 196616 | tf_op jit(solution)/shard_map/ppermute | solution.py:13
  8.6 5.0 %collective-permute-start.1 = (bf16[2,1,16,1024]{3,2,0,1:T(8,128)(2,1)S(1)}, bf16[2,1,16,1024]{3,2,0,1:T(8,128)(2,1)S(1)}, u32[]{:S(2)}, u32[]{:S(2)}) collective-permute-start(bf16[2,1,16,1024]{3,2,0,1:T(8,128)(2,1)S(1)} %maximum_select_fusion.8), channel_id=1, source_target_pairs={{0,8},{4,12},{8,0},{12,4},{16,24},{20,28},{24,16},{28,20},{1,9},{5... | collective-permute-start | bytes 196616 | tf_op jit(solution)/shard_map/ppermute | solution.py:13
  11.2 5.0 %collective-permute-start.6 = (bf16[2,1,32,1024]{3,2,0,1:T(8,128)(2,1)S(1)}, bf16[2,1,32,1024]{3,2,0,1:T(8,128)(2,1)S(1)}, u32[]{:S(2)}, u32[]{:S(2)}) collective-permute-start(bf16[2,1,32,1024]{3,2,0,1:T(8,128)(2,1)S(1)} %maximum_select_fusion.7), channel_id=1, source_target_pairs={{0,8},{4,12},{8,0},{12,4},{16,24},{20,28},{24,16},{28,20},{1,9},{5... | collective-permute-start | bytes 393224 | tf_op jit(solution)/shard_map/ppermute | solution.py:13
  13.6 6.3 %collective-permute-start.2 = (bf16[4,1,16,1024]{3,2,0,1:T(8,128)(2,1)S(1)}, bf16[4,1,16,1024]{3,2,0,1:T(8,128)(2,1)S(1)}, u32[]{:S(2)}, u32[]{:S(2)}) collective-permute-start(bf16[4,1,16,1024]{3,2,0,1:T(8,128)(2,1)S(1)} %bitcast.173), channel_id=1, source_target_pairs={{0,4},{4,0},{8,12},{12,8},{16,20},{20,16},{24,28},{28,24},{1,5},{5... | collective-permute-start | bytes 393224 | tf_op jit(solution)/shard_map/ppermute | solution.py:13
  16.3 7.5 %collective-permute-start.7 = (bf16[4,1,32,1024]{3,2,0,1:T(8,128)(2,1)S(1)}, bf16[4,1,32,1024]{3,2,0,1:T(8,128)(2,1)S(1)}, u32[]{:S(2)}, u32[]{:S(2)}) collective-permute-start(bf16[4,1,32,1024]{3,2,0,1:T(8,128)(2,1)S(1)} %bitcast.169), channel_id=1, source_target_pairs={{0,4},{4,0},{8,12},{12,8},{16,20},{20,16},{24,28},{28,24},{1,5},{5... | collective-permute-start | bytes 786440 | tf_op jit(solution)/shard_map/ppermute | solution.py:13
  20.7 6.4 %collective-permute-start.3 = (bf16[1,8,16,1024]{3,2,1,0:T(8,128)(2,1)S(1)}, bf16[1,8,16,1024]{3,2,1,0:T(8,128)(2,1)S(1)}, u32[]{:S(2)}, u32[]{:S(2)}) collective-permute-start(bf16[1,8,16,1024]{3,2,1,0:T(8,128)(2,1)S(1)} %bitcast_select_fusion), channel_id=1, source_target_pairs={{0,2},{1,3},{2,0},{3,1},{4,6},{5,7},{6,4},{7,5},{8,10},{9,11},{10,... | collective-permute-start | bytes 786440 | tf_op jit(solution)/shard_map/ppermute | solution.py:13
  27.1 0.7 copy-start.5
  27.2 5.1 %collective-permute-start.4 = (bf16[2,8,16,1024]{3,2,1,0:T(8,128)(2,1)S(1)}, bf16[2,8,16,1024]{3,2,1,0:T(8,128)(2,1)S(1)}, u32[]{:S(2)}, u32[]{:S(2)}) collective-permute-start(bf16[2,8,16,1024]{3,2,1,0:T(8,128)(2,1)S(1)} %maximum_select_fusion.2), channel_id=1, source_target_pairs={{0,1},{1,0},{2,3},{3,2},{4,5},{5,4},{6,7},{7,6},{8,9},{9,8},{10,11... | collective-permute-start | bytes 1572872 | tf_op jit(solution)/shard_map/ppermute | solution.py:13
  27.8 4.4 %copy-start.6 = (bf16[1,8,16,1024]{3,2,1,0:T(8,128)(2,1)S(1)}, bf16[1,8,16,1024]{3,2,1,0:T(8,128)(2,1)}, u32[]{:S(2)}) copy-start(bf16[1,8,16,1024]{3,2,1,0:T(8,128)(2,1)} %copy-done.5) | copy-start | bytes 786436
  38.2 9.4 %slice-start = ((s8[8388608]{0:T(1024)(128)(4,1)}), s8[4194304]{0:T(1024)(128)(4,1)S(1)}, s32[]{:S(2)}) async-start(s8[8388608]{0:T(1024)(128)(4,1)} %bitcast.181), calls=%async_computation | async-start | bytes 8388608
  39.7 7.9 %slice-start.1 = ((s8[8388608]{0:T(1024)(128)(4,1)}), s8[4194304]{0:T(1024)(128)(4,1)S(1)}, s32[]{:S(2)}) async-start(s8[8388608]{0:T(1024)(128)(4,1)} %bitcast.181), calls=%async_computation.1 | async-start | bytes 8388608
  47.6 4.5 %copy-start.2 = (bf16[2,8,32,1024]{3,2,1,0:T(8,128)(2,1)S(1)}, bf16[2,8,32,1024]{3,2,1,0:T(8,128)(2,1)}, u32[]{:S(2)}) copy-start(bf16[2,8,32,1024]{3,2,1,0:T(8,128)(2,1)} %get-tuple-element.36) | copy-start | bytes 3145732
  47.6 5.0 %copy-start.1 = (bf16[2,8,32,1024]{3,2,1,0:T(8,128)(2,1)S(1)}, bf16[2,8,32,1024]{3,2,1,0:T(8,128)(2,1)}, u32[]{:S(2)}) copy-start(bf16[2,8,32,1024]{3,2,1,0:T(8,128)(2,1)} %get-tuple-element.37) | copy-start | bytes 3145732
  52.1 1.2 %copy-start = (bf16[2,8,32,1024]{3,2,1,0:T(8,128)(2,1)S(1)}, bf16[2,8,32,1024]{3,2,1,0:T(8,128)(2,1)}, u32[]{:S(2)}) copy-start(bf16[2,8,32,1024]{3,2,1,0:T(8,128)(2,1)} %get-tuple-element.22) | copy-start | bytes 3145732
  53.2 2.7 %collective-permute-start.8 = (f32[2,2,256,256]{3,2,1,0:T(8,128)S(1)}, f32[2,2,256,256]{3,2,1,0:T(8,128)S(1)}, u32[]{:S(2)}, u32[]{:S(2)}) collective-permute-start(f32[2,2,256,256]{3,2,1,0:T(8,128)S(1)} %pad_maximum_fusion), channel_id=1, source_target_pairs={{0,1},{1,0},{2,3},{3,2},{4,5},{5,4},{6,7},{7,6},{8,9},{9,8},{10,11... | collective-permute-start | bytes 3145736 | tf_op jit(solution)/shard_map/ppermute | solution.py:13
  53.9 2.0 %copy-start.4 = (bf16[2,8,32,1024]{3,2,1,0:T(8,128)(2,1)S(1)}, bf16[2,8,32,1024]{3,2,1,0:T(8,128)(2,1)}, u32[]{:S(2)}) copy-start(bf16[2,8,32,1024]{3,2,1,0:T(8,128)(2,1)} %get-tuple-element.38) | copy-start | bytes 3145732
  54.5 4.4 %copy-start.3 = (bf16[2,8,32,1024]{3,2,1,0:T(8,128)(2,1)S(1)}, bf16[2,8,32,1024]{3,2,1,0:T(8,128)(2,1)}, u32[]{:S(2)}) copy-start(bf16[2,8,32,1024]{3,2,1,0:T(8,128)(2,1)} %get-tuple-element.21) | copy-start | bytes 3145732
  54.5 4.4 %collective-permute-start.10 = (f32[2,2,256,256]{3,2,1,0:T(8,128)S(1)}, f32[2,2,256,256]{3,2,1,0:T(8,128)S(1)}, u32[]{:S(2)}, u32[]{:S(2)}) collective-permute-start(f32[2,2,256,256]{3,2,1,0:T(8,128)S(1)} %pad_maximum_fusion.1), channel_id=1, source_target_pairs={{0,1},{1,0},{2,3},{3,2},{4,5},{5,4},{6,7},{7,6},{8,9},{9,8},{10,11... | collective-permute-start | bytes 3145736 | tf_op jit(solution)/shard_map/ppermute | solution.py:13
  56.5 9.2 %collective-permute-start.9 = (bf16[1,2,256,256]{3,2,1,0:T(8,128)(2,1)S(1)}, bf16[1,2,256,256]{3,2,1,0:T(8,128)(2,1)S(1)}, u32[]{:S(2)}, u32[]{:S(2)}) collective-permute-start(bf16[1,2,256,256]{3,2,1,0:T(8,128)(2,1)S(1)} %fusion.18), channel_id=1, source_target_pairs={{0,2},{1,3},{2,0},{3,1},{4,6},{5,7},{6,4},{7,5},{8,10},{9,11},{10,... | collective-permute-start | bytes 786440 | tf_op jit(solution)/shard_map/ppermute | solution.py:13
  59.5 11.2 %collective-permute-start.11 = (bf16[1,2,256,256]{3,2,1,0:T(8,128)(2,1)S(1)}, bf16[1,2,256,256]{3,2,1,0:T(8,128)(2,1)S(1)}, u32[]{:S(2)}, u32[]{:S(2)}) collective-permute-start(bf16[1,2,256,256]{3,2,1,0:T(8,128)(2,1)S(1)} %fusion.19), channel_id=1, source_target_pairs={{0,2},{1,3},{2,0},{3,1},{4,6},{5,7},{6,4},{7,5},{8,10},{9,11},{10,... | collective-permute-start | bytes 786440 | tf_op jit(solution)/shard_map/ppermute | solution.py:13

commit v9 on v7

--- a/solution.py
+++ b/solution.py
@@ -52,14 +52,15 @@
 
 
 def screened_of(valence_a, valence_b, screening):
-    chunk = valence_a.shape[0]
+    col_count, chunk, _, mu_cols = valence_a.shape
     valence_a = valence_a.astype(jnp.float32)
     valence_b = valence_b.astype(jnp.float32)
-    val_pairs = (valence_a[:, :, None, :] * valence_b[:, None, :, :]).astype(jnp.bfloat16)
-    val_pairs = val_pairs.reshape(chunk * NV * NV, valence_a.shape[2])
-    screened = jnp.dot(val_pairs, screening, preferred_element_type=jnp.float32).astype(
-        jnp.bfloat16
-    )
+    val_pairs = (valence_a[:, :, :, None, :] * valence_b[:, :, None, :, :]).astype(jnp.bfloat16)
+    val_pairs = val_pairs.reshape(col_count, chunk * NV * NV, mu_cols)
+    screen = screening.reshape(col_count, mu_cols, screening.shape[1])
+    screened = lax.dot_general(
+        val_pairs, screen, (((0, 2), (0, 1)), ((), ())), preferred_element_type=jnp.float32
+    ).astype(jnp.bfloat16)
     return screened.reshape(chunk, NV * NV, screening.shape[1])
 
 
@@ -81,16 +82,16 @@
     )
 
     valence = gather_axis(jnp.take(held_valence, wanted, axis=0), "col")
-    valence = jnp.transpose(valence, (1, 2, 0, 3)).reshape(
-        2 * pair_count, NV, col_count * mu_cols
-    )
     conduction = jnp.take(held_conduction, wanted, axis=0).astype(jnp.float32)
     rows_per_block = NC // col_count
     chunk = pair_count // PAIR_CHUNKS
     starts = list(range(0, pair_count, chunk))
 
     def valence_of(first):
-        return valence[first : first + chunk], valence[pair_count + first : pair_count + first + chunk]
+        return (
+            valence[:, first : first + chunk],
+            valence[:, pair_count + first : pair_count + first + chunk],
+        )
 
     results = []
     screened = screened_of(*valence_of(starts[0]), screening[0])

time: 78.7 us -> 63.4 us (0.81)
  local copies, waits for them, and re-layouts: 13.3 us -> 3.95 us
  other arithmetic: 13.8 us -> 10.6 us
  matrix products: 15.7 us -> 12.8 us
    convert_element_type x4 -> x0, local copies, waits for them, and re-layouts: 8.87 us -> none  [the longest x2 4.44 us: screened_of(): valence_a = valence_a.astype(jnp.float32)]
    dot_general x2, matrix products: 12 us -> 9.05 us  [screened_of(): lax.dot_general(val_pairs, screen, (((0, 2), (0, 1)), ((), ())), preferre...]
    convert_element_type x1, other arithmetic: 1.71 us -> 0.21 us  [screened_of(): valence_a = valence_a.astype(jnp.float32)]
    convert_element_type x1, other arithmetic: 4.34 us -> 3.07 us  [own_block(): (rows[:, :, None, :] * cond_b[:, None, :, :]).astype(jnp.bfloat16)]
    convert_element_type x2 -> x1, other arithmetic: 2.78 us -> 2.34 us  [screened_of(): (valence_a[:, :, :, None, :] * valence_b[:, :, None, :, :]).astype(jnp.bf...]
  transfers between devices with their start and end apart: 12 -> 12, of which waited for: 9 -> 9; matrix products, arithmetic and copies ran while one was open for 17% -> 18% of each run, Pallas kernels for 0% -> 0%
where the time goes in v9:
time: 63.4 us; the launch traced here: 63.1 us
  waiting for transfers between devices  19.4 us (31%)
  starting transfers between devices  16 us (25%)
  matrix products  12.8 us (20%)
  other arithmetic  10.6 us (17%)
  local copies, waits for them, and re-layouts  3.95 us (6%)
    ppermute x12, waiting for transfers between devices, swap(): return lax.ppermute(x, axis, [(i, i ^ bit) for i in range(size)])  19.4 us
    ppermute x12, starting transfers between devices, swap(): return lax.ppermute(x, axis, [(i, i ^ bit) for i in range(size)])  16 us
    dot_general x2, matrix products, screened_of(): lax.dot_general(val_pairs, screen, (((0, 2), (0, 1)), ((), ())), preferre...  9.05 us
    dot_general x8, matrix products, own_block(): jnp.einsum('pan,pbn->pab', screened, cond_pairs, preferred_element_type=j...  3.74 us
    convert_element_type x1, other arithmetic, own_block(): (rows[:, :, None, :] * cond_b[:, None, :, :]).astype(jnp.bfloat16)  3.07 us
    convert_element_type x1, other arithmetic, screened_of(): (valence_a[:, :, :, None, :] * valence_b[:, :, None, :, :]).astype(jnp.bf...  2.34 us
    another operation x2, local copies, waits for them, and re-layouts, gather_axis(): cur = jnp.where(low, jnp.stack([cur, got], 1), jnp.stack([got, cur], 1))  1.61 us
  transfers between devices with their start and end apart: 12, of which 9 were waited for; matrix products, arithmetic and copies ran while one was open for 18% of the time, Pallas kernels for 0%

profile of v9, /device:TPU:0, one launch (start us, length us, event | category | flops | bytes accessed | tf_op | source)
XLA Modules:
  0.0 63.1 jit_solution(3881832081778883936)
XLA Ops:
  0.0 0.8 %slice_bitcast_fusion.7 = (bf16[1,1,1,16,1024]{4,3,2,1,0:T(8,128)(2,1)S(1)}, bf16[1,1,16,1024]{3,2,0,1:T(8,128)(2,1)S(1)}) fusion(bf16[1,48,1024]{2,1,0:T(8,128)(2,1)} %param.3), kind=kLoop, calls=%fused_computation.59 | loop fusion | bytes 98304 | tf_op jit(solution)/shard_map/stack | solution.py:24
  0.8 4.0 %collective-permute-start = (bf16[1,1,16,1024]{3,2,0,1:T(8,128)(2,1)S(1)}, bf16[1,1,16,1024]{3,2,0,1:T(8,128)(2,1)S(1)}, u32[]{:S(2)}, u32[]{:S(2)}) collective-permute-start(bf16[1,1,16,1024]{3,2,0,1:T(8,128)(2,1)S(1)} %get-tuple-element.32), channel_id=1, source_target_pairs={{0,16},{4,20},{8,24},{12,28},{16,0},{20,4},{24,8},{28,12},{1,17},{... | collective-permute-start | bytes 98312 | tf_op jit(solution)/shard_map/ppermute | solution.py:13
  4.8 0.8 %slice_bitcast_fusion.5 = (bf16[1,1,1,32,1024]{4,3,2,1,0:T(8,128)(2,1)S(1)}, bf16[1,1,32,1024]{3,2,0,1:T(8,128)(2,1)S(1)}) fusion(bf16[1,48,1024]{2,1,0:T(8,128)(2,1)} %param.3), kind=kLoop, calls=%fused_computation.57 | loop fusion | bytes 196608 | tf_op jit(solution)/shard_map/stack | solution.py:24
  5.7 0.7 %fusion.38 = s32[4,1]{0,1:T(1,128)S(1)} fusion(s32[]{:T(128)S(6)} %axis_index.17, s32[1,4]{1,0:T(1,128)} %param.5), kind=kLoop, calls=%fused_computation.81 | loop fusion | flops 48 | bytes 36 | tf_op jit(solution)/shard_map/concatenate | solution.py:78
  6.4 0.7 %and_select_fusion = s32[4]{0:T(128)S(1)} fusion(s32[]{:T(128)S(6)} %axis_index.17, s32[1,4]{1,0:T(1,128)} %param.5), kind=kLoop, calls=%fused_computation.74 | loop fusion | flops 48 | bytes 36 | tf_op jit(solution)/shard_map/jit(remainder)/select_n | solution.py:75
  7.1 0.7 %fusion.13 = s32[8]{0:T(128)S(1)} fusion(s32[4,1]{0,1:T(1,128)S(1)} %fusion.38, s32[4,1]{0,1:T(1,128)} %bitcast.176), kind=kLoop, calls=%fused_computation.76 | loop fusion | flops 32 | bytes 64 | tf_op jit(solution)/shard_map/jit(_take)/jit(_where)/select_n | solution.py:84
  7.8 0.7 %compare_and_fusion = pred[8]{0:T(512)(128)(4,1)S(1)} fusion(s32[4]{0:T(128)S(1)} %and_select_fusion, s32[4]{0:T(128)} %bitcast.177), kind=kLoop, calls=%fused_computation.73 | loop fusion | flops 56 | bytes 40 | tf_op jit(solution)/shard_map/jit(_take)/and | solution.py:84
  8.6 2.0 %collective-permute-start.1 = (bf16[2,1,16,1024]{3,2,0,1:T(8,128)(2,1)S(1)}, bf16[2,1,16,1024]{3,2,0,1:T(8,128)(2,1)S(1)}, u32[]{:S(2)}, u32[]{:S(2)}) collective-permute-start(bf16[2,1,16,1024]{3,2,0,1:T(8,128)(2,1)S(1)} %maximum_select_fusion.8), channel_id=1, source_target_pairs={{0,8},{4,12},{8,0},{12,4},{16,24},{20,28},{24,16},{28,20},{1,9},{5... | collective-permute-start | bytes 196616 | tf_op jit(solution)/shard_map/ppermute | solution.py:13
  10.5 0.7 %collective-permute-done.5 = bf16[1,1,32,1024]{3,2,0,1:T(8,128)(2,1)S(1)} collective-permute-done((bf16[1,1,32,1024]{3,2,0,1:T(8,128)(2,1)S(1)}, bf16[1,1,32,1024]{3,2,0,1:T(8,128)(2,1)S(1)}, u32[]{:S(2)}, u32[]{:S(2)}) %collective-permute-start.5) | collective-permute-done | bytes 65568 | tf_op jit(solution)/shard_map/ppermute | solution.py:13
  11.2 1.3 %collective-permute-start.6 = (bf16[2,1,32,1024]{3,2,0,1:T(8,128)(2,1)S(1)}, bf16[2,1,32,1024]{3,2,0,1:T(8,128)(2,1)S(1)}, u32[]{:S(2)}, u32[]{:S(2)}) collective-permute-start(bf16[2,1,32,1024]{3,2,0,1:T(8,128)(2,1)S(1)} %maximum_select_fusion.7), channel_id=1, source_target_pairs={{0,8},{4,12},{8,0},{12,4},{16,24},{20,28},{24,16},{28,20},{1,9},{5... | collective-permute-start | bytes 393224 | tf_op jit(solution)/shard_map/ppermute | solution.py:13
  12.5 1.0 %collective-permute-done.1 = bf16[2,1,16,1024]{3,2,0,1:T(8,128)(2,1)S(1)} collective-permute-done((bf16[2,1,16,1024]{3,2,0,1:T(8,128)(2,1)S(1)}, bf16[2,1,16,1024]{3,2,0,1:T(8,128)(2,1)S(1)}, u32[]{:S(2)}, u32[]{:S(2)}) %collective-permute-start.1) | collective-permute-done | bytes 65568 | tf_op jit(solution)/shard_map/ppermute | solution.py:13
  13.6 1.9 %collective-permute-start.2 = (bf16[4,1,16,1024]{3,2,0,1:T(8,128)(2,1)S(1)}, bf16[4,1,16,1024]{3,2,0,1:T(8,128)(2,1)S(1)}, u32[]{:S(2)}, u32[]{:S(2)}) collective-permute-start(bf16[4,1,16,1024]{3,2,0,1:T(8,128)(2,1)S(1)} %bitcast.164), channel_id=1, source_target_pairs={{0,4},{4,0},{8,12},{12,8},{16,20},{20,16},{24,28},{28,24},{1,5},{5... | collective-permute-start | bytes 393224 | tf_op jit(solution)/shard_map/ppermute | solution.py:13
  15.5 0.8 %collective-permute-done.6 = bf16[2,1,32,1024]{3,2,0,1:T(8,128)(2,1)S(1)} collective-permute-done((bf16[2,1,32,1024]{3,2,0,1:T(8,128)(2,1)S(1)}, bf16[2,1,32,1024]{3,2,0,1:T(8,128)(2,1)S(1)}, u32[]{:S(2)}, u32[]{:S(2)}) %collective-permute-start.6) | collective-permute-done | bytes 131104 | tf_op jit(solution)/shard_map/ppermute | solution.py:13
  16.3 1.6 %collective-permute-start.7 = (bf16[4,1,32,1024]{3,2,0,1:T(8,128)(2,1)S(1)}, bf16[4,1,32,1024]{3,2,0,1:T(8,128)(2,1)S(1)}, u32[]{:S(2)}, u32[]{:S(2)}) collective-permute-start(bf16[4,1,32,1024]{3,2,0,1:T(8,128)(2,1)S(1)} %bitcast.160), channel_id=1, source_target_pairs={{0,4},{4,0},{8,12},{12,8},{16,20},{20,16},{24,28},{28,24},{1,5},{5... | collective-permute-start | bytes 786440 | tf_op jit(solution)/shard_map/ppermute | solution.py:13
  17.9 2.0 %collective-permute-done.2 = bf16[4,1,16,1024]{3,2,0,1:T(8,128)(2,1)S(1)} collective-permute-done((bf16[4,1,16,1024]{3,2,0,1:T(8,128)(2,1)S(1)}, bf16[4,1,16,1024]{3,2,0,1:T(8,128)(2,1)S(1)}, u32[]{:S(2)}, u32[]{:S(2)}) %collective-permute-start.2) | collective-permute-done | bytes 131104 | tf_op jit(solution)/shard_map/ppermute | solution.py:13
  20.0 0.6 gather_fusion
  20.7 1.9 %collective-permute-start.3 = (bf16[1,8,16,1024]{3,2,1,0:T(8,128)(2,1)S(1)}, bf16[1,8,16,1024]{3,2,1,0:T(8,128)(2,1)S(1)}, u32[]{:S(2)}, u32[]{:S(2)}) collective-permute-start(bf16[1,8,16,1024]{3,2,1,0:T(8,128)(2,1)S(1)} %bitcast_select_fusion), channel_id=1, source_target_pairs={{0,2},{1,3},{2,0},{3,1},{4,6},{5,7},{6,4},{7,5},{8,10},{9,11},{10,... | collective-permute-start | bytes 786440 | tf_op jit(solution)/shard_map/ppermute | solution.py:13
  22.7 1.1 %collective-permute-done.7 = bf16[4,1,32,1024]{3,2,0,1:T(8,128)(2,1)S(1)} collective-permute-done((bf16[4,1,32,1024]{3,2,0,1:T(8,128)(2,1)S(1)}, bf16[4,1,32,1024]{3,2,0,1:T(8,128)(2,1)S(1)}, u32[]{:S(2)}, u32[]{:S(2)}) %collective-permute-start.7) | collective-permute-done | bytes 262176 | tf_op jit(solution)/shard_map/ppermute | solution.py:13
  24.0 0.6 gather_fusion.1
  24.9 2.2 %collective-permute-done.3 = bf16[1,8,16,1024]{3,2,1,0:T(8,128)(2,1)S(1)} collective-permute-done((bf16[1,8,16,1024]{3,2,1,0:T(8,128)(2,1)S(1)}, bf16[1,8,16,1024]{3,2,1,0:T(8,128)(2,1)S(1)}, u32[]{:S(2)}, u32[]{:S(2)}) %collective-permute-start.3) | collective-permute-done | bytes 262176 | tf_op jit(solution)/shard_map/ppermute | solution.py:13
  27.3 3.1 %multiply_convert_fusion.2 = (bf16[2,8,32,1024]{3,2,1,0:T(8,128)(2,1)S(1)}, bf16[2,8,32,1024]{3,2,1,0:T(8,128)(2,1)S(1)}, bf16[2,8,32,1024]{3,2,1,0:T(8,128)(2,1...) fusion(f32[2,8,1024]{2,1,0:T(8,128)S(1)} %get-tuple-element.25,, ...), kind=kLoop, calls=%fused_computation.6 | loop fusion | flops 8388608 | bytes 9437184 | tf_op jit(solution)/shard_map/convert_element_type | solution.py:105
  31.0 2.3 %multiply_convert_fusion = (bf16[4,2,16,16,1024]{4,3,2,1,0:T(8,128)(2,1)S(1)}, bf16[4,2,16,16,1024]{4,3,2,1,0:T(8,128)(2,1)S(1)}) fusion(f32[4,2,16,1024]{3,2,1,0:T(8,128)S(1)} %get-tuple-element.10, f32[4,2,16,1024]{3,2,1,0:T(8,128)S(1)} %get-tuple-element.11, f32[4,2,16,1024]{3,2,1,0:T(8,128)S(1)} %get-tuple-element.12, ...), kind=kLoop, calls=%fused_computation.2 | loop fusion | flops 8388608 | bytes 10485760 | tf_op jit(solution)/shard_map/convert_element_type | solution.py:58
  33.3 0.8 %slice-done.1 = s8[4194304]{0:T(1024)(128)(4,1)S(1)} async-done(((s8[8388608]{0:T(1024)(128)(4,1)}), s8[4194304]{0:T(1024)(128)(4,1)S(1)}, s32[]{:S(2)}) %slice-start.1) | async-done | bytes 4194328
  34.2 4.5 %bitcast_convert_fusion = bf16[512,1024]{1,0:T(8,128)(2,1)S(1)} fusion(bf16[4,512,1024]{2,1,0:T(8,128)(2,1)S(1)} %bitcast.155, bf16[4,1024,1024]{2,1,0:T(8,128)(2,1)S(1)} %bitcast.174), kind=kOutput, calls=%fused_computation.4 | convolution fusion | flops 4295491584 | bytes 13631488 | tf_op jit(solution)/shard_map/dot_general | solution.py:61
  38.7 4.5 %bitcast_convert_fusion.1 = bf16[512,1024]{1,0:T(8,128)(2,1)S(1)} fusion(bf16[4,512,1024]{2,1,0:T(8,128)(2,1)S(1)} %bitcast.154, bf16[4,1024,1024]{2,1,0:T(8,128)(2,1)S(1)} %bitcast.175), kind=kOutput, calls=%fused_computation.5 | convolution fusion | flops 4295491584 | bytes 13631488 | tf_op jit(solution)/shard_map/dot_general | solution.py:61
  44.3 0.6 collective-permute-start.8
  46.4 0.7 %collective-permute-done.8 = f32[2,2,256,256]{3,2,1,0:T(8,128)S(1)} collective-permute-done((f32[2,2,256,256]{3,2,1,0:T(8,128)S(1)}, f32[2,2,256,256]{3,2,1,0:T(8,128)S(1)}, u32[]{:S(2)}, u32[]{:S(2)}) %collective-permute-start.8) | collective-permute-done | bytes 1048608 | tf_op jit(solution)/shard_map/ppermute | solution.py:13
  47.6 1.9 %collective-permute-start.9 = (bf16[1,2,256,256]{3,2,1,0:T(8,128)(2,1)S(1)}, bf16[1,2,256,256]{3,2,1,0:T(8,128)(2,1)S(1)}, u32[]{:S(2)}, u32[]{:S(2)}) collective-permute-start(bf16[1,2,256,256]{3,2,1,0:T(8,128)(2,1)S(1)} %fusion.8), channel_id=1, source_target_pairs={{0,2},{1,3},{2,0},{3,1},{4,6},{5,7},{6,4},{7,5},{8,10},{9,11},{10,... | collective-permute-start | bytes 786440 | tf_op jit(solution)/shard_map/ppermute | solution.py:13
  50.5 0.5 collective-permute-start.11
  51.0 5.7 %collective-permute-done.9 = bf16[1,2,256,256]{3,2,1,0:T(8,128)(2,1)S(1)} collective-permute-done((bf16[1,2,256,256]{3,2,1,0:T(8,128)(2,1)S(1)}, bf16[1,2,256,256]{3,2,1,0:T(8,128)(2,1)S(1)}, u32[]{:S(2)}, u32[]{:S(2)}) %collective-permute-start.9) | collective-permute-done | bytes 262176 | tf_op jit(solution)/shard_map/ppermute | solution.py:13
  56.9 5.1 %collective-permute-done.11 = bf16[1,2,256,256]{3,2,1,0:T(8,128)(2,1)S(1)} collective-permute-done((bf16[1,2,256,256]{3,2,1,0:T(8,128)(2,1)S(1)}, bf16[1,2,256,256]{3,2,1,0:T(8,128)(2,1)S(1)}, u32[]{:S(2)}, u32[]{:S(2)}) %collective-permute-start.11) | collective-permute-done | bytes 262176 | tf_op jit(solution)/shard_map/ppermute | solution.py:13
  62.1 1.0 %maximum_bitcast_fusion = f32[1,4,256,256]{3,2,1,0:T(8,128)} fusion(f32[2,256,256]{2,1,0:T(8,128)S(1)} %fusion.3, f32[2,256,256]{2,1,0:T(8,128)S(1)} %fusion.7), kind=kLoop, calls=%fused_computation.21 | loop fusion | flops 262144 | bytes 2097152 | tf_op jit(solution)/shard_map/broadcast_in_dim | solution.py:119
  (44 shorter events, 5.7 us)
Async XLA Ops:
  0.8 7.8 %collective-permute-start = (bf16[1,1,16,1024]{3,2,0,1:T(8,128)(2,1)S(1)}, bf16[1,1,16,1024]{3,2,0,1:T(8,128)(2,1)S(1)}, u32[]{:S(2)}, u32[]{:S(2)}) collective-permute-start(bf16[1,1,16,1024]{3,2,0,1:T(8,128)(2,1)S(1)} %get-tuple-element.32), channel_id=1, source_target_pairs={{0,16},{4,20},{8,24},{12,28},{16,0},{20,4},{24,8},{28,12},{1,17},{... | collective-permute-start | bytes 98312 | tf_op jit(solution)/shard_map/ppermute | solution.py:13
  5.7 5.6 %collective-permute-start.5 = (bf16[1,1,32,1024]{3,2,0,1:T(8,128)(2,1)S(1)}, bf16[1,1,32,1024]{3,2,0,1:T(8,128)(2,1)S(1)}, u32[]{:S(2)}, u32[]{:S(2)}) collective-permute-start(bf16[1,1,32,1024]{3,2,0,1:T(8,128)(2,1)S(1)} %get-tuple-element.30), channel_id=1, source_target_pairs={{0,16},{4,20},{8,24},{12,28},{16,0},{20,4},{24,8},{28,12},{1,17},{... | collective-permute-start | bytes 196616 | tf_op jit(solution)/shard_map/ppermute | solution.py:13
  8.6 5.0 %collective-permute-start.1 = (bf16[2,1,16,1024]{3,2,0,1:T(8,128)(2,1)S(1)}, bf16[2,1,16,1024]{3,2,0,1:T(8,128)(2,1)S(1)}, u32[]{:S(2)}, u32[]{:S(2)}) collective-permute-start(bf16[2,1,16,1024]{3,2,0,1:T(8,128)(2,1)S(1)} %maximum_select_fusion.8), channel_id=1, source_target_pairs={{0,8},{4,12},{8,0},{12,4},{16,24},{20,28},{24,16},{28,20},{1,9},{5... | collective-permute-start | bytes 196616 | tf_op jit(solution)/shard_map/ppermute | solution.py:13
  11.2 5.0 %collective-permute-start.6 = (bf16[2,1,32,1024]{3,2,0,1:T(8,128)(2,1)S(1)}, bf16[2,1,32,1024]{3,2,0,1:T(8,128)(2,1)S(1)}, u32[]{:S(2)}, u32[]{:S(2)}) collective-permute-start(bf16[2,1,32,1024]{3,2,0,1:T(8,128)(2,1)S(1)} %maximum_select_fusion.7), channel_id=1, source_target_pairs={{0,8},{4,12},{8,0},{12,4},{16,24},{20,28},{24,16},{28,20},{1,9},{5... | collective-permute-start | bytes 393224 | tf_op jit(solution)/shard_map/ppermute | solution.py:13
  13.6 6.3 %collective-permute-start.2 = (bf16[4,1,16,1024]{3,2,0,1:T(8,128)(2,1)S(1)}, bf16[4,1,16,1024]{3,2,0,1:T(8,128)(2,1)S(1)}, u32[]{:S(2)}, u32[]{:S(2)}) collective-permute-start(bf16[4,1,16,1024]{3,2,0,1:T(8,128)(2,1)S(1)} %bitcast.164), channel_id=1, source_target_pairs={{0,4},{4,0},{8,12},{12,8},{16,20},{20,16},{24,28},{28,24},{1,5},{5... | collective-permute-start | bytes 393224 | tf_op jit(solution)/shard_map/ppermute | solution.py:13
  16.3 7.5 %collective-permute-start.7 = (bf16[4,1,32,1024]{3,2,0,1:T(8,128)(2,1)S(1)}, bf16[4,1,32,1024]{3,2,0,1:T(8,128)(2,1)S(1)}, u32[]{:S(2)}, u32[]{:S(2)}) collective-permute-start(bf16[4,1,32,1024]{3,2,0,1:T(8,128)(2,1)S(1)} %bitcast.160), channel_id=1, source_target_pairs={{0,4},{4,0},{8,12},{12,8},{16,20},{20,16},{24,28},{28,24},{1,5},{5... | collective-permute-start | bytes 786440 | tf_op jit(solution)/shard_map/ppermute | solution.py:13
  20.7 6.4 %collective-permute-start.3 = (bf16[1,8,16,1024]{3,2,1,0:T(8,128)(2,1)S(1)}, bf16[1,8,16,1024]{3,2,1,0:T(8,128)(2,1)S(1)}, u32[]{:S(2)}, u32[]{:S(2)}) collective-permute-start(bf16[1,8,16,1024]{3,2,1,0:T(8,128)(2,1)S(1)} %bitcast_select_fusion), channel_id=1, source_target_pairs={{0,2},{1,3},{2,0},{3,1},{4,6},{5,7},{6,4},{7,5},{8,10},{9,11},{10,... | collective-permute-start | bytes 786440 | tf_op jit(solution)/shard_map/ppermute | solution.py:13
  27.2 3.2 %collective-permute-start.4 = (bf16[2,8,16,1024]{3,2,1,0:T(8,128)(2,1)S(1)}, bf16[2,8,16,1024]{3,2,1,0:T(8,128)(2,1)S(1)}, u32[]{:S(2)}, u32[]{:S(2)}) collective-permute-start(bf16[2,8,16,1024]{3,2,1,0:T(8,128)(2,1)S(1)} %maximum_select_fusion.2), channel_id=1, source_target_pairs={{0,1},{1,0},{2,3},{3,2},{4,5},{5,4},{6,7},{7,6},{8,9},{9,8},{10,11... | collective-permute-start | bytes 1572872 | tf_op jit(solution)/shard_map/ppermute | solution.py:13
  30.6 2.7 %slice-start = ((s8[8388608]{0:T(1024)(128)(4,1)}), s8[4194304]{0:T(1024)(128)(4,1)S(1)}, s32[]{:S(2)}) async-start(s8[8388608]{0:T(1024)(128)(4,1)} %bitcast.172), calls=%async_computation | async-start | bytes 8388608
  31.0 3.2 %slice-start.1 = ((s8[8388608]{0:T(1024)(128)(4,1)}), s8[4194304]{0:T(1024)(128)(4,1)S(1)}, s32[]{:S(2)}) async-start(s8[8388608]{0:T(1024)(128)(4,1)} %bitcast.172), calls=%async_computation.1 | async-start | bytes 8388608
  44.3 2.8 %collective-permute-start.8 = (f32[2,2,256,256]{3,2,1,0:T(8,128)S(1)}, f32[2,2,256,256]{3,2,1,0:T(8,128)S(1)}, u32[]{:S(2)}, u32[]{:S(2)}) collective-permute-start(f32[2,2,256,256]{3,2,1,0:T(8,128)S(1)} %pad_maximum_fusion), channel_id=1, source_target_pairs={{0,1},{1,0},{2,3},{3,2},{4,5},{5,4},{6,7},{7,6},{8,9},{9,8},{10,11... | collective-permute-start | bytes 3145736 | tf_op jit(solution)/shard_map/ppermute | solution.py:13
  45.9 4.1 %collective-permute-start.10 = (f32[2,2,256,256]{3,2,1,0:T(8,128)S(1)}, f32[2,2,256,256]{3,2,1,0:T(8,128)S(1)}, u32[]{:S(2)}, u32[]{:S(2)}) collective-permute-start(f32[2,2,256,256]{3,2,1,0:T(8,128)S(1)} %pad_maximum_fusion.1), channel_id=1, source_target_pairs={{0,1},{1,0},{2,3},{3,2},{4,5},{5,4},{6,7},{7,6},{8,9},{9,8},{10,11... | collective-permute-start | bytes 3145736 | tf_op jit(solution)/shard_map/ppermute | solution.py:13
  47.6 9.2 %collective-permute-start.9 = (bf16[1,2,256,256]{3,2,1,0:T(8,128)(2,1)S(1)}, bf16[1,2,256,256]{3,2,1,0:T(8,128)(2,1)S(1)}, u32[]{:S(2)}, u32[]{:S(2)}) collective-permute-start(bf16[1,2,256,256]{3,2,1,0:T(8,128)(2,1)S(1)} %fusion.8), channel_id=1, source_target_pairs={{0,2},{1,3},{2,0},{3,1},{4,6},{5,7},{6,4},{7,5},{8,10},{9,11},{10,... | collective-permute-start | bytes 786440 | tf_op jit(solution)/shard_map/ppermute | solution.py:13
  50.5 11.5 %collective-permute-start.11 = (bf16[1,2,256,256]{3,2,1,0:T(8,128)(2,1)S(1)}, bf16[1,2,256,256]{3,2,1,0:T(8,128)(2,1)S(1)}, u32[]{:S(2)}, u32[]{:S(2)}) collective-permute-start(bf16[1,2,256,256]{3,2,1,0:T(8,128)(2,1)S(1)} %fusion.9), channel_id=1, source_target_pairs={{0,2},{1,3},{2,0},{3,1},{4,6},{5,7},{6,4},{7,5},{8,10},{9,11},{10,... | collective-permute-start | bytes 786440 | tf_op jit(solution)/shard_map/ppermute | solution.py:13

commit v10 on v9

--- a/solution.py
+++ b/solution.py
@@ -5,7 +5,7 @@
 
 NV = 16
 NC = 32
-PAIR_CHUNKS = 2
+PAIR_CHUNKS = 1
 
 
 def swap(x, axis, bit):

time: 63.4 us -> 73.8 us (1.16)
  other arithmetic: 10.6 us -> 15.8 us
  waiting for transfers between devices: 19.4 us -> 23.2 us
  matrix products: 12.8 us -> 14.9 us
    ppermute x12 -> x10, waiting for transfers between devices: 19.4 us -> 23.2 us  [swap(): return lax.ppermute(x, axis, [(i, i ^ bit) for i in range(size)])]
    dot_general x2 -> x1, matrix products: 9.05 us -> 11.5 us  [screened_of(): lax.dot_general(val_pairs, screen, (((0, 2), (0, 1)), ((), ())), preferre...]
    convert_element_type x1, other arithmetic: 3.07 us -> 5.43 us  [own_block(): (rows[:, :, None, :] * cond_b[:, None, :, :]).astype(jnp.bfloat16)]
    convert_element_type x1, other arithmetic: 2.34 us -> 4.28 us  [screened_of(): (valence_a[:, :, :, None, :] * valence_b[:, :, None, :, :]).astype(jnp.bf...]
    convert_element_type x1, other arithmetic: 0.21 us -> 1.15 us  [screened_of(): valence_a = valence_a.astype(jnp.float32)]
    ppermute x12 -> x10, starting transfers between devices: 16 us -> 15.4 us  [swap(): return lax.ppermute(x, axis, [(i, i ^ bit) for i in range(size)])]
    dot_general x8 -> x4, matrix products: 3.74 us -> 3.38 us  [own_block(): jnp.einsum('pan,pbn->pab', screened, cond_pairs, preferred_element_type=j...]
  transfers between devices with their start and end apart: 12 -> 10, of which waited for: 9 -> 8; matrix products, arithmetic and copies ran while one was open for 18% -> 16% of each run, Pallas kernels for 0% -> 0%
where the time goes in v10:
time: 73.8 us; the launch traced here: 73.5 us
  waiting for transfers between devices  23.2 us (31%)
  other arithmetic  15.8 us (21%)
  starting transfers between devices  15.4 us (21%)
  matrix products  14.9 us (20%)
  local copies, waits for them, and re-layouts  3.89 us (5%)
    ppermute x10, waiting for transfers between devices, swap(): return lax.ppermute(x, axis, [(i, i ^ bit) for i in range(size)])  23.2 us
    ppermute x10, starting transfers between devices, swap(): return lax.ppermute(x, axis, [(i, i ^ bit) for i in range(size)])  15.4 us
    dot_general x1, matrix products, screened_of(): lax.dot_general(val_pairs, screen, (((0, 2), (0, 1)), ((), ())), preferre...  11.5 us
    convert_element_type x1, other arithmetic, own_block(): (rows[:, :, None, :] * cond_b[:, None, :, :]).astype(jnp.bfloat16)  5.43 us
    convert_element_type x1, other arithmetic, screened_of(): (valence_a[:, :, :, None, :] * valence_b[:, :, None, :, :]).astype(jnp.bf...  4.28 us
    dot_general x4, matrix products, own_block(): jnp.einsum('pan,pbn->pab', screened, cond_pairs, preferred_element_type=j...  3.38 us
    another operation x2, local copies, waits for them, and re-layouts, gather_axis(): cur = jnp.where(low, jnp.stack([cur, got], 1), jnp.stack([got, cur], 1))  1.61 us
  transfers between devices with their start and end apart: 10, of which 8 were waited for; matrix products, arithmetic and copies ran while one was open for 16% of the time, Pallas kernels for 0%

profile of v10, /device:TPU:0, one launch (start us, length us, event | category | flops | bytes accessed | tf_op | source)
XLA Modules:
  0.0 73.5 jit_solution(1549564506032144001)
XLA Ops:
  0.0 0.8 %slice_bitcast_fusion.5 = (bf16[1,1,1,16,1024]{4,3,2,1,0:T(8,128)(2,1)S(1)}, bf16[1,1,16,1024]{3,2,0,1:T(8,128)(2,1)S(1)}) fusion(bf16[1,48,1024]{2,1,0:T(8,128)(2,1)} %param.3), kind=kLoop, calls=%fused_computation.41 | loop fusion | bytes 98304 | tf_op jit(solution)/shard_map/stack | solution.py:24
  0.8 4.0 %collective-permute-start = (bf16[1,1,16,1024]{3,2,0,1:T(8,128)(2,1)S(1)}, bf16[1,1,16,1024]{3,2,0,1:T(8,128)(2,1)S(1)}, u32[]{:S(2)}, u32[]{:S(2)}) collective-permute-start(bf16[1,1,16,1024]{3,2,0,1:T(8,128)(2,1)S(1)} %get-tuple-element.20), channel_id=1, source_target_pairs={{0,16},{4,20},{8,24},{12,28},{16,0},{20,4},{24,8},{28,12},{1,17},{... | collective-permute-start | bytes 98312 | tf_op jit(solution)/shard_map/ppermute | solution.py:13
  4.8 0.8 %slice_bitcast_fusion.3 = (bf16[1,1,1,32,1024]{4,3,2,1,0:T(8,128)(2,1)S(1)}, bf16[1,1,32,1024]{3,2,0,1:T(8,128)(2,1)S(1)}) fusion(bf16[1,48,1024]{2,1,0:T(8,128)(2,1)} %param.3), kind=kLoop, calls=%fused_computation.39 | loop fusion | bytes 196608 | tf_op jit(solution)/shard_map/stack | solution.py:24
  5.7 0.7 fusion.23
  6.4 0.7 and_select_fusion
  7.1 0.7 fusion.9
  7.8 0.7 compare_and_fusion
  8.6 2.0 %collective-permute-start.1 = (bf16[2,1,16,1024]{3,2,0,1:T(8,128)(2,1)S(1)}, bf16[2,1,16,1024]{3,2,0,1:T(8,128)(2,1)S(1)}, u32[]{:S(2)}, u32[]{:S(2)}) collective-permute-start(bf16[2,1,16,1024]{3,2,0,1:T(8,128)(2,1)S(1)} %maximum_select_fusion.8), channel_id=1, source_target_pairs={{0,8},{4,12},{8,0},{12,4},{16,24},{20,28},{24,16},{28,20},{1,9},{5... | collective-permute-start | bytes 196616 | tf_op jit(solution)/shard_map/ppermute | solution.py:13
  10.5 0.7 collective-permute-done.5
  11.2 1.3 %collective-permute-start.6 = (bf16[2,1,32,1024]{3,2,0,1:T(8,128)(2,1)S(1)}, bf16[2,1,32,1024]{3,2,0,1:T(8,128)(2,1)S(1)}, u32[]{:S(2)}, u32[]{:S(2)}) collective-permute-start(bf16[2,1,32,1024]{3,2,0,1:T(8,128)(2,1)S(1)} %maximum_select_fusion.7), channel_id=1, source_target_pairs={{0,8},{4,12},{8,0},{12,4},{16,24},{20,28},{24,16},{28,20},{1,9},{5... | collective-permute-start | bytes 393224 | tf_op jit(solution)/shard_map/ppermute | solution.py:13
  12.5 1.0 %collective-permute-done.1 = bf16[2,1,16,1024]{3,2,0,1:T(8,128)(2,1)S(1)} collective-permute-done((bf16[2,1,16,1024]{3,2,0,1:T(8,128)(2,1)S(1)}, bf16[2,1,16,1024]{3,2,0,1:T(8,128)(2,1)S(1)}, u32[]{:S(2)}, u32[]{:S(2)}) %collective-permute-start.1) | collective-permute-done | bytes 65568 | tf_op jit(solution)/shard_map/ppermute | solution.py:13
  13.6 1.9 %collective-permute-start.2 = (bf16[4,1,16,1024]{3,2,0,1:T(8,128)(2,1)S(1)}, bf16[4,1,16,1024]{3,2,0,1:T(8,128)(2,1)S(1)}, u32[]{:S(2)}, u32[]{:S(2)}) collective-permute-start(bf16[4,1,16,1024]{3,2,0,1:T(8,128)(2,1)S(1)} %bitcast.116), channel_id=1, source_target_pairs={{0,4},{4,0},{8,12},{12,8},{16,20},{20,16},{24,28},{28,24},{1,5},{5... | collective-permute-start | bytes 393224 | tf_op jit(solution)/shard_map/ppermute | solution.py:13
  15.5 0.8 %collective-permute-done.6 = bf16[2,1,32,1024]{3,2,0,1:T(8,128)(2,1)S(1)} collective-permute-done((bf16[2,1,32,1024]{3,2,0,1:T(8,128)(2,1)S(1)}, bf16[2,1,32,1024]{3,2,0,1:T(8,128)(2,1)S(1)}, u32[]{:S(2)}, u32[]{:S(2)}) %collective-permute-start.6) | collective-permute-done | bytes 131104 | tf_op jit(solution)/shard_map/ppermute | solution.py:13
  16.3 1.6 %collective-permute-start.7 = (bf16[4,1,32,1024]{3,2,0,1:T(8,128)(2,1)S(1)}, bf16[4,1,32,1024]{3,2,0,1:T(8,128)(2,1)S(1)}, u32[]{:S(2)}, u32[]{:S(2)}) collective-permute-start(bf16[4,1,32,1024]{3,2,0,1:T(8,128)(2,1)S(1)} %bitcast.112), channel_id=1, source_target_pairs={{0,4},{4,0},{8,12},{12,8},{16,20},{20,16},{24,28},{28,24},{1,5},{5... | collective-permute-start | bytes 786440 | tf_op jit(solution)/shard_map/ppermute | solution.py:13
  17.9 2.0 %collective-permute-done.2 = bf16[4,1,16,1024]{3,2,0,1:T(8,128)(2,1)S(1)} collective-permute-done((bf16[4,1,16,1024]{3,2,0,1:T(8,128)(2,1)S(1)}, bf16[4,1,16,1024]{3,2,0,1:T(8,128)(2,1)S(1)}, u32[]{:S(2)}, u32[]{:S(2)}) %collective-permute-start.2) | collective-permute-done | bytes 131104 | tf_op jit(solution)/shard_map/ppermute | solution.py:13
  20.7 1.9 %collective-permute-start.3 = (bf16[1,8,16,1024]{3,2,1,0:T(8,128)(2,1)S(1)}, bf16[1,8,16,1024]{3,2,1,0:T(8,128)(2,1)S(1)}, u32[]{:S(2)}, u32[]{:S(2)}) collective-permute-start(bf16[1,8,16,1024]{3,2,1,0:T(8,128)(2,1)S(1)} %bitcast_select_fusion), channel_id=1, source_target_pairs={{0,2},{1,3},{2,0},{3,1},{4,6},{5,7},{6,4},{7,5},{8,10},{9,11},{10,... | collective-permute-start | bytes 786440 | tf_op jit(solution)/shard_map/ppermute | solution.py:13
  22.7 1.1 %collective-permute-done.7 = bf16[4,1,32,1024]{3,2,0,1:T(8,128)(2,1)S(1)} collective-permute-done((bf16[4,1,32,1024]{3,2,0,1:T(8,128)(2,1)S(1)}, bf16[4,1,32,1024]{3,2,0,1:T(8,128)(2,1)S(1)}, u32[]{:S(2)}, u32[]{:S(2)}) %collective-permute-start.7) | collective-permute-done | bytes 262176 | tf_op jit(solution)/shard_map/ppermute | solution.py:13
  23.9 0.6 gather_fusion.1
  24.8 2.3 %collective-permute-done.3 = bf16[1,8,16,1024]{3,2,1,0:T(8,128)(2,1)S(1)} collective-permute-done((bf16[1,8,16,1024]{3,2,1,0:T(8,128)(2,1)S(1)}, bf16[1,8,16,1024]{3,2,1,0:T(8,128)(2,1)S(1)}, u32[]{:S(2)}, u32[]{:S(2)}) %collective-permute-start.3) | collective-permute-done | bytes 262176 | tf_op jit(solution)/shard_map/ppermute | solution.py:13
  27.3 5.4 %multiply_convert_fusion.1 = (bf16[4,8,32,1024]{3,2,1,0:T(8,128)(2,1)}, bf16[4,8,32,1024]{3,2,1,0:T(8,128)(2,1)}, bf16[4,8,32,1024]{3,2,1,0:T(8,128)(2,1)}, bf16[4,8,32,1024]{3,2,1,0:T(8,128)(2,1)}) fusion(f32[4,8,1024]{2,1,0:T(8,128)S(1)} %get-tuple-element.13, f32[4,32,1024]{2,1,0:T(8,128)S(1)} %get-tuple-element.6, ...), kind=kLoop, calls=%fused_computation.4 | loop fusion | flops 8388608 | bytes 9437184 | tf_op jit(solution)/shard_map/convert_element_type | solution.py:105
  33.1 1.1 %slice_convert_fusion.1 = (f32[4,4,16,1024]{3,2,1,0:T(8,128)S(1)}, f32[4,4,16,1024]{3,2,1,0:T(8,128)}) fusion(bf16[4,8,16,1024]{3,2,1,0:T(8,128)(2,1)S(1)} %bitcast.109), kind=kLoop, calls=%fused_computation.21 | loop fusion | flops 524288 | bytes 3145728 | tf_op jit(solution)/shard_map/convert_element_type | solution.py:56
  34.2 4.3 %multiply_convert_fusion = bf16[4,4,16,16,1024]{4,3,2,1,0:T(8,128)(2,1)S(1)} fusion(f32[4,4,16,1024]{3,2,1,0:T(8,128)} %get-tuple-element.8, f32[4,4,16,1024]{3,2,1,0:T(8,128)S(1)} %get-tuple-element.7), kind=kLoop, calls=%fused_computation.2 | loop fusion | flops 8388608 | bytes 10485760 | tf_op jit(solution)/shard_map/convert_element_type | solution.py:58
  38.5 11.5 %bitcast_convert_fusion = bf16[1024,1024]{1,0:T(8,128)(2,1)S(1)} fusion(bf16[4,1024,1024]{2,1,0:T(8,128)(2,1)S(1)} %bitcast.104, bf16[4,1024,1024]{2,1,0:T(8,128)(2,1)} %bitcast.124), kind=kOutput, calls=%fused_computation.3 | convolution fusion | flops 8590983168 | bytes 18874368 | tf_op jit(solution)/shard_map/dot_general | solution.py:61
  50.1 0.7 %convolution_bitcast_fusion.1 = f32[1,4,256,256]{3,2,1,0:T(8,128)S(1)} fusion(bf16[4,256,1024]{2,1,0:T(8,128)(2,1)S(1)} %bitcast.100, bf16[4,256,1024]{2,1,0:T(8,128)(2,1)S(1)} %bitcast.107), kind=kOutput, calls=%fused_computation.10 | convolution fusion | flops 536870912 | bytes 5242880 | tf_op jit(solution)/shard_map/pan,pbn->pab/dot_general | solution.py:107
  50.8 0.8 %copy-done.1 = bf16[4,8,32,1024]{3,2,1,0:T(8,128)(2,1)S(1)} copy-done((bf16[4,8,32,1024]{3,2,1,0:T(8,128)(2,1)S(1)}, bf16[4,8,32,1024]{3,2,1,0:T(8,128)(2,1)}, u32[]{:S(2)}) %copy-start.1) | copy-done | bytes 2097176
  51.7 0.7 %convolution_bitcast_fusion = f32[1,4,256,256]{3,2,1,0:T(8,128)S(1)} fusion(bf16[4,256,1024]{2,1,0:T(8,128)(2,1)S(1)} %bitcast.101, bf16[4,256,1024]{2,1,0:T(8,128)(2,1)S(1)} %bitcast.106), kind=kOutput, calls=%fused_computation.9 | convolution fusion | flops 536870912 | bytes 5242880 | tf_op jit(solution)/shard_map/pan,pbn->pab/dot_general | solution.py:107
  53.1 3.8 %collective-permute-done.8 = f32[2,4,256,256]{3,2,1,0:T(8,128)S(1)} collective-permute-done((f32[2,4,256,256]{3,2,1,0:T(8,128)S(1)}, f32[2,4,256,256]{3,2,1,0:T(8,128)S(1)}, u32[]{:S(2)}, u32[]{:S(2)}) %collective-permute-start.8) | collective-permute-done | bytes 2097184 | tf_op jit(solution)/shard_map/ppermute | solution.py:13
  56.9 1.0 %fusion.5 = bf16[1,4,256,256]{3,2,1,0:T(8,128)(2,1)S(1)} fusion(f32[2,4,256,256]{3,2,1,0:T(8,128)S(1)} %collective-permute-done.8, bf16[4,256,1024]{2,1,0:T(8,128)(2,1)S(1)} %bitcast.102, bf16[4,256,1024]{2,1,0:T(8,128)(2,1)S(1)} %bitcast.108), kind=kOutput, calls=%fused_computation.19 | convolution fusion | flops 537395200 | bytes 5767168 | tf_op jit(solution)/shard_map/pan,pbn->pab/dot_general | solution.py:107
  57.9 2.0 %collective-permute-start.9 = (bf16[1,4,256,256]{3,2,1,0:T(8,128)(2,1)S(1)}, bf16[1,4,256,256]{3,2,1,0:T(8,128)(2,1)S(1)}, u32[]{:S(2)}, u32[]{:S(2)}) collective-permute-start(bf16[1,4,256,256]{3,2,1,0:T(8,128)(2,1)S(1)} %fusion.5), channel_id=1, source_target_pairs={{0,2},{1,3},{2,0},{3,1},{4,6},{5,7},{6,4},{7,5},{8,10},{9,11},{10,... | collective-permute-start | bytes 1572872 | tf_op jit(solution)/shard_map/ppermute | solution.py:13
  59.9 1.0 %fusion.11 = f32[4,256,256]{2,1,0:T(8,128)S(1)} fusion(bf16[4,256,1024]{2,1,0:T(8,128)(2,1)S(1)} %bitcast.103, bf16[4,256,1024]{2,1,0:T(8,128)(2,1)S(1)} %bitcast.105), kind=kOutput, calls=%fused_computation.56 | convolution fusion | flops 536870912 | bytes 5242880 | tf_op jit(solution)/shard_map/pan,pbn->pab/dot_general | solution.py:107
  60.8 11.5 %collective-permute-done.9 = bf16[1,4,256,256]{3,2,1,0:T(8,128)(2,1)S(1)} collective-permute-done((bf16[1,4,256,256]{3,2,1,0:T(8,128)(2,1)S(1)}, bf16[1,4,256,256]{3,2,1,0:T(8,128)(2,1)S(1)}, u32[]{:S(2)}, u32[]{:S(2)}) %collective-permute-start.9) | collective-permute-done | bytes 524320 | tf_op jit(solution)/shard_map/ppermute | solution.py:13
  72.3 1.2 %fusion.4 = f32[1,4,256,256]{3,2,1,0:T(8,128)} fusion(f32[4,256,256]{2,1,0:T(8,128)S(1)} %fusion.11, f32[2,4,256,256]{3,2,1,0:T(8,128)S(1)} %collective-permute-done.8, bf16[1,4,256,256]{3,2,1,0:T(8,128)(2,1)S(1)} %collective-permute-done.9), kind=kLoop, calls=%fused_computation.17 | loop fusion | flops 786432 | bytes 3670016 | tf_op jit(solution)/shard_map/broadcast_in_dim | solution.py:119
  (34 shorter events, 2.6 us)
Async XLA Ops:
  0.8 7.8 %collective-permute-start = (bf16[1,1,16,1024]{3,2,0,1:T(8,128)(2,1)S(1)}, bf16[1,1,16,1024]{3,2,0,1:T(8,128)(2,1)S(1)}, u32[]{:S(2)}, u32[]{:S(2)}) collective-permute-start(bf16[1,1,16,1024]{3,2,0,1:T(8,128)(2,1)S(1)} %get-tuple-element.20), channel_id=1, source_target_pairs={{0,16},{4,20},{8,24},{12,28},{16,0},{20,4},{24,8},{28,12},{1,17},{... | collective-permute-start | bytes 98312 | tf_op jit(solution)/shard_map/ppermute | solution.py:13
  5.7 5.6 %collective-permute-start.5 = (bf16[1,1,32,1024]{3,2,0,1:T(8,128)(2,1)S(1)}, bf16[1,1,32,1024]{3,2,0,1:T(8,128)(2,1)S(1)}, u32[]{:S(2)}, u32[]{:S(2)}) collective-permute-start(bf16[1,1,32,1024]{3,2,0,1:T(8,128)(2,1)S(1)} %get-tuple-element.18), channel_id=1, source_target_pairs={{0,16},{4,20},{8,24},{12,28},{16,0},{20,4},{24,8},{28,12},{1,17},{... | collective-permute-start | bytes 196616 | tf_op jit(solution)/shard_map/ppermute | solution.py:13
  8.6 5.0 %collective-permute-start.1 = (bf16[2,1,16,1024]{3,2,0,1:T(8,128)(2,1)S(1)}, bf16[2,1,16,1024]{3,2,0,1:T(8,128)(2,1)S(1)}, u32[]{:S(2)}, u32[]{:S(2)}) collective-permute-start(bf16[2,1,16,1024]{3,2,0,1:T(8,128)(2,1)S(1)} %maximum_select_fusion.8), channel_id=1, source_target_pairs={{0,8},{4,12},{8,0},{12,4},{16,24},{20,28},{24,16},{28,20},{1,9},{5... | collective-permute-start | bytes 196616 | tf_op jit(solution)/shard_map/ppermute | solution.py:13
  11.2 5.0 %collective-permute-start.6 = (bf16[2,1,32,1024]{3,2,0,1:T(8,128)(2,1)S(1)}, bf16[2,1,32,1024]{3,2,0,1:T(8,128)(2,1)S(1)}, u32[]{:S(2)}, u32[]{:S(2)}) collective-permute-start(bf16[2,1,32,1024]{3,2,0,1:T(8,128)(2,1)S(1)} %maximum_select_fusion.7), channel_id=1, source_target_pairs={{0,8},{4,12},{8,0},{12,4},{16,24},{20,28},{24,16},{28,20},{1,9},{5... | collective-permute-start | bytes 393224 | tf_op jit(solution)/shard_map/ppermute | solution.py:13
  13.6 6.3 %collective-permute-start.2 = (bf16[4,1,16,1024]{3,2,0,1:T(8,128)(2,1)S(1)}, bf16[4,1,16,1024]{3,2,0,1:T(8,128)(2,1)S(1)}, u32[]{:S(2)}, u32[]{:S(2)}) collective-permute-start(bf16[4,1,16,1024]{3,2,0,1:T(8,128)(2,1)S(1)} %bitcast.116), channel_id=1, source_target_pairs={{0,4},{4,0},{8,12},{12,8},{16,20},{20,16},{24,28},{28,24},{1,5},{5... | collective-permute-start | bytes 393224 | tf_op jit(solution)/shard_map/ppermute | solution.py:13
  16.3 7.5 %collective-permute-start.7 = (bf16[4,1,32,1024]{3,2,0,1:T(8,128)(2,1)S(1)}, bf16[4,1,32,1024]{3,2,0,1:T(8,128)(2,1)S(1)}, u32[]{:S(2)}, u32[]{:S(2)}) collective-permute-start(bf16[4,1,32,1024]{3,2,0,1:T(8,128)(2,1)S(1)} %bitcast.112), channel_id=1, source_target_pairs={{0,4},{4,0},{8,12},{12,8},{16,20},{20,16},{24,28},{28,24},{1,5},{5... | collective-permute-start | bytes 786440 | tf_op jit(solution)/shard_map/ppermute | solution.py:13
  20.7 6.4 %collective-permute-start.3 = (bf16[1,8,16,1024]{3,2,1,0:T(8,128)(2,1)S(1)}, bf16[1,8,16,1024]{3,2,1,0:T(8,128)(2,1)S(1)}, u32[]{:S(2)}, u32[]{:S(2)}) collective-permute-start(bf16[1,8,16,1024]{3,2,1,0:T(8,128)(2,1)S(1)} %bitcast_select_fusion), channel_id=1, source_target_pairs={{0,2},{1,3},{2,0},{3,1},{4,6},{5,7},{6,4},{7,5},{8,10},{9,11},{10,... | collective-permute-start | bytes 786440 | tf_op jit(solution)/shard_map/ppermute | solution.py:13
  27.2 5.6 %collective-permute-start.4 = (bf16[2,8,16,1024]{3,2,1,0:T(8,128)(2,1)S(1)}, bf16[2,8,16,1024]{3,2,1,0:T(8,128)(2,1)S(1)}, u32[]{:S(2)}, u32[]{:S(2)}) collective-permute-start(bf16[2,8,16,1024]{3,2,1,0:T(8,128)(2,1)S(1)} %maximum_select_fusion.2), channel_id=1, source_target_pairs={{0,1},{1,0},{2,3},{3,2},{4,5},{5,4},{6,7},{7,6},{8,9},{9,8},{10,11... | collective-permute-start | bytes 1572872 | tf_op jit(solution)/shard_map/ppermute | solution.py:13
  38.5 11.5 %copy-start.2 = (bf16[4,8,32,1024]{3,2,1,0:T(8,128)(2,1)S(1)}, bf16[4,8,32,1024]{3,2,1,0:T(8,128)(2,1)}, u32[]{:S(2)}) copy-start(bf16[4,8,32,1024]{3,2,1,0:T(8,128)(2,1)} %get-tuple-element.10) | copy-start | bytes 6291460
  50.1 1.6 %copy-start.1 = (bf16[4,8,32,1024]{3,2,1,0:T(8,128)(2,1)S(1)}, bf16[4,8,32,1024]{3,2,1,0:T(8,128)(2,1)}, u32[]{:S(2)}) copy-start(bf16[4,8,32,1024]{3,2,1,0:T(8,128)(2,1)} %get-tuple-element.11) | copy-start | bytes 6291460
  52.4 4.5 %copy-start.3 = (bf16[4,8,32,1024]{3,2,1,0:T(8,128)(2,1)S(1)}, bf16[4,8,32,1024]{3,2,1,0:T(8,128)(2,1)}, u32[]{:S(2)}) copy-start(bf16[4,8,32,1024]{3,2,1,0:T(8,128)(2,1)} %get-tuple-element.9) | copy-start | bytes 6291460
  52.6 4.3 %collective-permute-start.8 = (f32[2,4,256,256]{3,2,1,0:T(8,128)S(1)}, f32[2,4,256,256]{3,2,1,0:T(8,128)S(1)}, u32[]{:S(2)}, u32[]{:S(2)}) collective-permute-start(f32[2,4,256,256]{3,2,1,0:T(8,128)S(1)} %pad_maximum_fusion), channel_id=1, source_target_pairs={{0,1},{1,0},{2,3},{3,2},{4,5},{5,4},{6,7},{7,6},{8,9},{9,8},{10,11... | collective-permute-start | bytes 6291464 | tf_op jit(solution)/shard_map/ppermute | solution.py:13
  56.9 2.9 %copy-start = (bf16[4,8,32,1024]{3,2,1,0:T(8,128)(2,1)S(1)}, bf16[4,8,32,1024]{3,2,1,0:T(8,128)(2,1)}, u32[]{:S(2)}) copy-start(bf16[4,8,32,1024]{3,2,1,0:T(8,128)(2,1)} %get-tuple-element.12) | copy-start | bytes 6291460
  57.9 14.4 %collective-permute-start.9 = (bf16[1,4,256,256]{3,2,1,0:T(8,128)(2,1)S(1)}, bf16[1,4,256,256]{3,2,1,0:T(8,128)(2,1)S(1)}, u32[]{:S(2)}, u32[]{:S(2)}) collective-permute-start(bf16[1,4,256,256]{3,2,1,0:T(8,128)(2,1)S(1)} %fusion.5), channel_id=1, source_target_pairs={{0,2},{1,3},{2,0},{3,1},{4,6},{5,7},{6,4},{7,5},{8,10},{9,11},{10,... | collective-permute-start | bytes 1572872 | tf_op jit(solution)/shard_map/ppermute | solution.py:13

commit v11 on v9

--- a/solution.py
+++ b/solution.py
@@ -13,18 +13,22 @@
     return lax.ppermute(x, axis, [(i, i ^ bit) for i in range(size)])
 
 
-def gather_axis(mine, axis):
+def gather_axis(mine, axis, tie=None):
     count = lax.axis_size(axis)
     me = lax.axis_index(axis)
     cur = mine[None]
     bit = count // 2
     while bit >= 1:
         got = swap(cur, axis, bit)
+        if tie is not None and bit > 1:
+            got, tie = lax.optimization_barrier((got, tie))
         low = (me & bit) == 0
         cur = jnp.where(low, jnp.stack([cur, got], 1), jnp.stack([got, cur], 1))
         cur = cur.reshape((-1,) + mine.shape)
         bit //= 2
-    return cur
+    if tie is None:
+        return cur
+    return cur, tie
 
 
 def scatter_sum_col(own_block, last_swap):
@@ -81,11 +85,25 @@
         kpoint_count, orb_count - NV, mu_cols
     )
 
-    valence = gather_axis(jnp.take(held_valence, wanted, axis=0), "col")
     conduction = jnp.take(held_conduction, wanted, axis=0).astype(jnp.float32)
     rows_per_block = NC // col_count
     chunk = pair_count // PAIR_CHUNKS
     starts = list(range(0, pair_count, chunk))
+
+    def cond_block(first, delta):
+        cond_a = conduction[first : first + chunk]
+        cond_b = conduction[pair_count + first : pair_count + first + chunk]
+        rows = lax.dynamic_slice_in_dim(
+            cond_a, (col_index ^ delta) * rows_per_block, rows_per_block, 1
+        )
+        cond_pairs = (rows[:, :, None, :] * cond_b[:, None, :, :]).astype(jnp.bfloat16)
+        return cond_pairs.reshape(chunk, rows_per_block * NC, mu_cols)
+
+    cond_blocks = [[cond_block(first, d) for d in range(col_count)] for first in starts]
+
+    valence, cond_blocks = gather_axis(
+        jnp.take(held_valence, wanted, axis=0), "col", tie=cond_blocks
+    )
 
     def valence_of(first):
         return (
@@ -96,14 +114,9 @@
     results = []
     screened = screened_of(*valence_of(starts[0]), screening[0])
     for n_chunk, first in enumerate(starts):
-        cond_a = conduction[first : first + chunk]
-        cond_b = conduction[pair_count + first : pair_count + first + chunk]
 
-        def own_block(delta, screened=screened, cond_a=cond_a, cond_b=cond_b):
-            block = col_index ^ delta
-            rows = lax.dynamic_slice_in_dim(cond_a, block * rows_per_block, rows_per_block, 1)
-            cond_pairs = (rows[:, :, None, :] * cond_b[:, None, :, :]).astype(jnp.bfloat16)
-            cond_pairs = cond_pairs.reshape(chunk, rows_per_block * NC, mu_cols)
+        def own_block(delta, screened=screened, blocks=cond_blocks[n_chunk]):
+            cond_pairs = blocks[delta]
             return jnp.einsum(
                 "pan,pbn->pab", screened, cond_pairs, preferred_element_type=jnp.float32
             )

time: 63.4 us -> 69.3 us (1.093)
  other arithmetic: 10.6 us -> 17.2 us
  waiting for transfers between devices: 19.4 us -> 16 us
  matrix products: 12.8 us -> 15.8 us
  local copies, waits for them, and re-layouts: 3.95 us -> 3.11 us
    select_n x11, other arithmetic: 0.52 us -> 4.76 us  [gather_axis(): cur = jnp.where(low, jnp.stack([cur, got], 1), jnp.stack([got, cur], 1))]
    ppermute x12, waiting for transfers between devices: 19.4 us -> 16 us  [swap(): return lax.ppermute(x, axis, [(i, i ^ bit) for i in range(size)])]
    dot_general x2, matrix products: 9.05 us -> 12 us  [screened_of(): lax.dot_general(val_pairs, screen, (((0, 2), (0, 1)), ((), ())), preferre...]
    convert_element_type x1, other arithmetic: 3.07 us -> 4.34 us  [cond_block(): (rows[:, :, None, :] * cond_b[:, None, :, :]).astype(jnp.bfloat16)]
    unnamed x4 -> x14, local copies, waits for them, and re-layouts: 0.86 us -> 0.04 us
    select_n x2, other arithmetic: 0.82 us -> 1.52 us  [body(): jnp.take(held_valence, wanted, axis=0)]
    convert_element_type x1 -> x2, other arithmetic: 2.34 us -> 2.8 us  [screened_of(): (valence_a[:, :, :, None, :] * valence_b[:, :, None, :, :]).astype(jnp.bf...]
  transfers between devices with their start and end apart: 12 -> 12, of which waited for: 9 -> 9; matrix products, arithmetic and copies ran while one was open for 18% -> 29% of each run, Pallas kernels for 0% -> 0%
where the time goes in v11:
time: 69.3 us; the launch traced here: 69 us
  other arithmetic  17.2 us (25%)
  starting transfers between devices  16.6 us (24%)
  waiting for transfers between devices  16 us (23%)
  matrix products  15.8 us (23%)
  local copies, waits for them, and re-layouts  3.11 us (4%)
    ppermute x12, starting transfers between devices, swap(): return lax.ppermute(x, axis, [(i, i ^ bit) for i in range(size)])  16.6 us
    ppermute x12, waiting for transfers between devices, swap(): return lax.ppermute(x, axis, [(i, i ^ bit) for i in range(size)])  16 us
    dot_general x2, matrix products, screened_of(): lax.dot_general(val_pairs, screen, (((0, 2), (0, 1)), ((), ())), preferre...  12 us
    select_n x11, other arithmetic, gather_axis(): cur = jnp.where(low, jnp.stack([cur, got], 1), jnp.stack([got, cur], 1))  4.76 us
    convert_element_type x1, other arithmetic, cond_block(): (rows[:, :, None, :] * cond_b[:, None, :, :]).astype(jnp.bfloat16)  4.34 us
    dot_general x8, matrix products, own_block(): jnp.einsum('pan,pbn->pab', screened, cond_pairs, preferred_element_type=j...  3.77 us
    convert_element_type x2, other arithmetic, screened_of(): (valence_a[:, :, :, None, :] * valence_b[:, :, None, :, :]).astype(jnp.bf...  2.8 us
    another operation x2, local copies, waits for them, and re-layouts, gather_axis(): cur = jnp.where(low, jnp.stack([cur, got], 1), jnp.stack([got, cur], 1))  1.61 us
  transfers between devices with their start and end apart: 12, of which 9 were waited for; matrix products, arithmetic and copies ran while one was open for 29% of the time, Pallas kernels for 0%

profile of v11, /device:TPU:0, one launch (start us, length us, event | category | flops | bytes accessed | tf_op | source)
XLA Modules:
  0.0 69.0 jit_solution(4023723803461993177)
XLA Ops:
  0.0 0.8 %slice_bitcast_fusion.7 = (bf16[1,1,1,16,1024]{4,3,2,1,0:T(8,128)(2,1)S(1)}, bf16[1,1,16,1024]{3,2,0,1:T(8,128)(2,1)S(1)}) fusion(bf16[1,48,1024]{2,1,0:T(8,128)(2,1)} %param.3), kind=kLoop, calls=%fused_computation.59 | loop fusion | bytes 98304 | tf_op jit(solution)/shard_map/stack | solution.py:26
  0.8 4.0 %collective-permute-start = (bf16[1,1,16,1024]{3,2,0,1:T(8,128)(2,1)S(1)}, bf16[1,1,16,1024]{3,2,0,1:T(8,128)(2,1)S(1)}, u32[]{:S(2)}, u32[]{:S(2)}) collective-permute-start(bf16[1,1,16,1024]{3,2,0,1:T(8,128)(2,1)S(1)} %get-tuple-element.50), channel_id=1, source_target_pairs={{0,16},{4,20},{8,24},{12,28},{16,0},{20,4},{24,8},{28,12},{1,17},{... | collective-permute-start | bytes 98312 | tf_op jit(solution)/shard_map/ppermute | solution.py:13
  4.8 0.8 %slice_bitcast_fusion.5 = (bf16[1,1,1,32,1024]{4,3,2,1,0:T(8,128)(2,1)S(1)}, bf16[1,1,32,1024]{3,2,0,1:T(8,128)(2,1)S(1)}) fusion(bf16[1,48,1024]{2,1,0:T(8,128)(2,1)} %param.3), kind=kLoop, calls=%fused_computation.57 | loop fusion | bytes 196608 | tf_op jit(solution)/shard_map/stack | solution.py:26
  5.7 0.7 fusion.32
  6.4 0.7 and_select_fusion
  7.1 0.7 %fusion.9 = s32[8]{0:T(128)S(1)} fusion(s32[4,1]{0,1:T(1,128)S(1)} %fusion.32, s32[4,1]{0,1:T(1,128)} %bitcast.162), kind=kLoop, calls=%fused_computation.76 | loop fusion | flops 32 | bytes 64 | tf_op jit(solution)/shard_map/jit(_take)/jit(_where)/select_n | solution.py:105
  7.8 0.7 %compare_and_fusion = pred[8]{0:T(512)(128)(4,1)S(1)} fusion(s32[4]{0:T(128)S(1)} %and_select_fusion, s32[4]{0:T(128)} %bitcast.163), kind=kLoop, calls=%fused_computation.73 | loop fusion | flops 56 | bytes 40 | tf_op jit(solution)/shard_map/jit(_take)/and | solution.py:105
  8.6 2.0 %collective-permute-start.1 = (bf16[2,1,16,1024]{3,2,0,1:T(8,128)(2,1)S(1)}, bf16[2,1,16,1024]{3,2,0,1:T(8,128)(2,1)S(1)}, u32[]{:S(2)}, u32[]{:S(2)}) collective-permute-start(bf16[2,1,16,1024]{3,2,0,1:T(8,128)(2,1)S(1)} %maximum_select_fusion.8), channel_id=1, source_target_pairs={{0,8},{4,12},{8,0},{12,4},{16,24},{20,28},{24,16},{28,20},{1,9},{5... | collective-permute-start | bytes 196616 | tf_op jit(solution)/shard_map/ppermute | solution.py:13
  10.5 0.7 %collective-permute-done.4 = bf16[1,1,32,1024]{3,2,0,1:T(8,128)(2,1)S(1)} collective-permute-done((bf16[1,1,32,1024]{3,2,0,1:T(8,128)(2,1)S(1)}, bf16[1,1,32,1024]{3,2,0,1:T(8,128)(2,1)S(1)}, u32[]{:S(2)}, u32[]{:S(2)}) %collective-permute-start.4) | collective-permute-done | bytes 65568 | tf_op jit(solution)/shard_map/ppermute | solution.py:13
  11.2 1.3 %collective-permute-start.5 = (bf16[2,1,32,1024]{3,2,0,1:T(8,128)(2,1)S(1)}, bf16[2,1,32,1024]{3,2,0,1:T(8,128)(2,1)S(1)}, u32[]{:S(2)}, u32[]{:S(2)}) collective-permute-start(bf16[2,1,32,1024]{3,2,0,1:T(8,128)(2,1)S(1)} %maximum_select_fusion.7), channel_id=1, source_target_pairs={{0,8},{4,12},{8,0},{12,4},{16,24},{20,28},{24,16},{28,20},{1,9},{5... | collective-permute-start | bytes 393224 | tf_op jit(solution)/shard_map/ppermute | solution.py:13
  12.5 1.0 %collective-permute-done.1 = bf16[2,1,16,1024]{3,2,0,1:T(8,128)(2,1)S(1)} collective-permute-done((bf16[2,1,16,1024]{3,2,0,1:T(8,128)(2,1)S(1)}, bf16[2,1,16,1024]{3,2,0,1:T(8,128)(2,1)S(1)}, u32[]{:S(2)}, u32[]{:S(2)}) %collective-permute-start.1) | collective-permute-done | bytes 65568 | tf_op jit(solution)/shard_map/ppermute | solution.py:13
  13.6 1.9 %collective-permute-start.2 = (bf16[4,1,16,1024]{3,2,0,1:T(8,128)(2,1)S(1)}, bf16[4,1,16,1024]{3,2,0,1:T(8,128)(2,1)S(1)}, u32[]{:S(2)}, u32[]{:S(2)}) collective-permute-start(bf16[4,1,16,1024]{3,2,0,1:T(8,128)(2,1)S(1)} %bitcast.150), channel_id=1, source_target_pairs={{0,4},{4,0},{8,12},{12,8},{16,20},{20,16},{24,28},{28,24},{1,5},{5... | collective-permute-start | bytes 393224 | tf_op jit(solution)/shard_map/ppermute | solution.py:13
  15.5 0.8 %collective-permute-done.5 = bf16[2,1,32,1024]{3,2,0,1:T(8,128)(2,1)S(1)} collective-permute-done((bf16[2,1,32,1024]{3,2,0,1:T(8,128)(2,1)S(1)}, bf16[2,1,32,1024]{3,2,0,1:T(8,128)(2,1)S(1)}, u32[]{:S(2)}, u32[]{:S(2)}) %collective-permute-start.5) | collective-permute-done | bytes 131104 | tf_op jit(solution)/shard_map/ppermute | solution.py:13
  16.3 1.6 %collective-permute-start.6 = (bf16[4,1,32,1024]{3,2,0,1:T(8,128)(2,1)S(1)}, bf16[4,1,32,1024]{3,2,0,1:T(8,128)(2,1)S(1)}, u32[]{:S(2)}, u32[]{:S(2)}) collective-permute-start(bf16[4,1,32,1024]{3,2,0,1:T(8,128)(2,1)S(1)} %bitcast.148), channel_id=1, source_target_pairs={{0,4},{4,0},{8,12},{12,8},{16,20},{20,16},{24,28},{28,24},{1,5},{5... | collective-permute-start | bytes 786440 | tf_op jit(solution)/shard_map/ppermute | solution.py:13
  17.9 2.0 %collective-permute-done.2 = bf16[4,1,16,1024]{3,2,0,1:T(8,128)(2,1)S(1)} collective-permute-done((bf16[4,1,16,1024]{3,2,0,1:T(8,128)(2,1)S(1)}, bf16[4,1,16,1024]{3,2,0,1:T(8,128)(2,1)S(1)}, u32[]{:S(2)}, u32[]{:S(2)}) %collective-permute-start.2) | collective-permute-done | bytes 131104 | tf_op jit(solution)/shard_map/ppermute | solution.py:13
  20.6 0.8 %bitcast_select_fusion = bf16[1,8,16,1024]{3,2,1,0:T(8,128)(2,1)} fusion(bf16[8,16,1024]{2,1,0:T(8,128)(2,1)S(1)} %gather_fusion, pred[8]{0:T(512)(128)(4,1)S(1)} %compare_and_fusion), kind=kLoop, calls=%fused_computation.46 | loop fusion | flops 131072 | bytes 524296 | tf_op jit(solution)/shard_map/jit(_take)/select_n | solution.py:105
  21.4 1.9 %collective-permute-start.3 = (bf16[1,8,16,1024]{3,2,1,0:T(8,128)(2,1)}, bf16[1,8,16,1024]{3,2,1,0:T(8,128)(2,1)}, u32[]{:S(2)}, u32[]{:S(2)}) collective-permute-start(bf16[1,8,16,1024]{3,2,1,0:T(8,128)(2,1)} %bitcast_select_fusion), channel_id=1, source_target_pairs={{0,2},{1,3},{2,0},{3,1},{4,6},{5,7},{6,4},{7,5},{8,10},{9,11},{10,... | collective-permute-start | bytes 786440 | tf_op jit(solution)/shard_map/ppermute | solution.py:13
  23.2 0.6 collective-permute-done.6
  24.9 4.3 %multiply_convert_fusion.2 = (bf16[2,8,32,1024]{3,2,1,0:T(8,128)(2,1)}, bf16[2,8,32,1024]{3,2,1,0:T(8,128)(2,1)S(1)}, bf16[2,8,32,1024]{3,2,1,0:T(8,128)(2,1)}, ...) fusion(f32[2,8,1024]{2,1,0:T(8,128)S(1)} %get-tuple-element.35,, ...), kind=kLoop, calls=%fused_computation.6 | loop fusion | flops 8388608 | bytes 9437184 | tf_op jit(solution)/shard_map/convert_element_type | solution.py:99
  29.2 2.1 %maximum_select_fusion.3 = bf16[2,8,16,1024]{3,2,1,0:T(8,128)(2,1)} fusion(bf16[1,8,16,1024]{3,2,1,0:T(8,128)(2,1)} %collective-permute-done.3, bf16[1,8,16,1024]{3,2,1,0:T(8,128)(2,1)} %bitcast_select_fusion, pred[]{:T(512)S(6)} %eq.21), kind=kLoop, calls=%fused_computation.38 | loop fusion | flops 786432 | bytes 1048577 | tf_op jit(solution)/shard_map/jit(_where)/select_n | solution.py:26
  31.4 1.1 %maximum_select_fusion.2 = bf16[2,1,8,16,1024]{4,3,2,0,1:T(8,128)(2,1)S(1)} fusion(bf16[1,1,8,16,1024]{4,3,2,0,1:T(8,128)(2,1)} %bitcast.34, bf16[1,1,8,16,1024]{4,3,2,0,1:T(8,128)(2,1)S(1)} %fusion.31, pred[]{:T(512)S(6)} %eq.21), kind=kLoop, calls=%fused_computation.37 | loop fusion | flops 786432 | bytes 1048577 | tf_op jit(solution)/shard_map/jit(_where)/select_n | solution.py:26
  32.5 1.0 %collective-permute-done.7 = bf16[2,8,16,1024]{3,2,1,0:T(8,128)(2,1)} collective-permute-done((bf16[2,8,16,1024]{3,2,1,0:T(8,128)(2,1)}, bf16[2,8,16,1024]{3,2,1,0:T(8,128)(2,1)}, u32[]{:S(2)}, u32[]{:S(2)}) %collective-permute-start.7) | collective-permute-done | bytes 524320 | tf_op jit(solution)/shard_map/ppermute | solution.py:13
  33.5 1.4 %maximum_select_fusion = bf16[2,2,8,16,1024]{4,3,2,0,1:T(8,128)(2,1)S(1)} fusion(bf16[2,1,8,16,1024]{4,3,2,0,1:T(8,128)(2,1)} %bitcast.35, bf16[2,1,8,16,1024]{4,3,2,0,1:T(8,128)(2,1)S(1)} %maximum_select_fusion.2, pred[]{:T(512)S(6)} %eq.20), kind=kLoop, calls=%fused_computation.28 | loop fusion | flops 1572864 | bytes 2097153 | tf_op jit(solution)/shard_map/jit(_where)/select_n | solution.py:26
  35.3 1.4 %multiply_convert_fusion.1 = bf16[4,2,16,16,1024]{4,3,2,1,0:T(8,128)(2,1)S(1)} fusion(f32[4,2,16,1024]{3,2,1,0:T(8,128)S(1)} %get-tuple-element.26, f32[4,2,16,1024]{3,2,1,0:T(8,128)S(1)} %get-tuple-element.23), kind=kLoop, calls=%fused_computation.3 | loop fusion | flops 4194304 | bytes 5242880 | tf_op jit(solution)/shard_map/convert_element_type | solution.py:62
  36.7 7.4 %bitcast_convert_fusion.1 = bf16[512,1024]{1,0:T(8,128)(2,1)S(1)} fusion(bf16[4,512,1024]{2,1,0:T(8,128)(2,1)S(1)} %bitcast.135, bf16[4,1024,1024]{2,1,0:T(8,128)(2,1)} %bitcast.158), kind=kOutput, calls=%fused_computation.5 | convolution fusion | flops 4295491584 | bytes 13631488 | tf_op jit(solution)/shard_map/dot_general | solution.py:65
  45.4 1.4 %multiply_convert_fusion = bf16[4,2,16,16,1024]{4,3,2,1,0:T(8,128)(2,1)S(1)} fusion(f32[4,2,16,1024]{3,2,1,0:T(8,128)S(1)} %get-tuple-element.24, f32[4,2,16,1024]{3,2,1,0:T(8,128)S(1)} %get-tuple-element.25), kind=kLoop, calls=%fused_computation.2 | loop fusion | flops 4194304 | bytes 5242880 | tf_op jit(solution)/shard_map/convert_element_type | solution.py:62
  46.9 4.6 %bitcast_convert_fusion = bf16[512,1024]{1,0:T(8,128)(2,1)S(1)} fusion(bf16[4,512,1024]{2,1,0:T(8,128)(2,1)S(1)} %bitcast.136, bf16[4,1024,1024]{2,1,0:T(8,128)(2,1)S(1)} %bitcast.161), kind=kOutput, calls=%fused_computation.4 | convolution fusion | flops 4295491584 | bytes 13631488 | tf_op jit(solution)/shard_map/dot_general | solution.py:65
  53.5 1.6 %collective-permute-start.9 = (bf16[1,2,256,256]{3,2,1,0:T(8,128)(2,1)S(1)}, bf16[1,2,256,256]{3,2,1,0:T(8,128)(2,1)S(1)}, u32[]{:S(2)}, u32[]{:S(2)}) collective-permute-start(bf16[1,2,256,256]{3,2,1,0:T(8,128)(2,1)S(1)} %fusion.5), channel_id=1, source_target_pairs={{0,2},{1,3},{2,0},{3,1},{4,6},{5,7},{6,4},{7,5},{8,10},{9,11},{10,... | collective-permute-start | bytes 786440 | tf_op jit(solution)/shard_map/ppermute | solution.py:13
  55.7 1.6 %collective-permute-start.11 = (bf16[1,2,256,256]{3,2,1,0:T(8,128)(2,1)S(1)}, bf16[1,2,256,256]{3,2,1,0:T(8,128)(2,1)S(1)}, u32[]{:S(2)}, u32[]{:S(2)}) collective-permute-start(bf16[1,2,256,256]{3,2,1,0:T(8,128)(2,1)S(1)} %fusion.4), channel_id=1, source_target_pairs={{0,2},{1,3},{2,0},{3,1},{4,6},{5,7},{6,4},{7,5},{8,10},{9,11},{10,... | collective-permute-start | bytes 786440 | tf_op jit(solution)/shard_map/ppermute | solution.py:13
  57.3 5.3 %collective-permute-done.9 = bf16[1,2,256,256]{3,2,1,0:T(8,128)(2,1)S(1)} collective-permute-done((bf16[1,2,256,256]{3,2,1,0:T(8,128)(2,1)S(1)}, bf16[1,2,256,256]{3,2,1,0:T(8,128)(2,1)S(1)}, u32[]{:S(2)}, u32[]{:S(2)}) %collective-permute-start.9) | collective-permute-done | bytes 262176 | tf_op jit(solution)/shard_map/ppermute | solution.py:13
  63.2 4.3 %collective-permute-done.11 = bf16[1,2,256,256]{3,2,1,0:T(8,128)(2,1)S(1)} collective-permute-done((bf16[1,2,256,256]{3,2,1,0:T(8,128)(2,1)S(1)}, bf16[1,2,256,256]{3,2,1,0:T(8,128)(2,1)S(1)}, u32[]{:S(2)}, u32[]{:S(2)}) %collective-permute-start.11) | collective-permute-done | bytes 262176 | tf_op jit(solution)/shard_map/ppermute | solution.py:13
  68.0 1.0 %maximum_bitcast_fusion = f32[1,4,256,256]{3,2,1,0:T(8,128)} fusion(f32[2,256,256]{2,1,0:T(8,128)S(1)} %fusion.1, f32[2,256,256]{2,1,0:T(8,128)S(1)} %fusion), kind=kLoop, calls=%fused_computation.31 | loop fusion | flops 262144 | bytes 2097152 | tf_op jit(solution)/shard_map/broadcast_in_dim | solution.py:132
  (53 shorter events, 7.1 us)
Async XLA Ops:
  0.8 7.8 %collective-permute-start = (bf16[1,1,16,1024]{3,2,0,1:T(8,128)(2,1)S(1)}, bf16[1,1,16,1024]{3,2,0,1:T(8,128)(2,1)S(1)}, u32[]{:S(2)}, u32[]{:S(2)}) collective-permute-start(bf16[1,1,16,1024]{3,2,0,1:T(8,128)(2,1)S(1)} %get-tuple-element.50), channel_id=1, source_target_pairs={{0,16},{4,20},{8,24},{12,28},{16,0},{20,4},{24,8},{28,12},{1,17},{... | collective-permute-start | bytes 98312 | tf_op jit(solution)/shard_map/ppermute | solution.py:13
  5.7 5.6 %collective-permute-start.4 = (bf16[1,1,32,1024]{3,2,0,1:T(8,128)(2,1)S(1)}, bf16[1,1,32,1024]{3,2,0,1:T(8,128)(2,1)S(1)}, u32[]{:S(2)}, u32[]{:S(2)}) collective-permute-start(bf16[1,1,32,1024]{3,2,0,1:T(8,128)(2,1)S(1)} %get-tuple-element.48), channel_id=1, source_target_pairs={{0,16},{4,20},{8,24},{12,28},{16,0},{20,4},{24,8},{28,12},{1,17},{... | collective-permute-start | bytes 196616 | tf_op jit(solution)/shard_map/ppermute | solution.py:13
  8.6 5.0 %collective-permute-start.1 = (bf16[2,1,16,1024]{3,2,0,1:T(8,128)(2,1)S(1)}, bf16[2,1,16,1024]{3,2,0,1:T(8,128)(2,1)S(1)}, u32[]{:S(2)}, u32[]{:S(2)}) collective-permute-start(bf16[2,1,16,1024]{3,2,0,1:T(8,128)(2,1)S(1)} %maximum_select_fusion.8), channel_id=1, source_target_pairs={{0,8},{4,12},{8,0},{12,4},{16,24},{20,28},{24,16},{28,20},{1,9},{5... | collective-permute-start | bytes 196616 | tf_op jit(solution)/shard_map/ppermute | solution.py:13
  11.2 5.0 %collective-permute-start.5 = (bf16[2,1,32,1024]{3,2,0,1:T(8,128)(2,1)S(1)}, bf16[2,1,32,1024]{3,2,0,1:T(8,128)(2,1)S(1)}, u32[]{:S(2)}, u32[]{:S(2)}) collective-permute-start(bf16[2,1,32,1024]{3,2,0,1:T(8,128)(2,1)S(1)} %maximum_select_fusion.7), channel_id=1, source_target_pairs={{0,8},{4,12},{8,0},{12,4},{16,24},{20,28},{24,16},{28,20},{1,9},{5... | collective-permute-start | bytes 393224 | tf_op jit(solution)/shard_map/ppermute | solution.py:13
  13.6 6.3 %collective-permute-start.2 = (bf16[4,1,16,1024]{3,2,0,1:T(8,128)(2,1)S(1)}, bf16[4,1,16,1024]{3,2,0,1:T(8,128)(2,1)S(1)}, u32[]{:S(2)}, u32[]{:S(2)}) collective-permute-start(bf16[4,1,16,1024]{3,2,0,1:T(8,128)(2,1)S(1)} %bitcast.150), channel_id=1, source_target_pairs={{0,4},{4,0},{8,12},{12,8},{16,20},{20,16},{24,28},{28,24},{1,5},{5... | collective-permute-start | bytes 393224 | tf_op jit(solution)/shard_map/ppermute | solution.py:13
  16.3 7.5 %collective-permute-start.6 = (bf16[4,1,32,1024]{3,2,0,1:T(8,128)(2,1)S(1)}, bf16[4,1,32,1024]{3,2,0,1:T(8,128)(2,1)S(1)}, u32[]{:S(2)}, u32[]{:S(2)}) collective-permute-start(bf16[4,1,32,1024]{3,2,0,1:T(8,128)(2,1)S(1)} %bitcast.148), channel_id=1, source_target_pairs={{0,4},{4,0},{8,12},{12,8},{16,20},{20,16},{24,28},{28,24},{1,5},{5... | collective-permute-start | bytes 786440 | tf_op jit(solution)/shard_map/ppermute | solution.py:13
  21.4 7.9 %collective-permute-start.3 = (bf16[1,8,16,1024]{3,2,1,0:T(8,128)(2,1)}, bf16[1,8,16,1024]{3,2,1,0:T(8,128)(2,1)}, u32[]{:S(2)}, u32[]{:S(2)}) collective-permute-start(bf16[1,8,16,1024]{3,2,1,0:T(8,128)(2,1)} %bitcast_select_fusion), channel_id=1, source_target_pairs={{0,2},{1,3},{2,0},{3,1},{4,6},{5,7},{6,4},{7,5},{8,10},{9,11},{10,... | collective-permute-start | bytes 786440 | tf_op jit(solution)/shard_map/ppermute | solution.py:13
  31.3 2.3 %collective-permute-start.7 = (bf16[2,8,16,1024]{3,2,1,0:T(8,128)(2,1)}, bf16[2,8,16,1024]{3,2,1,0:T(8,128)(2,1)}, u32[]{:S(2)}, u32[]{:S(2)}) collective-permute-start(bf16[2,8,16,1024]{3,2,1,0:T(8,128)(2,1)} %maximum_select_fusion.3), channel_id=1, source_target_pairs={{0,1},{1,0},{2,3},{3,2},{4,5},{5,4},{6,7},{7,6},{8,9},{9,8},{10,11... | collective-permute-start | bytes 1572872 | tf_op jit(solution)/shard_map/ppermute | solution.py:13
  35.3 11.6 %slice-start = ((s8[8388608]{0:T(1024)(128)(4,1)}), s8[4194304]{0:T(1024)(128)(4,1)S(1)}, s32[]{:S(2)}) async-start(s8[8388608]{0:T(1024)(128)(4,1)} %bitcast.159), calls=%async_computation | async-start | bytes 8388608
  36.7 7.5 %copy-start.2 = (bf16[2,8,32,1024]{3,2,1,0:T(8,128)(2,1)S(1)}, bf16[2,8,32,1024]{3,2,1,0:T(8,128)(2,1)}, u32[]{:S(2)}) copy-start(bf16[2,8,32,1024]{3,2,1,0:T(8,128)(2,1)} %get-tuple-element.54) | copy-start | bytes 3145732
  36.7 8.0 %copy-start.1 = (bf16[2,8,32,1024]{3,2,1,0:T(8,128)(2,1)S(1)}, bf16[2,8,32,1024]{3,2,1,0:T(8,128)(2,1)}, u32[]{:S(2)}) copy-start(bf16[2,8,32,1024]{3,2,1,0:T(8,128)(2,1)} %get-tuple-element.53) | copy-start | bytes 3145732
  36.7 10.1 %slice-start.1 = ((s8[8388608]{0:T(1024)(128)(4,1)}), s8[4194304]{0:T(1024)(128)(4,1)S(1)}, s32[]{:S(2)}) async-start(s8[8388608]{0:T(1024)(128)(4,1)} %bitcast.159), calls=%async_computation.1 | async-start | bytes 8388608
  45.2 7.7 %collective-permute-start.8 = (f32[2,2,256,256]{3,2,1,0:T(8,128)S(1)}, f32[2,2,256,256]{3,2,1,0:T(8,128)S(1)}, u32[]{:S(2)}, u32[]{:S(2)}) collective-permute-start(f32[2,2,256,256]{3,2,1,0:T(8,128)S(1)} %pad_maximum_fusion), channel_id=1, source_target_pairs={{0,1},{1,0},{2,3},{3,2},{4,5},{5,4},{6,7},{7,6},{8,9},{9,8},{10,11... | collective-permute-start | bytes 3145736 | tf_op jit(solution)/shard_map/ppermute | solution.py:13
  46.9 4.6 %copy-start = (bf16[2,8,32,1024]{3,2,1,0:T(8,128)(2,1)S(1)}, bf16[2,8,32,1024]{3,2,1,0:T(8,128)(2,1)}, u32[]{:S(2)}) copy-start(bf16[2,8,32,1024]{3,2,1,0:T(8,128)(2,1)} %get-tuple-element.31) | copy-start | bytes 3145732
  51.4 1.5 %copy-start.4 = (bf16[2,8,32,1024]{3,2,1,0:T(8,128)(2,1)S(1)}, bf16[2,8,32,1024]{3,2,1,0:T(8,128)(2,1)}, u32[]{:S(2)}) copy-start(bf16[2,8,32,1024]{3,2,1,0:T(8,128)(2,1)} %get-tuple-element.52) | copy-start | bytes 3145732
  51.9 3.3 %copy-start.3 = (bf16[2,8,32,1024]{3,2,1,0:T(8,128)(2,1)S(1)}, bf16[2,8,32,1024]{3,2,1,0:T(8,128)(2,1)}, u32[]{:S(2)}) copy-start(bf16[2,8,32,1024]{3,2,1,0:T(8,128)(2,1)} %get-tuple-element.33) | copy-start | bytes 3145732
  52.5 2.7 %collective-permute-start.10 = (f32[2,2,256,256]{3,2,1,0:T(8,128)S(1)}, f32[2,2,256,256]{3,2,1,0:T(8,128)S(1)}, u32[]{:S(2)}, u32[]{:S(2)}) collective-permute-start(f32[2,2,256,256]{3,2,1,0:T(8,128)S(1)} %pad_maximum_fusion.1), channel_id=1, source_target_pairs={{0,1},{1,0},{2,3},{3,2},{4,5},{5,4},{6,7},{7,6},{8,9},{9,8},{10,11... | collective-permute-start | bytes 3145736 | tf_op jit(solution)/shard_map/ppermute | solution.py:13
  53.5 9.2 %collective-permute-start.9 = (bf16[1,2,256,256]{3,2,1,0:T(8,128)(2,1)S(1)}, bf16[1,2,256,256]{3,2,1,0:T(8,128)(2,1)S(1)}, u32[]{:S(2)}, u32[]{:S(2)}) collective-permute-start(bf16[1,2,256,256]{3,2,1,0:T(8,128)(2,1)S(1)} %fusion.5), channel_id=1, source_target_pairs={{0,2},{1,3},{2,0},{3,1},{4,6},{5,7},{6,4},{7,5},{8,10},{9,11},{10,... | collective-permute-start | bytes 786440 | tf_op jit(solution)/shard_map/ppermute | solution.py:13
  55.7 11.7 %collective-permute-start.11 = (bf16[1,2,256,256]{3,2,1,0:T(8,128)(2,1)S(1)}, bf16[1,2,256,256]{3,2,1,0:T(8,128)(2,1)S(1)}, u32[]{:S(2)}, u32[]{:S(2)}) collective-permute-start(bf16[1,2,256,256]{3,2,1,0:T(8,128)(2,1)S(1)} %fusion.4), channel_id=1, source_target_pairs={{0,2},{1,3},{2,0},{3,1},{4,6},{5,7},{6,4},{7,5},{8,10},{9,11},{10,... | collective-permute-start | bytes 786440 | tf_op jit(solution)/shard_map/ppermute | solution.py:13

commit v12 on v9

--- a/solution.py
+++ b/solution.py
@@ -77,11 +77,15 @@
 
     wanted = jnp.concatenate([kpoint_a, kpoint_b])
     held_valence = gather_axis(orbitals[:, :NV, :], "pb").reshape(kpoint_count, NV, mu_cols)
-    held_conduction = gather_axis(orbitals[:, NV:, :], "pb").reshape(
+    chosen_valence = jnp.take(held_valence, wanted, axis=0)
+    conduction_mine, chosen_valence = lax.optimization_barrier(
+        (orbitals[:, NV:, :], chosen_valence)
+    )
+    held_conduction = gather_axis(conduction_mine, "pb").reshape(
         kpoint_count, orb_count - NV, mu_cols
     )
 
-    valence = gather_axis(jnp.take(held_valence, wanted, axis=0), "col")
+    valence = gather_axis(chosen_valence, "col")
     conduction = jnp.take(held_conduction, wanted, axis=0).astype(jnp.float32)
     rows_per_block = NC // col_count
     chunk = pair_count // PAIR_CHUNKS

time: 63.4 us -> 70.6 us (1.11)
  waiting for transfers between devices: 19.4 us -> 24.3 us
  starting transfers between devices: 16 us -> 18.5 us
    ppermute x12, waiting for transfers between devices: 19.4 us -> 24.3 us  [swap(): return lax.ppermute(x, axis, [(i, i ^ bit) for i in range(size)])]
    ppermute x12, starting transfers between devices: 16 us -> 18.5 us  [swap(): return lax.ppermute(x, axis, [(i, i ^ bit) for i in range(size)])]
    another operation x2 -> x1, local copies, waits for them, and re-layouts: 1.61 us -> 0.76 us  [gather_axis(): cur = jnp.where(low, jnp.stack([cur, got], 1), jnp.stack([got, cur], 1))]
    slice x0 -> x1, local copies, waits for them, and re-layouts: none -> 0.84 us  [body(): orbitals[:, NV:, :]]
  transfers between devices with their start and end apart: 12 -> 12, of which waited for: 9 -> 9; matrix products, arithmetic and copies ran while one was open for 18% -> 15% of each run, Pallas kernels for 0% -> 0%
where the time goes in v12:
time: 70.6 us; the launch traced here: 70.3 us
  waiting for transfers between devices  24.3 us (34%)
  starting transfers between devices  18.5 us (26%)
  matrix products  12.8 us (18%)
  other arithmetic  10.5 us (15%)
  local copies, waits for them, and re-layouts  3.94 us (6%)
    ppermute x12, waiting for transfers between devices, swap(): return lax.ppermute(x, axis, [(i, i ^ bit) for i in range(size)])  24.3 us
    ppermute x12, starting transfers between devices, swap(): return lax.ppermute(x, axis, [(i, i ^ bit) for i in range(size)])  18.5 us
    dot_general x2, matrix products, screened_of(): lax.dot_general(val_pairs, screen, (((0, 2), (0, 1)), ((), ())), preferre...  9.04 us
    dot_general x8, matrix products, own_block(): jnp.einsum('pan,pbn->pab', screened, cond_pairs, preferred_element_type=j...  3.75 us
    convert_element_type x1, other arithmetic, own_block(): (rows[:, :, None, :] * cond_b[:, None, :, :]).astype(jnp.bfloat16)  3.02 us
    convert_element_type x1, other arithmetic, screened_of(): (valence_a[:, :, :, None, :] * valence_b[:, :, None, :, :]).astype(jnp.bf...  2.34 us
  transfers between devices with their start and end apart: 12, of which 9 were waited for; matrix products, arithmetic and copies ran while one was open for 15% of the time, Pallas kernels for 0%

profile of v12, /device:TPU:0, one launch (start us, length us, event | category | flops | bytes accessed | tf_op | source)
XLA Modules:
  0.0 70.3 jit_solution(9426984221919556611)
XLA Ops:
  0.0 0.8 %slice_bitcast_fusion.5 = (bf16[1,1,1,16,1024]{4,3,2,1,0:T(8,128)(2,1)S(1)}, bf16[1,1,16,1024]{3,2,0,1:T(8,128)(2,1)S(1)}) fusion(bf16[1,48,1024]{2,1,0:T(8,128)(2,1)} %param.3), kind=kLoop, calls=%fused_computation.57 | loop fusion | bytes 98304 | tf_op jit(solution)/shard_map/stack | solution.py:24
  0.8 4.0 %collective-permute-start = (bf16[1,1,16,1024]{3,2,0,1:T(8,128)(2,1)S(1)}, bf16[1,1,16,1024]{3,2,0,1:T(8,128)(2,1)S(1)}, u32[]{:S(2)}, u32[]{:S(2)}) collective-permute-start(bf16[1,1,16,1024]{3,2,0,1:T(8,128)(2,1)S(1)} %get-tuple-element.34), channel_id=1, source_target_pairs={{0,16},{4,20},{8,24},{12,28},{16,0},{20,4},{24,8},{28,12},{1,17},{... | collective-permute-start | bytes 98312 | tf_op jit(solution)/shard_map/ppermute | solution.py:13
  4.8 0.7 fusion.37
  5.5 0.7 and_select_fusion
  6.1 0.7 %compare_and_fusion = pred[8]{0:T(512)(128)(4,1)S(1)} fusion(s32[4]{0:T(128)S(1)} %and_select_fusion, s32[4]{0:T(128)} %bitcast.176), kind=kLoop, calls=%fused_computation.71 | loop fusion | flops 56 | bytes 40 | tf_op jit(solution)/shard_map/jit(_take)/and | solution.py:80
  7.1 1.6 %collective-permute-start.1 = (bf16[2,1,16,1024]{3,2,0,1:T(8,128)(2,1)S(1)}, bf16[2,1,16,1024]{3,2,0,1:T(8,128)(2,1)S(1)}, u32[]{:S(2)}, u32[]{:S(2)}) collective-permute-start(bf16[2,1,16,1024]{3,2,0,1:T(8,128)(2,1)S(1)} %maximum_select_fusion.8), channel_id=1, source_target_pairs={{0,8},{4,12},{8,0},{12,4},{16,24},{20,28},{24,16},{28,20},{1,9},{5... | collective-permute-start | bytes 196616 | tf_op jit(solution)/shard_map/ppermute | solution.py:13
  8.7 2.7 %collective-permute-done.1 = bf16[2,1,16,1024]{3,2,0,1:T(8,128)(2,1)S(1)} collective-permute-done((bf16[2,1,16,1024]{3,2,0,1:T(8,128)(2,1)S(1)}, bf16[2,1,16,1024]{3,2,0,1:T(8,128)(2,1)S(1)}, u32[]{:S(2)}, u32[]{:S(2)}) %collective-permute-start.1) | collective-permute-done | bytes 65568 | tf_op jit(solution)/shard_map/ppermute | solution.py:13
  11.4 1.8 %collective-permute-start.2 = (bf16[4,1,16,1024]{3,2,0,1:T(8,128)(2,1)S(1)}, bf16[4,1,16,1024]{3,2,0,1:T(8,128)(2,1)S(1)}, u32[]{:S(2)}, u32[]{:S(2)}) collective-permute-start(bf16[4,1,16,1024]{3,2,0,1:T(8,128)(2,1)S(1)} %bitcast.164), channel_id=1, source_target_pairs={{0,4},{4,0},{8,12},{12,8},{16,20},{20,16},{24,28},{28,24},{1,5},{5... | collective-permute-start | bytes 393224 | tf_op jit(solution)/shard_map/ppermute | solution.py:13
  13.2 0.7 %fusion.13 = s32[8]{0:T(128)S(1)} fusion(s32[4,1]{0,1:T(1,128)S(1)} %fusion.37, s32[4,1]{0,1:T(1,128)} %bitcast.177), kind=kLoop, calls=%fused_computation.74 | loop fusion | flops 32 | bytes 64 | tf_op jit(solution)/shard_map/jit(_take)/jit(_where)/select_n | solution.py:80
  13.9 0.8 %slice.42 = bf16[1,32,1024]{2,1,0:T(8,128)(2,1)S(1)} slice(bf16[1,48,1024]{2,1,0:T(8,128)(2,1)} %param.3), slice={[0:1], [16:48], [0:1024]} | slice | bytes 131072 | tf_op jit(solution)/shard_map/slice | solution.py:82
  14.8 1.7 %collective-permute-done.2 = bf16[4,1,16,1024]{3,2,0,1:T(8,128)(2,1)S(1)} collective-permute-done((bf16[4,1,16,1024]{3,2,0,1:T(8,128)(2,1)S(1)}, bf16[4,1,16,1024]{3,2,0,1:T(8,128)(2,1)S(1)}, u32[]{:S(2)}, u32[]{:S(2)}) %collective-permute-start.2) | collective-permute-done | bytes 131104 | tf_op jit(solution)/shard_map/ppermute | solution.py:13
  16.5 0.6 gather_fusion
  17.2 2.7 %collective-permute-start.5 = (bf16[1,1,32,1024]{3,2,0,1:T(8,128)(2,1)S(1)}, bf16[1,1,32,1024]{3,2,0,1:T(8,128)(2,1)S(1)}, u32[]{:S(2)}, u32[]{:S(2)}) collective-permute-start(bf16[1,1,32,1024]{3,2,0,1:T(8,128)(2,1)S(1)} %bitcast.160), channel_id=1, source_target_pairs={{0,16},{4,20},{8,24},{12,28},{16,0},{20,4},{24,8},{28,12},{1,17},{... | collective-permute-start | bytes 196616 | tf_op jit(solution)/shard_map/ppermute | solution.py:13
  19.8 1.5 %collective-permute-start.3 = (bf16[1,8,16,1024]{3,2,1,0:T(8,128)(2,1)S(1)}, bf16[1,8,16,1024]{3,2,1,0:T(8,128)(2,1)S(1)}, u32[]{:S(2)}, u32[]{:S(2)}) collective-permute-start(bf16[1,8,16,1024]{3,2,1,0:T(8,128)(2,1)S(1)} %bitcast.152), channel_id=1, source_target_pairs={{0,2},{1,3},{2,0},{3,1},{4,6},{5,7},{6,4},{7,5},{8,10},{9,11},{10,... | collective-permute-start | bytes 786440 | tf_op jit(solution)/shard_map/ppermute | solution.py:13
  21.3 1.2 %collective-permute-done.5 = bf16[1,1,32,1024]{3,2,0,1:T(8,128)(2,1)S(1)} collective-permute-done((bf16[1,1,32,1024]{3,2,0,1:T(8,128)(2,1)S(1)}, bf16[1,1,32,1024]{3,2,0,1:T(8,128)(2,1)S(1)}, u32[]{:S(2)}, u32[]{:S(2)}) %collective-permute-start.5) | collective-permute-done | bytes 65568 | tf_op jit(solution)/shard_map/ppermute | solution.py:13
  22.5 2.1 %collective-permute-start.6 = (bf16[2,1,32,1024]{3,2,0,1:T(8,128)(2,1)S(1)}, bf16[2,1,32,1024]{3,2,0,1:T(8,128)(2,1)S(1)}, u32[]{:S(2)}, u32[]{:S(2)}) collective-permute-start(bf16[2,1,32,1024]{3,2,0,1:T(8,128)(2,1)S(1)} %maximum_select_fusion.7), channel_id=1, source_target_pairs={{0,8},{4,12},{8,0},{12,4},{16,24},{20,28},{24,16},{28,20},{1,9},{5... | collective-permute-start | bytes 393224 | tf_op jit(solution)/shard_map/ppermute | solution.py:13
  24.6 2.9 %collective-permute-done.6 = bf16[2,1,32,1024]{3,2,0,1:T(8,128)(2,1)S(1)} collective-permute-done((bf16[2,1,32,1024]{3,2,0,1:T(8,128)(2,1)S(1)}, bf16[2,1,32,1024]{3,2,0,1:T(8,128)(2,1)S(1)}, u32[]{:S(2)}, u32[]{:S(2)}) %collective-permute-start.6) | collective-permute-done | bytes 131104 | tf_op jit(solution)/shard_map/ppermute | solution.py:13
  27.6 1.8 %collective-permute-start.7 = (bf16[4,1,32,1024]{3,2,0,1:T(8,128)(2,1)S(1)}, bf16[4,1,32,1024]{3,2,0,1:T(8,128)(2,1)S(1)}, u32[]{:S(2)}, u32[]{:S(2)}) collective-permute-start(bf16[4,1,32,1024]{3,2,0,1:T(8,128)(2,1)S(1)} %bitcast.157), channel_id=1, source_target_pairs={{0,4},{4,0},{8,12},{12,8},{16,20},{20,16},{24,28},{28,24},{1,5},{5... | collective-permute-start | bytes 786440 | tf_op jit(solution)/shard_map/ppermute | solution.py:13
  29.6 4.4 %collective-permute-done.7 = bf16[4,1,32,1024]{3,2,0,1:T(8,128)(2,1)S(1)} collective-permute-done((bf16[4,1,32,1024]{3,2,0,1:T(8,128)(2,1)S(1)}, bf16[4,1,32,1024]{3,2,0,1:T(8,128)(2,1)S(1)}, u32[]{:S(2)}, u32[]{:S(2)}) %collective-permute-start.7) | collective-permute-done | bytes 262176 | tf_op jit(solution)/shard_map/ppermute | solution.py:13
  34.2 0.6 gather_fusion.1
  35.1 3.0 %multiply_convert_fusion.2 = (bf16[2,8,32,1024]{3,2,1,0:T(8,128)(2,1)S(1)}, bf16[2,8,32,1024]{3,2,1,0:T(8,128)(2,1)S(1)}, bf16[2,8,32,1024]{3,2,1,0:T(8,128)(2,1...) fusion(f32[2,8,1024]{2,1,0:T(8,128)S(1)} %get-tuple-element.29,, ...), kind=kLoop, calls=%fused_computation.6 | loop fusion | flops 8388608 | bytes 9437184 | tf_op jit(solution)/shard_map/convert_element_type | solution.py:109
  38.7 2.3 %multiply_convert_fusion = (bf16[4,2,16,16,1024]{4,3,2,1,0:T(8,128)(2,1)S(1)}, bf16[4,2,16,16,1024]{4,3,2,1,0:T(8,128)(2,1)S(1)}) fusion(f32[4,2,16,1024]{3,2,1,0:T(8,128)S(1)} %get-tuple-element.14, f32[4,2,16,1024]{3,2,1,0:T(8,128)S(1)} %get-tuple-element.15, f32[4,2,16,1024]{3,2,1,0:T(8,128)S(1)} %get-tuple-element.16, ...), kind=kLoop, calls=%fused_computation.2 | loop fusion | flops 8388608 | bytes 10485760 | tf_op jit(solution)/shard_map/convert_element_type | solution.py:58
  41.0 0.8 %slice-done.1 = s8[4194304]{0:T(1024)(128)(4,1)S(1)} async-done(((s8[8388608]{0:T(1024)(128)(4,1)}), s8[4194304]{0:T(1024)(128)(4,1)S(1)}, s32[]{:S(2)}) %slice-start.1) | async-done | bytes 4194328
  41.9 4.5 %bitcast_convert_fusion = bf16[512,1024]{1,0:T(8,128)(2,1)S(1)} fusion(bf16[4,512,1024]{2,1,0:T(8,128)(2,1)S(1)} %bitcast.149, bf16[4,1024,1024]{2,1,0:T(8,128)(2,1)S(1)} %bitcast.174), kind=kOutput, calls=%fused_computation.4 | convolution fusion | flops 4295491584 | bytes 13631488 | tf_op jit(solution)/shard_map/dot_general | solution.py:61
  46.4 4.5 %bitcast_convert_fusion.1 = bf16[512,1024]{1,0:T(8,128)(2,1)S(1)} fusion(bf16[4,512,1024]{2,1,0:T(8,128)(2,1)S(1)} %bitcast.148, bf16[4,1024,1024]{2,1,0:T(8,128)(2,1)S(1)} %bitcast.175), kind=kOutput, calls=%fused_computation.5 | convolution fusion | flops 4295491584 | bytes 13631488 | tf_op jit(solution)/shard_map/dot_general | solution.py:61
  53.1 0.6 collective-permute-start.10
  54.1 0.6 collective-permute-done.8
  55.2 1.8 %collective-permute-start.9 = (bf16[1,2,256,256]{3,2,1,0:T(8,128)(2,1)S(1)}, bf16[1,2,256,256]{3,2,1,0:T(8,128)(2,1)S(1)}, u32[]{:S(2)}, u32[]{:S(2)}) collective-permute-start(bf16[1,2,256,256]{3,2,1,0:T(8,128)(2,1)S(1)} %fusion.8), channel_id=1, source_target_pairs={{0,2},{1,3},{2,0},{3,1},{4,6},{5,7},{6,4},{7,5},{8,10},{9,11},{10,... | collective-permute-start | bytes 786440 | tf_op jit(solution)/shard_map/ppermute | solution.py:13
  57.9 0.5 collective-permute-start.11
  58.4 5.9 %collective-permute-done.9 = bf16[1,2,256,256]{3,2,1,0:T(8,128)(2,1)S(1)} collective-permute-done((bf16[1,2,256,256]{3,2,1,0:T(8,128)(2,1)S(1)}, bf16[1,2,256,256]{3,2,1,0:T(8,128)(2,1)S(1)}, u32[]{:S(2)}, u32[]{:S(2)}) %collective-permute-start.9) | collective-permute-done | bytes 262176 | tf_op jit(solution)/shard_map/ppermute | solution.py:13
  64.5 4.7 %collective-permute-done.11 = bf16[1,2,256,256]{3,2,1,0:T(8,128)(2,1)S(1)} collective-permute-done((bf16[1,2,256,256]{3,2,1,0:T(8,128)(2,1)S(1)}, bf16[1,2,256,256]{3,2,1,0:T(8,128)(2,1)S(1)}, u32[]{:S(2)}, u32[]{:S(2)}) %collective-permute-start.11) | collective-permute-done | bytes 262176 | tf_op jit(solution)/shard_map/ppermute | solution.py:13
  69.3 1.0 %maximum_bitcast_fusion = f32[1,4,256,256]{3,2,1,0:T(8,128)} fusion(f32[2,256,256]{2,1,0:T(8,128)S(1)} %fusion.3, f32[2,256,256]{2,1,0:T(8,128)S(1)} %fusion.7), kind=kLoop, calls=%fused_computation.21 | loop fusion | flops 262144 | bytes 2097152 | tf_op jit(solution)/shard_map/broadcast_in_dim | solution.py:123
  (43 shorter events, 5.7 us)
Async XLA Ops:
  0.8 6.3 %collective-permute-start = (bf16[1,1,16,1024]{3,2,0,1:T(8,128)(2,1)S(1)}, bf16[1,1,16,1024]{3,2,0,1:T(8,128)(2,1)S(1)}, u32[]{:S(2)}, u32[]{:S(2)}) collective-permute-start(bf16[1,1,16,1024]{3,2,0,1:T(8,128)(2,1)S(1)} %get-tuple-element.34), channel_id=1, source_target_pairs={{0,16},{4,20},{8,24},{12,28},{16,0},{20,4},{24,8},{28,12},{1,17},{... | collective-permute-start | bytes 98312 | tf_op jit(solution)/shard_map/ppermute | solution.py:13
  7.1 4.3 %collective-permute-start.1 = (bf16[2,1,16,1024]{3,2,0,1:T(8,128)(2,1)S(1)}, bf16[2,1,16,1024]{3,2,0,1:T(8,128)(2,1)S(1)}, u32[]{:S(2)}, u32[]{:S(2)}) collective-permute-start(bf16[2,1,16,1024]{3,2,0,1:T(8,128)(2,1)S(1)} %maximum_select_fusion.8), channel_id=1, source_target_pairs={{0,8},{4,12},{8,0},{12,4},{16,24},{20,28},{24,16},{28,20},{1,9},{5... | collective-permute-start | bytes 196616 | tf_op jit(solution)/shard_map/ppermute | solution.py:13
  11.4 5.0 %collective-permute-start.2 = (bf16[4,1,16,1024]{3,2,0,1:T(8,128)(2,1)S(1)}, bf16[4,1,16,1024]{3,2,0,1:T(8,128)(2,1)S(1)}, u32[]{:S(2)}, u32[]{:S(2)}) collective-permute-start(bf16[4,1,16,1024]{3,2,0,1:T(8,128)(2,1)S(1)} %bitcast.164), channel_id=1, source_target_pairs={{0,4},{4,0},{8,12},{12,8},{16,20},{20,16},{24,28},{28,24},{1,5},{5... | collective-permute-start | bytes 393224 | tf_op jit(solution)/shard_map/ppermute | solution.py:13
  17.2 5.3 %collective-permute-start.5 = (bf16[1,1,32,1024]{3,2,0,1:T(8,128)(2,1)S(1)}, bf16[1,1,32,1024]{3,2,0,1:T(8,128)(2,1)S(1)}, u32[]{:S(2)}, u32[]{:S(2)}) collective-permute-start(bf16[1,1,32,1024]{3,2,0,1:T(8,128)(2,1)S(1)} %bitcast.160), channel_id=1, source_target_pairs={{0,16},{4,20},{8,24},{12,28},{16,0},{20,4},{24,8},{28,12},{1,17},{... | collective-permute-start | bytes 196616 | tf_op jit(solution)/shard_map/ppermute | solution.py:13
  19.8 9.6 %collective-permute-start.3 = (bf16[1,8,16,1024]{3,2,1,0:T(8,128)(2,1)S(1)}, bf16[1,8,16,1024]{3,2,1,0:T(8,128)(2,1)S(1)}, u32[]{:S(2)}, u32[]{:S(2)}) collective-permute-start(bf16[1,8,16,1024]{3,2,1,0:T(8,128)(2,1)S(1)} %bitcast.152), channel_id=1, source_target_pairs={{0,2},{1,3},{2,0},{3,1},{4,6},{5,7},{6,4},{7,5},{8,10},{9,11},{10,... | collective-permute-start | bytes 786440 | tf_op jit(solution)/shard_map/ppermute | solution.py:13
  22.5 5.0 %collective-permute-start.6 = (bf16[2,1,32,1024]{3,2,0,1:T(8,128)(2,1)S(1)}, bf16[2,1,32,1024]{3,2,0,1:T(8,128)(2,1)S(1)}, u32[]{:S(2)}, u32[]{:S(2)}) collective-permute-start(bf16[2,1,32,1024]{3,2,0,1:T(8,128)(2,1)S(1)} %maximum_select_fusion.7), channel_id=1, source_target_pairs={{0,8},{4,12},{8,0},{12,4},{16,24},{20,28},{24,16},{28,20},{1,9},{5... | collective-permute-start | bytes 393224 | tf_op jit(solution)/shard_map/ppermute | solution.py:13
  27.6 6.4 %collective-permute-start.7 = (bf16[4,1,32,1024]{3,2,0,1:T(8,128)(2,1)S(1)}, bf16[4,1,32,1024]{3,2,0,1:T(8,128)(2,1)S(1)}, u32[]{:S(2)}, u32[]{:S(2)}) collective-permute-start(bf16[4,1,32,1024]{3,2,0,1:T(8,128)(2,1)S(1)} %bitcast.157), channel_id=1, source_target_pairs={{0,4},{4,0},{8,12},{12,8},{16,20},{20,16},{24,28},{28,24},{1,5},{5... | collective-permute-start | bytes 786440 | tf_op jit(solution)/shard_map/ppermute | solution.py:13
  29.5 8.6 %collective-permute-start.4 = (bf16[2,8,16,1024]{3,2,1,0:T(8,128)(2,1)S(1)}, bf16[2,8,16,1024]{3,2,1,0:T(8,128)(2,1)S(1)}, u32[]{:S(2)}, u32[]{:S(2)}) collective-permute-start(bf16[2,8,16,1024]{3,2,1,0:T(8,128)(2,1)S(1)} %maximum_select_fusion.2), channel_id=1, source_target_pairs={{0,1},{1,0},{2,3},{3,2},{4,5},{5,4},{6,7},{7,6},{8,9},{9,8},{10,11... | collective-permute-start | bytes 1572872 | tf_op jit(solution)/shard_map/ppermute | solution.py:13
  38.3 2.7 %slice-start = ((s8[8388608]{0:T(1024)(128)(4,1)}), s8[4194304]{0:T(1024)(128)(4,1)S(1)}, s32[]{:S(2)}) async-start(s8[8388608]{0:T(1024)(128)(4,1)} %bitcast.172), calls=%async_computation | async-start | bytes 8388608
  38.6 3.2 %slice-start.1 = ((s8[8388608]{0:T(1024)(128)(4,1)}), s8[4194304]{0:T(1024)(128)(4,1)S(1)}, s32[]{:S(2)}) async-start(s8[8388608]{0:T(1024)(128)(4,1)} %bitcast.172), calls=%async_computation.1 | async-start | bytes 8388608
  52.0 2.7 %collective-permute-start.8 = (f32[2,2,256,256]{3,2,1,0:T(8,128)S(1)}, f32[2,2,256,256]{3,2,1,0:T(8,128)S(1)}, u32[]{:S(2)}, u32[]{:S(2)}) collective-permute-start(f32[2,2,256,256]{3,2,1,0:T(8,128)S(1)} %pad_maximum_fusion), channel_id=1, source_target_pairs={{0,1},{1,0},{2,3},{3,2},{4,5},{5,4},{6,7},{7,6},{8,9},{9,8},{10,11... | collective-permute-start | bytes 3145736 | tf_op jit(solution)/shard_map/ppermute | solution.py:13
  53.1 4.3 %collective-permute-start.10 = (f32[2,2,256,256]{3,2,1,0:T(8,128)S(1)}, f32[2,2,256,256]{3,2,1,0:T(8,128)S(1)}, u32[]{:S(2)}, u32[]{:S(2)}) collective-permute-start(f32[2,2,256,256]{3,2,1,0:T(8,128)S(1)} %pad_maximum_fusion.1), channel_id=1, source_target_pairs={{0,1},{1,0},{2,3},{3,2},{4,5},{5,4},{6,7},{7,6},{8,9},{9,8},{10,11... | collective-permute-start | bytes 3145736 | tf_op jit(solution)/shard_map/ppermute | solution.py:13
  55.2 9.2 %collective-permute-start.9 = (bf16[1,2,256,256]{3,2,1,0:T(8,128)(2,1)S(1)}, bf16[1,2,256,256]{3,2,1,0:T(8,128)(2,1)S(1)}, u32[]{:S(2)}, u32[]{:S(2)}) collective-permute-start(bf16[1,2,256,256]{3,2,1,0:T(8,128)(2,1)S(1)} %fusion.8), channel_id=1, source_target_pairs={{0,2},{1,3},{2,0},{3,1},{4,6},{5,7},{6,4},{7,5},{8,10},{9,11},{10,... | collective-permute-start | bytes 786440 | tf_op jit(solution)/shard_map/ppermute | solution.py:13
  57.9 11.3 %collective-permute-start.11 = (bf16[1,2,256,256]{3,2,1,0:T(8,128)(2,1)S(1)}, bf16[1,2,256,256]{3,2,1,0:T(8,128)(2,1)S(1)}, u32[]{:S(2)}, u32[]{:S(2)}) collective-permute-start(bf16[1,2,256,256]{3,2,1,0:T(8,128)(2,1)S(1)} %fusion.9), channel_id=1, source_target_pairs={{0,2},{1,3},{2,0},{3,1},{4,6},{5,7},{6,4},{7,5},{8,10},{9,11},{10,... | collective-permute-start | bytes 786440 | tf_op jit(solution)/shard_map/ppermute | solution.py:13

commit v13 on v11

--- a/solution.py
+++ b/solution.py
@@ -13,22 +13,18 @@
     return lax.ppermute(x, axis, [(i, i ^ bit) for i in range(size)])
 
 
-def gather_axis(mine, axis, tie=None):
+def gather_axis(mine, axis):
     count = lax.axis_size(axis)
     me = lax.axis_index(axis)
     cur = mine[None]
     bit = count // 2
     while bit >= 1:
         got = swap(cur, axis, bit)
-        if tie is not None and bit > 1:
-            got, tie = lax.optimization_barrier((got, tie))
         low = (me & bit) == 0
         cur = jnp.where(low, jnp.stack([cur, got], 1), jnp.stack([got, cur], 1))
         cur = cur.reshape((-1,) + mine.shape)
         bit //= 2
-    if tie is None:
-        return cur
-    return cur, tie
+    return cur
 
 
 def scatter_sum_col(own_block, last_swap):
@@ -85,6 +81,7 @@
         kpoint_count, orb_count - NV, mu_cols
     )
 
+    valence = gather_axis(jnp.take(held_valence, wanted, axis=0), "col")
     conduction = jnp.take(held_conduction, wanted, axis=0).astype(jnp.float32)
     rows_per_block = NC // col_count
     chunk = pair_count // PAIR_CHUNKS
@@ -100,10 +97,7 @@
         return cond_pairs.reshape(chunk, rows_per_block * NC, mu_cols)
 
     cond_blocks = [[cond_block(first, d) for d in range(col_count)] for first in starts]
-
-    valence, cond_blocks = gather_axis(
-        jnp.take(held_valence, wanted, axis=0), "col", tie=cond_blocks
-    )
+    valence, cond_blocks = lax.optimization_barrier((valence, cond_blocks))
 
     def valence_of(first):
         return (

time: 69.3 us -> 63 us (0.909)
  other arithmetic: 17.2 us -> 11.2 us
  matrix products: 15.8 us -> 13 us
  waiting for transfers between devices: 16 us -> 18.2 us
    select_n x11, other arithmetic: 4.76 us -> 0.52 us  [gather_axis(): cur = jnp.where(low, jnp.stack([cur, got], 1), jnp.stack([got, cur], 1))]
    dot_general x2, matrix products: 12 us -> 9.3 us  [screened_of(): lax.dot_general(val_pairs, screen, (((0, 2), (0, 1)), ((), ())), preferre...]
    ppermute x12, waiting for transfers between devices: 16 us -> 18.2 us  [swap(): return lax.ppermute(x, axis, [(i, i ^ bit) for i in range(size)])]
    convert_element_type x1, other arithmetic: 4.34 us -> 3.08 us  [cond_block(): (rows[:, :, None, :] * cond_b[:, None, :, :]).astype(jnp.bfloat16)]
    select_n x2, other arithmetic: 1.52 us -> 0.82 us  [body(): valence = gather_axis(jnp.take(held_valence, wanted, axis=0), 'col')]
  transfers between devices with their start and end apart: 12 -> 12, of which waited for: 9 -> 8; matrix products, arithmetic and copies ran while one was open for 29% -> 28% of each run, Pallas kernels for 0% -> 0%
where the time goes in v13:
time: 63 us; the launch traced here: 62.7 us
  waiting for transfers between devices  18.2 us (29%)
  starting transfers between devices  16.7 us (27%)
  matrix products  13 us (21%)
  other arithmetic  11.2 us (18%)
  local copies, waits for them, and re-layouts  3.32 us (5%)
    ppermute x12, waiting for transfers between devices, swap(): return lax.ppermute(x, axis, [(i, i ^ bit) for i in range(size)])  18.2 us
    ppermute x12, starting transfers between devices, swap(): return lax.ppermute(x, axis, [(i, i ^ bit) for i in range(size)])  16.7 us
    dot_general x2, matrix products, screened_of(): lax.dot_general(val_pairs, screen, (((0, 2), (0, 1)), ((), ())), preferre...  9.3 us
    dot_general x8, matrix products, own_block(): jnp.einsum('pan,pbn->pab', screened, cond_pairs, preferred_element_type=j...  3.75 us
    convert_element_type x1, other arithmetic, cond_block(): (rows[:, :, None, :] * cond_b[:, None, :, :]).astype(jnp.bfloat16)  3.08 us
    convert_element_type x2, other arithmetic, screened_of(): (valence_a[:, :, :, None, :] * valence_b[:, :, None, :, :]).astype(jnp.bf...  2.78 us
    another operation x2, local copies, waits for them, and re-layouts, gather_axis(): cur = jnp.where(low, jnp.stack([cur, got], 1), jnp.stack([got, cur], 1))  1.61 us
  transfers between devices with their start and end apart: 12, of which 8 were waited for; matrix products, arithmetic and copies ran while one was open for 28% of the time, Pallas kernels for 0%

profile of v13, /device:TPU:0, one launch (start us, length us, event | category | flops | bytes accessed | tf_op | source)
XLA Modules:
  0.0 62.7 jit_solution(13872367823866094748)
XLA Ops:
  0.0 0.8 %slice_bitcast_fusion.7 = (bf16[1,1,1,16,1024]{4,3,2,1,0:T(8,128)(2,1)S(1)}, bf16[1,1,16,1024]{3,2,0,1:T(8,128)(2,1)S(1)}) fusion(bf16[1,48,1024]{2,1,0:T(8,128)(2,1)} %param.3), kind=kLoop, calls=%fused_computation.59 | loop fusion | bytes 98304 | tf_op jit(solution)/shard_map/stack | solution.py:24
  0.8 4.0 %collective-permute-start = (bf16[1,1,16,1024]{3,2,0,1:T(8,128)(2,1)S(1)}, bf16[1,1,16,1024]{3,2,0,1:T(8,128)(2,1)S(1)}, u32[]{:S(2)}, u32[]{:S(2)}) collective-permute-start(bf16[1,1,16,1024]{3,2,0,1:T(8,128)(2,1)S(1)} %get-tuple-element.50), channel_id=1, source_target_pairs={{0,16},{4,20},{8,24},{12,28},{16,0},{20,4},{24,8},{28,12},{1,17},{... | collective-permute-start | bytes 98312 | tf_op jit(solution)/shard_map/ppermute | solution.py:13
  4.8 0.8 %slice_bitcast_fusion.5 = (bf16[1,1,1,32,1024]{4,3,2,1,0:T(8,128)(2,1)S(1)}, bf16[1,1,32,1024]{3,2,0,1:T(8,128)(2,1)S(1)}) fusion(bf16[1,48,1024]{2,1,0:T(8,128)(2,1)} %param.3), kind=kLoop, calls=%fused_computation.57 | loop fusion | bytes 196608 | tf_op jit(solution)/shard_map/stack | solution.py:24
  5.7 0.7 %fusion.38 = s32[4,1]{0,1:T(1,128)S(1)} fusion(s32[]{:T(128)S(6)} %axis_index.17, s32[1,4]{1,0:T(1,128)} %param.5), kind=kLoop, calls=%fused_computation.81 | loop fusion | flops 48 | bytes 36 | tf_op jit(solution)/shard_map/concatenate | solution.py:78
  6.4 0.7 %and_select_fusion = s32[4]{0:T(128)S(1)} fusion(s32[]{:T(128)S(6)} %axis_index.17, s32[1,4]{1,0:T(1,128)} %param.5), kind=kLoop, calls=%fused_computation.74 | loop fusion | flops 48 | bytes 36 | tf_op jit(solution)/shard_map/jit(remainder)/select_n | solution.py:75
  7.1 0.7 %fusion.13 = s32[8]{0:T(128)S(1)} fusion(s32[4,1]{0,1:T(1,128)S(1)} %fusion.38, s32[4,1]{0,1:T(1,128)} %bitcast.176), kind=kLoop, calls=%fused_computation.76 | loop fusion | flops 32 | bytes 64 | tf_op jit(solution)/shard_map/jit(_take)/jit(_where)/select_n | solution.py:84
  7.8 0.7 %compare_and_fusion = pred[8]{0:T(512)(128)(4,1)S(1)} fusion(s32[4]{0:T(128)S(1)} %and_select_fusion, s32[4]{0:T(128)} %bitcast.177), kind=kLoop, calls=%fused_computation.73 | loop fusion | flops 56 | bytes 40 | tf_op jit(solution)/shard_map/jit(_take)/and | solution.py:84
  8.6 2.0 %collective-permute-start.1 = (bf16[2,1,16,1024]{3,2,0,1:T(8,128)(2,1)S(1)}, bf16[2,1,16,1024]{3,2,0,1:T(8,128)(2,1)S(1)}, u32[]{:S(2)}, u32[]{:S(2)}) collective-permute-start(bf16[2,1,16,1024]{3,2,0,1:T(8,128)(2,1)S(1)} %maximum_select_fusion.8), channel_id=1, source_target_pairs={{0,8},{4,12},{8,0},{12,4},{16,24},{20,28},{24,16},{28,20},{1,9},{5... | collective-permute-start | bytes 196616 | tf_op jit(solution)/shard_map/ppermute | solution.py:13
  10.5 0.7 %collective-permute-done.5 = bf16[1,1,32,1024]{3,2,0,1:T(8,128)(2,1)S(1)} collective-permute-done((bf16[1,1,32,1024]{3,2,0,1:T(8,128)(2,1)S(1)}, bf16[1,1,32,1024]{3,2,0,1:T(8,128)(2,1)S(1)}, u32[]{:S(2)}, u32[]{:S(2)}) %collective-permute-start.5) | collective-permute-done | bytes 65568 | tf_op jit(solution)/shard_map/ppermute | solution.py:13
  11.2 1.3 %collective-permute-start.6 = (bf16[2,1,32,1024]{3,2,0,1:T(8,128)(2,1)S(1)}, bf16[2,1,32,1024]{3,2,0,1:T(8,128)(2,1)S(1)}, u32[]{:S(2)}, u32[]{:S(2)}) collective-permute-start(bf16[2,1,32,1024]{3,2,0,1:T(8,128)(2,1)S(1)} %maximum_select_fusion.7), channel_id=1, source_target_pairs={{0,8},{4,12},{8,0},{12,4},{16,24},{20,28},{24,16},{28,20},{1,9},{5... | collective-permute-start | bytes 393224 | tf_op jit(solution)/shard_map/ppermute | solution.py:13
  12.5 1.0 %collective-permute-done.1 = bf16[2,1,16,1024]{3,2,0,1:T(8,128)(2,1)S(1)} collective-permute-done((bf16[2,1,16,1024]{3,2,0,1:T(8,128)(2,1)S(1)}, bf16[2,1,16,1024]{3,2,0,1:T(8,128)(2,1)S(1)}, u32[]{:S(2)}, u32[]{:S(2)}) %collective-permute-start.1) | collective-permute-done | bytes 65568 | tf_op jit(solution)/shard_map/ppermute | solution.py:13
  13.6 1.9 %collective-permute-start.2 = (bf16[4,1,16,1024]{3,2,0,1:T(8,128)(2,1)S(1)}, bf16[4,1,16,1024]{3,2,0,1:T(8,128)(2,1)S(1)}, u32[]{:S(2)}, u32[]{:S(2)}) collective-permute-start(bf16[4,1,16,1024]{3,2,0,1:T(8,128)(2,1)S(1)} %bitcast.164), channel_id=1, source_target_pairs={{0,4},{4,0},{8,12},{12,8},{16,20},{20,16},{24,28},{28,24},{1,5},{5... | collective-permute-start | bytes 393224 | tf_op jit(solution)/shard_map/ppermute | solution.py:13
  15.5 0.8 %collective-permute-done.6 = bf16[2,1,32,1024]{3,2,0,1:T(8,128)(2,1)S(1)} collective-permute-done((bf16[2,1,32,1024]{3,2,0,1:T(8,128)(2,1)S(1)}, bf16[2,1,32,1024]{3,2,0,1:T(8,128)(2,1)S(1)}, u32[]{:S(2)}, u32[]{:S(2)}) %collective-permute-start.6) | collective-permute-done | bytes 131104 | tf_op jit(solution)/shard_map/ppermute | solution.py:13
  16.3 1.6 %collective-permute-start.7 = (bf16[4,1,32,1024]{3,2,0,1:T(8,128)(2,1)S(1)}, bf16[4,1,32,1024]{3,2,0,1:T(8,128)(2,1)S(1)}, u32[]{:S(2)}, u32[]{:S(2)}) collective-permute-start(bf16[4,1,32,1024]{3,2,0,1:T(8,128)(2,1)S(1)} %bitcast.160), channel_id=1, source_target_pairs={{0,4},{4,0},{8,12},{12,8},{16,20},{20,16},{24,28},{28,24},{1,5},{5... | collective-permute-start | bytes 786440 | tf_op jit(solution)/shard_map/ppermute | solution.py:13
  17.9 2.0 %collective-permute-done.2 = bf16[4,1,16,1024]{3,2,0,1:T(8,128)(2,1)S(1)} collective-permute-done((bf16[4,1,16,1024]{3,2,0,1:T(8,128)(2,1)S(1)}, bf16[4,1,16,1024]{3,2,0,1:T(8,128)(2,1)S(1)}, u32[]{:S(2)}, u32[]{:S(2)}) %collective-permute-start.2) | collective-permute-done | bytes 131104 | tf_op jit(solution)/shard_map/ppermute | solution.py:13
  20.0 0.6 gather_fusion
  20.7 1.9 %collective-permute-start.3 = (bf16[1,8,16,1024]{3,2,1,0:T(8,128)(2,1)S(1)}, bf16[1,8,16,1024]{3,2,1,0:T(8,128)(2,1)S(1)}, u32[]{:S(2)}, u32[]{:S(2)}) collective-permute-start(bf16[1,8,16,1024]{3,2,1,0:T(8,128)(2,1)S(1)} %bitcast_select_fusion), channel_id=1, source_target_pairs={{0,2},{1,3},{2,0},{3,1},{4,6},{5,7},{6,4},{7,5},{8,10},{9,11},{10,... | collective-permute-start | bytes 786440 | tf_op jit(solution)/shard_map/ppermute | solution.py:13
  22.7 1.1 %collective-permute-done.7 = bf16[4,1,32,1024]{3,2,0,1:T(8,128)(2,1)S(1)} collective-permute-done((bf16[4,1,32,1024]{3,2,0,1:T(8,128)(2,1)S(1)}, bf16[4,1,32,1024]{3,2,0,1:T(8,128)(2,1)S(1)}, u32[]{:S(2)}, u32[]{:S(2)}) %collective-permute-start.7) | collective-permute-done | bytes 262176 | tf_op jit(solution)/shard_map/ppermute | solution.py:13
  24.0 0.6 gather_fusion.1
  24.9 2.2 %collective-permute-done.3 = bf16[1,8,16,1024]{3,2,1,0:T(8,128)(2,1)S(1)} collective-permute-done((bf16[1,8,16,1024]{3,2,1,0:T(8,128)(2,1)S(1)}, bf16[1,8,16,1024]{3,2,1,0:T(8,128)(2,1)S(1)}, u32[]{:S(2)}, u32[]{:S(2)}) %collective-permute-start.3) | collective-permute-done | bytes 262176 | tf_op jit(solution)/shard_map/ppermute | solution.py:13
  27.3 3.1 %multiply_convert_fusion.2 = (bf16[2,8,32,1024]{3,2,1,0:T(8,128)(2,1)S(1)}, bf16[2,8,32,1024]{3,2,1,0:T(8,128)(2,1)S(1)}, bf16[2,8,32,1024]{3,2,1,0:T(8,128)(2,1...) fusion(f32[2,8,1024]{2,1,0:T(8,128)S(1)} %get-tuple-element.35,, ...), kind=kLoop, calls=%fused_computation.6 | loop fusion | flops 8388608 | bytes 9437184 | tf_op jit(solution)/shard_map/convert_element_type | solution.py:96
  31.0 1.4 %multiply_convert_fusion.1 = bf16[4,2,16,16,1024]{4,3,2,1,0:T(8,128)(2,1)S(1)} fusion(f32[4,2,16,1024]{3,2,1,0:T(8,128)S(1)} %get-tuple-element.26, f32[4,2,16,1024]{3,2,1,0:T(8,128)S(1)} %get-tuple-element.23), kind=kLoop, calls=%fused_computation.3 | loop fusion | flops 4194304 | bytes 5242880 | tf_op jit(solution)/shard_map/convert_element_type | solution.py:58
  32.6 4.6 %bitcast_convert_fusion.1 = bf16[512,1024]{1,0:T(8,128)(2,1)S(1)} fusion(bf16[4,512,1024]{2,1,0:T(8,128)(2,1)S(1)} %bitcast.147, bf16[4,1024,1024]{2,1,0:T(8,128)(2,1)S(1)} %bitcast.174), kind=kOutput, calls=%fused_computation.5 | convolution fusion | flops 4295491584 | bytes 13631488 | tf_op jit(solution)/shard_map/dot_general | solution.py:61
  38.2 0.5 collective-permute-start.8
  38.8 1.4 %multiply_convert_fusion = bf16[4,2,16,16,1024]{4,3,2,1,0:T(8,128)(2,1)S(1)} fusion(f32[4,2,16,1024]{3,2,1,0:T(8,128)S(1)} %get-tuple-element.24, f32[4,2,16,1024]{3,2,1,0:T(8,128)S(1)} %get-tuple-element.25), kind=kLoop, calls=%fused_computation.2 | loop fusion | flops 4194304 | bytes 5242880 | tf_op jit(solution)/shard_map/convert_element_type | solution.py:58
  40.2 4.7 %bitcast_convert_fusion = bf16[512,1024]{1,0:T(8,128)(2,1)S(1)} fusion(bf16[4,512,1024]{2,1,0:T(8,128)(2,1)S(1)} %bitcast.148, bf16[4,1024,1024]{2,1,0:T(8,128)(2,1)S(1)} %bitcast.175), kind=kOutput, calls=%fused_computation.4 | convolution fusion | flops 4295491584 | bytes 13631488 | tf_op jit(solution)/shard_map/dot_general | solution.py:61
  47.0 1.9 %collective-permute-start.9 = (bf16[1,2,256,256]{3,2,1,0:T(8,128)(2,1)S(1)}, bf16[1,2,256,256]{3,2,1,0:T(8,128)(2,1)S(1)}, u32[]{:S(2)}, u32[]{:S(2)}) collective-permute-start(bf16[1,2,256,256]{3,2,1,0:T(8,128)(2,1)S(1)} %fusion.8), channel_id=1, source_target_pairs={{0,2},{1,3},{2,0},{3,1},{4,6},{5,7},{6,4},{7,5},{8,10},{9,11},{10,... | collective-permute-start | bytes 786440 | tf_op jit(solution)/shard_map/ppermute | solution.py:13
  49.5 0.5 fusion.9
  50.0 1.2 %collective-permute-start.11 = (bf16[1,2,256,256]{3,2,1,0:T(8,128)(2,1)S(1)}, bf16[1,2,256,256]{3,2,1,0:T(8,128)(2,1)S(1)}, u32[]{:S(2)}, u32[]{:S(2)}) collective-permute-start(bf16[1,2,256,256]{3,2,1,0:T(8,128)(2,1)S(1)} %fusion.9), channel_id=1, source_target_pairs={{0,2},{1,3},{2,0},{3,1},{4,6},{5,7},{6,4},{7,5},{8,10},{9,11},{10,... | collective-permute-start | bytes 786440 | tf_op jit(solution)/shard_map/ppermute | solution.py:13
  51.1 5.1 %collective-permute-done.9 = bf16[1,2,256,256]{3,2,1,0:T(8,128)(2,1)S(1)} collective-permute-done((bf16[1,2,256,256]{3,2,1,0:T(8,128)(2,1)S(1)}, bf16[1,2,256,256]{3,2,1,0:T(8,128)(2,1)S(1)}, u32[]{:S(2)}, u32[]{:S(2)}) %collective-permute-start.9) | collective-permute-done | bytes 262176 | tf_op jit(solution)/shard_map/ppermute | solution.py:13
  56.4 5.2 %collective-permute-done.11 = bf16[1,2,256,256]{3,2,1,0:T(8,128)(2,1)S(1)} collective-permute-done((bf16[1,2,256,256]{3,2,1,0:T(8,128)(2,1)S(1)}, bf16[1,2,256,256]{3,2,1,0:T(8,128)(2,1)S(1)}, u32[]{:S(2)}, u32[]{:S(2)}) %collective-permute-start.11) | collective-permute-done | bytes 262176 | tf_op jit(solution)/shard_map/ppermute | solution.py:13
  61.7 1.0 %maximum_bitcast_fusion = f32[1,4,256,256]{3,2,1,0:T(8,128)} fusion(f32[2,256,256]{2,1,0:T(8,128)S(1)} %fusion.3, f32[2,256,256]{2,1,0:T(8,128)S(1)} %fusion.7), kind=kLoop, calls=%fused_computation.21 | loop fusion | flops 262144 | bytes 2097152 | tf_op jit(solution)/shard_map/broadcast_in_dim | solution.py:126
  (45 shorter events, 5.6 us)
Async XLA Ops:
  0.8 7.8 %collective-permute-start = (bf16[1,1,16,1024]{3,2,0,1:T(8,128)(2,1)S(1)}, bf16[1,1,16,1024]{3,2,0,1:T(8,128)(2,1)S(1)}, u32[]{:S(2)}, u32[]{:S(2)}) collective-permute-start(bf16[1,1,16,1024]{3,2,0,1:T(8,128)(2,1)S(1)} %get-tuple-element.50), channel_id=1, source_target_pairs={{0,16},{4,20},{8,24},{12,28},{16,0},{20,4},{24,8},{28,12},{1,17},{... | collective-permute-start | bytes 98312 | tf_op jit(solution)/shard_map/ppermute | solution.py:13
  5.7 5.6 %collective-permute-start.5 = (bf16[1,1,32,1024]{3,2,0,1:T(8,128)(2,1)S(1)}, bf16[1,1,32,1024]{3,2,0,1:T(8,128)(2,1)S(1)}, u32[]{:S(2)}, u32[]{:S(2)}) collective-permute-start(bf16[1,1,32,1024]{3,2,0,1:T(8,128)(2,1)S(1)} %get-tuple-element.48), channel_id=1, source_target_pairs={{0,16},{4,20},{8,24},{12,28},{16,0},{20,4},{24,8},{28,12},{1,17},{... | collective-permute-start | bytes 196616 | tf_op jit(solution)/shard_map/ppermute | solution.py:13
  8.6 5.0 %collective-permute-start.1 = (bf16[2,1,16,1024]{3,2,0,1:T(8,128)(2,1)S(1)}, bf16[2,1,16,1024]{3,2,0,1:T(8,128)(2,1)S(1)}, u32[]{:S(2)}, u32[]{:S(2)}) collective-permute-start(bf16[2,1,16,1024]{3,2,0,1:T(8,128)(2,1)S(1)} %maximum_select_fusion.8), channel_id=1, source_target_pairs={{0,8},{4,12},{8,0},{12,4},{16,24},{20,28},{24,16},{28,20},{1,9},{5... | collective-permute-start | bytes 196616 | tf_op jit(solution)/shard_map/ppermute | solution.py:13
  11.2 5.0 %collective-permute-start.6 = (bf16[2,1,32,1024]{3,2,0,1:T(8,128)(2,1)S(1)}, bf16[2,1,32,1024]{3,2,0,1:T(8,128)(2,1)S(1)}, u32[]{:S(2)}, u32[]{:S(2)}) collective-permute-start(bf16[2,1,32,1024]{3,2,0,1:T(8,128)(2,1)S(1)} %maximum_select_fusion.7), channel_id=1, source_target_pairs={{0,8},{4,12},{8,0},{12,4},{16,24},{20,28},{24,16},{28,20},{1,9},{5... | collective-permute-start | bytes 393224 | tf_op jit(solution)/shard_map/ppermute | solution.py:13
  13.6 6.3 %collective-permute-start.2 = (bf16[4,1,16,1024]{3,2,0,1:T(8,128)(2,1)S(1)}, bf16[4,1,16,1024]{3,2,0,1:T(8,128)(2,1)S(1)}, u32[]{:S(2)}, u32[]{:S(2)}) collective-permute-start(bf16[4,1,16,1024]{3,2,0,1:T(8,128)(2,1)S(1)} %bitcast.164), channel_id=1, source_target_pairs={{0,4},{4,0},{8,12},{12,8},{16,20},{20,16},{24,28},{28,24},{1,5},{5... | collective-permute-start | bytes 393224 | tf_op jit(solution)/shard_map/ppermute | solution.py:13
  16.3 7.5 %collective-permute-start.7 = (bf16[4,1,32,1024]{3,2,0,1:T(8,128)(2,1)S(1)}, bf16[4,1,32,1024]{3,2,0,1:T(8,128)(2,1)S(1)}, u32[]{:S(2)}, u32[]{:S(2)}) collective-permute-start(bf16[4,1,32,1024]{3,2,0,1:T(8,128)(2,1)S(1)} %bitcast.160), channel_id=1, source_target_pairs={{0,4},{4,0},{8,12},{12,8},{16,20},{20,16},{24,28},{28,24},{1,5},{5... | collective-permute-start | bytes 786440 | tf_op jit(solution)/shard_map/ppermute | solution.py:13
  20.7 6.4 %collective-permute-start.3 = (bf16[1,8,16,1024]{3,2,1,0:T(8,128)(2,1)S(1)}, bf16[1,8,16,1024]{3,2,1,0:T(8,128)(2,1)S(1)}, u32[]{:S(2)}, u32[]{:S(2)}) collective-permute-start(bf16[1,8,16,1024]{3,2,1,0:T(8,128)(2,1)S(1)} %bitcast_select_fusion), channel_id=1, source_target_pairs={{0,2},{1,3},{2,0},{3,1},{4,6},{5,7},{6,4},{7,5},{8,10},{9,11},{10,... | collective-permute-start | bytes 786440 | tf_op jit(solution)/shard_map/ppermute | solution.py:13
  27.2 3.3 %collective-permute-start.4 = (bf16[2,8,16,1024]{3,2,1,0:T(8,128)(2,1)S(1)}, bf16[2,8,16,1024]{3,2,1,0:T(8,128)(2,1)S(1)}, u32[]{:S(2)}, u32[]{:S(2)}) collective-permute-start(bf16[2,8,16,1024]{3,2,1,0:T(8,128)(2,1)S(1)} %maximum_select_fusion.2), channel_id=1, source_target_pairs={{0,1},{1,0},{2,3},{3,2},{4,5},{5,4},{6,7},{7,6},{8,9},{9,8},{10,11... | collective-permute-start | bytes 1572872 | tf_op jit(solution)/shard_map/ppermute | solution.py:13
  27.3 5.2 %slice-start = ((s8[8388608]{0:T(1024)(128)(4,1)}), s8[4194304]{0:T(1024)(128)(4,1)S(1)}, s32[]{:S(2)}) async-start(s8[8388608]{0:T(1024)(128)(4,1)} %bitcast.172), calls=%async_computation | async-start | bytes 8388608
  30.5 2.2 %slice-start.1 = ((s8[8388608]{0:T(1024)(128)(4,1)}), s8[4194304]{0:T(1024)(128)(4,1)S(1)}, s32[]{:S(2)}) async-start(s8[8388608]{0:T(1024)(128)(4,1)} %bitcast.172), calls=%async_computation.1 | async-start | bytes 8388608
  38.2 8.3 %collective-permute-start.8 = (f32[2,2,256,256]{3,2,1,0:T(8,128)S(1)}, f32[2,2,256,256]{3,2,1,0:T(8,128)S(1)}, u32[]{:S(2)}, u32[]{:S(2)}) collective-permute-start(f32[2,2,256,256]{3,2,1,0:T(8,128)S(1)} %pad_maximum_fusion), channel_id=1, source_target_pairs={{0,1},{1,0},{2,3},{3,2},{4,5},{5,4},{6,7},{7,6},{8,9},{9,8},{10,11... | collective-permute-start | bytes 3145736 | tf_op jit(solution)/shard_map/ppermute | solution.py:13
  46.0 3.5 %collective-permute-start.10 = (f32[2,2,256,256]{3,2,1,0:T(8,128)S(1)}, f32[2,2,256,256]{3,2,1,0:T(8,128)S(1)}, u32[]{:S(2)}, u32[]{:S(2)}) collective-permute-start(f32[2,2,256,256]{3,2,1,0:T(8,128)S(1)} %pad_maximum_fusion.1), channel_id=1, source_target_pairs={{0,1},{1,0},{2,3},{3,2},{4,5},{5,4},{6,7},{7,6},{8,9},{9,8},{10,11... | collective-permute-start | bytes 3145736 | tf_op jit(solution)/shard_map/ppermute | solution.py:13
  47.0 9.2 %collective-permute-start.9 = (bf16[1,2,256,256]{3,2,1,0:T(8,128)(2,1)S(1)}, bf16[1,2,256,256]{3,2,1,0:T(8,128)(2,1)S(1)}, u32[]{:S(2)}, u32[]{:S(2)}) collective-permute-start(bf16[1,2,256,256]{3,2,1,0:T(8,128)(2,1)S(1)} %fusion.8), channel_id=1, source_target_pairs={{0,2},{1,3},{2,0},{3,1},{4,6},{5,7},{6,4},{7,5},{8,10},{9,11},{10,... | collective-permute-start | bytes 786440 | tf_op jit(solution)/shard_map/ppermute | solution.py:13
  50.0 11.6 %collective-permute-start.11 = (bf16[1,2,256,256]{3,2,1,0:T(8,128)(2,1)S(1)}, bf16[1,2,256,256]{3,2,1,0:T(8,128)(2,1)S(1)}, u32[]{:S(2)}, u32[]{:S(2)}) collective-permute-start(bf16[1,2,256,256]{3,2,1,0:T(8,128)(2,1)S(1)} %fusion.9), channel_id=1, source_target_pairs={{0,2},{1,3},{2,0},{3,1},{4,6},{5,7},{6,4},{7,5},{8,10},{9,11},{10,... | collective-permute-start | bytes 786440 | tf_op jit(solution)/shard_map/ppermute | solution.py:13

commit v14 on v11

--- a/solution.py
+++ b/solution.py
@@ -20,11 +20,11 @@
     bit = count // 2
     while bit >= 1:
         got = swap(cur, axis, bit)
-        if tie is not None and bit > 1:
-            got, tie = lax.optimization_barrier((got, tie))
         low = (me & bit) == 0
         cur = jnp.where(low, jnp.stack([cur, got], 1), jnp.stack([got, cur], 1))
         cur = cur.reshape((-1,) + mine.shape)
+        if tie is not None and bit > 1:
+            cur, tie = lax.optimization_barrier((cur, tie))
         bit //= 2
     if tie is None:
         return cur
@@ -100,7 +100,6 @@
         return cond_pairs.reshape(chunk, rows_per_block * NC, mu_cols)
 
     cond_blocks = [[cond_block(first, d) for d in range(col_count)] for first in starts]
-
     valence, cond_blocks = gather_axis(
         jnp.take(held_valence, wanted, axis=0), "col", tie=cond_blocks
     )

time: 69.3 us -> 69.4 us (level)
  waiting for transfers between devices: 16 us -> 17.9 us
  other arithmetic: 17.2 us -> 15.4 us
    ppermute x12, waiting for transfers between devices: 16 us -> 17.9 us  [swap(): return lax.ppermute(x, axis, [(i, i ^ bit) for i in range(size)])]
    select_n x11 -> x10, other arithmetic: 4.76 us -> 3.82 us  [gather_axis(): cur = jnp.where(low, jnp.stack([cur, got], 1), jnp.stack([got, cur], 1))]
    select_n x2, other arithmetic: 1.52 us -> 0.82 us  [body(): jnp.take(held_valence, wanted, axis=0)]
  transfers between devices with their start and end apart: 12 -> 12, of which waited for: 9 -> 9; matrix products, arithmetic and copies ran while one was open for 29% -> 26% of each run, Pallas kernels for 0% -> 0%
where the time goes in v14:
time: 69.4 us; the launch traced here: 69.1 us
  waiting for transfers between devices  17.9 us (26%)
  starting transfers between devices  16.6 us (24%)
  matrix products  15.7 us (23%)
  other arithmetic  15.4 us (22%)
  local copies, waits for them, and re-layouts  3.08 us (4%)
    ppermute x12, waiting for transfers between devices, swap(): return lax.ppermute(x, axis, [(i, i ^ bit) for i in range(size)])  17.9 us
    ppermute x12, starting transfers between devices, swap(): return lax.ppermute(x, axis, [(i, i ^ bit) for i in range(size)])  16.6 us
    dot_general x2, matrix products, screened_of(): lax.dot_general(val_pairs, screen, (((0, 2), (0, 1)), ((), ())), preferre...  11.9 us
    convert_element_type x1, other arithmetic, cond_block(): (rows[:, :, None, :] * cond_b[:, None, :, :]).astype(jnp.bfloat16)  4.34 us
    select_n x10, other arithmetic, gather_axis(): cur = jnp.where(low, jnp.stack([cur, got], 1), jnp.stack([got, cur], 1))  3.82 us
    dot_general x8, matrix products, own_block(): jnp.einsum('pan,pbn->pab', screened, cond_pairs, preferred_element_type=j...  3.77 us
    convert_element_type x2, other arithmetic, screened_of(): (valence_a[:, :, :, None, :] * valence_b[:, :, None, :, :]).astype(jnp.bf...  2.78 us
    another operation x2, local copies, waits for them, and re-layouts, gather_axis(): cur = jnp.where(low, jnp.stack([cur, got], 1), jnp.stack([got, cur], 1))  1.61 us
  transfers between devices with their start and end apart: 12, of which 9 were waited for; matrix products, arithmetic and copies ran while one was open for 26% of the time, Pallas kernels for 0%

profile of v14, /device:TPU:0, one launch (start us, length us, event | category | flops | bytes accessed | tf_op | source)
XLA Modules:
  0.0 69.1 jit_solution(9873245304883645483)
XLA Ops:
  0.0 0.8 %slice_bitcast_fusion.7 = (bf16[1,1,1,16,1024]{4,3,2,1,0:T(8,128)(2,1)S(1)}, bf16[1,1,16,1024]{3,2,0,1:T(8,128)(2,1)S(1)}) fusion(bf16[1,48,1024]{2,1,0:T(8,128)(2,1)} %param.3), kind=kLoop, calls=%fused_computation.58 | loop fusion | bytes 98304 | tf_op jit(solution)/shard_map/stack | solution.py:24
  0.8 4.0 %collective-permute-start = (bf16[1,1,16,1024]{3,2,0,1:T(8,128)(2,1)S(1)}, bf16[1,1,16,1024]{3,2,0,1:T(8,128)(2,1)S(1)}, u32[]{:S(2)}, u32[]{:S(2)}) collective-permute-start(bf16[1,1,16,1024]{3,2,0,1:T(8,128)(2,1)S(1)} %get-tuple-element.50), channel_id=1, source_target_pairs={{0,16},{4,20},{8,24},{12,28},{16,0},{20,4},{24,8},{28,12},{1,17},{... | collective-permute-start | bytes 98312 | tf_op jit(solution)/shard_map/ppermute | solution.py:13
  4.8 0.8 %slice_bitcast_fusion.5 = (bf16[1,1,1,32,1024]{4,3,2,1,0:T(8,128)(2,1)S(1)}, bf16[1,1,32,1024]{3,2,0,1:T(8,128)(2,1)S(1)}) fusion(bf16[1,48,1024]{2,1,0:T(8,128)(2,1)} %param.3), kind=kLoop, calls=%fused_computation.56 | loop fusion | bytes 196608 | tf_op jit(solution)/shard_map/stack | solution.py:24
  5.7 0.7 fusion.35
  6.4 0.7 and_select_fusion
  7.1 0.7 %fusion.13 = s32[8]{0:T(128)S(1)} fusion(s32[4,1]{0,1:T(1,128)S(1)} %fusion.35, s32[4,1]{0,1:T(1,128)} %bitcast.170), kind=kLoop, calls=%fused_computation.75 | loop fusion | flops 32 | bytes 64 | tf_op jit(solution)/shard_map/jit(_take)/jit(_where)/select_n | solution.py:104
  7.8 0.7 %compare_and_fusion = pred[8]{0:T(512)(128)(4,1)S(1)} fusion(s32[4]{0:T(128)S(1)} %and_select_fusion, s32[4]{0:T(128)} %bitcast.171), kind=kLoop, calls=%fused_computation.72 | loop fusion | flops 56 | bytes 40 | tf_op jit(solution)/shard_map/jit(_take)/and | solution.py:104
  8.6 2.0 %collective-permute-start.1 = (bf16[2,1,16,1024]{3,2,0,1:T(8,128)(2,1)S(1)}, bf16[2,1,16,1024]{3,2,0,1:T(8,128)(2,1)S(1)}, u32[]{:S(2)}, u32[]{:S(2)}) collective-permute-start(bf16[2,1,16,1024]{3,2,0,1:T(8,128)(2,1)S(1)} %maximum_select_fusion.7), channel_id=1, source_target_pairs={{0,8},{4,12},{8,0},{12,4},{16,24},{20,28},{24,16},{28,20},{1,9},{5... | collective-permute-start | bytes 196616 | tf_op jit(solution)/shard_map/ppermute | solution.py:13
  10.5 0.7 %collective-permute-done.4 = bf16[1,1,32,1024]{3,2,0,1:T(8,128)(2,1)S(1)} collective-permute-done((bf16[1,1,32,1024]{3,2,0,1:T(8,128)(2,1)S(1)}, bf16[1,1,32,1024]{3,2,0,1:T(8,128)(2,1)S(1)}, u32[]{:S(2)}, u32[]{:S(2)}) %collective-permute-start.4) | collective-permute-done | bytes 65568 | tf_op jit(solution)/shard_map/ppermute | solution.py:13
  11.2 1.3 %collective-permute-start.5 = (bf16[2,1,32,1024]{3,2,0,1:T(8,128)(2,1)S(1)}, bf16[2,1,32,1024]{3,2,0,1:T(8,128)(2,1)S(1)}, u32[]{:S(2)}, u32[]{:S(2)}) collective-permute-start(bf16[2,1,32,1024]{3,2,0,1:T(8,128)(2,1)S(1)} %maximum_select_fusion.6), channel_id=1, source_target_pairs={{0,8},{4,12},{8,0},{12,4},{16,24},{20,28},{24,16},{28,20},{1,9},{5... | collective-permute-start | bytes 393224 | tf_op jit(solution)/shard_map/ppermute | solution.py:13
  12.5 1.0 %collective-permute-done.1 = bf16[2,1,16,1024]{3,2,0,1:T(8,128)(2,1)S(1)} collective-permute-done((bf16[2,1,16,1024]{3,2,0,1:T(8,128)(2,1)S(1)}, bf16[2,1,16,1024]{3,2,0,1:T(8,128)(2,1)S(1)}, u32[]{:S(2)}, u32[]{:S(2)}) %collective-permute-start.1) | collective-permute-done | bytes 65568 | tf_op jit(solution)/shard_map/ppermute | solution.py:13
  13.6 1.9 %collective-permute-start.2 = (bf16[4,1,16,1024]{3,2,0,1:T(8,128)(2,1)S(1)}, bf16[4,1,16,1024]{3,2,0,1:T(8,128)(2,1)S(1)}, u32[]{:S(2)}, u32[]{:S(2)}) collective-permute-start(bf16[4,1,16,1024]{3,2,0,1:T(8,128)(2,1)S(1)} %bitcast.158), channel_id=1, source_target_pairs={{0,4},{4,0},{8,12},{12,8},{16,20},{20,16},{24,28},{28,24},{1,5},{5... | collective-permute-start | bytes 393224 | tf_op jit(solution)/shard_map/ppermute | solution.py:13
  15.5 0.8 %collective-permute-done.5 = bf16[2,1,32,1024]{3,2,0,1:T(8,128)(2,1)S(1)} collective-permute-done((bf16[2,1,32,1024]{3,2,0,1:T(8,128)(2,1)S(1)}, bf16[2,1,32,1024]{3,2,0,1:T(8,128)(2,1)S(1)}, u32[]{:S(2)}, u32[]{:S(2)}) %collective-permute-start.5) | collective-permute-done | bytes 131104 | tf_op jit(solution)/shard_map/ppermute | solution.py:13
  16.3 1.6 %collective-permute-start.6 = (bf16[4,1,32,1024]{3,2,0,1:T(8,128)(2,1)S(1)}, bf16[4,1,32,1024]{3,2,0,1:T(8,128)(2,1)S(1)}, u32[]{:S(2)}, u32[]{:S(2)}) collective-permute-start(bf16[4,1,32,1024]{3,2,0,1:T(8,128)(2,1)S(1)} %bitcast.156), channel_id=1, source_target_pairs={{0,4},{4,0},{8,12},{12,8},{16,20},{20,16},{24,28},{28,24},{1,5},{5... | collective-permute-start | bytes 786440 | tf_op jit(solution)/shard_map/ppermute | solution.py:13
  17.9 2.0 %collective-permute-done.2 = bf16[4,1,16,1024]{3,2,0,1:T(8,128)(2,1)S(1)} collective-permute-done((bf16[4,1,16,1024]{3,2,0,1:T(8,128)(2,1)S(1)}, bf16[4,1,16,1024]{3,2,0,1:T(8,128)(2,1)S(1)}, u32[]{:S(2)}, u32[]{:S(2)}) %collective-permute-start.2) | collective-permute-done | bytes 131104 | tf_op jit(solution)/shard_map/ppermute | solution.py:13
  20.0 0.6 gather_fusion
  20.7 1.9 %collective-permute-start.3 = (bf16[1,8,16,1024]{3,2,1,0:T(8,128)(2,1)S(1)}, bf16[1,8,16,1024]{3,2,1,0:T(8,128)(2,1)}, u32[]{:S(2)}, u32[]{:S(2)}) collective-permute-start(bf16[1,8,16,1024]{3,2,1,0:T(8,128)(2,1)S(1)} %bitcast_select_fusion), channel_id=1, source_target_pairs={{0,2},{1,3},{2,0},{3,1},{4,6},{5,7},{6,4},{7,5},{8,10},{9,11},{10,... | collective-permute-start | bytes 786440 | tf_op jit(solution)/shard_map/ppermute | solution.py:13
  22.6 1.2 %collective-permute-done.6 = bf16[4,1,32,1024]{3,2,0,1:T(8,128)(2,1)S(1)} collective-permute-done((bf16[4,1,32,1024]{3,2,0,1:T(8,128)(2,1)S(1)}, bf16[4,1,32,1024]{3,2,0,1:T(8,128)(2,1)S(1)}, u32[]{:S(2)}, u32[]{:S(2)}) %collective-permute-start.6) | collective-permute-done | bytes 262176 | tf_op jit(solution)/shard_map/ppermute | solution.py:13
  23.9 0.6 gather_fusion.1
  24.8 4.3 %multiply_convert_fusion.2 = (bf16[2,8,32,1024]{3,2,1,0:T(8,128)(2,1)}, bf16[2,8,32,1024]{3,2,1,0:T(8,128)(2,1)S(1)}, bf16[2,8,32,1024]{3,2,1,0:T(8,128)(2,1)}, ...) fusion(f32[2,8,1024]{2,1,0:T(8,128)S(1)} %get-tuple-element.35,, ...), kind=kLoop, calls=%fused_computation.6 | loop fusion | flops 8388608 | bytes 9437184 | tf_op jit(solution)/shard_map/convert_element_type | solution.py:99
  29.2 1.9 %maximum_select_fusion.1 = bf16[2,8,16,1024]{3,2,1,0:T(8,128)(2,1)} fusion(bf16[1,8,16,1024]{3,2,1,0:T(8,128)(2,1)} %collective-permute-done.3, bf16[1,8,16,1024]{3,2,1,0:T(8,128)(2,1)S(1)} %bitcast_select_fusion, pred[]{:T(512)S(6)} %eq.21), kind=kLoop, calls=%fused_computation.34 | loop fusion | flops 786432 | bytes 1048577 | tf_op jit(solution)/shard_map/jit(_where)/select_n | solution.py:24
  31.1 2.2 %collective-permute-done.7 = bf16[2,8,16,1024]{3,2,1,0:T(8,128)(2,1)} collective-permute-done((bf16[2,8,16,1024]{3,2,1,0:T(8,128)(2,1)}, bf16[2,8,16,1024]{3,2,1,0:T(8,128)(2,1)}, u32[]{:S(2)}, u32[]{:S(2)}) %collective-permute-start.7) | collective-permute-done | bytes 524320 | tf_op jit(solution)/shard_map/ppermute | solution.py:13
  33.4 1.7 %maximum_select_fusion = bf16[2,2,8,16,1024]{4,3,2,0,1:T(8,128)(2,1)S(1)} fusion(bf16[2,1,8,16,1024]{4,3,2,0,1:T(8,128)(2,1)} %bitcast.34, bf16[2,1,8,16,1024]{4,3,2,0,1:T(8,128)(2,1)} %bitcast.33, pred[]{:T(512)S(6)} %eq.20), kind=kLoop, calls=%fused_computation.18 | loop fusion | flops 1572864 | bytes 2097153 | tf_op jit(solution)/shard_map/jit(_where)/select_n | solution.py:24
  35.5 1.4 %multiply_convert_fusion.1 = bf16[4,2,16,16,1024]{4,3,2,1,0:T(8,128)(2,1)S(1)} fusion(f32[4,2,16,1024]{3,2,1,0:T(8,128)S(1)} %get-tuple-element.26, f32[4,2,16,1024]{3,2,1,0:T(8,128)S(1)} %get-tuple-element.23), kind=kLoop, calls=%fused_computation.3 | loop fusion | flops 4194304 | bytes 5242880 | tf_op jit(solution)/shard_map/convert_element_type | solution.py:62
  36.9 7.4 %bitcast_convert_fusion.1 = bf16[512,1024]{1,0:T(8,128)(2,1)S(1)} fusion(bf16[4,512,1024]{2,1,0:T(8,128)(2,1)S(1)} %bitcast.143, bf16[4,1024,1024]{2,1,0:T(8,128)(2,1)} %bitcast.166), kind=kOutput, calls=%fused_computation.5 | convolution fusion | flops 4295491584 | bytes 13631488 | tf_op jit(solution)/shard_map/dot_general | solution.py:65
  45.5 1.4 %multiply_convert_fusion = bf16[4,2,16,16,1024]{4,3,2,1,0:T(8,128)(2,1)S(1)} fusion(f32[4,2,16,1024]{3,2,1,0:T(8,128)S(1)} %get-tuple-element.24, f32[4,2,16,1024]{3,2,1,0:T(8,128)S(1)} %get-tuple-element.25), kind=kLoop, calls=%fused_computation.2 | loop fusion | flops 4194304 | bytes 5242880 | tf_op jit(solution)/shard_map/convert_element_type | solution.py:62
  47.0 4.6 %bitcast_convert_fusion = bf16[512,1024]{1,0:T(8,128)(2,1)S(1)} fusion(bf16[4,512,1024]{2,1,0:T(8,128)(2,1)S(1)} %bitcast.144, bf16[4,1024,1024]{2,1,0:T(8,128)(2,1)S(1)} %bitcast.169), kind=kOutput, calls=%fused_computation.4 | convolution fusion | flops 4295491584 | bytes 13631488 | tf_op jit(solution)/shard_map/dot_general | solution.py:65
  53.6 1.6 %collective-permute-start.9 = (bf16[1,2,256,256]{3,2,1,0:T(8,128)(2,1)S(1)}, bf16[1,2,256,256]{3,2,1,0:T(8,128)(2,1)S(1)}, u32[]{:S(2)}, u32[]{:S(2)}) collective-permute-start(bf16[1,2,256,256]{3,2,1,0:T(8,128)(2,1)S(1)} %fusion.8), channel_id=1, source_target_pairs={{0,2},{1,3},{2,0},{3,1},{4,6},{5,7},{6,4},{7,5},{8,10},{9,11},{10,... | collective-permute-start | bytes 786440 | tf_op jit(solution)/shard_map/ppermute | solution.py:13
  55.8 1.6 %collective-permute-start.11 = (bf16[1,2,256,256]{3,2,1,0:T(8,128)(2,1)S(1)}, bf16[1,2,256,256]{3,2,1,0:T(8,128)(2,1)S(1)}, u32[]{:S(2)}, u32[]{:S(2)}) collective-permute-start(bf16[1,2,256,256]{3,2,1,0:T(8,128)(2,1)S(1)} %fusion.9), channel_id=1, source_target_pairs={{0,2},{1,3},{2,0},{3,1},{4,6},{5,7},{6,4},{7,5},{8,10},{9,11},{10,... | collective-permute-start | bytes 786440 | tf_op jit(solution)/shard_map/ppermute | solution.py:13
  57.4 5.3 %collective-permute-done.9 = bf16[1,2,256,256]{3,2,1,0:T(8,128)(2,1)S(1)} collective-permute-done((bf16[1,2,256,256]{3,2,1,0:T(8,128)(2,1)S(1)}, bf16[1,2,256,256]{3,2,1,0:T(8,128)(2,1)S(1)}, u32[]{:S(2)}, u32[]{:S(2)}) %collective-permute-start.9) | collective-permute-done | bytes 262176 | tf_op jit(solution)/shard_map/ppermute | solution.py:13
  63.3 4.3 %collective-permute-done.11 = bf16[1,2,256,256]{3,2,1,0:T(8,128)(2,1)S(1)} collective-permute-done((bf16[1,2,256,256]{3,2,1,0:T(8,128)(2,1)S(1)}, bf16[1,2,256,256]{3,2,1,0:T(8,128)(2,1)S(1)}, u32[]{:S(2)}, u32[]{:S(2)}) %collective-permute-start.11) | collective-permute-done | bytes 262176 | tf_op jit(solution)/shard_map/ppermute | solution.py:13
  68.1 1.0 %maximum_bitcast_fusion = f32[1,4,256,256]{3,2,1,0:T(8,128)} fusion(f32[2,256,256]{2,1,0:T(8,128)S(1)} %fusion.3, f32[2,256,256]{2,1,0:T(8,128)S(1)} %fusion.7), kind=kLoop, calls=%fused_computation.21 | loop fusion | flops 262144 | bytes 2097152 | tf_op jit(solution)/shard_map/broadcast_in_dim | solution.py:131
  (51 shorter events, 5.9 us)
Async XLA Ops:
  0.8 7.8 %collective-permute-start = (bf16[1,1,16,1024]{3,2,0,1:T(8,128)(2,1)S(1)}, bf16[1,1,16,1024]{3,2,0,1:T(8,128)(2,1)S(1)}, u32[]{:S(2)}, u32[]{:S(2)}) collective-permute-start(bf16[1,1,16,1024]{3,2,0,1:T(8,128)(2,1)S(1)} %get-tuple-element.50), channel_id=1, source_target_pairs={{0,16},{4,20},{8,24},{12,28},{16,0},{20,4},{24,8},{28,12},{1,17},{... | collective-permute-start | bytes 98312 | tf_op jit(solution)/shard_map/ppermute | solution.py:13
  5.7 5.6 %collective-permute-start.4 = (bf16[1,1,32,1024]{3,2,0,1:T(8,128)(2,1)S(1)}, bf16[1,1,32,1024]{3,2,0,1:T(8,128)(2,1)S(1)}, u32[]{:S(2)}, u32[]{:S(2)}) collective-permute-start(bf16[1,1,32,1024]{3,2,0,1:T(8,128)(2,1)S(1)} %get-tuple-element.48), channel_id=1, source_target_pairs={{0,16},{4,20},{8,24},{12,28},{16,0},{20,4},{24,8},{28,12},{1,17},{... | collective-permute-start | bytes 196616 | tf_op jit(solution)/shard_map/ppermute | solution.py:13
  8.6 5.0 %collective-permute-start.1 = (bf16[2,1,16,1024]{3,2,0,1:T(8,128)(2,1)S(1)}, bf16[2,1,16,1024]{3,2,0,1:T(8,128)(2,1)S(1)}, u32[]{:S(2)}, u32[]{:S(2)}) collective-permute-start(bf16[2,1,16,1024]{3,2,0,1:T(8,128)(2,1)S(1)} %maximum_select_fusion.7), channel_id=1, source_target_pairs={{0,8},{4,12},{8,0},{12,4},{16,24},{20,28},{24,16},{28,20},{1,9},{5... | collective-permute-start | bytes 196616 | tf_op jit(solution)/shard_map/ppermute | solution.py:13
  11.2 5.0 %collective-permute-start.5 = (bf16[2,1,32,1024]{3,2,0,1:T(8,128)(2,1)S(1)}, bf16[2,1,32,1024]{3,2,0,1:T(8,128)(2,1)S(1)}, u32[]{:S(2)}, u32[]{:S(2)}) collective-permute-start(bf16[2,1,32,1024]{3,2,0,1:T(8,128)(2,1)S(1)} %maximum_select_fusion.6), channel_id=1, source_target_pairs={{0,8},{4,12},{8,0},{12,4},{16,24},{20,28},{24,16},{28,20},{1,9},{5... | collective-permute-start | bytes 393224 | tf_op jit(solution)/shard_map/ppermute | solution.py:13
  13.6 6.3 %collective-permute-start.2 = (bf16[4,1,16,1024]{3,2,0,1:T(8,128)(2,1)S(1)}, bf16[4,1,16,1024]{3,2,0,1:T(8,128)(2,1)S(1)}, u32[]{:S(2)}, u32[]{:S(2)}) collective-permute-start(bf16[4,1,16,1024]{3,2,0,1:T(8,128)(2,1)S(1)} %bitcast.158), channel_id=1, source_target_pairs={{0,4},{4,0},{8,12},{12,8},{16,20},{20,16},{24,28},{28,24},{1,5},{5... | collective-permute-start | bytes 393224 | tf_op jit(solution)/shard_map/ppermute | solution.py:13
  16.3 7.5 %collective-permute-start.6 = (bf16[4,1,32,1024]{3,2,0,1:T(8,128)(2,1)S(1)}, bf16[4,1,32,1024]{3,2,0,1:T(8,128)(2,1)S(1)}, u32[]{:S(2)}, u32[]{:S(2)}) collective-permute-start(bf16[4,1,32,1024]{3,2,0,1:T(8,128)(2,1)S(1)} %bitcast.156), channel_id=1, source_target_pairs={{0,4},{4,0},{8,12},{12,8},{16,20},{20,16},{24,28},{28,24},{1,5},{5... | collective-permute-start | bytes 786440 | tf_op jit(solution)/shard_map/ppermute | solution.py:13
  20.7 8.5 %collective-permute-start.3 = (bf16[1,8,16,1024]{3,2,1,0:T(8,128)(2,1)S(1)}, bf16[1,8,16,1024]{3,2,1,0:T(8,128)(2,1)}, u32[]{:S(2)}, u32[]{:S(2)}) collective-permute-start(bf16[1,8,16,1024]{3,2,1,0:T(8,128)(2,1)S(1)} %bitcast_select_fusion), channel_id=1, source_target_pairs={{0,2},{1,3},{2,0},{3,1},{4,6},{5,7},{6,4},{7,5},{8,10},{9,11},{10,... | collective-permute-start | bytes 786440 | tf_op jit(solution)/shard_map/ppermute | solution.py:13
  31.1 2.3 %collective-permute-start.7 = (bf16[2,8,16,1024]{3,2,1,0:T(8,128)(2,1)}, bf16[2,8,16,1024]{3,2,1,0:T(8,128)(2,1)}, u32[]{:S(2)}, u32[]{:S(2)}) collective-permute-start(bf16[2,8,16,1024]{3,2,1,0:T(8,128)(2,1)} %maximum_select_fusion.1), channel_id=1, source_target_pairs={{0,1},{1,0},{2,3},{3,2},{4,5},{5,4},{6,7},{7,6},{8,9},{9,8},{10,11... | collective-permute-start | bytes 1572872 | tf_op jit(solution)/shard_map/ppermute | solution.py:13
  35.4 11.5 %slice-start = ((s8[8388608]{0:T(1024)(128)(4,1)}), s8[4194304]{0:T(1024)(128)(4,1)S(1)}, s32[]{:S(2)}) async-start(s8[8388608]{0:T(1024)(128)(4,1)} %bitcast.167), calls=%async_computation | async-start | bytes 8388608
  36.8 7.4 %copy-start.2 = (bf16[2,8,32,1024]{3,2,1,0:T(8,128)(2,1)S(1)}, bf16[2,8,32,1024]{3,2,1,0:T(8,128)(2,1)}, u32[]{:S(2)}) copy-start(bf16[2,8,32,1024]{3,2,1,0:T(8,128)(2,1)} %get-tuple-element.54) | copy-start | bytes 3145732
  36.9 7.9 %copy-start.1 = (bf16[2,8,32,1024]{3,2,1,0:T(8,128)(2,1)S(1)}, bf16[2,8,32,1024]{3,2,1,0:T(8,128)(2,1)}, u32[]{:S(2)}) copy-start(bf16[2,8,32,1024]{3,2,1,0:T(8,128)(2,1)} %get-tuple-element.53) | copy-start | bytes 3145732
  36.9 10.1 %slice-start.1 = ((s8[8388608]{0:T(1024)(128)(4,1)}), s8[4194304]{0:T(1024)(128)(4,1)S(1)}, s32[]{:S(2)}) async-start(s8[8388608]{0:T(1024)(128)(4,1)} %bitcast.167), calls=%async_computation.1 | async-start | bytes 8388608
  45.3 7.7 %collective-permute-start.8 = (f32[2,2,256,256]{3,2,1,0:T(8,128)S(1)}, f32[2,2,256,256]{3,2,1,0:T(8,128)S(1)}, u32[]{:S(2)}, u32[]{:S(2)}) collective-permute-start(f32[2,2,256,256]{3,2,1,0:T(8,128)S(1)} %pad_maximum_fusion), channel_id=1, source_target_pairs={{0,1},{1,0},{2,3},{3,2},{4,5},{5,4},{6,7},{7,6},{8,9},{9,8},{10,11... | collective-permute-start | bytes 3145736 | tf_op jit(solution)/shard_map/ppermute | solution.py:13
  47.0 4.6 %copy-start = (bf16[2,8,32,1024]{3,2,1,0:T(8,128)(2,1)S(1)}, bf16[2,8,32,1024]{3,2,1,0:T(8,128)(2,1)}, u32[]{:S(2)}) copy-start(bf16[2,8,32,1024]{3,2,1,0:T(8,128)(2,1)} %get-tuple-element.31) | copy-start | bytes 3145732
  51.5 1.5 %copy-start.4 = (bf16[2,8,32,1024]{3,2,1,0:T(8,128)(2,1)S(1)}, bf16[2,8,32,1024]{3,2,1,0:T(8,128)(2,1)}, u32[]{:S(2)}) copy-start(bf16[2,8,32,1024]{3,2,1,0:T(8,128)(2,1)} %get-tuple-element.52) | copy-start | bytes 3145732
  52.0 3.3 %copy-start.3 = (bf16[2,8,32,1024]{3,2,1,0:T(8,128)(2,1)S(1)}, bf16[2,8,32,1024]{3,2,1,0:T(8,128)(2,1)}, u32[]{:S(2)}) copy-start(bf16[2,8,32,1024]{3,2,1,0:T(8,128)(2,1)} %get-tuple-element.33) | copy-start | bytes 3145732
  52.6 2.7 %collective-permute-start.10 = (f32[2,2,256,256]{3,2,1,0:T(8,128)S(1)}, f32[2,2,256,256]{3,2,1,0:T(8,128)S(1)}, u32[]{:S(2)}, u32[]{:S(2)}) collective-permute-start(f32[2,2,256,256]{3,2,1,0:T(8,128)S(1)} %pad_maximum_fusion.1), channel_id=1, source_target_pairs={{0,1},{1,0},{2,3},{3,2},{4,5},{5,4},{6,7},{7,6},{8,9},{9,8},{10,11... | collective-permute-start | bytes 3145736 | tf_op jit(solution)/shard_map/ppermute | solution.py:13
  53.6 9.2 %collective-permute-start.9 = (bf16[1,2,256,256]{3,2,1,0:T(8,128)(2,1)S(1)}, bf16[1,2,256,256]{3,2,1,0:T(8,128)(2,1)S(1)}, u32[]{:S(2)}, u32[]{:S(2)}) collective-permute-start(bf16[1,2,256,256]{3,2,1,0:T(8,128)(2,1)S(1)} %fusion.8), channel_id=1, source_target_pairs={{0,2},{1,3},{2,0},{3,1},{4,6},{5,7},{6,4},{7,5},{8,10},{9,11},{10,... | collective-permute-start | bytes 786440 | tf_op jit(solution)/shard_map/ppermute | solution.py:13
  55.8 11.7 %collective-permute-start.11 = (bf16[1,2,256,256]{3,2,1,0:T(8,128)(2,1)S(1)}, bf16[1,2,256,256]{3,2,1,0:T(8,128)(2,1)S(1)}, u32[]{:S(2)}, u32[]{:S(2)}) collective-permute-start(bf16[1,2,256,256]{3,2,1,0:T(8,128)(2,1)S(1)} %fusion.9), channel_id=1, source_target_pairs={{0,2},{1,3},{2,0},{3,1},{4,6},{5,7},{6,4},{7,5},{8,10},{9,11},{10,... | collective-permute-start | bytes 786440 | tf_op jit(solution)/shard_map/ppermute | solution.py:13

commit v15 on v13

--- a/solution.py
+++ b/solution.py
@@ -5,7 +5,6 @@
 
 NV = 16
 NC = 32
-PAIR_CHUNKS = 2
 
 
 def swap(x, axis, bit):
@@ -84,10 +83,10 @@
     valence = gather_axis(jnp.take(held_valence, wanted, axis=0), "col")
     conduction = jnp.take(held_conduction, wanted, axis=0).astype(jnp.float32)
     rows_per_block = NC // col_count
-    chunk = pair_count // PAIR_CHUNKS
-    starts = list(range(0, pair_count, chunk))
+    first_size = max(1, pair_count // 4)
+    bounds = [(0, first_size), (first_size, pair_count - first_size)]
 
-    def cond_block(first, delta):
+    def cond_block(first, chunk, delta):
         cond_a = conduction[first : first + chunk]
         cond_b = conduction[pair_count + first : pair_count + first + chunk]
         rows = lax.dynamic_slice_in_dim(
@@ -96,33 +95,39 @@
         cond_pairs = (rows[:, :, None, :] * cond_b[:, None, :, :]).astype(jnp.bfloat16)
         return cond_pairs.reshape(chunk, rows_per_block * NC, mu_cols)
 
-    cond_blocks = [[cond_block(first, d) for d in range(col_count)] for first in starts]
+    cond_blocks = [[cond_block(first, size, d) for d in range(col_count)] for first, size in bounds]
     valence, cond_blocks = lax.optimization_barrier((valence, cond_blocks))
 
-    def valence_of(first):
+    def valence_of(first, chunk):
         return (
             valence[:, first : first + chunk],
             valence[:, pair_count + first : pair_count + first + chunk],
         )
 
     results = []
-    screened = screened_of(*valence_of(starts[0]), screening[0])
-    for n_chunk, first in enumerate(starts):
+    screened = screened_of(*valence_of(*bounds[0]), screening[0])
+    for n_chunk, (first, chunk) in enumerate(bounds):
 
-        def own_block(delta, screened=screened, blocks=cond_blocks[n_chunk]):
+        def own_block(delta, screened=screened, blocks=cond_blocks[n_chunk], chunk=chunk):
             cond_pairs = blocks[delta]
             return jnp.einsum(
                 "pan,pbn->pab", screened, cond_pairs, preferred_element_type=jnp.float32
             )
 
-        def last_swap(send, bit):
-            got = swap(send.astype(jnp.bfloat16), "col", bit)
-            return got.astype(jnp.float32), None
+        following = valence_of(*bounds[n_chunk + 1]) if n_chunk + 1 < len(bounds) else None
 
-        summed, _ = scatter_sum_col(own_block, last_swap)
+        def last_swap(send, bit, following=following):
+            send = send.astype(jnp.bfloat16)
+            if following is None:
+                return swap(send, "col", bit).astype(jnp.float32), None
+            send, following = lax.optimization_barrier((send, following))
+            got = swap(send, "col", bit)
+            screened_next = screened_of(*following, screening[0])
+            got, screened_next = lax.optimization_barrier((got, screened_next))
+            return got.astype(jnp.float32), screened_next
+
+        summed, screened = scatter_sum_col(own_block, last_swap)
         results.append(summed)
-        if n_chunk + 1 < len(starts):
-            screened = screened_of(*valence_of(starts[n_chunk + 1]), screening[0])
     return jnp.concatenate(results, 0)[None]
 
 

time: 63 us -> 70 us (1.11)
  waiting for transfers between devices: 18.2 us -> 22.8 us
  matrix products: 13 us -> 15.7 us
  local copies, waits for them, and re-layouts: 3.32 us -> 4.36 us
  starting transfers between devices: 16.7 us -> 15.8 us
    ppermute x12, waiting for transfers between devices: 18.2 us -> 22.8 us  [swap(): return lax.ppermute(x, axis, [(i, i ^ bit) for i in range(size)])]
    dot_general x2, matrix products: 9.3 us -> 11.6 us  [screened_of(): lax.dot_general(val_pairs, screen, (((0, 2), (0, 1)), ((), ())), preferre...]
    unnamed x4, local copies, waits for them, and re-layouts: 0.23 us -> 1.24 us
    ppermute x12, starting transfers between devices: 16.7 us -> 15.8 us  [swap(): return lax.ppermute(x, axis, [(i, i ^ bit) for i in range(size)])]
    convert_element_type x1 -> x2, other arithmetic: 3.08 us -> 2.76 us  [cond_block(): (rows[:, :, None, :] * cond_b[:, None, :, :]).astype(jnp.bfloat16)]
  transfers between devices with their start and end apart: 12 -> 12, of which waited for: 8 -> 9; matrix products, arithmetic and copies ran while one was open for 28% -> 30% of each run, Pallas kernels for 0% -> 0%
where the time goes in v15:
time: 70 us; the launch traced here: 69.7 us
  waiting for transfers between devices  22.8 us (33%)
  starting transfers between devices  15.8 us (23%)
  matrix products  15.7 us (22%)
  other arithmetic  10.7 us (15%)
  local copies, waits for them, and re-layouts  4.36 us (6%)
    ppermute x12, waiting for transfers between devices, swap(): return lax.ppermute(x, axis, [(i, i ^ bit) for i in range(size)])  22.8 us
    ppermute x12, starting transfers between devices, swap(): return lax.ppermute(x, axis, [(i, i ^ bit) for i in range(size)])  15.8 us
    dot_general x2, matrix products, screened_of(): lax.dot_general(val_pairs, screen, (((0, 2), (0, 1)), ((), ())), preferre...  11.6 us
    dot_general x8, matrix products, own_block(): jnp.einsum('pan,pbn->pab', screened, cond_pairs, preferred_element_type=j...  4.07 us
    convert_element_type x2, other arithmetic, screened_of(): (valence_a[:, :, :, None, :] * valence_b[:, :, None, :, :]).astype(jnp.bf...  2.91 us
    convert_element_type x2, other arithmetic, cond_block(): (rows[:, :, None, :] * cond_b[:, None, :, :]).astype(jnp.bfloat16)  2.76 us
    another operation x2, local copies, waits for them, and re-layouts, gather_axis(): cur = jnp.where(low, jnp.stack([cur, got], 1), jnp.stack([got, cur], 1))  1.61 us
  transfers between devices with their start and end apart: 12, of which 9 were waited for; matrix products, arithmetic and copies ran while one was open for 30% of the time, Pallas kernels for 0%

profile of v15, /device:TPU:0, one launch (start us, length us, event | category | flops | bytes accessed | tf_op | source)
XLA Modules:
  0.0 69.7 jit_solution(9666540790546259166)
XLA Ops:
  0.0 0.8 %slice_bitcast_fusion.8 = (bf16[1,1,1,16,1024]{4,3,2,1,0:T(8,128)(2,1)S(1)}, bf16[1,1,16,1024]{3,2,0,1:T(8,128)(2,1)S(1)}) fusion(bf16[1,48,1024]{2,1,0:T(8,128)(2,1)} %param.3), kind=kLoop, calls=%fused_computation.70 | loop fusion | bytes 98304 | tf_op jit(solution)/shard_map/stack | solution.py:23
  0.8 4.0 %collective-permute-start = (bf16[1,1,16,1024]{3,2,0,1:T(8,128)(2,1)S(1)}, bf16[1,1,16,1024]{3,2,0,1:T(8,128)(2,1)S(1)}, u32[]{:S(2)}, u32[]{:S(2)}) collective-permute-start(bf16[1,1,16,1024]{3,2,0,1:T(8,128)(2,1)S(1)} %get-tuple-element.60), channel_id=1, source_target_pairs={{0,16},{4,20},{8,24},{12,28},{16,0},{20,4},{24,8},{28,12},{1,17},{... | collective-permute-start | bytes 98312 | tf_op jit(solution)/shard_map/ppermute | solution.py:12
  4.8 0.8 %slice_bitcast_fusion.6 = (bf16[1,1,1,32,1024]{4,3,2,1,0:T(8,128)(2,1)S(1)}, bf16[1,1,32,1024]{3,2,0,1:T(8,128)(2,1)S(1)}) fusion(bf16[1,48,1024]{2,1,0:T(8,128)(2,1)} %param.3), kind=kLoop, calls=%fused_computation.64 | loop fusion | bytes 196608 | tf_op jit(solution)/shard_map/stack | solution.py:23
  5.7 0.7 fusion.42
  6.4 0.7 and_select_fusion
  7.1 0.7 %fusion.19 = s32[8]{0:T(128)S(1)} fusion(s32[4,1]{0,1:T(1,128)S(1)} %fusion.42, s32[4,1]{0,1:T(1,128)} %bitcast.198), kind=kLoop, calls=%fused_computation.83 | loop fusion | flops 32 | bytes 64 | tf_op jit(solution)/shard_map/jit(_take)/jit(_where)/select_n | solution.py:83
  7.8 0.7 %compare_and_fusion = pred[8]{0:T(512)(128)(4,1)S(1)} fusion(s32[4]{0:T(128)S(1)} %and_select_fusion, s32[4]{0:T(128)} %bitcast.199), kind=kLoop, calls=%fused_computation.80 | loop fusion | flops 56 | bytes 40 | tf_op jit(solution)/shard_map/jit(_take)/and | solution.py:83
  8.6 2.0 %collective-permute-start.1 = (bf16[2,1,16,1024]{3,2,0,1:T(8,128)(2,1)S(1)}, bf16[2,1,16,1024]{3,2,0,1:T(8,128)(2,1)S(1)}, u32[]{:S(2)}, u32[]{:S(2)}) collective-permute-start(bf16[2,1,16,1024]{3,2,0,1:T(8,128)(2,1)S(1)} %maximum_select_fusion.8), channel_id=1, source_target_pairs={{0,8},{4,12},{8,0},{12,4},{16,24},{20,28},{24,16},{28,20},{1,9},{5... | collective-permute-start | bytes 196616 | tf_op jit(solution)/shard_map/ppermute | solution.py:12
  10.5 0.7 collective-permute-done.5
  11.2 1.3 %collective-permute-start.6 = (bf16[2,1,32,1024]{3,2,0,1:T(8,128)(2,1)S(1)}, bf16[2,1,32,1024]{3,2,0,1:T(8,128)(2,1)S(1)}, u32[]{:S(2)}, u32[]{:S(2)}) collective-permute-start(bf16[2,1,32,1024]{3,2,0,1:T(8,128)(2,1)S(1)} %maximum_select_fusion.7), channel_id=1, source_target_pairs={{0,8},{4,12},{8,0},{12,4},{16,24},{20,28},{24,16},{28,20},{1,9},{5... | collective-permute-start | bytes 393224 | tf_op jit(solution)/shard_map/ppermute | solution.py:12
  12.5 1.0 %collective-permute-done.1 = bf16[2,1,16,1024]{3,2,0,1:T(8,128)(2,1)S(1)} collective-permute-done((bf16[2,1,16,1024]{3,2,0,1:T(8,128)(2,1)S(1)}, bf16[2,1,16,1024]{3,2,0,1:T(8,128)(2,1)S(1)}, u32[]{:S(2)}, u32[]{:S(2)}) %collective-permute-start.1) | collective-permute-done | bytes 65568 | tf_op jit(solution)/shard_map/ppermute | solution.py:12
  13.6 1.9 %collective-permute-start.2 = (bf16[4,1,16,1024]{3,2,0,1:T(8,128)(2,1)S(1)}, bf16[4,1,16,1024]{3,2,0,1:T(8,128)(2,1)S(1)}, u32[]{:S(2)}, u32[]{:S(2)}) collective-permute-start(bf16[4,1,16,1024]{3,2,0,1:T(8,128)(2,1)S(1)} %bitcast.186), channel_id=1, source_target_pairs={{0,4},{4,0},{8,12},{12,8},{16,20},{20,16},{24,28},{28,24},{1,5},{5... | collective-permute-start | bytes 393224 | tf_op jit(solution)/shard_map/ppermute | solution.py:12
  15.5 0.8 %collective-permute-done.6 = bf16[2,1,32,1024]{3,2,0,1:T(8,128)(2,1)S(1)} collective-permute-done((bf16[2,1,32,1024]{3,2,0,1:T(8,128)(2,1)S(1)}, bf16[2,1,32,1024]{3,2,0,1:T(8,128)(2,1)S(1)}, u32[]{:S(2)}, u32[]{:S(2)}) %collective-permute-start.6) | collective-permute-done | bytes 131104 | tf_op jit(solution)/shard_map/ppermute | solution.py:12
  16.3 1.6 %collective-permute-start.7 = (bf16[4,1,32,1024]{3,2,0,1:T(8,128)(2,1)S(1)}, bf16[4,1,32,1024]{3,2,0,1:T(8,128)(2,1)S(1)}, u32[]{:S(2)}, u32[]{:S(2)}) collective-permute-start(bf16[4,1,32,1024]{3,2,0,1:T(8,128)(2,1)S(1)} %bitcast.182), channel_id=1, source_target_pairs={{0,4},{4,0},{8,12},{12,8},{16,20},{20,16},{24,28},{28,24},{1,5},{5... | collective-permute-start | bytes 786440 | tf_op jit(solution)/shard_map/ppermute | solution.py:12
  17.9 2.0 %collective-permute-done.2 = bf16[4,1,16,1024]{3,2,0,1:T(8,128)(2,1)S(1)} collective-permute-done((bf16[4,1,16,1024]{3,2,0,1:T(8,128)(2,1)S(1)}, bf16[4,1,16,1024]{3,2,0,1:T(8,128)(2,1)S(1)}, u32[]{:S(2)}, u32[]{:S(2)}) %collective-permute-start.2) | collective-permute-done | bytes 131104 | tf_op jit(solution)/shard_map/ppermute | solution.py:12
  20.7 1.9 %collective-permute-start.3 = (bf16[1,8,16,1024]{3,2,1,0:T(8,128)(2,1)S(1)}, bf16[1,8,16,1024]{3,2,1,0:T(8,128)(2,1)S(1)}, u32[]{:S(2)}, u32[]{:S(2)}) collective-permute-start(bf16[1,8,16,1024]{3,2,1,0:T(8,128)(2,1)S(1)} %bitcast_select_fusion), channel_id=1, source_target_pairs={{0,2},{1,3},{2,0},{3,1},{4,6},{5,7},{6,4},{7,5},{8,10},{9,11},{10,... | collective-permute-start | bytes 786440 | tf_op jit(solution)/shard_map/ppermute | solution.py:12
  22.7 1.1 %collective-permute-done.7 = bf16[4,1,32,1024]{3,2,0,1:T(8,128)(2,1)S(1)} collective-permute-done((bf16[4,1,32,1024]{3,2,0,1:T(8,128)(2,1)S(1)}, bf16[4,1,32,1024]{3,2,0,1:T(8,128)(2,1)S(1)}, u32[]{:S(2)}, u32[]{:S(2)}) %collective-permute-start.7) | collective-permute-done | bytes 262176 | tf_op jit(solution)/shard_map/ppermute | solution.py:12
  25.4 1.7 %collective-permute-done.3 = bf16[1,8,16,1024]{3,2,1,0:T(8,128)(2,1)S(1)} collective-permute-done((bf16[1,8,16,1024]{3,2,1,0:T(8,128)(2,1)S(1)}, bf16[1,8,16,1024]{3,2,1,0:T(8,128)(2,1)S(1)}, u32[]{:S(2)}, u32[]{:S(2)}) %collective-permute-start.3) | collective-permute-done | bytes 262176 | tf_op jit(solution)/shard_map/ppermute | solution.py:12
  27.3 2.3 %multiply_convert_fusion.2 = (bf16[3,8,32,1024]{3,2,1,0:T(8,128)(2,1)S(1)}, bf16[3,8,32,1024]{3,2,1,0:T(8,128)(2,1)S(1)}, bf16[3,8,32,1024]{3,2,1,0:T(8,128)(2,1)S(1)}, bf16[3,8,32,1024]{3,2,1,0:T(8,128)(2,1)S(1)}) fusion(f32[3,8,1024]{2,1,0:T(8,128)S(1)} %get-tuple-element.45, f32[3,32,1024]{2,1,0:T(8,128)S(1)} %get-tuple-element.38, ...), kind=kLoop, calls=%fused_computation.5 | loop fusion | flops 6291456 | bytes 7077888 | tf_op jit(solution)/shard_map/convert_element_type | solution.py:95
  30.5 1.2 %slice-done.1 = s8[4194304]{0:T(1024)(128)(4,1)S(1)} async-done(((s8[8388608]{0:T(1024)(128)(4,1)}), s8[4194304]{0:T(1024)(128)(4,1)S(1)}, s32[]{:S(2)}) %slice-start.1) | async-done | bytes 4194328
  31.7 2.4 %fusion = bf16[256,1024]{1,0:T(8,128)(2,1)S(1)} fusion(bf16[4,256,1024]{2,1,0:T(8,128)(2,1)S(1)} %bitcast.175, bf16[4,1024,1024]{2,1,0:T(8,128)(2,1)S(1)} %bitcast.197), kind=kOutput, calls=%fused_computation.11 | convolution fusion | flops 2147745792 | bytes 11010048 | tf_op jit(solution)/shard_map/dot_general | solution.py:60
  35.5 1.5 %collective-permute-done.8 = f32[2,1,256,256]{3,2,1,0:T(8,128)S(1)} collective-permute-done((f32[2,1,256,256]{3,2,1,0:T(8,128)S(1)}, f32[2,1,256,256]{3,2,1,0:T(8,128)S(1)}, u32[]{:S(2)}, u32[]{:S(2)}) %collective-permute-start.8) | collective-permute-done | bytes 524320 | tf_op jit(solution)/shard_map/ppermute | solution.py:12
  37.3 2.0 %collective-permute-start.9 = (bf16[1,1,256,256]{3,2,1,0:T(8,128)(2,1)S(1)}, bf16[1,1,256,256]{3,2,1,0:T(8,128)(2,1)S(1)}, u32[]{:S(2)}, u32[]{:S(2)}) collective-permute-start(bf16[1,1,256,256]{3,2,1,0:T(8,128)(2,1)S(1)} %fusion.15), channel_id=1, source_target_pairs={{0,2},{1,3},{2,0},{3,1},{4,6},{5,7},{6,4},{7,5},{8,10},{9,11},{10,... | collective-permute-start | bytes 393224 | tf_op jit(solution)/shard_map/ppermute | solution.py:12
  39.5 2.4 %multiply_convert_fusion = bf16[4,3,16,16,1024]{4,3,2,1,0:T(8,128)(2,1)S(1)} fusion(f32[4,3,16,1024]{3,2,1,0:T(8,128)S(1)} %convert_element_type.172, f32[4,3,16,1024]{3,2,1,0:T(8,128)S(1)} %convert_element_type.171), kind=kLoop, calls=%fused_computation.2 | loop fusion | flops 6291456 | bytes 7864320 | tf_op jit(solution)/shard_map/convert_element_type | solution.py:57
  41.9 9.2 %bitcast_convert_fusion = bf16[768,1024]{1,0:T(8,128)(2,1)S(1)} fusion(bf16[4,768,1024]{2,1,0:T(8,128)(2,1)S(1)} %bitcast.172, bf16[4,1024,1024]{2,1,0:T(8,128)(2,1)} %bitcast.194), kind=kOutput, calls=%fused_computation.4 | convolution fusion | flops 6443237376 | bytes 16252928 | tf_op jit(solution)/shard_map/dot_general | solution.py:60
  51.1 0.7 convolution_bitcast_fusion.1
  51.8 0.7 convolution_bitcast_fusion.2
  52.7 3.3 %collective-permute-done.10 = f32[2,3,256,256]{3,2,1,0:T(8,128)S(1)} collective-permute-done((f32[2,3,256,256]{3,2,1,0:T(8,128)S(1)}, f32[2,3,256,256]{3,2,1,0:T(8,128)S(1)}, u32[]{:S(2)}, u32[]{:S(2)}) %collective-permute-start.10) | collective-permute-done | bytes 1572896 | tf_op jit(solution)/shard_map/ppermute | solution.py:12
  56.0 0.7 fusion.3
  57.4 10.6 %collective-permute-done.11 = bf16[1,3,256,256]{3,2,1,0:T(8,128)(2,1)S(1)} collective-permute-done((bf16[1,3,256,256]{3,2,1,0:T(8,128)(2,1)S(1)}, bf16[1,3,256,256]{3,2,1,0:T(8,128)(2,1)S(1)}, u32[]{:S(2)}, u32[]{:S(2)}) %collective-permute-start.11) | collective-permute-done | bytes 393248 | tf_op jit(solution)/shard_map/ppermute | solution.py:12
  68.0 0.7 %fusion.1 = f32[3,256,256]{2,1,0:T(8,128)S(1)} fusion(bf16[3,256,1024]{2,1,0:T(8,128)(2,1)S(1)} %bitcast.167, bf16[3,256,1024]{2,1,0:T(8,128)(2,1)S(1)} %bitcast.168, f32[2,3,256,256]{3,2,1,0:T(8,128)S(1)} %collective-permute-done.10, bf16[1,3,256,256]{3,2,1,0:T(8,128)(2,1)S(1)} %collective-permute-done.11), kind=kOutput, calls=%fused_computation.16 | convolution fusion | flops 403243008 | bytes 5111808 | tf_op jit(solution)/shard_map/pan,pbn->pab/dot_general | solution.py:113
  68.7 1.0 %maximum_bitcast_fusion = f32[1,4,256,256]{3,2,1,0:T(8,128)} fusion(f32[3,256,256]{2,1,0:T(8,128)S(1)} %fusion.1, f32[1,256,256]{2,1,0:T(8,128)S(1)} %fusion.14), kind=kLoop, calls=%fused_computation.22 | loop fusion | flops 262144 | bytes 2097152 | tf_op jit(solution)/shard_map/broadcast_in_dim | solution.py:131
  (49 shorter events, 6.2 us)
Async XLA Ops:
  0.8 7.8 %collective-permute-start = (bf16[1,1,16,1024]{3,2,0,1:T(8,128)(2,1)S(1)}, bf16[1,1,16,1024]{3,2,0,1:T(8,128)(2,1)S(1)}, u32[]{:S(2)}, u32[]{:S(2)}) collective-permute-start(bf16[1,1,16,1024]{3,2,0,1:T(8,128)(2,1)S(1)} %get-tuple-element.60), channel_id=1, source_target_pairs={{0,16},{4,20},{8,24},{12,28},{16,0},{20,4},{24,8},{28,12},{1,17},{... | collective-permute-start | bytes 98312 | tf_op jit(solution)/shard_map/ppermute | solution.py:12
  5.7 5.6 %collective-permute-start.5 = (bf16[1,1,32,1024]{3,2,0,1:T(8,128)(2,1)S(1)}, bf16[1,1,32,1024]{3,2,0,1:T(8,128)(2,1)S(1)}, u32[]{:S(2)}, u32[]{:S(2)}) collective-permute-start(bf16[1,1,32,1024]{3,2,0,1:T(8,128)(2,1)S(1)} %get-tuple-element.58), channel_id=1, source_target_pairs={{0,16},{4,20},{8,24},{12,28},{16,0},{20,4},{24,8},{28,12},{1,17},{... | collective-permute-start | bytes 196616 | tf_op jit(solution)/shard_map/ppermute | solution.py:12
  8.6 5.0 %collective-permute-start.1 = (bf16[2,1,16,1024]{3,2,0,1:T(8,128)(2,1)S(1)}, bf16[2,1,16,1024]{3,2,0,1:T(8,128)(2,1)S(1)}, u32[]{:S(2)}, u32[]{:S(2)}) collective-permute-start(bf16[2,1,16,1024]{3,2,0,1:T(8,128)(2,1)S(1)} %maximum_select_fusion.8), channel_id=1, source_target_pairs={{0,8},{4,12},{8,0},{12,4},{16,24},{20,28},{24,16},{28,20},{1,9},{5... | collective-permute-start | bytes 196616 | tf_op jit(solution)/shard_map/ppermute | solution.py:12
  11.2 5.0 %collective-permute-start.6 = (bf16[2,1,32,1024]{3,2,0,1:T(8,128)(2,1)S(1)}, bf16[2,1,32,1024]{3,2,0,1:T(8,128)(2,1)S(1)}, u32[]{:S(2)}, u32[]{:S(2)}) collective-permute-start(bf16[2,1,32,1024]{3,2,0,1:T(8,128)(2,1)S(1)} %maximum_select_fusion.7), channel_id=1, source_target_pairs={{0,8},{4,12},{8,0},{12,4},{16,24},{20,28},{24,16},{28,20},{1,9},{5... | collective-permute-start | bytes 393224 | tf_op jit(solution)/shard_map/ppermute | solution.py:12
  13.6 6.3 %collective-permute-start.2 = (bf16[4,1,16,1024]{3,2,0,1:T(8,128)(2,1)S(1)}, bf16[4,1,16,1024]{3,2,0,1:T(8,128)(2,1)S(1)}, u32[]{:S(2)}, u32[]{:S(2)}) collective-permute-start(bf16[4,1,16,1024]{3,2,0,1:T(8,128)(2,1)S(1)} %bitcast.186), channel_id=1, source_target_pairs={{0,4},{4,0},{8,12},{12,8},{16,20},{20,16},{24,28},{28,24},{1,5},{5... | collective-permute-start | bytes 393224 | tf_op jit(solution)/shard_map/ppermute | solution.py:12
  16.3 7.5 %collective-permute-start.7 = (bf16[4,1,32,1024]{3,2,0,1:T(8,128)(2,1)S(1)}, bf16[4,1,32,1024]{3,2,0,1:T(8,128)(2,1)S(1)}, u32[]{:S(2)}, u32[]{:S(2)}) collective-permute-start(bf16[4,1,32,1024]{3,2,0,1:T(8,128)(2,1)S(1)} %bitcast.182), channel_id=1, source_target_pairs={{0,4},{4,0},{8,12},{12,8},{16,20},{20,16},{24,28},{28,24},{1,5},{5... | collective-permute-start | bytes 786440 | tf_op jit(solution)/shard_map/ppermute | solution.py:12
  20.7 6.4 %collective-permute-start.3 = (bf16[1,8,16,1024]{3,2,1,0:T(8,128)(2,1)S(1)}, bf16[1,8,16,1024]{3,2,1,0:T(8,128)(2,1)S(1)}, u32[]{:S(2)}, u32[]{:S(2)}) collective-permute-start(bf16[1,8,16,1024]{3,2,1,0:T(8,128)(2,1)S(1)} %bitcast_select_fusion), channel_id=1, source_target_pairs={{0,2},{1,3},{2,0},{3,1},{4,6},{5,7},{6,4},{7,5},{8,10},{9,11},{10,... | collective-permute-start | bytes 786440 | tf_op jit(solution)/shard_map/ppermute | solution.py:12
  27.2 2.5 %collective-permute-start.4 = (bf16[2,8,16,1024]{3,2,1,0:T(8,128)(2,1)S(1)}, bf16[2,8,16,1024]{3,2,1,0:T(8,128)(2,1)S(1)}, u32[]{:S(2)}, u32[]{:S(2)}) collective-permute-start(bf16[2,8,16,1024]{3,2,1,0:T(8,128)(2,1)S(1)} %maximum_select_fusion.2), channel_id=1, source_target_pairs={{0,1},{1,0},{2,3},{3,2},{4,5},{5,4},{6,7},{7,6},{8,9},{9,8},{10,11... | collective-permute-start | bytes 1572872 | tf_op jit(solution)/shard_map/ppermute | solution.py:12
  27.3 3.2 %slice-start = ((s8[8388608]{0:T(1024)(128)(4,1)}), s8[4194304]{0:T(1024)(128)(4,1)S(1)}, s32[]{:S(2)}) async-start(s8[8388608]{0:T(1024)(128)(4,1)} %bitcast.195), calls=%async_computation | async-start | bytes 8388608
  29.5 2.2 %slice-start.1 = ((s8[8388608]{0:T(1024)(128)(4,1)}), s8[4194304]{0:T(1024)(128)(4,1)S(1)}, s32[]{:S(2)}) async-start(s8[8388608]{0:T(1024)(128)(4,1)} %bitcast.195), calls=%async_computation.1 | async-start | bytes 8388608
  34.9 2.1 %collective-permute-start.8 = (f32[2,1,256,256]{3,2,1,0:T(8,128)S(1)}, f32[2,1,256,256]{3,2,1,0:T(8,128)S(1)}, u32[]{:S(2)}, u32[]{:S(2)}) collective-permute-start(f32[2,1,256,256]{3,2,1,0:T(8,128)S(1)} %pad_maximum_fusion.1), channel_id=1, source_target_pairs={{0,1},{1,0},{2,3},{3,2},{4,5},{5,4},{6,7},{7,6},{8,9},{9,8},{10,11... | collective-permute-start | bytes 1572872 | tf_op jit(solution)/shard_map/ppermute | solution.py:12
  37.3 13.8 %collective-permute-start.9 = (bf16[1,1,256,256]{3,2,1,0:T(8,128)(2,1)S(1)}, bf16[1,1,256,256]{3,2,1,0:T(8,128)(2,1)S(1)}, u32[]{:S(2)}, u32[]{:S(2)}) collective-permute-start(bf16[1,1,256,256]{3,2,1,0:T(8,128)(2,1)S(1)} %fusion.15), channel_id=1, source_target_pairs={{0,2},{1,3},{2,0},{3,1},{4,6},{5,7},{6,4},{7,5},{8,10},{9,11},{10,... | collective-permute-start | bytes 393224 | tf_op jit(solution)/shard_map/ppermute | solution.py:12
  52.6 3.5 %collective-permute-start.10 = (f32[2,3,256,256]{3,2,1,0:T(8,128)S(1)}, f32[2,3,256,256]{3,2,1,0:T(8,128)S(1)}, u32[]{:S(2)}, u32[]{:S(2)}) collective-permute-start(f32[2,3,256,256]{3,2,1,0:T(8,128)S(1)} %pad_maximum_fusion), channel_id=1, source_target_pairs={{0,1},{1,0},{2,3},{3,2},{4,5},{5,4},{6,7},{7,6},{8,9},{9,8},{10,11... | collective-permute-start | bytes 4718600 | tf_op jit(solution)/shard_map/ppermute | solution.py:12
  56.7 11.2 %collective-permute-start.11 = (bf16[1,3,256,256]{3,2,1,0:T(8,128)(2,1)S(1)}, bf16[1,3,256,256]{3,2,1,0:T(8,128)(2,1)S(1)}, u32[]{:S(2)}, u32[]{:S(2)}) collective-permute-start(bf16[1,3,256,256]{3,2,1,0:T(8,128)(2,1)S(1)} %fusion.3), channel_id=1, source_target_pairs={{0,2},{1,3},{2,0},{3,1},{4,6},{5,7},{6,4},{7,5},{8,10},{9,11},{10,... | collective-permute-start | bytes 1179656 | tf_op jit(solution)/shard_map/ppermute | solution.py:12

commit v16 on v13

--- a/solution.py
+++ b/solution.py
@@ -5,7 +5,7 @@
 
 NV = 16
 NC = 32
-PAIR_CHUNKS = 2
+PAIR_CHUNKS = 4
 
 
 def swap(x, axis, bit):

time: 63 us -> 64.4 us (1.022)
  waiting for transfers between devices: 18.2 us -> 15.7 us
  matrix products: 13 us -> 15.2 us
  starting transfers between devices: 16.7 us -> 18.5 us
  other arithmetic: 11.2 us -> 9.86 us
  local copies, waits for them, and re-layouts: 3.32 us -> 4.46 us
    ppermute x12 -> x16, waiting for transfers between devices: 18.2 us -> 15.7 us  [swap(): return lax.ppermute(x, axis, [(i, i ^ bit) for i in range(size)])]
    ppermute x12 -> x16, starting transfers between devices: 16.7 us -> 18.5 us  [swap(): return lax.ppermute(x, axis, [(i, i ^ bit) for i in range(size)])]
    dot_general x8 -> x16, matrix products: 3.75 us -> 5.43 us  [own_block(): jnp.einsum('pan,pbn->pab', screened, cond_pairs, preferred_element_type=j...]
    unnamed x4, local copies, waits for them, and re-layouts: 0.23 us -> 1.36 us
    convert_element_type x2 -> x4, other arithmetic: 2.78 us -> 1.97 us  [screened_of(): (valence_a[:, :, :, None, :] * valence_b[:, :, None, :, :]).astype(jnp.bf...]
    dot_general x2 -> x4, matrix products: 9.3 us -> 9.73 us  [screened_of(): lax.dot_general(val_pairs, screen, (((0, 2), (0, 1)), ((), ())), preferre...]
    convert_element_type x1 -> x2, other arithmetic: 3.08 us -> 2.67 us  [cond_block(): (rows[:, :, None, :] * cond_b[:, None, :, :]).astype(jnp.bfloat16)]
  transfers between devices with their start and end apart: 12 -> 16, of which waited for: 8 -> 11; matrix products, arithmetic and copies ran while one was open for 28% -> 34% of each run, Pallas kernels for 0% -> 0%
where the time goes in v16:
time: 64.4 us; the launch traced here: 64.2 us
  starting transfers between devices  18.5 us (29%)
  waiting for transfers between devices  15.7 us (24%)
  matrix products  15.2 us (24%)
  other arithmetic  9.86 us (15%)
  local copies, waits for them, and re-layouts  4.46 us (7%)
    ppermute x16, starting transfers between devices, swap(): return lax.ppermute(x, axis, [(i, i ^ bit) for i in range(size)])  18.5 us
    ppermute x16, waiting for transfers between devices, swap(): return lax.ppermute(x, axis, [(i, i ^ bit) for i in range(size)])  15.7 us
    dot_general x4, matrix products, screened_of(): lax.dot_general(val_pairs, screen, (((0, 2), (0, 1)), ((), ())), preferre...  9.73 us
    dot_general x16, matrix products, own_block(): jnp.einsum('pan,pbn->pab', screened, cond_pairs, preferred_element_type=j...  5.43 us
    convert_element_type x2, other arithmetic, cond_block(): (rows[:, :, None, :] * cond_b[:, None, :, :]).astype(jnp.bfloat16)  2.67 us
    convert_element_type x4, other arithmetic, screened_of(): (valence_a[:, :, :, None, :] * valence_b[:, :, None, :, :]).astype(jnp.bf...  1.97 us
    another operation x2, local copies, waits for them, and re-layouts, gather_axis(): cur = jnp.where(low, jnp.stack([cur, got], 1), jnp.stack([got, cur], 1))  1.61 us
    unnamed x4, local copies, waits for them, and re-layouts  1.36 us
  transfers between devices with their start and end apart: 16, of which 11 were waited for; matrix products, arithmetic and copies ran while one was open for 34% of the time, Pallas kernels for 0%

profile of v16, /device:TPU:0, one launch (start us, length us, event | category | flops | bytes accessed | tf_op | source)
XLA Modules:
  0.0 64.2 jit_solution(10381734267524095580)
XLA Ops:
  0.0 0.8 %slice_bitcast_fusion.15 = (bf16[1,1,1,16,1024]{4,3,2,1,0:T(8,128)(2,1)S(1)}, bf16[1,1,16,1024]{3,2,0,1:T(8,128)(2,1)S(1)}) fusion(bf16[1,48,1024]{2,1,0:T(8,128)(2,1)} %param.3), kind=kLoop, calls=%fused_computation.147 | loop fusion | bytes 98304 | tf_op jit(solution)/shard_map/stack | solution.py:24
  0.8 4.0 %collective-permute-start = (bf16[1,1,16,1024]{3,2,0,1:T(8,128)(2,1)S(1)}, bf16[1,1,16,1024]{3,2,0,1:T(8,128)(2,1)S(1)}, u32[]{:S(2)}, u32[]{:S(2)}) collective-permute-start(bf16[1,1,16,1024]{3,2,0,1:T(8,128)(2,1)S(1)} %get-tuple-element.90), channel_id=1, source_target_pairs={{0,16},{4,20},{8,24},{12,28},{16,0},{20,4},{24,8},{28,12},{1,17},{... | collective-permute-start | bytes 98312 | tf_op jit(solution)/shard_map/ppermute | solution.py:13
  4.8 0.8 %slice_bitcast_fusion.13 = (bf16[1,1,1,32,1024]{4,3,2,1,0:T(8,128)(2,1)S(1)}, bf16[1,1,32,1024]{3,2,0,1:T(8,128)(2,1)S(1)}) fusion(bf16[1,48,1024]{2,1,0:T(8,128)(2,1)} %param.3), kind=kLoop, calls=%fused_computation.129 | loop fusion | bytes 196608 | tf_op jit(solution)/shard_map/stack | solution.py:24
  5.7 0.7 %fusion.90 = s32[4,1]{0,1:T(1,128)S(1)} fusion(s32[]{:T(128)S(6)} %axis_index.17, s32[1,4]{1,0:T(1,128)} %param.5), kind=kLoop, calls=%fused_computation.159 | loop fusion | flops 48 | bytes 36 | tf_op jit(solution)/shard_map/concatenate | solution.py:78
  6.4 0.7 %and_select_fusion = s32[4]{0:T(128)S(1)} fusion(s32[]{:T(128)S(6)} %axis_index.17, s32[1,4]{1,0:T(1,128)} %param.5), kind=kLoop, calls=%fused_computation.154 | loop fusion | flops 48 | bytes 36 | tf_op jit(solution)/shard_map/jit(remainder)/select_n | solution.py:75
  7.1 0.7 %fusion.55 = s32[8]{0:T(128)S(1)} fusion(s32[4,1]{0,1:T(1,128)S(1)} %fusion.90, s32[4,1]{0,1:T(1,128)} %bitcast.386), kind=kLoop, calls=%fused_computation.156 | loop fusion | flops 32 | bytes 64 | tf_op jit(solution)/shard_map/jit(_take)/jit(_where)/select_n | solution.py:84
  7.8 0.7 %compare_and_fusion = pred[8]{0:T(512)(128)(4,1)S(1)} fusion(s32[4]{0:T(128)S(1)} %and_select_fusion, s32[4]{0:T(128)} %bitcast.387), kind=kLoop, calls=%fused_computation.153 | loop fusion | flops 56 | bytes 40 | tf_op jit(solution)/shard_map/jit(_take)/and | solution.py:84
  8.6 2.0 %collective-permute-start.1 = (bf16[2,1,16,1024]{3,2,0,1:T(8,128)(2,1)S(1)}, bf16[2,1,16,1024]{3,2,0,1:T(8,128)(2,1)S(1)}, u32[]{:S(2)}, u32[]{:S(2)}) collective-permute-start(bf16[2,1,16,1024]{3,2,0,1:T(8,128)(2,1)S(1)} %maximum_select_fusion.8), channel_id=1, source_target_pairs={{0,8},{4,12},{8,0},{12,4},{16,24},{20,28},{24,16},{28,20},{1,9},{5... | collective-permute-start | bytes 196616 | tf_op jit(solution)/shard_map/ppermute | solution.py:13
  10.5 0.7 %collective-permute-done.5 = bf16[1,1,32,1024]{3,2,0,1:T(8,128)(2,1)S(1)} collective-permute-done((bf16[1,1,32,1024]{3,2,0,1:T(8,128)(2,1)S(1)}, bf16[1,1,32,1024]{3,2,0,1:T(8,128)(2,1)S(1)}, u32[]{:S(2)}, u32[]{:S(2)}) %collective-permute-start.5) | collective-permute-done | bytes 65568 | tf_op jit(solution)/shard_map/ppermute | solution.py:13
  11.2 1.3 %collective-permute-start.6 = (bf16[2,1,32,1024]{3,2,0,1:T(8,128)(2,1)S(1)}, bf16[2,1,32,1024]{3,2,0,1:T(8,128)(2,1)S(1)}, u32[]{:S(2)}, u32[]{:S(2)}) collective-permute-start(bf16[2,1,32,1024]{3,2,0,1:T(8,128)(2,1)S(1)} %maximum_select_fusion.7), channel_id=1, source_target_pairs={{0,8},{4,12},{8,0},{12,4},{16,24},{20,28},{24,16},{28,20},{1,9},{5... | collective-permute-start | bytes 393224 | tf_op jit(solution)/shard_map/ppermute | solution.py:13
  12.5 1.0 %collective-permute-done.1 = bf16[2,1,16,1024]{3,2,0,1:T(8,128)(2,1)S(1)} collective-permute-done((bf16[2,1,16,1024]{3,2,0,1:T(8,128)(2,1)S(1)}, bf16[2,1,16,1024]{3,2,0,1:T(8,128)(2,1)S(1)}, u32[]{:S(2)}, u32[]{:S(2)}) %collective-permute-start.1) | collective-permute-done | bytes 65568 | tf_op jit(solution)/shard_map/ppermute | solution.py:13
  13.6 1.9 %collective-permute-start.2 = (bf16[4,1,16,1024]{3,2,0,1:T(8,128)(2,1)S(1)}, bf16[4,1,16,1024]{3,2,0,1:T(8,128)(2,1)S(1)}, u32[]{:S(2)}, u32[]{:S(2)}) collective-permute-start(bf16[4,1,16,1024]{3,2,0,1:T(8,128)(2,1)S(1)} %bitcast.372), channel_id=1, source_target_pairs={{0,4},{4,0},{8,12},{12,8},{16,20},{20,16},{24,28},{28,24},{1,5},{5... | collective-permute-start | bytes 393224 | tf_op jit(solution)/shard_map/ppermute | solution.py:13
  15.5 0.8 %collective-permute-done.6 = bf16[2,1,32,1024]{3,2,0,1:T(8,128)(2,1)S(1)} collective-permute-done((bf16[2,1,32,1024]{3,2,0,1:T(8,128)(2,1)S(1)}, bf16[2,1,32,1024]{3,2,0,1:T(8,128)(2,1)S(1)}, u32[]{:S(2)}, u32[]{:S(2)}) %collective-permute-start.6) | collective-permute-done | bytes 131104 | tf_op jit(solution)/shard_map/ppermute | solution.py:13
  16.3 1.6 %collective-permute-start.7 = (bf16[4,1,32,1024]{3,2,0,1:T(8,128)(2,1)S(1)}, bf16[4,1,32,1024]{3,2,0,1:T(8,128)(2,1)S(1)}, u32[]{:S(2)}, u32[]{:S(2)}) collective-permute-start(bf16[4,1,32,1024]{3,2,0,1:T(8,128)(2,1)S(1)} %bitcast.368), channel_id=1, source_target_pairs={{0,4},{4,0},{8,12},{12,8},{16,20},{20,16},{24,28},{28,24},{1,5},{5... | collective-permute-start | bytes 786440 | tf_op jit(solution)/shard_map/ppermute | solution.py:13
  17.9 2.0 %collective-permute-done.2 = bf16[4,1,16,1024]{3,2,0,1:T(8,128)(2,1)S(1)} collective-permute-done((bf16[4,1,16,1024]{3,2,0,1:T(8,128)(2,1)S(1)}, bf16[4,1,16,1024]{3,2,0,1:T(8,128)(2,1)S(1)}, u32[]{:S(2)}, u32[]{:S(2)}) %collective-permute-start.2) | collective-permute-done | bytes 131104 | tf_op jit(solution)/shard_map/ppermute | solution.py:13
  20.7 1.9 %collective-permute-start.3 = (bf16[1,8,16,1024]{3,2,1,0:T(8,128)(2,1)S(1)}, bf16[1,8,16,1024]{3,2,1,0:T(8,128)(2,1)S(1)}, u32[]{:S(2)}, u32[]{:S(2)}) collective-permute-start(bf16[1,8,16,1024]{3,2,1,0:T(8,128)(2,1)S(1)} %bitcast_select_fusion), channel_id=1, source_target_pairs={{0,2},{1,3},{2,0},{3,1},{4,6},{5,7},{6,4},{7,5},{8,10},{9,11},{10,... | collective-permute-start | bytes 786440 | tf_op jit(solution)/shard_map/ppermute | solution.py:13
  22.7 1.1 %collective-permute-done.7 = bf16[4,1,32,1024]{3,2,0,1:T(8,128)(2,1)S(1)} collective-permute-done((bf16[4,1,32,1024]{3,2,0,1:T(8,128)(2,1)S(1)}, bf16[4,1,32,1024]{3,2,0,1:T(8,128)(2,1)S(1)}, u32[]{:S(2)}, u32[]{:S(2)}) %collective-permute-start.7) | collective-permute-done | bytes 262176 | tf_op jit(solution)/shard_map/ppermute | solution.py:13
  24.9 1.3 %multiply_convert_fusion.12 = (bf16[8,32,1024]{2,1,0:T(8,128)(2,1)S(1)}, bf16[8,32,1024]{2,1,0:T(8,128)(2,1)S(1)}, bf16[8,32,1024]{2,1,0:T(8,128)(2,1)S(1)}, bf1...) fusion(f32[8,1024]{1,0:T(8,128)S(1)} %get-tuple-element.75, ...), kind=kLoop, calls=%fused_computation.32 | loop fusion | flops 4194304 | bytes 4718592 | tf_op jit(solution)/shard_map/convert_element_type | solution.py:96
  26.2 0.9 %collective-permute-done.3 = bf16[1,8,16,1024]{3,2,1,0:T(8,128)(2,1)S(1)} collective-permute-done((bf16[1,8,16,1024]{3,2,1,0:T(8,128)(2,1)S(1)}, bf16[1,8,16,1024]{3,2,1,0:T(8,128)(2,1)S(1)}, u32[]{:S(2)}, u32[]{:S(2)}) %collective-permute-start.3) | collective-permute-done | bytes 262176 | tf_op jit(solution)/shard_map/ppermute | solution.py:13
  27.3 1.3 %multiply_convert_fusion.4 = (bf16[8,32,1024]{2,1,0:T(8,128)(2,1)S(1)}, bf16[8,32,1024]{2,1,0:T(8,128)(2,1)S(1)}, bf16[8,32,1024]{2,1,0:T(8,128)(2,1)S(1)}, bf16...) fusion(f32[8,1024]{1,0:T(8,128)S(1)} %get-tuple-element.59, ...), kind=kLoop, calls=%fused_computation.24 | loop fusion | flops 4194304 | bytes 4718592 | tf_op jit(solution)/shard_map/convert_element_type | solution.py:96
  30.2 1.4 %slice-done.1 = s8[4194304]{0:T(1024)(128)(4,1)S(1)} async-done(((s8[8388608]{0:T(1024)(128)(4,1)}), s8[4194304]{0:T(1024)(128)(4,1)S(1)}, s32[]{:S(2)}) %slice-start.1) | async-done | bytes 4194328
  31.6 2.4 %fusion = bf16[256,1024]{1,0:T(8,128)(2,1)S(1)} fusion(bf16[4,256,1024]{2,1,0:T(8,128)(2,1)S(1)} %bitcast.346, bf16[4,1024,1024]{2,1,0:T(8,128)(2,1)S(1)} %bitcast.382), kind=kOutput, calls=%fused_computation.10 | convolution fusion | flops 2147745792 | bytes 11010048 | tf_op jit(solution)/shard_map/dot_general | solution.py:61
  35.8 2.4 %fusion.3 = bf16[256,1024]{1,0:T(8,128)(2,1)S(1)} fusion(bf16[4,256,1024]{2,1,0:T(8,128)(2,1)S(1)} %bitcast.347, bf16[4,1024,1024]{2,1,0:T(8,128)(2,1)S(1)} %bitcast.383), kind=kOutput, calls=%fused_computation.13 | convolution fusion | flops 2147745792 | bytes 11010048 | tf_op jit(solution)/shard_map/dot_general | solution.py:61
  40.1 2.6 %fusion.2 = bf16[256,1024]{1,0:T(8,128)(2,1)S(1)} fusion(bf16[4,256,1024]{2,1,0:T(8,128)(2,1)S(1)} %bitcast.348, bf16[4,1024,1024]{2,1,0:T(8,128)(2,1)S(1)} %bitcast.384), kind=kOutput, calls=%fused_computation.12 | convolution fusion | flops 2147745792 | bytes 11010048 | tf_op jit(solution)/shard_map/dot_general | solution.py:61
  44.6 2.4 %fusion.1 = bf16[256,1024]{1,0:T(8,128)(2,1)S(1)} fusion(bf16[4,256,1024]{2,1,0:T(8,128)(2,1)S(1)} %bitcast.349, bf16[4,1024,1024]{2,1,0:T(8,128)(2,1)S(1)} %bitcast.385), kind=kOutput, calls=%fused_computation.11 | convolution fusion | flops 2147745792 | bytes 11010048 | tf_op jit(solution)/shard_map/dot_general | solution.py:61
  48.8 2.0 %collective-permute-start.9 = (bf16[1,1,256,256]{3,2,1,0:T(8,128)(2,1)S(1)}, bf16[1,1,256,256]{3,2,1,0:T(8,128)(2,1)S(1)}, u32[]{:S(2)}, u32[]{:S(2)}) collective-permute-start(bf16[1,1,256,256]{3,2,1,0:T(8,128)(2,1)S(1)} %fusion.48), channel_id=1, source_target_pairs={{0,2},{1,3},{2,0},{3,1},{4,6},{5,7},{6,4},{7,5},{8,10},{9,11},{10,... | collective-permute-start | bytes 393224 | tf_op jit(solution)/shard_map/ppermute | solution.py:13
  51.7 2.0 %collective-permute-start.13 = (bf16[1,1,256,256]{3,2,1,0:T(8,128)(2,1)S(1)}, bf16[1,1,256,256]{3,2,1,0:T(8,128)(2,1)S(1)}, u32[]{:S(2)}, u32[]{:S(2)}) collective-permute-start(bf16[1,1,256,256]{3,2,1,0:T(8,128)(2,1)S(1)} %fusion.50), channel_id=1, source_target_pairs={{0,2},{1,3},{2,0},{3,1},{4,6},{5,7},{6,4},{7,5},{8,10},{9,11},{10,... | collective-permute-start | bytes 393224 | tf_op jit(solution)/shard_map/ppermute | solution.py:13
  54.2 1.0 %collective-permute-done.9 = bf16[1,1,256,256]{3,2,1,0:T(8,128)(2,1)S(1)} collective-permute-done((bf16[1,1,256,256]{3,2,1,0:T(8,128)(2,1)S(1)}, bf16[1,1,256,256]{3,2,1,0:T(8,128)(2,1)S(1)}, u32[]{:S(2)}, u32[]{:S(2)}) %collective-permute-start.9) | collective-permute-done | bytes 131104 | tf_op jit(solution)/shard_map/ppermute | solution.py:13
  55.2 2.8 %collective-permute-done.15 = bf16[1,1,256,256]{3,2,1,0:T(8,128)(2,1)S(1)} collective-permute-done((bf16[1,1,256,256]{3,2,1,0:T(8,128)(2,1)S(1)}, bf16[1,1,256,256]{3,2,1,0:T(8,128)(2,1)S(1)}, u32[]{:S(2)}, u32[]{:S(2)}) %collective-permute-start.15) | collective-permute-done | bytes 131104 | tf_op jit(solution)/shard_map/ppermute | solution.py:13
  58.0 2.8 %collective-permute-done.13 = bf16[1,1,256,256]{3,2,1,0:T(8,128)(2,1)S(1)} collective-permute-done((bf16[1,1,256,256]{3,2,1,0:T(8,128)(2,1)S(1)}, bf16[1,1,256,256]{3,2,1,0:T(8,128)(2,1)S(1)}, u32[]{:S(2)}, u32[]{:S(2)}) %collective-permute-start.13) | collective-permute-done | bytes 131104 | tf_op jit(solution)/shard_map/ppermute | solution.py:13
  60.8 2.2 %collective-permute-done.11 = bf16[1,1,256,256]{3,2,1,0:T(8,128)(2,1)S(1)} collective-permute-done((bf16[1,1,256,256]{3,2,1,0:T(8,128)(2,1)S(1)}, bf16[1,1,256,256]{3,2,1,0:T(8,128)(2,1)S(1)}, u32[]{:S(2)}, u32[]{:S(2)}) %collective-permute-start.11) | collective-permute-done | bytes 131104 | tf_op jit(solution)/shard_map/ppermute | solution.py:13
  63.1 1.0 %maximum_bitcast_fusion = f32[1,4,256,256]{3,2,1,0:T(8,128)} fusion(f32[1,256,256]{2,1,0:T(8,128)S(1)} %fusion.32, f32[1,256,256]{2,1,0:T(8,128)S(1)} %fusion.37, f32[1,256,256]{2,1,0:T(8,128)S(1)} %fusion.42, f32[1,256,256]{2,1,0:T(8,128)S(1)} %fusion.47), kind=kLoop, calls=%fused_computation.23 | loop fusion | flops 786432 | bytes 2097152 | tf_op jit(solution)/shard_map/broadcast_in_dim | solution.py:126
  (72 shorter events, 12.5 us)
Async XLA Ops:
  0.8 7.8 %collective-permute-start = (bf16[1,1,16,1024]{3,2,0,1:T(8,128)(2,1)S(1)}, bf16[1,1,16,1024]{3,2,0,1:T(8,128)(2,1)S(1)}, u32[]{:S(2)}, u32[]{:S(2)}) collective-permute-start(bf16[1,1,16,1024]{3,2,0,1:T(8,128)(2,1)S(1)} %get-tuple-element.90), channel_id=1, source_target_pairs={{0,16},{4,20},{8,24},{12,28},{16,0},{20,4},{24,8},{28,12},{1,17},{... | collective-permute-start | bytes 98312 | tf_op jit(solution)/shard_map/ppermute | solution.py:13
  5.7 5.6 %collective-permute-start.5 = (bf16[1,1,32,1024]{3,2,0,1:T(8,128)(2,1)S(1)}, bf16[1,1,32,1024]{3,2,0,1:T(8,128)(2,1)S(1)}, u32[]{:S(2)}, u32[]{:S(2)}) collective-permute-start(bf16[1,1,32,1024]{3,2,0,1:T(8,128)(2,1)S(1)} %get-tuple-element.88), channel_id=1, source_target_pairs={{0,16},{4,20},{8,24},{12,28},{16,0},{20,4},{24,8},{28,12},{1,17},{... | collective-permute-start | bytes 196616 | tf_op jit(solution)/shard_map/ppermute | solution.py:13
  8.6 5.0 %collective-permute-start.1 = (bf16[2,1,16,1024]{3,2,0,1:T(8,128)(2,1)S(1)}, bf16[2,1,16,1024]{3,2,0,1:T(8,128)(2,1)S(1)}, u32[]{:S(2)}, u32[]{:S(2)}) collective-permute-start(bf16[2,1,16,1024]{3,2,0,1:T(8,128)(2,1)S(1)} %maximum_select_fusion.8), channel_id=1, source_target_pairs={{0,8},{4,12},{8,0},{12,4},{16,24},{20,28},{24,16},{28,20},{1,9},{5... | collective-permute-start | bytes 196616 | tf_op jit(solution)/shard_map/ppermute | solution.py:13
  11.2 5.0 %collective-permute-start.6 = (bf16[2,1,32,1024]{3,2,0,1:T(8,128)(2,1)S(1)}, bf16[2,1,32,1024]{3,2,0,1:T(8,128)(2,1)S(1)}, u32[]{:S(2)}, u32[]{:S(2)}) collective-permute-start(bf16[2,1,32,1024]{3,2,0,1:T(8,128)(2,1)S(1)} %maximum_select_fusion.7), channel_id=1, source_target_pairs={{0,8},{4,12},{8,0},{12,4},{16,24},{20,28},{24,16},{28,20},{1,9},{5... | collective-permute-start | bytes 393224 | tf_op jit(solution)/shard_map/ppermute | solution.py:13
  13.6 6.3 %collective-permute-start.2 = (bf16[4,1,16,1024]{3,2,0,1:T(8,128)(2,1)S(1)}, bf16[4,1,16,1024]{3,2,0,1:T(8,128)(2,1)S(1)}, u32[]{:S(2)}, u32[]{:S(2)}) collective-permute-start(bf16[4,1,16,1024]{3,2,0,1:T(8,128)(2,1)S(1)} %bitcast.372), channel_id=1, source_target_pairs={{0,4},{4,0},{8,12},{12,8},{16,20},{20,16},{24,28},{28,24},{1,5},{5... | collective-permute-start | bytes 393224 | tf_op jit(solution)/shard_map/ppermute | solution.py:13
  16.3 7.5 %collective-permute-start.7 = (bf16[4,1,32,1024]{3,2,0,1:T(8,128)(2,1)S(1)}, bf16[4,1,32,1024]{3,2,0,1:T(8,128)(2,1)S(1)}, u32[]{:S(2)}, u32[]{:S(2)}) collective-permute-start(bf16[4,1,32,1024]{3,2,0,1:T(8,128)(2,1)S(1)} %bitcast.368), channel_id=1, source_target_pairs={{0,4},{4,0},{8,12},{12,8},{16,20},{20,16},{24,28},{28,24},{1,5},{5... | collective-permute-start | bytes 786440 | tf_op jit(solution)/shard_map/ppermute | solution.py:13
  20.7 6.4 %collective-permute-start.3 = (bf16[1,8,16,1024]{3,2,1,0:T(8,128)(2,1)S(1)}, bf16[1,8,16,1024]{3,2,1,0:T(8,128)(2,1)S(1)}, u32[]{:S(2)}, u32[]{:S(2)}) collective-permute-start(bf16[1,8,16,1024]{3,2,1,0:T(8,128)(2,1)S(1)} %bitcast_select_fusion), channel_id=1, source_target_pairs={{0,2},{1,3},{2,0},{3,1},{4,6},{5,7},{6,4},{7,5},{8,10},{9,11},{10,... | collective-permute-start | bytes 786440 | tf_op jit(solution)/shard_map/ppermute | solution.py:13
  27.2 2.0 %collective-permute-start.4 = (bf16[2,8,16,1024]{3,2,1,0:T(8,128)(2,1)S(1)}, bf16[2,8,16,1024]{3,2,1,0:T(8,128)(2,1)S(1)}, u32[]{:S(2)}, u32[]{:S(2)}) collective-permute-start(bf16[2,8,16,1024]{3,2,1,0:T(8,128)(2,1)S(1)} %maximum_select_fusion.2), channel_id=1, source_target_pairs={{0,1},{1,0},{2,3},{3,2},{4,5},{5,4},{6,7},{7,6},{8,9},{9,8},{10,11... | collective-permute-start | bytes 1572872 | tf_op jit(solution)/shard_map/ppermute | solution.py:13
  27.3 2.9 %slice-start = ((s8[8388608]{0:T(1024)(128)(4,1)}), s8[4194304]{0:T(1024)(128)(4,1)S(1)}, s32[]{:S(2)}) async-start(s8[8388608]{0:T(1024)(128)(4,1)} %bitcast.380), calls=%async_computation | async-start | bytes 8388608
  29.3 2.2 %slice-start.1 = ((s8[8388608]{0:T(1024)(128)(4,1)}), s8[4194304]{0:T(1024)(128)(4,1)S(1)}, s32[]{:S(2)}) async-start(s8[8388608]{0:T(1024)(128)(4,1)} %bitcast.380), calls=%async_computation.1 | async-start | bytes 8388608
  35.0 13.4 %collective-permute-start.8 = (f32[2,1,256,256]{3,2,1,0:T(8,128)S(1)}, f32[2,1,256,256]{3,2,1,0:T(8,128)S(1)}, u32[]{:S(2)}, u32[]{:S(2)}) collective-permute-start(f32[2,1,256,256]{3,2,1,0:T(8,128)S(1)} %pad_maximum_fusion), channel_id=1, source_target_pairs={{0,1},{1,0},{2,3},{3,2},{4,5},{5,4},{6,7},{7,6},{8,9},{9,8},{10,11... | collective-permute-start | bytes 1572872 | tf_op jit(solution)/shard_map/ppermute | solution.py:13
  39.3 11.5 %collective-permute-start.14 = (f32[2,1,256,256]{3,2,1,0:T(8,128)S(1)}, f32[2,1,256,256]{3,2,1,0:T(8,128)S(1)}, u32[]{:S(2)}, u32[]{:S(2)}) collective-permute-start(f32[2,1,256,256]{3,2,1,0:T(8,128)S(1)} %pad_maximum_fusion.3), channel_id=1, source_target_pairs={{0,1},{1,0},{2,3},{3,2},{4,5},{5,4},{6,7},{7,6},{8,9},{9,8},{10,11... | collective-permute-start | bytes 1572872 | tf_op jit(solution)/shard_map/ppermute | solution.py:13
  43.8 7.5 %collective-permute-start.12 = (f32[2,1,256,256]{3,2,1,0:T(8,128)S(1)}, f32[2,1,256,256]{3,2,1,0:T(8,128)S(1)}, u32[]{:S(2)}, u32[]{:S(2)}) collective-permute-start(f32[2,1,256,256]{3,2,1,0:T(8,128)S(1)} %pad_maximum_fusion.2), channel_id=1, source_target_pairs={{0,1},{1,0},{2,3},{3,2},{4,5},{5,4},{6,7},{7,6},{8,9},{9,8},{10,11... | collective-permute-start | bytes 1572872 | tf_op jit(solution)/shard_map/ppermute | solution.py:13
  47.8 5.9 %collective-permute-start.10 = (f32[2,1,256,256]{3,2,1,0:T(8,128)S(1)}, f32[2,1,256,256]{3,2,1,0:T(8,128)S(1)}, u32[]{:S(2)}, u32[]{:S(2)}) collective-permute-start(f32[2,1,256,256]{3,2,1,0:T(8,128)S(1)} %pad_maximum_fusion.1), channel_id=1, source_target_pairs={{0,1},{1,0},{2,3},{3,2},{4,5},{5,4},{6,7},{7,6},{8,9},{9,8},{10,11... | collective-permute-start | bytes 1572872 | tf_op jit(solution)/shard_map/ppermute | solution.py:13
  48.8 6.4 %collective-permute-start.9 = (bf16[1,1,256,256]{3,2,1,0:T(8,128)(2,1)S(1)}, bf16[1,1,256,256]{3,2,1,0:T(8,128)(2,1)S(1)}, u32[]{:S(2)}, u32[]{:S(2)}) collective-permute-start(bf16[1,1,256,256]{3,2,1,0:T(8,128)(2,1)S(1)} %fusion.48), channel_id=1, source_target_pairs={{0,2},{1,3},{2,0},{3,1},{4,6},{5,7},{6,4},{7,5},{8,10},{9,11},{10,... | collective-permute-start | bytes 393224 | tf_op jit(solution)/shard_map/ppermute | solution.py:13
  51.1 6.9 %collective-permute-start.15 = (bf16[1,1,256,256]{3,2,1,0:T(8,128)(2,1)S(1)}, bf16[1,1,256,256]{3,2,1,0:T(8,128)(2,1)S(1)}, u32[]{:S(2)}, u32[]{:S(2)}) collective-permute-start(bf16[1,1,256,256]{3,2,1,0:T(8,128)(2,1)S(1)} %fusion.51), channel_id=1, source_target_pairs={{0,2},{1,3},{2,0},{3,1},{4,6},{5,7},{6,4},{7,5},{8,10},{9,11},{10,... | collective-permute-start | bytes 393224 | tf_op jit(solution)/shard_map/ppermute | solution.py:13
  51.7 9.1 %collective-permute-start.13 = (bf16[1,1,256,256]{3,2,1,0:T(8,128)(2,1)S(1)}, bf16[1,1,256,256]{3,2,1,0:T(8,128)(2,1)S(1)}, u32[]{:S(2)}, u32[]{:S(2)}) collective-permute-start(bf16[1,1,256,256]{3,2,1,0:T(8,128)(2,1)S(1)} %fusion.50), channel_id=1, source_target_pairs={{0,2},{1,3},{2,0},{3,1},{4,6},{5,7},{6,4},{7,5},{8,10},{9,11},{10,... | collective-permute-start | bytes 393224 | tf_op jit(solution)/shard_map/ppermute | solution.py:13
  54.0 9.1 %collective-permute-start.11 = (bf16[1,1,256,256]{3,2,1,0:T(8,128)(2,1)S(1)}, bf16[1,1,256,256]{3,2,1,0:T(8,128)(2,1)S(1)}, u32[]{:S(2)}, u32[]{:S(2)}) collective-permute-start(bf16[1,1,256,256]{3,2,1,0:T(8,128)(2,1)S(1)} %fusion.49), channel_id=1, source_target_pairs={{0,2},{1,3},{2,0},{3,1},{4,6},{5,7},{6,4},{7,5},{8,10},{9,11},{10,... | collective-permute-start | bytes 393224 | tf_op jit(solution)/shard_map/ppermute | solution.py:13

commit v17 on v13

--- a/solution.py
+++ b/solution.py
@@ -6,6 +6,19 @@
 NV = 16
 NC = 32
 PAIR_CHUNKS = 2
+
+
+def gather_axis_low_first(mine, axis):
+    count = lax.axis_size(axis)
+    me = lax.axis_index(axis)
+    cur = mine[None]
+    bit = 1
+    while bit < count:
+        got = swap(cur, axis, bit)
+        low = (me & bit) == 0
+        cur = jnp.where(low, jnp.concatenate([cur, got], 0), jnp.concatenate([got, cur], 0))
+        bit *= 2
+    return cur
 
 
 def swap(x, axis, bit):
@@ -77,7 +90,7 @@
 
     wanted = jnp.concatenate([kpoint_a, kpoint_b])
     held_valence = gather_axis(orbitals[:, :NV, :], "pb").reshape(kpoint_count, NV, mu_cols)
-    held_conduction = gather_axis(orbitals[:, NV:, :], "pb").reshape(
+    held_conduction = gather_axis_low_first(orbitals[:, NV:, :], "pb").reshape(
         kpoint_count, orb_count - NV, mu_cols
     )
 

time: 63 us -> 67.2 us (1.067)
  waiting for transfers between devices: 18.2 us -> 25.2 us
  starting transfers between devices: 16.7 us -> 13.8 us
    ppermute x12, waiting for transfers between devices: 18.2 us -> 25.2 us  [swap(): return lax.ppermute(x, axis, [(i, i ^ bit) for i in range(size)])]
    ppermute x12, starting transfers between devices: 16.7 us -> 13.8 us  [swap(): return lax.ppermute(x, axis, [(i, i ^ bit) for i in range(size)])]
    another operation x2 -> x1, local copies, waits for them, and re-layouts: 1.61 us -> 0.76 us  [gather_axis(): cur = jnp.where(low, jnp.stack([cur, got], 1), jnp.stack([got, cur], 1))]
    slice x0 -> x1, local copies, waits for them, and re-layouts: none -> 0.85 us  [body(): orbitals[:, NV:, :]]
  transfers between devices with their start and end apart: 12 -> 12, of which waited for: 8 -> 6; matrix products, arithmetic and copies ran while one was open for 28% -> 27% of each run, Pallas kernels for 0% -> 0%
where the time goes in v17:
time: 67.2 us; the launch traced here: 66.9 us
  waiting for transfers between devices  25.2 us (38%)
  starting transfers between devices  13.8 us (21%)
  matrix products  13.1 us (19%)
  other arithmetic  11.2 us (17%)
  local copies, waits for them, and re-layouts  3.26 us (5%)
    ppermute x12, waiting for transfers between devices, swap(): return lax.ppermute(x, axis, [(i, i ^ bit) for i in range(size)])  25.2 us
    ppermute x12, starting transfers between devices, swap(): return lax.ppermute(x, axis, [(i, i ^ bit) for i in range(size)])  13.8 us
    dot_general x2, matrix products, screened_of(): lax.dot_general(val_pairs, screen, (((0, 2), (0, 1)), ((), ())), preferre...  9.29 us
    dot_general x8, matrix products, own_block(): jnp.einsum('pan,pbn->pab', screened, cond_pairs, preferred_element_type=j...  3.76 us
    convert_element_type x1, other arithmetic, cond_block(): (rows[:, :, None, :] * cond_b[:, None, :, :]).astype(jnp.bfloat16)  3.09 us
    convert_element_type x2, other arithmetic, screened_of(): (valence_a[:, :, :, None, :] * valence_b[:, :, None, :, :]).astype(jnp.bf...  2.78 us
  transfers between devices with their start and end apart: 12, of which 6 were waited for; matrix products, arithmetic and copies ran while one was open for 27% of the time, Pallas kernels for 0%

profile of v17, /device:TPU:0, one launch (start us, length us, event | category | flops | bytes accessed | tf_op | source)
XLA Modules:
  0.0 66.9 jit_solution(9319222266086577083)
XLA Ops:
  0.0 0.8 %slice_bitcast_fusion.5 = (bf16[1,1,1,16,1024]{4,3,2,1,0:T(8,128)(2,1)S(1)}, bf16[1,1,16,1024]{3,2,0,1:T(8,128)(2,1)S(1)}) fusion(bf16[1,48,1024]{2,1,0:T(8,128)(2,1)} %param.3), kind=kLoop, calls=%fused_computation.56 | loop fusion | bytes 98304 | tf_op jit(solution)/shard_map/stack | solution.py:37
  0.8 4.0 %collective-permute-start = (bf16[1,1,16,1024]{3,2,0,1:T(8,128)(2,1)S(1)}, bf16[1,1,16,1024]{3,2,0,1:T(8,128)(2,1)S(1)}, u32[]{:S(2)}, u32[]{:S(2)}) collective-permute-start(bf16[1,1,16,1024]{3,2,0,1:T(8,128)(2,1)S(1)} %get-tuple-element.50), channel_id=1, source_target_pairs={{0,16},{4,20},{8,24},{12,28},{16,0},{20,4},{24,8},{28,12},{1,17},{... | collective-permute-start | bytes 98312 | tf_op jit(solution)/shard_map/ppermute | solution.py:26
  4.8 0.8 %fusion.14 = (bf16[1,32,1024]{2,1,0:T(8,128)(2,1)S(1)}, bf16[1,1,32,1024]{3,2,0,1:T(8,128)(2,1)S(1)}) fusion(bf16[1,48,1024]{2,1,0:T(8,128)(2,1)} %param.3), kind=kLoop, calls=%fused_computation.76 | loop fusion | bytes 196608 | tf_op jit(solution)/shard_map/slice | solution.py:93
  5.7 1.6 %collective-permute-start.5 = (bf16[1,1,32,1024]{3,2,0,1:T(8,128)(2,1)S(1)}, bf16[1,1,32,1024]{3,2,0,1:T(8,128)(2,1)S(1)}, u32[]{:S(2)}, u32[]{:S(2)}) collective-permute-start(bf16[1,1,32,1024]{3,2,0,1:T(8,128)(2,1)S(1)} %get-tuple-element.48), channel_id=1, source_target_pairs={{0,4},{4,0},{8,12},{12,8},{16,20},{20,16},{24,28},{28,24},{1,5},{5... | collective-permute-start | bytes 196616 | tf_op jit(solution)/shard_map/ppermute | solution.py:26
  7.2 0.7 fusion.39
  7.9 0.7 and_select_fusion
  8.6 0.7 %fusion.12 = s32[8]{0:T(128)S(1)} fusion(s32[4,1]{0,1:T(1,128)S(1)} %fusion.39, s32[4,1]{0,1:T(1,128)} %bitcast.163), kind=kLoop, calls=%fused_computation.73 | loop fusion | flops 32 | bytes 64 | tf_op jit(solution)/shard_map/jit(_take)/jit(_where)/select_n | solution.py:97
  9.3 0.7 %compare_and_fusion = pred[8]{0:T(512)(128)(4,1)S(1)} fusion(s32[4]{0:T(128)S(1)} %and_select_fusion, s32[4]{0:T(128)} %bitcast.164), kind=kLoop, calls=%fused_computation.70 | loop fusion | flops 56 | bytes 40 | tf_op jit(solution)/shard_map/jit(_take)/and | solution.py:97
  10.1 1.6 %collective-permute-start.1 = (bf16[2,1,16,1024]{3,2,0,1:T(8,128)(2,1)S(1)}, bf16[2,1,16,1024]{3,2,0,1:T(8,128)(2,1)S(1)}, u32[]{:S(2)}, u32[]{:S(2)}) collective-permute-start(bf16[2,1,16,1024]{3,2,0,1:T(8,128)(2,1)S(1)} %maximum_select_fusion.10), channel_id=1, source_target_pairs={{0,8},{4,12},{8,0},{12,4},{16,24},{20,28},{24,16},{28,20},{1,9},{5... | collective-permute-start | bytes 196616 | tf_op jit(solution)/shard_map/ppermute | solution.py:26
  11.7 0.5 collective-permute-start.6
  12.3 2.8 %collective-permute-done.1 = bf16[2,1,16,1024]{3,2,0,1:T(8,128)(2,1)S(1)} collective-permute-done((bf16[2,1,16,1024]{3,2,0,1:T(8,128)(2,1)S(1)}, bf16[2,1,16,1024]{3,2,0,1:T(8,128)(2,1)S(1)}, u32[]{:S(2)}, u32[]{:S(2)}) %collective-permute-start.1) | collective-permute-done | bytes 65568 | tf_op jit(solution)/shard_map/ppermute | solution.py:26
  15.1 0.6 collective-permute-start.2
  15.7 1.2 %collective-permute-done.6 = bf16[2,1,32,1024]{3,2,0,1:T(8,128)(2,1)S(1)} collective-permute-done((bf16[2,1,32,1024]{3,2,0,1:T(8,128)(2,1)S(1)}, bf16[2,1,32,1024]{3,2,0,1:T(8,128)(2,1)S(1)}, u32[]{:S(2)}, u32[]{:S(2)}) %collective-permute-start.6) | collective-permute-done | bytes 131104 | tf_op jit(solution)/shard_map/ppermute | solution.py:26
  17.4 2.8 %collective-permute-done.2 = bf16[4,1,16,1024]{3,2,0,1:T(8,128)(2,1)S(1)} collective-permute-done((bf16[4,1,16,1024]{3,2,0,1:T(8,128)(2,1)S(1)}, bf16[4,1,16,1024]{3,2,0,1:T(8,128)(2,1)S(1)}, u32[]{:S(2)}, u32[]{:S(2)}) %collective-permute-start.2) | collective-permute-done | bytes 131104 | tf_op jit(solution)/shard_map/ppermute | solution.py:26
  20.2 0.6 gather_fusion
  20.9 1.6 %collective-permute-start.3 = (bf16[1,8,16,1024]{3,2,1,0:T(8,128)(2,1)S(1)}, bf16[1,8,16,1024]{3,2,1,0:T(8,128)(2,1)S(1)}, u32[]{:S(2)}, u32[]{:S(2)}) collective-permute-start(bf16[1,8,16,1024]{3,2,1,0:T(8,128)(2,1)S(1)} %bitcast_select_fusion), channel_id=1, source_target_pairs={{0,2},{1,3},{2,0},{3,1},{4,6},{5,7},{6,4},{7,5},{8,10},{9,11},{10,... | collective-permute-start | bytes 786440 | tf_op jit(solution)/shard_map/ppermute | solution.py:26
  22.5 7.9 %collective-permute-done.7 = bf16[4,1,32,1024]{3,2,0,1:T(8,128)(2,1)S(1)} collective-permute-done((bf16[4,1,32,1024]{3,2,0,1:T(8,128)(2,1)S(1)}, bf16[4,1,32,1024]{3,2,0,1:T(8,128)(2,1)S(1)}, u32[]{:S(2)}, u32[]{:S(2)}) %collective-permute-start.7) | collective-permute-done | bytes 262176 | tf_op jit(solution)/shard_map/ppermute | solution.py:26
  30.5 0.6 gather_fusion.1
  31.6 3.1 %multiply_convert_fusion.2 = (bf16[2,8,32,1024]{3,2,1,0:T(8,128)(2,1)S(1)}, bf16[2,8,32,1024]{3,2,1,0:T(8,128)(2,1)S(1)}, bf16[2,8,32,1024]{3,2,1,0:T(8,128)(2,1...) fusion(f32[2,8,1024]{2,1,0:T(8,128)S(1)} %get-tuple-element.35,, ...), kind=kLoop, calls=%fused_computation.6 | loop fusion | flops 8388608 | bytes 9437184 | tf_op jit(solution)/shard_map/convert_element_type | solution.py:109
  35.3 1.4 %multiply_convert_fusion.1 = bf16[4,2,16,16,1024]{4,3,2,1,0:T(8,128)(2,1)S(1)} fusion(f32[4,2,16,1024]{3,2,1,0:T(8,128)S(1)} %get-tuple-element.26, f32[4,2,16,1024]{3,2,1,0:T(8,128)S(1)} %get-tuple-element.23), kind=kLoop, calls=%fused_computation.3 | loop fusion | flops 4194304 | bytes 5242880 | tf_op jit(solution)/shard_map/convert_element_type | solution.py:71
  37.0 4.6 %bitcast_convert_fusion.1 = bf16[512,1024]{1,0:T(8,128)(2,1)S(1)} fusion(bf16[4,512,1024]{2,1,0:T(8,128)(2,1)S(1)} %bitcast.136, bf16[4,1024,1024]{2,1,0:T(8,128)(2,1)S(1)} %bitcast.161), kind=kOutput, calls=%fused_computation.5 | convolution fusion | flops 4295491584 | bytes 13631488 | tf_op jit(solution)/shard_map/dot_general | solution.py:74
  42.6 0.5 collective-permute-start.8
  43.1 1.4 %multiply_convert_fusion = bf16[4,2,16,16,1024]{4,3,2,1,0:T(8,128)(2,1)S(1)} fusion(f32[4,2,16,1024]{3,2,1,0:T(8,128)S(1)} %get-tuple-element.24, f32[4,2,16,1024]{3,2,1,0:T(8,128)S(1)} %get-tuple-element.25), kind=kLoop, calls=%fused_computation.2 | loop fusion | flops 4194304 | bytes 5242880 | tf_op jit(solution)/shard_map/convert_element_type | solution.py:71
  44.5 4.7 %bitcast_convert_fusion = bf16[512,1024]{1,0:T(8,128)(2,1)S(1)} fusion(bf16[4,512,1024]{2,1,0:T(8,128)(2,1)S(1)} %bitcast.137, bf16[4,1024,1024]{2,1,0:T(8,128)(2,1)S(1)} %bitcast.162), kind=kOutput, calls=%fused_computation.4 | convolution fusion | flops 4295491584 | bytes 13631488 | tf_op jit(solution)/shard_map/dot_general | solution.py:74
  49.3 0.5 convolution_bitcast_fusion
  49.7 0.5 convolution_bitcast_fusion.1
  50.9 0.5 fusion.8
  51.4 1.6 %collective-permute-start.9 = (bf16[1,2,256,256]{3,2,1,0:T(8,128)(2,1)S(1)}, bf16[1,2,256,256]{3,2,1,0:T(8,128)(2,1)S(1)}, u32[]{:S(2)}, u32[]{:S(2)}) collective-permute-start(bf16[1,2,256,256]{3,2,1,0:T(8,128)(2,1)S(1)} %fusion.8), channel_id=1, source_target_pairs={{0,2},{1,3},{2,0},{3,1},{4,6},{5,7},{6,4},{7,5},{8,10},{9,11},{10,... | collective-permute-start | bytes 786440 | tf_op jit(solution)/shard_map/ppermute | solution.py:26
  53.9 1.2 %collective-permute-start.11 = (bf16[1,2,256,256]{3,2,1,0:T(8,128)(2,1)S(1)}, bf16[1,2,256,256]{3,2,1,0:T(8,128)(2,1)S(1)}, u32[]{:S(2)}, u32[]{:S(2)}) collective-permute-start(bf16[1,2,256,256]{3,2,1,0:T(8,128)(2,1)S(1)} %fusion.9), channel_id=1, source_target_pairs={{0,2},{1,3},{2,0},{3,1},{4,6},{5,7},{6,4},{7,5},{8,10},{9,11},{10,... | collective-permute-start | bytes 786440 | tf_op jit(solution)/shard_map/ppermute | solution.py:26
  55.1 5.5 %collective-permute-done.9 = bf16[1,2,256,256]{3,2,1,0:T(8,128)(2,1)S(1)} collective-permute-done((bf16[1,2,256,256]{3,2,1,0:T(8,128)(2,1)S(1)}, bf16[1,2,256,256]{3,2,1,0:T(8,128)(2,1)S(1)}, u32[]{:S(2)}, u32[]{:S(2)}) %collective-permute-start.9) | collective-permute-done | bytes 262176 | tf_op jit(solution)/shard_map/ppermute | solution.py:26
  60.7 5.1 %collective-permute-done.11 = bf16[1,2,256,256]{3,2,1,0:T(8,128)(2,1)S(1)} collective-permute-done((bf16[1,2,256,256]{3,2,1,0:T(8,128)(2,1)S(1)}, bf16[1,2,256,256]{3,2,1,0:T(8,128)(2,1)S(1)}, u32[]{:S(2)}, u32[]{:S(2)}) %collective-permute-start.11) | collective-permute-done | bytes 262176 | tf_op jit(solution)/shard_map/ppermute | solution.py:26
  65.8 1.0 %maximum_bitcast_fusion = f32[1,4,256,256]{3,2,1,0:T(8,128)} fusion(f32[2,256,256]{2,1,0:T(8,128)S(1)} %fusion.3, f32[2,256,256]{2,1,0:T(8,128)S(1)} %fusion.7), kind=kLoop, calls=%fused_computation.21 | loop fusion | flops 262144 | bytes 2097152 | tf_op jit(solution)/shard_map/broadcast_in_dim | solution.py:139
  (46 shorter events, 5.0 us)
Async XLA Ops:
  0.8 9.3 %collective-permute-start = (bf16[1,1,16,1024]{3,2,0,1:T(8,128)(2,1)S(1)}, bf16[1,1,16,1024]{3,2,0,1:T(8,128)(2,1)S(1)}, u32[]{:S(2)}, u32[]{:S(2)}) collective-permute-start(bf16[1,1,16,1024]{3,2,0,1:T(8,128)(2,1)S(1)} %get-tuple-element.50), channel_id=1, source_target_pairs={{0,16},{4,20},{8,24},{12,28},{16,0},{20,4},{24,8},{28,12},{1,17},{... | collective-permute-start | bytes 98312 | tf_op jit(solution)/shard_map/ppermute | solution.py:26
  5.7 6.1 %collective-permute-start.5 = (bf16[1,1,32,1024]{3,2,0,1:T(8,128)(2,1)S(1)}, bf16[1,1,32,1024]{3,2,0,1:T(8,128)(2,1)S(1)}, u32[]{:S(2)}, u32[]{:S(2)}) collective-permute-start(bf16[1,1,32,1024]{3,2,0,1:T(8,128)(2,1)S(1)} %get-tuple-element.48), channel_id=1, source_target_pairs={{0,4},{4,0},{8,12},{12,8},{16,20},{20,16},{24,28},{28,24},{1,5},{5... | collective-permute-start | bytes 196616 | tf_op jit(solution)/shard_map/ppermute | solution.py:26
  10.1 5.0 %collective-permute-start.1 = (bf16[2,1,16,1024]{3,2,0,1:T(8,128)(2,1)S(1)}, bf16[2,1,16,1024]{3,2,0,1:T(8,128)(2,1)S(1)}, u32[]{:S(2)}, u32[]{:S(2)}) collective-permute-start(bf16[2,1,16,1024]{3,2,0,1:T(8,128)(2,1)S(1)} %maximum_select_fusion.10), channel_id=1, source_target_pairs={{0,8},{4,12},{8,0},{12,4},{16,24},{20,28},{24,16},{28,20},{1,9},{5... | collective-permute-start | bytes 196616 | tf_op jit(solution)/shard_map/ppermute | solution.py:26
  11.7 5.2 %collective-permute-start.6 = (bf16[2,1,32,1024]{3,2,0,1:T(8,128)(2,1)S(1)}, bf16[2,1,32,1024]{3,2,0,1:T(8,128)(2,1)S(1)}, u32[]{:S(2)}, u32[]{:S(2)}) collective-permute-start(bf16[2,1,32,1024]{3,2,0,1:T(8,128)(2,1)S(1)} %maximum_select_fusion.9), channel_id=1, source_target_pairs={{0,8},{4,12},{8,0},{12,4},{16,24},{20,28},{24,16},{28,20},{1,9},{5... | collective-permute-start | bytes 393224 | tf_op jit(solution)/shard_map/ppermute | solution.py:26
  15.1 5.0 %collective-permute-start.2 = (bf16[4,1,16,1024]{3,2,0,1:T(8,128)(2,1)S(1)}, bf16[4,1,16,1024]{3,2,0,1:T(8,128)(2,1)S(1)}, u32[]{:S(2)}, u32[]{:S(2)}) collective-permute-start(bf16[4,1,16,1024]{3,2,0,1:T(8,128)(2,1)S(1)} %bitcast.153), channel_id=1, source_target_pairs={{0,4},{4,0},{8,12},{12,8},{16,20},{20,16},{24,28},{28,24},{1,5},{5... | collective-permute-start | bytes 393224 | tf_op jit(solution)/shard_map/ppermute | solution.py:26
  16.9 13.4 %collective-permute-start.7 = (bf16[4,1,32,1024]{3,2,0,1:T(8,128)(2,1)S(1)}, bf16[4,1,32,1024]{3,2,0,1:T(8,128)(2,1)S(1)}, u32[]{:S(2)}, u32[]{:S(2)}) collective-permute-start(bf16[4,1,32,1024]{3,2,0,1:T(8,128)(2,1)S(1)} %maximum_select_fusion.6), channel_id=1, source_target_pairs={{0,16},{4,20},{8,24},{12,28},{16,0},{20,4},{24,8},{28,12},{1,17},{... | collective-permute-start | bytes 786440 | tf_op jit(solution)/shard_map/ppermute | solution.py:26
  20.9 10.5 %collective-permute-start.3 = (bf16[1,8,16,1024]{3,2,1,0:T(8,128)(2,1)S(1)}, bf16[1,8,16,1024]{3,2,1,0:T(8,128)(2,1)S(1)}, u32[]{:S(2)}, u32[]{:S(2)}) collective-permute-start(bf16[1,8,16,1024]{3,2,1,0:T(8,128)(2,1)S(1)} %bitcast_select_fusion), channel_id=1, source_target_pairs={{0,2},{1,3},{2,0},{3,1},{4,6},{5,7},{6,4},{7,5},{8,10},{9,11},{10,... | collective-permute-start | bytes 786440 | tf_op jit(solution)/shard_map/ppermute | solution.py:26
  31.5 3.3 %collective-permute-start.4 = (bf16[2,8,16,1024]{3,2,1,0:T(8,128)(2,1)S(1)}, bf16[2,8,16,1024]{3,2,1,0:T(8,128)(2,1)S(1)}, u32[]{:S(2)}, u32[]{:S(2)}) collective-permute-start(bf16[2,8,16,1024]{3,2,1,0:T(8,128)(2,1)S(1)} %maximum_select_fusion.2), channel_id=1, source_target_pairs={{0,1},{1,0},{2,3},{3,2},{4,5},{5,4},{6,7},{7,6},{8,9},{9,8},{10,11... | collective-permute-start | bytes 1572872 | tf_op jit(solution)/shard_map/ppermute | solution.py:26
  31.6 5.2 %slice-start = ((s8[8388608]{0:T(1024)(128)(4,1)}), s8[4194304]{0:T(1024)(128)(4,1)S(1)}, s32[]{:S(2)}) async-start(s8[8388608]{0:T(1024)(128)(4,1)} %bitcast.159), calls=%async_computation | async-start | bytes 8388608
  34.8 2.2 %slice-start.1 = ((s8[8388608]{0:T(1024)(128)(4,1)}), s8[4194304]{0:T(1024)(128)(4,1)S(1)}, s32[]{:S(2)}) async-start(s8[8388608]{0:T(1024)(128)(4,1)} %bitcast.159), calls=%async_computation.1 | async-start | bytes 8388608
  42.6 8.3 %collective-permute-start.8 = (f32[2,2,256,256]{3,2,1,0:T(8,128)S(1)}, f32[2,2,256,256]{3,2,1,0:T(8,128)S(1)}, u32[]{:S(2)}, u32[]{:S(2)}) collective-permute-start(f32[2,2,256,256]{3,2,1,0:T(8,128)S(1)} %pad_maximum_fusion), channel_id=1, source_target_pairs={{0,1},{1,0},{2,3},{3,2},{4,5},{5,4},{6,7},{7,6},{8,9},{9,8},{10,11... | collective-permute-start | bytes 3145736 | tf_op jit(solution)/shard_map/ppermute | solution.py:26
  50.3 3.1 %collective-permute-start.10 = (f32[2,2,256,256]{3,2,1,0:T(8,128)S(1)}, f32[2,2,256,256]{3,2,1,0:T(8,128)S(1)}, u32[]{:S(2)}, u32[]{:S(2)}) collective-permute-start(f32[2,2,256,256]{3,2,1,0:T(8,128)S(1)} %pad_maximum_fusion.1), channel_id=1, source_target_pairs={{0,1},{1,0},{2,3},{3,2},{4,5},{5,4},{6,7},{7,6},{8,9},{9,8},{10,11... | collective-permute-start | bytes 3145736 | tf_op jit(solution)/shard_map/ppermute | solution.py:26
  51.4 9.2 %collective-permute-start.9 = (bf16[1,2,256,256]{3,2,1,0:T(8,128)(2,1)S(1)}, bf16[1,2,256,256]{3,2,1,0:T(8,128)(2,1)S(1)}, u32[]{:S(2)}, u32[]{:S(2)}) collective-permute-start(bf16[1,2,256,256]{3,2,1,0:T(8,128)(2,1)S(1)} %fusion.8), channel_id=1, source_target_pairs={{0,2},{1,3},{2,0},{3,1},{4,6},{5,7},{6,4},{7,5},{8,10},{9,11},{10,... | collective-permute-start | bytes 786440 | tf_op jit(solution)/shard_map/ppermute | solution.py:26
  53.9 11.9 %collective-permute-start.11 = (bf16[1,2,256,256]{3,2,1,0:T(8,128)(2,1)S(1)}, bf16[1,2,256,256]{3,2,1,0:T(8,128)(2,1)S(1)}, u32[]{:S(2)}, u32[]{:S(2)}) collective-permute-start(bf16[1,2,256,256]{3,2,1,0:T(8,128)(2,1)S(1)} %fusion.9), channel_id=1, source_target_pairs={{0,2},{1,3},{2,0},{3,1},{4,6},{5,7},{6,4},{7,5},{8,10},{9,11},{10,... | collective-permute-start | bytes 786440 | tf_op jit(solution)/shard_map/ppermute | solution.py:26

commit v18 on v13

--- a/solution.py
+++ b/solution.py
@@ -51,12 +51,21 @@
     return (acc[0] if 0 in acc else own_block(0)), extra
 
 
-def screened_of(valence_a, valence_b, screening):
+def pairs_of(valence_a, valence_b):
     col_count, chunk, _, mu_cols = valence_a.shape
     valence_a = valence_a.astype(jnp.float32)
     valence_b = valence_b.astype(jnp.float32)
     val_pairs = (valence_a[:, :, :, None, :] * valence_b[:, :, None, :, :]).astype(jnp.bfloat16)
-    val_pairs = val_pairs.reshape(col_count, chunk * NV * NV, mu_cols)
+    return val_pairs.reshape(col_count, chunk * NV * NV, mu_cols)
+
+
+def screened_of(valence_a, valence_b, screening):
+    return dot_of(pairs_of(valence_a, valence_b), screening)
+
+
+def dot_of(val_pairs, screening):
+    col_count, rows, mu_cols = val_pairs.shape
+    chunk = rows // (NV * NV)
     screen = screening.reshape(col_count, mu_cols, screening.shape[1])
     screened = lax.dot_general(
         val_pairs, screen, (((0, 2), (0, 1)), ((), ())), preferred_element_type=jnp.float32
@@ -115,14 +124,21 @@
                 "pan,pbn->pab", screened, cond_pairs, preferred_element_type=jnp.float32
             )
 
-        def last_swap(send, bit):
-            got = swap(send.astype(jnp.bfloat16), "col", bit)
-            return got.astype(jnp.float32), None
+        following = valence_of(starts[n_chunk + 1]) if n_chunk + 1 < len(starts) else None
 
-        summed, _ = scatter_sum_col(own_block, last_swap)
+        def last_swap(send, bit, following=following):
+            send = send.astype(jnp.bfloat16)
+            if following is None:
+                return swap(send, "col", bit).astype(jnp.float32), None
+            val_next = pairs_of(*following)
+            send, val_next = lax.optimization_barrier((send, val_next))
+            got = swap(send, "col", bit)
+            screened_next = dot_of(val_next, screening[0])
+            got, screened_next = lax.optimization_barrier((got, screened_next))
+            return got.astype(jnp.float32), screened_next
+
+        summed, screened = scatter_sum_col(own_block, last_swap)
         results.append(summed)
-        if n_chunk + 1 < len(starts):
-            screened = screened_of(*valence_of(starts[n_chunk + 1]), screening[0])
     return jnp.concatenate(results, 0)[None]
 
 

time: 63 us -> 66.4 us (1.054)
  waiting for transfers between devices: 18.2 us -> 23.6 us
  starting transfers between devices: 16.7 us -> 14.7 us
    ppermute x12, waiting for transfers between devices: 18.2 us -> 23.6 us  [swap(): return lax.ppermute(x, axis, [(i, i ^ bit) for i in range(size)])]
    ppermute x12, starting transfers between devices: 16.7 us -> 14.7 us  [swap(): return lax.ppermute(x, axis, [(i, i ^ bit) for i in range(size)])]
  transfers between devices with their start and end apart: 12 -> 12, of which waited for: 8 -> 10; matrix products, arithmetic and copies ran while one was open for 28% -> 23% of each run, Pallas kernels for 0% -> 0%
where the time goes in v18:
time: 66.4 us; the launch traced here: 66.1 us
  waiting for transfers between devices  23.6 us (36%)
  starting transfers between devices  14.7 us (22%)
  matrix products  13.1 us (20%)
  other arithmetic  11.1 us (17%)
  local copies, waits for them, and re-layouts  3.32 us (5%)
    ppermute x12, waiting for transfers between devices, swap(): return lax.ppermute(x, axis, [(i, i ^ bit) for i in range(size)])  23.6 us
    ppermute x12, starting transfers between devices, swap(): return lax.ppermute(x, axis, [(i, i ^ bit) for i in range(size)])  14.7 us
    dot_general x2, matrix products, dot_of(): lax.dot_general(val_pairs, screen, (((0, 2), (0, 1)), ((), ())), preferre...  9.29 us
    dot_general x8, matrix products, own_block(): jnp.einsum('pan,pbn->pab', screened, cond_pairs, preferred_element_type=j...  3.76 us
    convert_element_type x1, other arithmetic, cond_block(): (rows[:, :, None, :] * cond_b[:, None, :, :]).astype(jnp.bfloat16)  3.08 us
    convert_element_type x2, other arithmetic, pairs_of(): (valence_a[:, :, :, None, :] * valence_b[:, :, None, :, :]).astype(jnp.bf...  2.78 us
    another operation x2, local copies, waits for them, and re-layouts, gather_axis(): cur = jnp.where(low, jnp.stack([cur, got], 1), jnp.stack([got, cur], 1))  1.61 us
  transfers between devices with their start and end apart: 12, of which 10 were waited for; matrix products, arithmetic and copies ran while one was open for 23% of the time, Pallas kernels for 0%

profile of v18, /device:TPU:0, one launch (start us, length us, event | category | flops | bytes accessed | tf_op | source)
XLA Modules:
  0.0 66.1 jit_solution(2798148461061889028)
XLA Ops:
  0.0 0.8 %slice_bitcast_fusion.5 = (bf16[1,1,1,32,1024]{4,3,2,1,0:T(8,128)(2,1)S(1)}, bf16[1,1,32,1024]{3,2,0,1:T(8,128)(2,1)S(1)}) fusion(bf16[1,48,1024]{2,1,0:T(8,128)(2,1)} %param.3), kind=kLoop, calls=%fused_computation.57 | loop fusion | bytes 196608 | tf_op jit(solution)/shard_map/stack | solution.py:24
  0.9 4.1 %collective-permute-start.5 = (bf16[1,1,32,1024]{3,2,0,1:T(8,128)(2,1)S(1)}, bf16[1,1,32,1024]{3,2,0,1:T(8,128)(2,1)S(1)}, u32[]{:S(2)}, u32[]{:S(2)}) collective-permute-start(bf16[1,1,32,1024]{3,2,0,1:T(8,128)(2,1)S(1)} %get-tuple-element.56), channel_id=1, source_target_pairs={{0,16},{4,20},{8,24},{12,28},{16,0},{20,4},{24,8},{28,12},{1,17},{... | collective-permute-start | bytes 196616 | tf_op jit(solution)/shard_map/ppermute | solution.py:13
  5.0 0.8 %slice_bitcast_fusion.7 = (bf16[1,1,1,16,1024]{4,3,2,1,0:T(8,128)(2,1)S(1)}, bf16[1,1,16,1024]{3,2,0,1:T(8,128)(2,1)S(1)}) fusion(bf16[1,48,1024]{2,1,0:T(8,128)(2,1)} %param.3), kind=kLoop, calls=%fused_computation.59 | loop fusion | bytes 98304 | tf_op jit(solution)/shard_map/stack | solution.py:24
  5.7 0.7 %fusion.35 = s32[4,1]{0,1:T(1,128)S(1)} fusion(s32[]{:T(128)S(6)} %axis_index.17, s32[1,4]{1,0:T(1,128)} %param.5), kind=kLoop, calls=%fused_computation.80 | loop fusion | flops 48 | bytes 36 | tf_op jit(solution)/shard_map/concatenate | solution.py:87
  6.4 0.7 %and_select_fusion = s32[4]{0:T(128)S(1)} fusion(s32[]{:T(128)S(6)} %axis_index.17, s32[1,4]{1,0:T(1,128)} %param.5), kind=kLoop, calls=%fused_computation.74 | loop fusion | flops 48 | bytes 36 | tf_op jit(solution)/shard_map/jit(remainder)/select_n | solution.py:84
  7.1 0.7 %fusion.11 = s32[8]{0:T(128)S(1)} fusion(s32[4,1]{0,1:T(1,128)S(1)} %fusion.35, s32[4,1]{0,1:T(1,128)} %bitcast.170), kind=kLoop, calls=%fused_computation.76 | loop fusion | flops 32 | bytes 64 | tf_op jit(solution)/shard_map/jit(_take)/jit(_where)/select_n | solution.py:93
  7.8 0.7 %compare_and_fusion = pred[8]{0:T(512)(128)(4,1)S(1)} fusion(s32[4]{0:T(128)S(1)} %and_select_fusion, s32[4]{0:T(128)} %bitcast.171), kind=kLoop, calls=%fused_computation.73 | loop fusion | flops 56 | bytes 40 | tf_op jit(solution)/shard_map/jit(_take)/and | solution.py:93
  8.5 2.0 %collective-permute-done = bf16[1,1,16,1024]{3,2,0,1:T(8,128)(2,1)S(1)} collective-permute-done((bf16[1,1,16,1024]{3,2,0,1:T(8,128)(2,1)S(1)}, bf16[1,1,16,1024]{3,2,0,1:T(8,128)(2,1)S(1)}, u32[]{:S(2)}, u32[]{:S(2)}) %collective-permute-start) | collective-permute-done | bytes 32800 | tf_op jit(solution)/shard_map/ppermute | solution.py:13
  10.5 1.6 %collective-permute-start.1 = (bf16[2,1,16,1024]{3,2,0,1:T(8,128)(2,1)S(1)}, bf16[2,1,16,1024]{3,2,0,1:T(8,128)(2,1)S(1)}, u32[]{:S(2)}, u32[]{:S(2)}) collective-permute-start(bf16[2,1,16,1024]{3,2,0,1:T(8,128)(2,1)S(1)} %maximum_select_fusion.8), channel_id=1, source_target_pairs={{0,8},{4,12},{8,0},{12,4},{16,24},{20,28},{24,16},{28,20},{1,9},{5... | collective-permute-start | bytes 196616 | tf_op jit(solution)/shard_map/ppermute | solution.py:13
  12.2 0.5 collective-permute-start.6
  12.7 2.5 %collective-permute-done.1 = bf16[2,1,16,1024]{3,2,0,1:T(8,128)(2,1)S(1)} collective-permute-done((bf16[2,1,16,1024]{3,2,0,1:T(8,128)(2,1)S(1)}, bf16[2,1,16,1024]{3,2,0,1:T(8,128)(2,1)S(1)}, u32[]{:S(2)}, u32[]{:S(2)}) %collective-permute-start.1) | collective-permute-done | bytes 65568 | tf_op jit(solution)/shard_map/ppermute | solution.py:13
  15.2 1.6 %collective-permute-start.2 = (bf16[4,1,16,1024]{3,2,0,1:T(8,128)(2,1)S(1)}, bf16[4,1,16,1024]{3,2,0,1:T(8,128)(2,1)S(1)}, u32[]{:S(2)}, u32[]{:S(2)}) collective-permute-start(bf16[4,1,16,1024]{3,2,0,1:T(8,128)(2,1)S(1)} %bitcast.158), channel_id=1, source_target_pairs={{0,4},{4,0},{8,12},{12,8},{16,20},{20,16},{24,28},{28,24},{1,5},{5... | collective-permute-start | bytes 393224 | tf_op jit(solution)/shard_map/ppermute | solution.py:13
  17.3 1.6 %collective-permute-start.7 = (bf16[4,1,32,1024]{3,2,0,1:T(8,128)(2,1)S(1)}, bf16[4,1,32,1024]{3,2,0,1:T(8,128)(2,1)S(1)}, u32[]{:S(2)}, u32[]{:S(2)}) collective-permute-start(bf16[4,1,32,1024]{3,2,0,1:T(8,128)(2,1)S(1)} %bitcast.154), channel_id=1, source_target_pairs={{0,4},{4,0},{8,12},{12,8},{16,20},{20,16},{24,28},{28,24},{1,5},{5... | collective-permute-start | bytes 786440 | tf_op jit(solution)/shard_map/ppermute | solution.py:13
  18.9 2.8 %collective-permute-done.2 = bf16[4,1,16,1024]{3,2,0,1:T(8,128)(2,1)S(1)} collective-permute-done((bf16[4,1,16,1024]{3,2,0,1:T(8,128)(2,1)S(1)}, bf16[4,1,16,1024]{3,2,0,1:T(8,128)(2,1)S(1)}, u32[]{:S(2)}, u32[]{:S(2)}) %collective-permute-start.2) | collective-permute-done | bytes 131104 | tf_op jit(solution)/shard_map/ppermute | solution.py:13
  21.7 0.6 gather_fusion
  22.4 1.5 %collective-permute-start.3 = (bf16[1,8,16,1024]{3,2,1,0:T(8,128)(2,1)S(1)}, bf16[1,8,16,1024]{3,2,1,0:T(8,128)(2,1)S(1)}, u32[]{:S(2)}, u32[]{:S(2)}) collective-permute-start(bf16[1,8,16,1024]{3,2,1,0:T(8,128)(2,1)S(1)} %bitcast_select_fusion), channel_id=1, source_target_pairs={{0,2},{1,3},{2,0},{3,1},{4,6},{5,7},{6,4},{7,5},{8,10},{9,11},{10,... | collective-permute-start | bytes 786440 | tf_op jit(solution)/shard_map/ppermute | solution.py:13
  24.0 0.6 collective-permute-done.7
  24.8 0.6 gather_fusion.1
  25.7 3.1 %collective-permute-done.3 = bf16[1,8,16,1024]{3,2,1,0:T(8,128)(2,1)S(1)} collective-permute-done((bf16[1,8,16,1024]{3,2,1,0:T(8,128)(2,1)S(1)}, bf16[1,8,16,1024]{3,2,1,0:T(8,128)(2,1)S(1)}, u32[]{:S(2)}, u32[]{:S(2)}) %collective-permute-start.3) | collective-permute-done | bytes 262176 | tf_op jit(solution)/shard_map/ppermute | solution.py:13
  29.0 3.1 %multiply_convert_fusion.2 = (bf16[2,8,32,1024]{3,2,1,0:T(8,128)(2,1)S(1)}, bf16[2,8,32,1024]{3,2,1,0:T(8,128)(2,1)S(1)}, bf16[2,8,32,1024]{3,2,1,0:T(8,128)(2,1...) fusion(f32[2,8,1024]{2,1,0:T(8,128)S(1)} %get-tuple-element.43,, ...), kind=kLoop, calls=%fused_computation.6 | loop fusion | flops 8388608 | bytes 9437184 | tf_op jit(solution)/shard_map/convert_element_type | solution.py:105
  32.8 1.4 %multiply_convert_fusion.1 = bf16[4,2,16,16,1024]{4,3,2,1,0:T(8,128)(2,1)S(1)} fusion(f32[4,2,16,1024]{3,2,1,0:T(8,128)S(1)} %get-tuple-element.33, f32[4,2,16,1024]{3,2,1,0:T(8,128)S(1)} %get-tuple-element.34), kind=kLoop, calls=%fused_computation.3 | loop fusion | flops 4194304 | bytes 5242880 | tf_op jit(solution)/shard_map/convert_element_type | solution.py:58
  34.4 4.5 %bitcast_convert_fusion.1 = bf16[512,1024]{1,0:T(8,128)(2,1)S(1)} fusion(bf16[4,512,1024]{2,1,0:T(8,128)(2,1)S(1)} %bitcast.142, bf16[4,1024,1024]{2,1,0:T(8,128)(2,1)S(1)} %bitcast.168), kind=kOutput, calls=%fused_computation.5 | convolution fusion | flops 4295491584 | bytes 13631488 | tf_op jit(solution)/shard_map/dot_general | solution.py:70
  40.0 0.5 collective-permute-start.8
  40.5 1.4 %multiply_convert_fusion = bf16[4,2,16,16,1024]{4,3,2,1,0:T(8,128)(2,1)S(1)} fusion(f32[4,2,16,1024]{3,2,1,0:T(8,128)S(1)} %get-tuple-element.32, f32[4,2,16,1024]{3,2,1,0:T(8,128)S(1)} %get-tuple-element.31), kind=kLoop, calls=%fused_computation.2 | loop fusion | flops 4194304 | bytes 5242880 | tf_op jit(solution)/shard_map/convert_element_type | solution.py:58
  41.9 0.9 %collective-permute-done.8 = f32[2,2,256,256]{3,2,1,0:T(8,128)S(1)} collective-permute-done((f32[2,2,256,256]{3,2,1,0:T(8,128)S(1)}, f32[2,2,256,256]{3,2,1,0:T(8,128)S(1)}, u32[]{:S(2)}, u32[]{:S(2)}) %collective-permute-start.8) | collective-permute-done | bytes 1048608 | tf_op jit(solution)/shard_map/ppermute | solution.py:13
  43.3 1.6 %collective-permute-start.9 = (bf16[1,2,256,256]{3,2,1,0:T(8,128)(2,1)S(1)}, bf16[1,2,256,256]{3,2,1,0:T(8,128)(2,1)S(1)}, u32[]{:S(2)}, u32[]{:S(2)}) collective-permute-start(bf16[1,2,256,256]{3,2,1,0:T(8,128)(2,1)S(1)} %fusion.7), channel_id=1, source_target_pairs={{0,2},{1,3},{2,0},{3,1},{4,6},{5,7},{6,4},{7,5},{8,10},{9,11},{10,... | collective-permute-start | bytes 786440 | tf_op jit(solution)/shard_map/ppermute | solution.py:13
  44.9 4.7 %bitcast_convert_fusion = bf16[512,1024]{1,0:T(8,128)(2,1)S(1)} fusion(bf16[4,512,1024]{2,1,0:T(8,128)(2,1)S(1)} %bitcast.141, bf16[4,1024,1024]{2,1,0:T(8,128)(2,1)S(1)} %bitcast.169), kind=kOutput, calls=%fused_computation.4 | convolution fusion | flops 4295491584 | bytes 13631488 | tf_op jit(solution)/shard_map/dot_general | solution.py:70
  49.6 2.3 %collective-permute-done.9 = bf16[1,2,256,256]{3,2,1,0:T(8,128)(2,1)S(1)} collective-permute-done((bf16[1,2,256,256]{3,2,1,0:T(8,128)(2,1)S(1)}, bf16[1,2,256,256]{3,2,1,0:T(8,128)(2,1)S(1)}, u32[]{:S(2)}, u32[]{:S(2)}) %collective-permute-start.9) | collective-permute-done | bytes 262176 | tf_op jit(solution)/shard_map/ppermute | solution.py:13
  53.6 2.2 %collective-permute-done.10 = f32[2,2,256,256]{3,2,1,0:T(8,128)S(1)} collective-permute-done((f32[2,2,256,256]{3,2,1,0:T(8,128)S(1)}, f32[2,2,256,256]{3,2,1,0:T(8,128)S(1)}, u32[]{:S(2)}, u32[]{:S(2)}) %collective-permute-start.10) | collective-permute-done | bytes 1048608 | tf_op jit(solution)/shard_map/ppermute | solution.py:13
  56.2 1.5 %collective-permute-start.11 = (bf16[1,2,256,256]{3,2,1,0:T(8,128)(2,1)S(1)}, bf16[1,2,256,256]{3,2,1,0:T(8,128)(2,1)S(1)}, u32[]{:S(2)}, u32[]{:S(2)}) collective-permute-start(bf16[1,2,256,256]{3,2,1,0:T(8,128)(2,1)S(1)} %fusion.2), channel_id=1, source_target_pairs={{0,2},{1,3},{2,0},{3,1},{4,6},{5,7},{6,4},{7,5},{8,10},{9,11},{10,... | collective-permute-start | bytes 786440 | tf_op jit(solution)/shard_map/ppermute | solution.py:13
  57.9 6.8 %collective-permute-done.11 = bf16[1,2,256,256]{3,2,1,0:T(8,128)(2,1)S(1)} collective-permute-done((bf16[1,2,256,256]{3,2,1,0:T(8,128)(2,1)S(1)}, bf16[1,2,256,256]{3,2,1,0:T(8,128)(2,1)S(1)}, u32[]{:S(2)}, u32[]{:S(2)}) %collective-permute-start.11) | collective-permute-done | bytes 262176 | tf_op jit(solution)/shard_map/ppermute | solution.py:13
  65.1 1.0 %maximum_bitcast_fusion = f32[1,4,256,256]{3,2,1,0:T(8,128)} fusion(f32[2,256,256]{2,1,0:T(8,128)S(1)} %fusion, f32[2,256,256]{2,1,0:T(8,128)S(1)} %fusion.6), kind=kLoop, calls=%fused_computation.26 | loop fusion | flops 262144 | bytes 2097152 | tf_op jit(solution)/shard_map/broadcast_in_dim | solution.py:142
  (44 shorter events, 6.3 us)
Async XLA Ops:
  0.9 11.3 %collective-permute-start.5 = (bf16[1,1,32,1024]{3,2,0,1:T(8,128)(2,1)S(1)}, bf16[1,1,32,1024]{3,2,0,1:T(8,128)(2,1)S(1)}, u32[]{:S(2)}, u32[]{:S(2)}) collective-permute-start(bf16[1,1,32,1024]{3,2,0,1:T(8,128)(2,1)S(1)} %get-tuple-element.56), channel_id=1, source_target_pairs={{0,16},{4,20},{8,24},{12,28},{16,0},{20,4},{24,8},{28,12},{1,17},{... | collective-permute-start | bytes 196616 | tf_op jit(solution)/shard_map/ppermute | solution.py:13
  5.7 4.8 %collective-permute-start = (bf16[1,1,16,1024]{3,2,0,1:T(8,128)(2,1)S(1)}, bf16[1,1,16,1024]{3,2,0,1:T(8,128)(2,1)S(1)}, u32[]{:S(2)}, u32[]{:S(2)}) collective-permute-start(bf16[1,1,16,1024]{3,2,0,1:T(8,128)(2,1)S(1)} %get-tuple-element.58), channel_id=1, source_target_pairs={{0,16},{4,20},{8,24},{12,28},{16,0},{20,4},{24,8},{28,12},{1,17},{... | collective-permute-start | bytes 98312 | tf_op jit(solution)/shard_map/ppermute | solution.py:13
  10.5 4.7 %collective-permute-start.1 = (bf16[2,1,16,1024]{3,2,0,1:T(8,128)(2,1)S(1)}, bf16[2,1,16,1024]{3,2,0,1:T(8,128)(2,1)S(1)}, u32[]{:S(2)}, u32[]{:S(2)}) collective-permute-start(bf16[2,1,16,1024]{3,2,0,1:T(8,128)(2,1)S(1)} %maximum_select_fusion.8), channel_id=1, source_target_pairs={{0,8},{4,12},{8,0},{12,4},{16,24},{20,28},{24,16},{28,20},{1,9},{5... | collective-permute-start | bytes 196616 | tf_op jit(solution)/shard_map/ppermute | solution.py:13
  12.2 5.0 %collective-permute-start.6 = (bf16[2,1,32,1024]{3,2,0,1:T(8,128)(2,1)S(1)}, bf16[2,1,32,1024]{3,2,0,1:T(8,128)(2,1)S(1)}, u32[]{:S(2)}, u32[]{:S(2)}) collective-permute-start(bf16[2,1,32,1024]{3,2,0,1:T(8,128)(2,1)S(1)} %maximum_select_fusion.7), channel_id=1, source_target_pairs={{0,8},{4,12},{8,0},{12,4},{16,24},{20,28},{24,16},{28,20},{1,9},{5... | collective-permute-start | bytes 393224 | tf_op jit(solution)/shard_map/ppermute | solution.py:13
  15.2 6.5 %collective-permute-start.2 = (bf16[4,1,16,1024]{3,2,0,1:T(8,128)(2,1)S(1)}, bf16[4,1,16,1024]{3,2,0,1:T(8,128)(2,1)S(1)}, u32[]{:S(2)}, u32[]{:S(2)}) collective-permute-start(bf16[4,1,16,1024]{3,2,0,1:T(8,128)(2,1)S(1)} %bitcast.158), channel_id=1, source_target_pairs={{0,4},{4,0},{8,12},{12,8},{16,20},{20,16},{24,28},{28,24},{1,5},{5... | collective-permute-start | bytes 393224 | tf_op jit(solution)/shard_map/ppermute | solution.py:13
  17.3 7.4 %collective-permute-start.7 = (bf16[4,1,32,1024]{3,2,0,1:T(8,128)(2,1)S(1)}, bf16[4,1,32,1024]{3,2,0,1:T(8,128)(2,1)S(1)}, u32[]{:S(2)}, u32[]{:S(2)}) collective-permute-start(bf16[4,1,32,1024]{3,2,0,1:T(8,128)(2,1)S(1)} %bitcast.154), channel_id=1, source_target_pairs={{0,4},{4,0},{8,12},{12,8},{16,20},{20,16},{24,28},{28,24},{1,5},{5... | collective-permute-start | bytes 786440 | tf_op jit(solution)/shard_map/ppermute | solution.py:13
  22.4 6.4 %collective-permute-start.3 = (bf16[1,8,16,1024]{3,2,1,0:T(8,128)(2,1)S(1)}, bf16[1,8,16,1024]{3,2,1,0:T(8,128)(2,1)S(1)}, u32[]{:S(2)}, u32[]{:S(2)}) collective-permute-start(bf16[1,8,16,1024]{3,2,1,0:T(8,128)(2,1)S(1)} %bitcast_select_fusion), channel_id=1, source_target_pairs={{0,2},{1,3},{2,0},{3,1},{4,6},{5,7},{6,4},{7,5},{8,10},{9,11},{10,... | collective-permute-start | bytes 786440 | tf_op jit(solution)/shard_map/ppermute | solution.py:13
  28.9 3.3 %collective-permute-start.4 = (bf16[2,8,16,1024]{3,2,1,0:T(8,128)(2,1)S(1)}, bf16[2,8,16,1024]{3,2,1,0:T(8,128)(2,1)S(1)}, u32[]{:S(2)}, u32[]{:S(2)}) collective-permute-start(bf16[2,8,16,1024]{3,2,1,0:T(8,128)(2,1)S(1)} %maximum_select_fusion.2), channel_id=1, source_target_pairs={{0,1},{1,0},{2,3},{3,2},{4,5},{5,4},{6,7},{7,6},{8,9},{9,8},{10,11... | collective-permute-start | bytes 1572872 | tf_op jit(solution)/shard_map/ppermute | solution.py:13
  29.0 5.2 %slice-start = ((s8[8388608]{0:T(1024)(128)(4,1)}), s8[4194304]{0:T(1024)(128)(4,1)S(1)}, s32[]{:S(2)}) async-start(s8[8388608]{0:T(1024)(128)(4,1)} %bitcast.166), calls=%async_computation | async-start | bytes 8388608
  32.2 2.2 %slice-start.1 = ((s8[8388608]{0:T(1024)(128)(4,1)}), s8[4194304]{0:T(1024)(128)(4,1)S(1)}, s32[]{:S(2)}) async-start(s8[8388608]{0:T(1024)(128)(4,1)} %bitcast.166), calls=%async_computation.1 | async-start | bytes 8388608
  40.0 2.8 %collective-permute-start.8 = (f32[2,2,256,256]{3,2,1,0:T(8,128)S(1)}, f32[2,2,256,256]{3,2,1,0:T(8,128)S(1)}, u32[]{:S(2)}, u32[]{:S(2)}) collective-permute-start(f32[2,2,256,256]{3,2,1,0:T(8,128)S(1)} %pad_maximum_fusion), channel_id=1, source_target_pairs={{0,1},{1,0},{2,3},{3,2},{4,5},{5,4},{6,7},{7,6},{8,9},{9,8},{10,11... | collective-permute-start | bytes 3145736 | tf_op jit(solution)/shard_map/ppermute | solution.py:13
  43.3 8.7 %collective-permute-start.9 = (bf16[1,2,256,256]{3,2,1,0:T(8,128)(2,1)S(1)}, bf16[1,2,256,256]{3,2,1,0:T(8,128)(2,1)S(1)}, u32[]{:S(2)}, u32[]{:S(2)}) collective-permute-start(bf16[1,2,256,256]{3,2,1,0:T(8,128)(2,1)S(1)} %fusion.7), channel_id=1, source_target_pairs={{0,2},{1,3},{2,0},{3,1},{4,6},{5,7},{6,4},{7,5},{8,10},{9,11},{10,... | collective-permute-start | bytes 786440 | tf_op jit(solution)/shard_map/ppermute | solution.py:13
  53.0 2.7 %collective-permute-start.10 = (f32[2,2,256,256]{3,2,1,0:T(8,128)S(1)}, f32[2,2,256,256]{3,2,1,0:T(8,128)S(1)}, u32[]{:S(2)}, u32[]{:S(2)}) collective-permute-start(f32[2,2,256,256]{3,2,1,0:T(8,128)S(1)} %pad_maximum_fusion.1), channel_id=1, source_target_pairs={{0,1},{1,0},{2,3},{3,2},{4,5},{5,4},{6,7},{7,6},{8,9},{9,8},{10,11... | collective-permute-start | bytes 3145736 | tf_op jit(solution)/shard_map/ppermute | solution.py:13
  56.2 8.4 %collective-permute-start.11 = (bf16[1,2,256,256]{3,2,1,0:T(8,128)(2,1)S(1)}, bf16[1,2,256,256]{3,2,1,0:T(8,128)(2,1)S(1)}, u32[]{:S(2)}, u32[]{:S(2)}) collective-permute-start(bf16[1,2,256,256]{3,2,1,0:T(8,128)(2,1)S(1)} %fusion.2), channel_id=1, source_target_pairs={{0,2},{1,3},{2,0},{3,1},{4,6},{5,7},{6,4},{7,5},{8,10},{9,11},{10,... | collective-permute-start | bytes 786440 | tf_op jit(solution)/shard_map/ppermute | solution.py:13

commit v19 on v13

--- a/solution.py
+++ b/solution.py
@@ -81,8 +81,11 @@
         kpoint_count, orb_count - NV, mu_cols
     )
 
-    valence = gather_axis(jnp.take(held_valence, wanted, axis=0), "col")
-    conduction = jnp.take(held_conduction, wanted, axis=0).astype(jnp.float32)
+    if kpoint_count <= wanted.shape[0]:
+        valence = jnp.take(gather_axis(held_valence, "col"), wanted, axis=1, mode="clip")
+    else:
+        valence = gather_axis(jnp.take(held_valence, wanted, axis=0, mode="clip"), "col")
+    conduction = jnp.take(held_conduction, wanted, axis=0, mode="clip").astype(jnp.float32)
     rows_per_block = NC // col_count
     chunk = pair_count // PAIR_CHUNKS
     starts = list(range(0, pair_count, chunk))

time: 63 us -> 69.1 us (1.097)
  matrix products: 13 us -> 15.7 us
  other arithmetic: 11.2 us -> 12.7 us
  waiting for transfers between devices: 18.2 us -> 19.3 us
  local copies, waits for them, and re-layouts: 3.32 us -> 4.37 us
    dot_general x2, matrix products: 9.3 us -> 12 us  [screened_of(): lax.dot_general(val_pairs, screen, (((0, 2), (0, 1)), ((), ())), preferre...]
    convert_element_type x1, other arithmetic: 3.08 us -> 4.68 us  [cond_block(): (rows[:, :, None, :] * cond_b[:, None, :, :]).astype(jnp.bfloat16)]
    gather x2, local copies, waits for them, and re-layouts: 1.15 us -> 2.42 us  [the longest x1 1.84 us: body(): jnp.take(gather_axis(held_valence, 'col'), wanted, axis=1, mode='clip')]
    ppermute x12, waiting for transfers between devices: 18.2 us -> 19.3 us  [swap(): return lax.ppermute(x, axis, [(i, i ^ bit) for i in range(size)])]
    select_n x11, other arithmetic: 0.52 us -> 1.47 us  [gather_axis(): cur = jnp.where(low, jnp.stack([cur, got], 1), jnp.stack([got, cur], 1))]
    select_n x2 -> x0, other arithmetic: 0.82 us -> none  [body(): valence = gather_axis(jnp.take(held_valence, wanted, axis=0), 'col')]
    convert_element_type x2, other arithmetic: 2.78 us -> 3.58 us  [screened_of(): (valence_a[:, :, :, None, :] * valence_b[:, :, None, :, :]).astype(jnp.bf...]
    and x1 -> x0, other arithmetic: 0.73 us -> none  [body(): valence = gather_axis(jnp.take(held_valence, wanted, axis=0), 'col')]
  transfers between devices with their start and end apart: 12 -> 12, of which waited for: 8 -> 8; matrix products, arithmetic and copies ran while one was open for 28% -> 25% of each run, Pallas kernels for 0% -> 0%
where the time goes in v19:
time: 69.1 us; the launch traced here: 68.8 us
  waiting for transfers between devices  19.3 us (28%)
  starting transfers between devices  16.3 us (24%)
  matrix products  15.7 us (23%)
  other arithmetic  12.7 us (18%)
  local copies, waits for them, and re-layouts  4.37 us (6%)
    ppermute x12, waiting for transfers between devices, swap(): return lax.ppermute(x, axis, [(i, i ^ bit) for i in range(size)])  19.3 us
    ppermute x12, starting transfers between devices, swap(): return lax.ppermute(x, axis, [(i, i ^ bit) for i in range(size)])  16.3 us
    dot_general x2, matrix products, screened_of(): lax.dot_general(val_pairs, screen, (((0, 2), (0, 1)), ((), ())), preferre...  12 us
    convert_element_type x1, other arithmetic, cond_block(): (rows[:, :, None, :] * cond_b[:, None, :, :]).astype(jnp.bfloat16)  4.68 us
    dot_general x8, matrix products, own_block(): jnp.einsum('pan,pbn->pab', screened, cond_pairs, preferred_element_type=j...  3.74 us
    convert_element_type x2, other arithmetic, screened_of(): (valence_a[:, :, :, None, :] * valence_b[:, :, None, :, :]).astype(jnp.bf...  3.58 us
    gather x1, local copies, waits for them, and re-layouts, body(): jnp.take(gather_axis(held_valence, 'col'), wanted, axis=1, mode='clip')  1.84 us
    another operation x2, local copies, waits for them, and re-layouts, gather_axis(): cur = jnp.where(low, jnp.stack([cur, got], 1), jnp.stack([got, cur], 1))  1.61 us
  transfers between devices with their start and end apart: 12, of which 8 were waited for; matrix products, arithmetic and copies ran while one was open for 25% of the time, Pallas kernels for 0%

profile of v19, /device:TPU:0, one launch (start us, length us, event | category | flops | bytes accessed | tf_op | source)
XLA Modules:
  0.0 68.8 jit_solution(3761161661496625232)
XLA Ops:
  0.0 0.8 %slice_bitcast_fusion.7 = (bf16[1,1,1,16,1024]{4,3,2,1,0:T(8,128)(2,1)S(1)}, bf16[1,1,16,1024]{3,2,0,1:T(8,128)(2,1)S(1)}) fusion(bf16[1,48,1024]{2,1,0:T(8,128)(2,1)} %param.3), kind=kLoop, calls=%fused_computation.57 | loop fusion | bytes 98304 | tf_op jit(solution)/shard_map/stack | solution.py:24
  0.8 4.0 %collective-permute-start = (bf16[1,1,16,1024]{3,2,0,1:T(8,128)(2,1)S(1)}, bf16[1,1,16,1024]{3,2,0,1:T(8,128)(2,1)S(1)}, u32[]{:S(2)}, u32[]{:S(2)}) collective-permute-start(bf16[1,1,16,1024]{3,2,0,1:T(8,128)(2,1)S(1)} %get-tuple-element.50), channel_id=1, source_target_pairs={{0,16},{4,20},{8,24},{12,28},{16,0},{20,4},{24,8},{28,12},{1,17},{... | collective-permute-start | bytes 98312 | tf_op jit(solution)/shard_map/ppermute | solution.py:13
  4.8 0.8 %slice_bitcast_fusion.5 = (bf16[1,1,1,32,1024]{4,3,2,1,0:T(8,128)(2,1)S(1)}, bf16[1,1,32,1024]{3,2,0,1:T(8,128)(2,1)S(1)}) fusion(bf16[1,48,1024]{2,1,0:T(8,128)(2,1)} %param.3), kind=kLoop, calls=%fused_computation.55 | loop fusion | bytes 196608 | tf_op jit(solution)/shard_map/stack | solution.py:24
  5.7 0.7 and_select_fusion
  6.4 0.6 collective-permute-done
  7.1 2.5 %collective-permute-start.1 = (bf16[2,1,16,1024]{3,2,0,1:T(8,128)(2,1)S(1)}, bf16[2,1,16,1024]{3,2,0,1:T(8,128)(2,1)S(1)}, u32[]{:S(2)}, u32[]{:S(2)}) collective-permute-start(bf16[2,1,16,1024]{3,2,0,1:T(8,128)(2,1)S(1)} %maximum_select_fusion.8), channel_id=1, source_target_pairs={{0,8},{4,12},{8,0},{12,4},{16,24},{20,28},{24,16},{28,20},{1,9},{5... | collective-permute-start | bytes 196616 | tf_op jit(solution)/shard_map/ppermute | solution.py:13
  9.5 1.6 %collective-permute-done.5 = bf16[1,1,32,1024]{3,2,0,1:T(8,128)(2,1)S(1)} collective-permute-done((bf16[1,1,32,1024]{3,2,0,1:T(8,128)(2,1)S(1)}, bf16[1,1,32,1024]{3,2,0,1:T(8,128)(2,1)S(1)}, u32[]{:S(2)}, u32[]{:S(2)}) %collective-permute-start.5) | collective-permute-done | bytes 65568 | tf_op jit(solution)/shard_map/ppermute | solution.py:13
  11.2 1.5 %collective-permute-start.6 = (bf16[2,1,32,1024]{3,2,0,1:T(8,128)(2,1)S(1)}, bf16[2,1,32,1024]{3,2,0,1:T(8,128)(2,1)S(1)}, u32[]{:S(2)}, u32[]{:S(2)}) collective-permute-start(bf16[2,1,32,1024]{3,2,0,1:T(8,128)(2,1)S(1)} %maximum_select_fusion.7), channel_id=1, source_target_pairs={{0,8},{4,12},{8,0},{12,4},{16,24},{20,28},{24,16},{28,20},{1,9},{5... | collective-permute-start | bytes 393224 | tf_op jit(solution)/shard_map/ppermute | solution.py:13
  12.8 1.6 %collective-permute-start.2 = (bf16[4,1,16,1024]{3,2,0,1:T(8,128)(2,1)S(1)}, bf16[4,1,16,1024]{3,2,0,1:T(8,128)(2,1)S(1)}, u32[]{:S(2)}, u32[]{:S(2)}) collective-permute-start(bf16[4,1,16,1024]{3,2,0,1:T(8,128)(2,1)S(1)} %bitcast.156), channel_id=1, source_target_pairs={{0,4},{4,0},{8,12},{12,8},{16,20},{20,16},{24,28},{28,24},{1,5},{5... | collective-permute-start | bytes 393224 | tf_op jit(solution)/shard_map/ppermute | solution.py:13
  14.4 1.9 %collective-permute-done.6 = bf16[2,1,32,1024]{3,2,0,1:T(8,128)(2,1)S(1)} collective-permute-done((bf16[2,1,32,1024]{3,2,0,1:T(8,128)(2,1)S(1)}, bf16[2,1,32,1024]{3,2,0,1:T(8,128)(2,1)S(1)}, u32[]{:S(2)}, u32[]{:S(2)}) %collective-permute-start.6) | collective-permute-done | bytes 131104 | tf_op jit(solution)/shard_map/ppermute | solution.py:13
  16.3 1.6 %collective-permute-start.7 = (bf16[4,1,32,1024]{3,2,0,1:T(8,128)(2,1)S(1)}, bf16[4,1,32,1024]{3,2,0,1:T(8,128)(2,1)S(1)}, u32[]{:S(2)}, u32[]{:S(2)}) collective-permute-start(bf16[4,1,32,1024]{3,2,0,1:T(8,128)(2,1)S(1)} %bitcast.152), channel_id=1, source_target_pairs={{0,4},{4,0},{8,12},{12,8},{16,20},{20,16},{24,28},{28,24},{1,5},{5... | collective-permute-start | bytes 786440 | tf_op jit(solution)/shard_map/ppermute | solution.py:13
  17.9 0.7 %pad_add_fusion = s32[8]{0:T(128)S(1)} fusion(s32[4]{0:T(128)S(1)} %and_select_fusion, s32[4]{0:T(128)} %bitcast.168), kind=kLoop, calls=%fused_computation.71 | loop fusion | flops 8 | bytes 64 | tf_op jit(solution)/shard_map/concatenate | solution.py:78
  18.6 0.5 collective-permute-done.2
  19.2 1.6 %collective-permute-start.3 = (bf16[1,8,16,1024]{3,2,1,0:T(8,128)(2,1)S(1)}, bf16[1,8,16,1024]{3,2,1,0:T(8,128)(2,1)S(1)}, u32[]{:S(2)}, u32[]{:S(2)}) collective-permute-start(bf16[1,8,16,1024]{3,2,1,0:T(8,128)(2,1)S(1)} %bitcast.148), channel_id=1, source_target_pairs={{0,2},{1,3},{2,0},{3,1},{4,6},{5,7},{6,4},{7,5},{8,10},{9,11},{10,... | collective-permute-start | bytes 786440 | tf_op jit(solution)/shard_map/ppermute | solution.py:13
  20.8 2.2 %collective-permute-done.7 = bf16[4,1,32,1024]{3,2,0,1:T(8,128)(2,1)S(1)} collective-permute-done((bf16[4,1,32,1024]{3,2,0,1:T(8,128)(2,1)S(1)}, bf16[4,1,32,1024]{3,2,0,1:T(8,128)(2,1)S(1)}, u32[]{:S(2)}, u32[]{:S(2)}) %collective-permute-start.7) | collective-permute-done | bytes 262176 | tf_op jit(solution)/shard_map/ppermute | solution.py:13
  23.1 0.6 gather_fusion.1
  23.9 1.7 %collective-permute-done.3 = bf16[1,8,16,1024]{3,2,1,0:T(8,128)(2,1)S(1)} collective-permute-done((bf16[1,8,16,1024]{3,2,1,0:T(8,128)(2,1)S(1)}, bf16[1,8,16,1024]{3,2,1,0:T(8,128)(2,1)S(1)}, u32[]{:S(2)}, u32[]{:S(2)}) %collective-permute-start.3) | collective-permute-done | bytes 262176 | tf_op jit(solution)/shard_map/ppermute | solution.py:13
  25.8 4.7 %multiply_convert_fusion.2 = (bf16[2,8,32,1024]{3,2,1,0:T(8,128)(2,1)}, bf16[2,8,32,1024]{3,2,1,0:T(8,128)(2,1)}, bf16[2,8,32,1024]{3,2,1,0:T(8,128)(2,1)}, bf16...) fusion(f32[2,8,1024]{2,1,0:T(8,128)S(1)} %get-tuple-element.35,, ...), kind=kLoop, calls=%fused_computation.6 | loop fusion | flops 8388608 | bytes 9437184 | tf_op jit(solution)/shard_map/convert_element_type | solution.py:99
  30.6 1.1 %maximum_select_fusion = bf16[2,2,8,16,1024]{4,3,2,1,0:T(8,128)(2,1)} fusion(bf16[2,1,8,16,1024]{4,3,2,1,0:T(8,128)(2,1)S(1)} %bitcast.155, bf16[2,1,8,16,1024]{4,3,2,1,0:T(8,128)(2,1)S(1)} %maximum_select_fusion.1, pred[]{:T(512)S(6)} %eq.20), kind=kLoop, calls=%fused_computation.18 | loop fusion | flops 1572864 | bytes 2097153 | tf_op jit(solution)/shard_map/jit(_where)/select_n | solution.py:24
  31.7 1.8 %gather_fusion = bf16[8,4,16,1024]{3,2,1,0:T(8,128)(2,1)S(1)} fusion(bf16[4,8,16,1024]{3,2,1,0:T(8,128)(2,1)} %bitcast.145, s32[1024]{0:T(1024)S(1)} %pad_clamp_fusion), kind=kCustom, calls=%fused_computation | custom fusion | bytes 2097184 | tf_op jit(solution)/shard_map/jit(_take)/gather | solution.py:85
  33.8 1.8 %multiply_convert_fusion.1 = bf16[4,2,16,16,1024]{4,3,2,1,0:T(8,128)(2,1)S(1)} fusion(f32[4,2,16,1024]{3,2,0,1:T(8,128)S(1)} %get-tuple-element.23, f32[4,2,16,1024]{3,2,0,1:T(8,128)S(1)} %get-tuple-element.26), kind=kLoop, calls=%fused_computation.3 | loop fusion | flops 4194304 | bytes 5242880 | tf_op jit(solution)/shard_map/convert_element_type | solution.py:58
  35.6 7.4 %bitcast_convert_fusion.1 = bf16[512,1024]{1,0:T(8,128)(2,1)S(1)} fusion(bf16[4,512,1024]{2,1,0:T(8,128)(2,1)S(1)} %bitcast.137, bf16[4,1024,1024]{2,1,0:T(8,128)(2,1)} %bitcast.164), kind=kOutput, calls=%fused_computation.5 | convolution fusion | flops 4295491584 | bytes 13631488 | tf_op jit(solution)/shard_map/dot_general | solution.py:61
  43.6 0.5 convolution_bitcast_fusion.3
  44.1 0.6 collective-permute-start.8
  44.7 1.8 %multiply_convert_fusion = bf16[4,2,16,16,1024]{4,3,2,1,0:T(8,128)(2,1)S(1)} fusion(f32[4,2,16,1024]{3,2,0,1:T(8,128)S(1)} %get-tuple-element.25, f32[4,2,16,1024]{3,2,0,1:T(8,128)S(1)} %get-tuple-element.24), kind=kLoop, calls=%fused_computation.2 | loop fusion | flops 4194304 | bytes 5242880 | tf_op jit(solution)/shard_map/convert_element_type | solution.py:58
  46.6 4.6 %bitcast_convert_fusion = bf16[512,1024]{1,0:T(8,128)(2,1)S(1)} fusion(bf16[4,512,1024]{2,1,0:T(8,128)(2,1)S(1)} %bitcast.138, bf16[4,1024,1024]{2,1,0:T(8,128)(2,1)S(1)} %bitcast.167), kind=kOutput, calls=%fused_computation.4 | convolution fusion | flops 4295491584 | bytes 13631488 | tf_op jit(solution)/shard_map/dot_general | solution.py:61
  53.3 1.6 %collective-permute-start.9 = (bf16[1,2,256,256]{3,2,1,0:T(8,128)(2,1)S(1)}, bf16[1,2,256,256]{3,2,1,0:T(8,128)(2,1)S(1)}, u32[]{:S(2)}, u32[]{:S(2)}) collective-permute-start(bf16[1,2,256,256]{3,2,1,0:T(8,128)(2,1)S(1)} %fusion.8), channel_id=1, source_target_pairs={{0,2},{1,3},{2,0},{3,1},{4,6},{5,7},{6,4},{7,5},{8,10},{9,11},{10,... | collective-permute-start | bytes 786440 | tf_op jit(solution)/shard_map/ppermute | solution.py:13
  55.4 0.5 fusion.9
  55.8 1.1 %collective-permute-start.11 = (bf16[1,2,256,256]{3,2,1,0:T(8,128)(2,1)S(1)}, bf16[1,2,256,256]{3,2,1,0:T(8,128)(2,1)S(1)}, u32[]{:S(2)}, u32[]{:S(2)}) collective-permute-start(bf16[1,2,256,256]{3,2,1,0:T(8,128)(2,1)S(1)} %fusion.9), channel_id=1, source_target_pairs={{0,2},{1,3},{2,0},{3,1},{4,6},{5,7},{6,4},{7,5},{8,10},{9,11},{10,... | collective-permute-start | bytes 786440 | tf_op jit(solution)/shard_map/ppermute | solution.py:13
  57.0 5.5 %collective-permute-done.9 = bf16[1,2,256,256]{3,2,1,0:T(8,128)(2,1)S(1)} collective-permute-done((bf16[1,2,256,256]{3,2,1,0:T(8,128)(2,1)S(1)}, bf16[1,2,256,256]{3,2,1,0:T(8,128)(2,1)S(1)}, u32[]{:S(2)}, u32[]{:S(2)}) %collective-permute-start.9) | collective-permute-done | bytes 262176 | tf_op jit(solution)/shard_map/ppermute | solution.py:13
  62.6 5.1 %collective-permute-done.11 = bf16[1,2,256,256]{3,2,1,0:T(8,128)(2,1)S(1)} collective-permute-done((bf16[1,2,256,256]{3,2,1,0:T(8,128)(2,1)S(1)}, bf16[1,2,256,256]{3,2,1,0:T(8,128)(2,1)S(1)}, u32[]{:S(2)}, u32[]{:S(2)}) %collective-permute-start.11) | collective-permute-done | bytes 262176 | tf_op jit(solution)/shard_map/ppermute | solution.py:13
  67.7 1.0 %maximum_bitcast_fusion = f32[1,4,256,256]{3,2,1,0:T(8,128)} fusion(f32[2,256,256]{2,1,0:T(8,128)S(1)} %fusion.3, f32[2,256,256]{2,1,0:T(8,128)S(1)} %fusion.7), kind=kLoop, calls=%fused_computation.21 | loop fusion | flops 262144 | bytes 2097152 | tf_op jit(solution)/shard_map/broadcast_in_dim | solution.py:129
  (51 shorter events, 4.3 us)
Async XLA Ops:
  0.8 6.3 %collective-permute-start = (bf16[1,1,16,1024]{3,2,0,1:T(8,128)(2,1)S(1)}, bf16[1,1,16,1024]{3,2,0,1:T(8,128)(2,1)S(1)}, u32[]{:S(2)}, u32[]{:S(2)}) collective-permute-start(bf16[1,1,16,1024]{3,2,0,1:T(8,128)(2,1)S(1)} %get-tuple-element.50), channel_id=1, source_target_pairs={{0,16},{4,20},{8,24},{12,28},{16,0},{20,4},{24,8},{28,12},{1,17},{... | collective-permute-start | bytes 98312 | tf_op jit(solution)/shard_map/ppermute | solution.py:13
  5.7 5.5 %collective-permute-start.5 = (bf16[1,1,32,1024]{3,2,0,1:T(8,128)(2,1)S(1)}, bf16[1,1,32,1024]{3,2,0,1:T(8,128)(2,1)S(1)}, u32[]{:S(2)}, u32[]{:S(2)}) collective-permute-start(bf16[1,1,32,1024]{3,2,0,1:T(8,128)(2,1)S(1)} %get-tuple-element.48), channel_id=1, source_target_pairs={{0,16},{4,20},{8,24},{12,28},{16,0},{20,4},{24,8},{28,12},{1,17},{... | collective-permute-start | bytes 196616 | tf_op jit(solution)/shard_map/ppermute | solution.py:13
  7.1 5.7 %collective-permute-start.1 = (bf16[2,1,16,1024]{3,2,0,1:T(8,128)(2,1)S(1)}, bf16[2,1,16,1024]{3,2,0,1:T(8,128)(2,1)S(1)}, u32[]{:S(2)}, u32[]{:S(2)}) collective-permute-start(bf16[2,1,16,1024]{3,2,0,1:T(8,128)(2,1)S(1)} %maximum_select_fusion.8), channel_id=1, source_target_pairs={{0,8},{4,12},{8,0},{12,4},{16,24},{20,28},{24,16},{28,20},{1,9},{5... | collective-permute-start | bytes 196616 | tf_op jit(solution)/shard_map/ppermute | solution.py:13
  11.2 5.0 %collective-permute-start.6 = (bf16[2,1,32,1024]{3,2,0,1:T(8,128)(2,1)S(1)}, bf16[2,1,32,1024]{3,2,0,1:T(8,128)(2,1)S(1)}, u32[]{:S(2)}, u32[]{:S(2)}) collective-permute-start(bf16[2,1,32,1024]{3,2,0,1:T(8,128)(2,1)S(1)} %maximum_select_fusion.7), channel_id=1, source_target_pairs={{0,8},{4,12},{8,0},{12,4},{16,24},{20,28},{24,16},{28,20},{1,9},{5... | collective-permute-start | bytes 393224 | tf_op jit(solution)/shard_map/ppermute | solution.py:13
  12.8 6.4 %collective-permute-start.2 = (bf16[4,1,16,1024]{3,2,0,1:T(8,128)(2,1)S(1)}, bf16[4,1,16,1024]{3,2,0,1:T(8,128)(2,1)S(1)}, u32[]{:S(2)}, u32[]{:S(2)}) collective-permute-start(bf16[4,1,16,1024]{3,2,0,1:T(8,128)(2,1)S(1)} %bitcast.156), channel_id=1, source_target_pairs={{0,4},{4,0},{8,12},{12,8},{16,20},{20,16},{24,28},{28,24},{1,5},{5... | collective-permute-start | bytes 393224 | tf_op jit(solution)/shard_map/ppermute | solution.py:13
  16.3 6.7 %collective-permute-start.7 = (bf16[4,1,32,1024]{3,2,0,1:T(8,128)(2,1)S(1)}, bf16[4,1,32,1024]{3,2,0,1:T(8,128)(2,1)S(1)}, u32[]{:S(2)}, u32[]{:S(2)}) collective-permute-start(bf16[4,1,32,1024]{3,2,0,1:T(8,128)(2,1)S(1)} %bitcast.152), channel_id=1, source_target_pairs={{0,4},{4,0},{8,12},{12,8},{16,20},{20,16},{24,28},{28,24},{1,5},{5... | collective-permute-start | bytes 786440 | tf_op jit(solution)/shard_map/ppermute | solution.py:13
  19.2 6.4 %collective-permute-start.3 = (bf16[1,8,16,1024]{3,2,1,0:T(8,128)(2,1)S(1)}, bf16[1,8,16,1024]{3,2,1,0:T(8,128)(2,1)S(1)}, u32[]{:S(2)}, u32[]{:S(2)}) collective-permute-start(bf16[1,8,16,1024]{3,2,1,0:T(8,128)(2,1)S(1)} %bitcast.148), channel_id=1, source_target_pairs={{0,2},{1,3},{2,0},{3,1},{4,6},{5,7},{6,4},{7,5},{8,10},{9,11},{10,... | collective-permute-start | bytes 786440 | tf_op jit(solution)/shard_map/ppermute | solution.py:13
  25.7 4.8 %collective-permute-start.4 = (bf16[2,8,16,1024]{3,2,1,0:T(8,128)(2,1)S(1)}, bf16[2,8,16,1024]{3,2,1,0:T(8,128)(2,1)S(1)}, u32[]{:S(2)}, u32[]{:S(2)}) collective-permute-start(bf16[2,8,16,1024]{3,2,1,0:T(8,128)(2,1)S(1)} %maximum_select_fusion.2), channel_id=1, source_target_pairs={{0,1},{1,0},{2,3},{3,2},{4,5},{5,4},{6,7},{7,6},{8,9},{9,8},{10,11... | collective-permute-start | bytes 1572872 | tf_op jit(solution)/shard_map/ppermute | solution.py:13
  33.8 12.7 %slice-start = ((s8[8388608]{0:T(1024)(128)(4,1)}), s8[4194304]{0:T(1024)(128)(4,1)S(1)}, s32[]{:S(2)}) async-start(s8[8388608]{0:T(1024)(128)(4,1)} %bitcast.165), calls=%async_computation | async-start | bytes 8388608
  35.6 7.5 %copy-start.3 = (bf16[2,8,32,1024]{3,2,1,0:T(8,128)(2,1)S(1)}, bf16[2,8,32,1024]{3,2,1,0:T(8,128)(2,1)}, u32[]{:S(2)}) copy-start(bf16[2,8,32,1024]{3,2,1,0:T(8,128)(2,1)} %get-tuple-element.54) | copy-start | bytes 3145732
  35.6 8.0 %copy-start.2 = (bf16[2,8,32,1024]{3,2,1,0:T(8,128)(2,1)S(1)}, bf16[2,8,32,1024]{3,2,1,0:T(8,128)(2,1)}, u32[]{:S(2)}) copy-start(bf16[2,8,32,1024]{3,2,1,0:T(8,128)(2,1)} %get-tuple-element.53) | copy-start | bytes 3145732
  35.6 10.9 %slice-start.1 = ((s8[8388608]{0:T(1024)(128)(4,1)}), s8[4194304]{0:T(1024)(128)(4,1)S(1)}, s32[]{:S(2)}) async-start(s8[8388608]{0:T(1024)(128)(4,1)} %bitcast.165), calls=%async_computation.1 | async-start | bytes 8388608
  44.1 8.6 %collective-permute-start.8 = (f32[2,2,256,256]{3,2,1,0:T(8,128)S(1)}, f32[2,2,256,256]{3,2,1,0:T(8,128)S(1)}, u32[]{:S(2)}, u32[]{:S(2)}) collective-permute-start(f32[2,2,256,256]{3,2,1,0:T(8,128)S(1)} %pad_maximum_fusion), channel_id=1, source_target_pairs={{0,1},{1,0},{2,3},{3,2},{4,5},{5,4},{6,7},{7,6},{8,9},{9,8},{10,11... | collective-permute-start | bytes 3145736 | tf_op jit(solution)/shard_map/ppermute | solution.py:13
  46.5 4.6 %copy-start.1 = (bf16[2,8,32,1024]{3,2,1,0:T(8,128)(2,1)S(1)}, bf16[2,8,32,1024]{3,2,1,0:T(8,128)(2,1)}, u32[]{:S(2)}) copy-start(bf16[2,8,32,1024]{3,2,1,0:T(8,128)(2,1)} %get-tuple-element.31) | copy-start | bytes 3145732
  46.5 5.1 %copy-start = (bf16[2,8,32,1024]{3,2,1,0:T(8,128)(2,1)S(1)}, bf16[2,8,32,1024]{3,2,1,0:T(8,128)(2,1)}, u32[]{:S(2)}) copy-start(bf16[2,8,32,1024]{3,2,1,0:T(8,128)(2,1)} %get-tuple-element.32) | copy-start | bytes 3145732
  51.6 1.2 %copy-start.5 = (bf16[2,8,32,1024]{3,2,1,0:T(8,128)(2,1)S(1)}, bf16[2,8,32,1024]{3,2,1,0:T(8,128)(2,1)}, u32[]{:S(2)}) copy-start(bf16[2,8,32,1024]{3,2,1,0:T(8,128)(2,1)} %get-tuple-element.52) | copy-start | bytes 3145732
  52.2 3.2 %copy-start.4 = (bf16[2,8,32,1024]{3,2,1,0:T(8,128)(2,1)S(1)}, bf16[2,8,32,1024]{3,2,1,0:T(8,128)(2,1)}, u32[]{:S(2)}) copy-start(bf16[2,8,32,1024]{3,2,1,0:T(8,128)(2,1)} %get-tuple-element.33) | copy-start | bytes 3145732
  52.2 3.2 %collective-permute-start.10 = (f32[2,2,256,256]{3,2,1,0:T(8,128)S(1)}, f32[2,2,256,256]{3,2,1,0:T(8,128)S(1)}, u32[]{:S(2)}, u32[]{:S(2)}) collective-permute-start(f32[2,2,256,256]{3,2,1,0:T(8,128)S(1)} %pad_maximum_fusion.1), channel_id=1, source_target_pairs={{0,1},{1,0},{2,3},{3,2},{4,5},{5,4},{6,7},{7,6},{8,9},{9,8},{10,11... | collective-permute-start | bytes 3145736 | tf_op jit(solution)/shard_map/ppermute | solution.py:13
  53.3 9.2 %collective-permute-start.9 = (bf16[1,2,256,256]{3,2,1,0:T(8,128)(2,1)S(1)}, bf16[1,2,256,256]{3,2,1,0:T(8,128)(2,1)S(1)}, u32[]{:S(2)}, u32[]{:S(2)}) collective-permute-start(bf16[1,2,256,256]{3,2,1,0:T(8,128)(2,1)S(1)} %fusion.8), channel_id=1, source_target_pairs={{0,2},{1,3},{2,0},{3,1},{4,6},{5,7},{6,4},{7,5},{8,10},{9,11},{10,... | collective-permute-start | bytes 786440 | tf_op jit(solution)/shard_map/ppermute | solution.py:13
  55.8 11.8 %collective-permute-start.11 = (bf16[1,2,256,256]{3,2,1,0:T(8,128)(2,1)S(1)}, bf16[1,2,256,256]{3,2,1,0:T(8,128)(2,1)S(1)}, u32[]{:S(2)}, u32[]{:S(2)}) collective-permute-start(bf16[1,2,256,256]{3,2,1,0:T(8,128)(2,1)S(1)} %fusion.9), channel_id=1, source_target_pairs={{0,2},{1,3},{2,0},{3,1},{4,6},{5,7},{6,4},{7,5},{8,10},{9,11},{10,... | collective-permute-start | bytes 786440 | tf_op jit(solution)/shard_map/ppermute | solution.py:13

commit v20 on v13

--- a/solution.py
+++ b/solution.py
@@ -81,8 +81,8 @@
         kpoint_count, orb_count - NV, mu_cols
     )
 
-    valence = gather_axis(jnp.take(held_valence, wanted, axis=0), "col")
-    conduction = jnp.take(held_conduction, wanted, axis=0).astype(jnp.float32)
+    valence = gather_axis(jnp.take(held_valence, wanted, axis=0, mode="clip"), "col")
+    conduction = jnp.take(held_conduction, wanted, axis=0, mode="clip").astype(jnp.float32)
     rows_per_block = NC // col_count
     chunk = pair_count // PAIR_CHUNKS
     starts = list(range(0, pair_count, chunk))

time: 63 us -> 62 us (0.984)
  other arithmetic: 11.2 us -> 9.45 us
  waiting for transfers between devices: 18.2 us -> 19.2 us
    ppermute x12, waiting for transfers between devices: 18.2 us -> 19.2 us  [swap(): return lax.ppermute(x, axis, [(i, i ^ bit) for i in range(size)])]
    select_n x2 -> x0, other arithmetic: 0.82 us -> none  [body(): valence = gather_axis(jnp.take(held_valence, wanted, axis=0), 'col')]
    and x1 -> x0, other arithmetic: 0.73 us -> none  [body(): valence = gather_axis(jnp.take(held_valence, wanted, axis=0), 'col')]
  transfers between devices with their start and end apart: 12 -> 12, of which waited for: 8 -> 8; matrix products, arithmetic and copies ran while one was open for 28% -> 26% of each run, Pallas kernels for 0% -> 0%
where the time goes in v20:
time: 62 us; the launch traced here: 61.7 us
  waiting for transfers between devices  19.2 us (31%)
  starting transfers between devices  16.3 us (26%)
  matrix products  13.1 us (21%)
  other arithmetic  9.45 us (15%)
  local copies, waits for them, and re-layouts  3.32 us (5%)
    ppermute x12, waiting for transfers between devices, swap(): return lax.ppermute(x, axis, [(i, i ^ bit) for i in range(size)])  19.2 us
    ppermute x12, starting transfers between devices, swap(): return lax.ppermute(x, axis, [(i, i ^ bit) for i in range(size)])  16.3 us
    dot_general x2, matrix products, screened_of(): lax.dot_general(val_pairs, screen, (((0, 2), (0, 1)), ((), ())), preferre...  9.3 us
    dot_general x8, matrix products, own_block(): jnp.einsum('pan,pbn->pab', screened, cond_pairs, preferred_element_type=j...  3.75 us
    convert_element_type x1, other arithmetic, cond_block(): (rows[:, :, None, :] * cond_b[:, None, :, :]).astype(jnp.bfloat16)  3.09 us
    convert_element_type x2, other arithmetic, screened_of(): (valence_a[:, :, :, None, :] * valence_b[:, :, None, :, :]).astype(jnp.bf...  2.78 us
    another operation x2, local copies, waits for them, and re-layouts, gather_axis(): cur = jnp.where(low, jnp.stack([cur, got], 1), jnp.stack([got, cur], 1))  1.61 us
  transfers between devices with their start and end apart: 12, of which 8 were waited for; matrix products, arithmetic and copies ran while one was open for 26% of the time, Pallas kernels for 0%

profile of v20, /device:TPU:0, one launch (start us, length us, event | category | flops | bytes accessed | tf_op | source)
XLA Modules:
  0.0 61.7 jit_solution(11896637537826503424)
XLA Ops:
  0.0 0.8 %slice_bitcast_fusion.7 = (bf16[1,1,1,16,1024]{4,3,2,1,0:T(8,128)(2,1)S(1)}, bf16[1,1,16,1024]{3,2,0,1:T(8,128)(2,1)S(1)}) fusion(bf16[1,48,1024]{2,1,0:T(8,128)(2,1)} %param.3), kind=kLoop, calls=%fused_computation.57 | loop fusion | bytes 98304 | tf_op jit(solution)/shard_map/stack | solution.py:24
  0.8 4.0 %collective-permute-start = (bf16[1,1,16,1024]{3,2,0,1:T(8,128)(2,1)S(1)}, bf16[1,1,16,1024]{3,2,0,1:T(8,128)(2,1)S(1)}, u32[]{:S(2)}, u32[]{:S(2)}) collective-permute-start(bf16[1,1,16,1024]{3,2,0,1:T(8,128)(2,1)S(1)} %get-tuple-element.50), channel_id=1, source_target_pairs={{0,16},{4,20},{8,24},{12,28},{16,0},{20,4},{24,8},{28,12},{1,17},{... | collective-permute-start | bytes 98312 | tf_op jit(solution)/shard_map/ppermute | solution.py:13
  4.8 0.8 %slice_bitcast_fusion.5 = (bf16[1,1,1,32,1024]{4,3,2,1,0:T(8,128)(2,1)S(1)}, bf16[1,1,32,1024]{3,2,0,1:T(8,128)(2,1)S(1)}) fusion(bf16[1,48,1024]{2,1,0:T(8,128)(2,1)} %param.3), kind=kLoop, calls=%fused_computation.55 | loop fusion | bytes 196608 | tf_op jit(solution)/shard_map/stack | solution.py:24
  5.7 0.7 %and_select_fusion = s32[4]{0:T(128)S(1)} fusion(s32[]{:T(128)S(6)} %axis_index.17, s32[1,4]{1,0:T(1,128)} %param.5), kind=kLoop, calls=%fused_computation.69 | loop fusion | flops 48 | bytes 36 | tf_op jit(solution)/shard_map/jit(remainder)/select_n | solution.py:75
  6.4 0.6 %collective-permute-done = bf16[1,1,16,1024]{3,2,0,1:T(8,128)(2,1)S(1)} collective-permute-done((bf16[1,1,16,1024]{3,2,0,1:T(8,128)(2,1)S(1)}, bf16[1,1,16,1024]{3,2,0,1:T(8,128)(2,1)S(1)}, u32[]{:S(2)}, u32[]{:S(2)}) %collective-permute-start) | collective-permute-done | bytes 32800 | tf_op jit(solution)/shard_map/ppermute | solution.py:13
  7.1 2.5 %collective-permute-start.1 = (bf16[2,1,16,1024]{3,2,0,1:T(8,128)(2,1)S(1)}, bf16[2,1,16,1024]{3,2,0,1:T(8,128)(2,1)S(1)}, u32[]{:S(2)}, u32[]{:S(2)}) collective-permute-start(bf16[2,1,16,1024]{3,2,0,1:T(8,128)(2,1)S(1)} %maximum_select_fusion.8), channel_id=1, source_target_pairs={{0,8},{4,12},{8,0},{12,4},{16,24},{20,28},{24,16},{28,20},{1,9},{5... | collective-permute-start | bytes 196616 | tf_op jit(solution)/shard_map/ppermute | solution.py:13
  9.5 1.6 %collective-permute-done.5 = bf16[1,1,32,1024]{3,2,0,1:T(8,128)(2,1)S(1)} collective-permute-done((bf16[1,1,32,1024]{3,2,0,1:T(8,128)(2,1)S(1)}, bf16[1,1,32,1024]{3,2,0,1:T(8,128)(2,1)S(1)}, u32[]{:S(2)}, u32[]{:S(2)}) %collective-permute-start.5) | collective-permute-done | bytes 65568 | tf_op jit(solution)/shard_map/ppermute | solution.py:13
  11.2 1.5 %collective-permute-start.6 = (bf16[2,1,32,1024]{3,2,0,1:T(8,128)(2,1)S(1)}, bf16[2,1,32,1024]{3,2,0,1:T(8,128)(2,1)S(1)}, u32[]{:S(2)}, u32[]{:S(2)}) collective-permute-start(bf16[2,1,32,1024]{3,2,0,1:T(8,128)(2,1)S(1)} %maximum_select_fusion.7), channel_id=1, source_target_pairs={{0,8},{4,12},{8,0},{12,4},{16,24},{20,28},{24,16},{28,20},{1,9},{5... | collective-permute-start | bytes 393224 | tf_op jit(solution)/shard_map/ppermute | solution.py:13
  12.8 1.6 %collective-permute-start.2 = (bf16[4,1,16,1024]{3,2,0,1:T(8,128)(2,1)S(1)}, bf16[4,1,16,1024]{3,2,0,1:T(8,128)(2,1)S(1)}, u32[]{:S(2)}, u32[]{:S(2)}) collective-permute-start(bf16[4,1,16,1024]{3,2,0,1:T(8,128)(2,1)S(1)} %bitcast.156), channel_id=1, source_target_pairs={{0,4},{4,0},{8,12},{12,8},{16,20},{20,16},{24,28},{28,24},{1,5},{5... | collective-permute-start | bytes 393224 | tf_op jit(solution)/shard_map/ppermute | solution.py:13
  14.4 1.9 %collective-permute-done.6 = bf16[2,1,32,1024]{3,2,0,1:T(8,128)(2,1)S(1)} collective-permute-done((bf16[2,1,32,1024]{3,2,0,1:T(8,128)(2,1)S(1)}, bf16[2,1,32,1024]{3,2,0,1:T(8,128)(2,1)S(1)}, u32[]{:S(2)}, u32[]{:S(2)}) %collective-permute-start.6) | collective-permute-done | bytes 131104 | tf_op jit(solution)/shard_map/ppermute | solution.py:13
  16.3 1.6 %collective-permute-start.7 = (bf16[4,1,32,1024]{3,2,0,1:T(8,128)(2,1)S(1)}, bf16[4,1,32,1024]{3,2,0,1:T(8,128)(2,1)S(1)}, u32[]{:S(2)}, u32[]{:S(2)}) collective-permute-start(bf16[4,1,32,1024]{3,2,0,1:T(8,128)(2,1)S(1)} %bitcast.152), channel_id=1, source_target_pairs={{0,4},{4,0},{8,12},{12,8},{16,20},{20,16},{24,28},{28,24},{1,5},{5... | collective-permute-start | bytes 786440 | tf_op jit(solution)/shard_map/ppermute | solution.py:13
  17.9 0.7 %pad_add_fusion = s32[8]{0:T(128)S(1)} fusion(s32[4]{0:T(128)S(1)} %and_select_fusion, s32[4]{0:T(128)} %bitcast.168), kind=kLoop, calls=%fused_computation.71 | loop fusion | flops 8 | bytes 64 | tf_op jit(solution)/shard_map/concatenate | solution.py:78
  18.6 0.5 collective-permute-done.2
  19.2 0.6 gather_fusion
  19.8 1.6 %collective-permute-start.3 = (bf16[1,8,16,1024]{3,2,1,0:T(8,128)(2,1)S(1)}, bf16[1,8,16,1024]{3,2,1,0:T(8,128)(2,1)S(1)}, u32[]{:S(2)}, u32[]{:S(2)}) collective-permute-start(bf16[1,8,16,1024]{3,2,1,0:T(8,128)(2,1)S(1)} %bitcast.147), channel_id=1, source_target_pairs={{0,2},{1,3},{2,0},{3,1},{4,6},{5,7},{6,4},{7,5},{8,10},{9,11},{10,... | collective-permute-start | bytes 786440 | tf_op jit(solution)/shard_map/ppermute | solution.py:13
  21.3 1.7 %collective-permute-done.7 = bf16[4,1,32,1024]{3,2,0,1:T(8,128)(2,1)S(1)} collective-permute-done((bf16[4,1,32,1024]{3,2,0,1:T(8,128)(2,1)S(1)}, bf16[4,1,32,1024]{3,2,0,1:T(8,128)(2,1)S(1)}, u32[]{:S(2)}, u32[]{:S(2)}) %collective-permute-start.7) | collective-permute-done | bytes 262176 | tf_op jit(solution)/shard_map/ppermute | solution.py:13
  23.1 0.6 gather_fusion.1
  23.9 2.3 %collective-permute-done.3 = bf16[1,8,16,1024]{3,2,1,0:T(8,128)(2,1)S(1)} collective-permute-done((bf16[1,8,16,1024]{3,2,1,0:T(8,128)(2,1)S(1)}, bf16[1,8,16,1024]{3,2,1,0:T(8,128)(2,1)S(1)}, u32[]{:S(2)}, u32[]{:S(2)}) %collective-permute-start.3) | collective-permute-done | bytes 262176 | tf_op jit(solution)/shard_map/ppermute | solution.py:13
  26.4 3.1 %multiply_convert_fusion.2 = (bf16[2,8,32,1024]{3,2,1,0:T(8,128)(2,1)S(1)}, bf16[2,8,32,1024]{3,2,1,0:T(8,128)(2,1)S(1)}, bf16[2,8,32,1024]{3,2,1,0:T(8,128)(2,1...) fusion(f32[2,8,1024]{2,1,0:T(8,128)S(1)} %get-tuple-element.35,, ...), kind=kLoop, calls=%fused_computation.6 | loop fusion | flops 8388608 | bytes 9437184 | tf_op jit(solution)/shard_map/convert_element_type | solution.py:96
  30.0 1.4 %multiply_convert_fusion.1 = bf16[4,2,16,16,1024]{4,3,2,1,0:T(8,128)(2,1)S(1)} fusion(f32[4,2,16,1024]{3,2,1,0:T(8,128)S(1)} %get-tuple-element.26, f32[4,2,16,1024]{3,2,1,0:T(8,128)S(1)} %get-tuple-element.23), kind=kLoop, calls=%fused_computation.3 | loop fusion | flops 4194304 | bytes 5242880 | tf_op jit(solution)/shard_map/convert_element_type | solution.py:58
  31.8 4.5 %bitcast_convert_fusion.1 = bf16[512,1024]{1,0:T(8,128)(2,1)S(1)} fusion(bf16[4,512,1024]{2,1,0:T(8,128)(2,1)S(1)} %bitcast.137, bf16[4,1024,1024]{2,1,0:T(8,128)(2,1)S(1)} %bitcast.166), kind=kOutput, calls=%fused_computation.5 | convolution fusion | flops 4295491584 | bytes 13631488 | tf_op jit(solution)/shard_map/dot_general | solution.py:61
  36.8 0.5 convolution_bitcast_fusion.3
  37.4 0.5 collective-permute-start.8
  37.9 1.4 %multiply_convert_fusion = bf16[4,2,16,16,1024]{4,3,2,1,0:T(8,128)(2,1)S(1)} fusion(f32[4,2,16,1024]{3,2,1,0:T(8,128)S(1)} %get-tuple-element.24, f32[4,2,16,1024]{3,2,1,0:T(8,128)S(1)} %get-tuple-element.25), kind=kLoop, calls=%fused_computation.2 | loop fusion | flops 4194304 | bytes 5242880 | tf_op jit(solution)/shard_map/convert_element_type | solution.py:58
  39.3 4.8 %bitcast_convert_fusion = bf16[512,1024]{1,0:T(8,128)(2,1)S(1)} fusion(bf16[4,512,1024]{2,1,0:T(8,128)(2,1)S(1)} %bitcast.138, bf16[4,1024,1024]{2,1,0:T(8,128)(2,1)S(1)} %bitcast.167), kind=kOutput, calls=%fused_computation.4 | convolution fusion | flops 4295491584 | bytes 13631488 | tf_op jit(solution)/shard_map/dot_general | solution.py:61
  45.7 0.5 fusion.8
  46.2 1.6 %collective-permute-start.9 = (bf16[1,2,256,256]{3,2,1,0:T(8,128)(2,1)S(1)}, bf16[1,2,256,256]{3,2,1,0:T(8,128)(2,1)S(1)}, u32[]{:S(2)}, u32[]{:S(2)}) collective-permute-start(bf16[1,2,256,256]{3,2,1,0:T(8,128)(2,1)S(1)} %fusion.8), channel_id=1, source_target_pairs={{0,2},{1,3},{2,0},{3,1},{4,6},{5,7},{6,4},{7,5},{8,10},{9,11},{10,... | collective-permute-start | bytes 786440 | tf_op jit(solution)/shard_map/ppermute | solution.py:13
  48.2 0.5 fusion.9
  48.7 1.2 %collective-permute-start.11 = (bf16[1,2,256,256]{3,2,1,0:T(8,128)(2,1)S(1)}, bf16[1,2,256,256]{3,2,1,0:T(8,128)(2,1)S(1)}, u32[]{:S(2)}, u32[]{:S(2)}) collective-permute-start(bf16[1,2,256,256]{3,2,1,0:T(8,128)(2,1)S(1)} %fusion.9), channel_id=1, source_target_pairs={{0,2},{1,3},{2,0},{3,1},{4,6},{5,7},{6,4},{7,5},{8,10},{9,11},{10,... | collective-permute-start | bytes 786440 | tf_op jit(solution)/shard_map/ppermute | solution.py:13
  49.9 5.5 %collective-permute-done.9 = bf16[1,2,256,256]{3,2,1,0:T(8,128)(2,1)S(1)} collective-permute-done((bf16[1,2,256,256]{3,2,1,0:T(8,128)(2,1)S(1)}, bf16[1,2,256,256]{3,2,1,0:T(8,128)(2,1)S(1)}, u32[]{:S(2)}, u32[]{:S(2)}) %collective-permute-start.9) | collective-permute-done | bytes 262176 | tf_op jit(solution)/shard_map/ppermute | solution.py:13
  55.5 5.1 %collective-permute-done.11 = bf16[1,2,256,256]{3,2,1,0:T(8,128)(2,1)S(1)} collective-permute-done((bf16[1,2,256,256]{3,2,1,0:T(8,128)(2,1)S(1)}, bf16[1,2,256,256]{3,2,1,0:T(8,128)(2,1)S(1)}, u32[]{:S(2)}, u32[]{:S(2)}) %collective-permute-start.11) | collective-permute-done | bytes 262176 | tf_op jit(solution)/shard_map/ppermute | solution.py:13
  60.7 1.0 %maximum_bitcast_fusion = f32[1,4,256,256]{3,2,1,0:T(8,128)} fusion(f32[2,256,256]{2,1,0:T(8,128)S(1)} %fusion.3, f32[2,256,256]{2,1,0:T(8,128)S(1)} %fusion.7), kind=kLoop, calls=%fused_computation.21 | loop fusion | flops 262144 | bytes 2097152 | tf_op jit(solution)/shard_map/broadcast_in_dim | solution.py:126
  (39 shorter events, 4.3 us)
Async XLA Ops:
  0.8 6.3 %collective-permute-start = (bf16[1,1,16,1024]{3,2,0,1:T(8,128)(2,1)S(1)}, bf16[1,1,16,1024]{3,2,0,1:T(8,128)(2,1)S(1)}, u32[]{:S(2)}, u32[]{:S(2)}) collective-permute-start(bf16[1,1,16,1024]{3,2,0,1:T(8,128)(2,1)S(1)} %get-tuple-element.50), channel_id=1, source_target_pairs={{0,16},{4,20},{8,24},{12,28},{16,0},{20,4},{24,8},{28,12},{1,17},{... | collective-permute-start | bytes 98312 | tf_op jit(solution)/shard_map/ppermute | solution.py:13
  5.7 5.5 %collective-permute-start.5 = (bf16[1,1,32,1024]{3,2,0,1:T(8,128)(2,1)S(1)}, bf16[1,1,32,1024]{3,2,0,1:T(8,128)(2,1)S(1)}, u32[]{:S(2)}, u32[]{:S(2)}) collective-permute-start(bf16[1,1,32,1024]{3,2,0,1:T(8,128)(2,1)S(1)} %get-tuple-element.48), channel_id=1, source_target_pairs={{0,16},{4,20},{8,24},{12,28},{16,0},{20,4},{24,8},{28,12},{1,17},{... | collective-permute-start | bytes 196616 | tf_op jit(solution)/shard_map/ppermute | solution.py:13
  7.1 5.7 %collective-permute-start.1 = (bf16[2,1,16,1024]{3,2,0,1:T(8,128)(2,1)S(1)}, bf16[2,1,16,1024]{3,2,0,1:T(8,128)(2,1)S(1)}, u32[]{:S(2)}, u32[]{:S(2)}) collective-permute-start(bf16[2,1,16,1024]{3,2,0,1:T(8,128)(2,1)S(1)} %maximum_select_fusion.8), channel_id=1, source_target_pairs={{0,8},{4,12},{8,0},{12,4},{16,24},{20,28},{24,16},{28,20},{1,9},{5... | collective-permute-start | bytes 196616 | tf_op jit(solution)/shard_map/ppermute | solution.py:13
  11.2 5.0 %collective-permute-start.6 = (bf16[2,1,32,1024]{3,2,0,1:T(8,128)(2,1)S(1)}, bf16[2,1,32,1024]{3,2,0,1:T(8,128)(2,1)S(1)}, u32[]{:S(2)}, u32[]{:S(2)}) collective-permute-start(bf16[2,1,32,1024]{3,2,0,1:T(8,128)(2,1)S(1)} %maximum_select_fusion.7), channel_id=1, source_target_pairs={{0,8},{4,12},{8,0},{12,4},{16,24},{20,28},{24,16},{28,20},{1,9},{5... | collective-permute-start | bytes 393224 | tf_op jit(solution)/shard_map/ppermute | solution.py:13
  12.8 6.4 %collective-permute-start.2 = (bf16[4,1,16,1024]{3,2,0,1:T(8,128)(2,1)S(1)}, bf16[4,1,16,1024]{3,2,0,1:T(8,128)(2,1)S(1)}, u32[]{:S(2)}, u32[]{:S(2)}) collective-permute-start(bf16[4,1,16,1024]{3,2,0,1:T(8,128)(2,1)S(1)} %bitcast.156), channel_id=1, source_target_pairs={{0,4},{4,0},{8,12},{12,8},{16,20},{20,16},{24,28},{28,24},{1,5},{5... | collective-permute-start | bytes 393224 | tf_op jit(solution)/shard_map/ppermute | solution.py:13
  16.3 6.7 %collective-permute-start.7 = (bf16[4,1,32,1024]{3,2,0,1:T(8,128)(2,1)S(1)}, bf16[4,1,32,1024]{3,2,0,1:T(8,128)(2,1)S(1)}, u32[]{:S(2)}, u32[]{:S(2)}) collective-permute-start(bf16[4,1,32,1024]{3,2,0,1:T(8,128)(2,1)S(1)} %bitcast.152), channel_id=1, source_target_pairs={{0,4},{4,0},{8,12},{12,8},{16,20},{20,16},{24,28},{28,24},{1,5},{5... | collective-permute-start | bytes 786440 | tf_op jit(solution)/shard_map/ppermute | solution.py:13
  19.8 6.4 %collective-permute-start.3 = (bf16[1,8,16,1024]{3,2,1,0:T(8,128)(2,1)S(1)}, bf16[1,8,16,1024]{3,2,1,0:T(8,128)(2,1)S(1)}, u32[]{:S(2)}, u32[]{:S(2)}) collective-permute-start(bf16[1,8,16,1024]{3,2,1,0:T(8,128)(2,1)S(1)} %bitcast.147), channel_id=1, source_target_pairs={{0,2},{1,3},{2,0},{3,1},{4,6},{5,7},{6,4},{7,5},{8,10},{9,11},{10,... | collective-permute-start | bytes 786440 | tf_op jit(solution)/shard_map/ppermute | solution.py:13
  26.3 3.3 %collective-permute-start.4 = (bf16[2,8,16,1024]{3,2,1,0:T(8,128)(2,1)S(1)}, bf16[2,8,16,1024]{3,2,1,0:T(8,128)(2,1)S(1)}, u32[]{:S(2)}, u32[]{:S(2)}) collective-permute-start(bf16[2,8,16,1024]{3,2,1,0:T(8,128)(2,1)S(1)} %maximum_select_fusion.2), channel_id=1, source_target_pairs={{0,1},{1,0},{2,3},{3,2},{4,5},{5,4},{6,7},{7,6},{8,9},{9,8},{10,11... | collective-permute-start | bytes 1572872 | tf_op jit(solution)/shard_map/ppermute | solution.py:13
  26.4 5.0 %slice-start = ((s8[8388608]{0:T(1024)(128)(4,1)}), s8[4194304]{0:T(1024)(128)(4,1)S(1)}, s32[]{:S(2)}) async-start(s8[8388608]{0:T(1024)(128)(4,1)} %bitcast.164), calls=%async_computation | async-start | bytes 8388608
  29.6 2.2 %slice-start.1 = ((s8[8388608]{0:T(1024)(128)(4,1)}), s8[4194304]{0:T(1024)(128)(4,1)S(1)}, s32[]{:S(2)}) async-start(s8[8388608]{0:T(1024)(128)(4,1)} %bitcast.164), calls=%async_computation.1 | async-start | bytes 8388608
  37.4 8.3 %collective-permute-start.8 = (f32[2,2,256,256]{3,2,1,0:T(8,128)S(1)}, f32[2,2,256,256]{3,2,1,0:T(8,128)S(1)}, u32[]{:S(2)}, u32[]{:S(2)}) collective-permute-start(f32[2,2,256,256]{3,2,1,0:T(8,128)S(1)} %pad_maximum_fusion), channel_id=1, source_target_pairs={{0,1},{1,0},{2,3},{3,2},{4,5},{5,4},{6,7},{7,6},{8,9},{9,8},{10,11... | collective-permute-start | bytes 3145736 | tf_op jit(solution)/shard_map/ppermute | solution.py:13
  45.1 3.1 %collective-permute-start.10 = (f32[2,2,256,256]{3,2,1,0:T(8,128)S(1)}, f32[2,2,256,256]{3,2,1,0:T(8,128)S(1)}, u32[]{:S(2)}, u32[]{:S(2)}) collective-permute-start(f32[2,2,256,256]{3,2,1,0:T(8,128)S(1)} %pad_maximum_fusion.1), channel_id=1, source_target_pairs={{0,1},{1,0},{2,3},{3,2},{4,5},{5,4},{6,7},{7,6},{8,9},{9,8},{10,11... | collective-permute-start | bytes 3145736 | tf_op jit(solution)/shard_map/ppermute | solution.py:13
  46.2 9.2 %collective-permute-start.9 = (bf16[1,2,256,256]{3,2,1,0:T(8,128)(2,1)S(1)}, bf16[1,2,256,256]{3,2,1,0:T(8,128)(2,1)S(1)}, u32[]{:S(2)}, u32[]{:S(2)}) collective-permute-start(bf16[1,2,256,256]{3,2,1,0:T(8,128)(2,1)S(1)} %fusion.8), channel_id=1, source_target_pairs={{0,2},{1,3},{2,0},{3,1},{4,6},{5,7},{6,4},{7,5},{8,10},{9,11},{10,... | collective-permute-start | bytes 786440 | tf_op jit(solution)/shard_map/ppermute | solution.py:13
  48.7 11.9 %collective-permute-start.11 = (bf16[1,2,256,256]{3,2,1,0:T(8,128)(2,1)S(1)}, bf16[1,2,256,256]{3,2,1,0:T(8,128)(2,1)S(1)}, u32[]{:S(2)}, u32[]{:S(2)}) collective-permute-start(bf16[1,2,256,256]{3,2,1,0:T(8,128)(2,1)S(1)} %fusion.9), channel_id=1, source_target_pairs={{0,2},{1,3},{2,0},{3,1},{4,6},{5,7},{6,4},{7,5},{8,10},{9,11},{10,... | collective-permute-start | bytes 786440 | tf_op jit(solution)/shard_map/ppermute | solution.py:13

commit v21 on v20

--- a/solution.py
+++ b/solution.py
@@ -6,6 +6,17 @@
 NV = 16
 NC = 32
 PAIR_CHUNKS = 2
+
+
+def gather_axis_xor(mine, axis):
+    count = lax.axis_size(axis)
+    cur = mine[None]
+    bit = count // 2
+    while bit >= 1:
+        got = swap(cur, axis, bit)
+        cur = jnp.stack([cur, got], 1).reshape((-1,) + mine.shape)
+        bit //= 2
+    return cur
 
 
 def swap(x, axis, bit):
@@ -76,8 +87,9 @@
     pair_count = kpoint_a.shape[0]
 
     wanted = jnp.concatenate([kpoint_a, kpoint_b])
-    held_valence = gather_axis(orbitals[:, :NV, :], "pb").reshape(kpoint_count, NV, mu_cols)
-    held_conduction = gather_axis(orbitals[:, NV:, :], "pb").reshape(
+    wanted = ((wanted // k_dev) ^ group_index) * k_dev + wanted % k_dev
+    held_valence = gather_axis_xor(orbitals[:, :NV, :], "pb").reshape(kpoint_count, NV, mu_cols)
+    held_conduction = gather_axis_xor(orbitals[:, NV:, :], "pb").reshape(
         kpoint_count, orb_count - NV, mu_cols
     )
 

time: 62 us -> 62.5 us (level)
  waiting for transfers between devices: 19.2 us -> 20 us
    ppermute x12, waiting for transfers between devices: 19.2 us -> 20 us  [swap(): return lax.ppermute(x, axis, [(i, i ^ bit) for i in range(size)])]
    xor x0 -> x1, other arithmetic: none -> 0.73 us  [body(): wanted = (wanted // k_dev ^ group_index) * k_dev + wanted % k_dev]
    select_n x1 -> x0, other arithmetic: 0.67 us -> none  [body(): kpoint_b = (kpoint_a - group_index) % kpoint_count]
    another operation x2 -> x4, local copies, waits for them, and re-layouts: 1.61 us -> 1.66 us  [gather_axis_xor(): cur = jnp.stack([cur, got], 1).reshape((-1,) + mine.shape)]
where the time goes in v21:
time: 62.5 us; the launch traced here: 62.2 us
  waiting for transfers between devices  20 us (32%)
  starting transfers between devices  16.1 us (26%)
  matrix products  13.1 us (21%)
  other arithmetic  9.4 us (15%)
  local copies, waits for them, and re-layouts  3.31 us (5%)
    ppermute x12, waiting for transfers between devices, swap(): return lax.ppermute(x, axis, [(i, i ^ bit) for i in range(size)])  20 us
    ppermute x12, starting transfers between devices, swap(): return lax.ppermute(x, axis, [(i, i ^ bit) for i in range(size)])  16.1 us
    dot_general x2, matrix products, screened_of(): lax.dot_general(val_pairs, screen, (((0, 2), (0, 1)), ((), ())), preferre...  9.3 us
    dot_general x8, matrix products, own_block(): jnp.einsum('pan,pbn->pab', screened, cond_pairs, preferred_element_type=j...  3.75 us
    convert_element_type x1, other arithmetic, cond_block(): (rows[:, :, None, :] * cond_b[:, None, :, :]).astype(jnp.bfloat16)  3.09 us
    convert_element_type x2, other arithmetic, screened_of(): (valence_a[:, :, :, None, :] * valence_b[:, :, None, :, :]).astype(jnp.bf...  2.78 us
    another operation x4, local copies, waits for them, and re-layouts, gather_axis_xor(): cur = jnp.stack([cur, got], 1).reshape((-1,) + mine.shape)  1.66 us
  transfers between devices with their start and end apart: 12, of which 8 were waited for; matrix products, arithmetic and copies ran while one was open for 26% of the time, Pallas kernels for 0%

profile of v21, /device:TPU:0, one launch (start us, length us, event | category | flops | bytes accessed | tf_op | source)
XLA Modules:
  0.0 62.2 jit_solution(2289294953379363781)
XLA Ops:
  0.0 0.8 %slice_bitcast_fusion.7 = (bf16[1,1,1,16,1024]{4,3,1,2,0:T(8,128)(2,1)S(1)}, bf16[1,1,16,1024]{3,2,1,0:T(8,128)(2,1)S(1)}) fusion(bf16[1,48,1024]{2,1,0:T(8,128)(2,1)} %param.3), kind=kLoop, calls=%fused_computation.55 | loop fusion | bytes 98304 | tf_op jit(solution)/shard_map/stack;broadcast_in_dim | solution.py:17
  0.8 4.0 %collective-permute-start = (bf16[1,1,16,1024]{3,2,1,0:T(8,128)(2,1)S(1)}, bf16[1,1,16,1024]{3,2,1,0:T(8,128)(2,1)S(1)}, u32[]{:S(2)}, u32[]{:S(2)}) collective-permute-start(bf16[1,1,16,1024]{3,2,1,0:T(8,128)(2,1)S(1)} %get-tuple-element.52), channel_id=1, source_target_pairs={{0,16},{4,20},{8,24},{12,28},{16,0},{20,4},{24,8},{28,12},{1,17},{... | collective-permute-start | bytes 98312 | tf_op jit(solution)/shard_map/ppermute | solution.py:24
  4.8 0.8 %slice_bitcast_fusion.5 = (bf16[1,1,1,32,1024]{4,3,1,2,0:T(8,128)(2,1)S(1)}, bf16[1,1,32,1024]{3,2,1,0:T(8,128)(2,1)S(1)}) fusion(bf16[1,48,1024]{2,1,0:T(8,128)(2,1)} %param.3), kind=kLoop, calls=%fused_computation.51 | loop fusion | bytes 196608 | tf_op jit(solution)/shard_map/stack;broadcast_in_dim | solution.py:17
  5.7 1.3 %collective-permute-done = bf16[1,1,16,1024]{3,2,1,0:T(8,128)(2,1)S(1)} collective-permute-done((bf16[1,1,16,1024]{3,2,1,0:T(8,128)(2,1)S(1)}, bf16[1,1,16,1024]{3,2,1,0:T(8,128)(2,1)S(1)}, u32[]{:S(2)}, u32[]{:S(2)}) %collective-permute-start) | collective-permute-done | bytes 32800 | tf_op jit(solution)/shard_map/ppermute | solution.py:24
  7.1 2.5 %collective-permute-start.1 = (bf16[2,1,16,1024]{3,2,0,1:T(8,128)(2,1)S(1)}, bf16[2,1,16,1024]{3,2,0,1:T(8,128)(2,1)S(1)}, u32[]{:S(2)}, u32[]{:S(2)}) collective-permute-start(bf16[2,1,16,1024]{3,2,0,1:T(8,128)(2,1)S(1)} %get-tuple-element.54), channel_id=1, source_target_pairs={{0,8},{4,12},{8,0},{12,4},{16,24},{20,28},{24,16},{28,20},{1,9},{5... | collective-permute-start | bytes 196616 | tf_op jit(solution)/shard_map/ppermute | solution.py:24
  9.5 1.7 %collective-permute-done.5 = bf16[1,1,32,1024]{3,2,1,0:T(8,128)(2,1)S(1)} collective-permute-done((bf16[1,1,32,1024]{3,2,1,0:T(8,128)(2,1)S(1)}, bf16[1,1,32,1024]{3,2,1,0:T(8,128)(2,1)S(1)}, u32[]{:S(2)}, u32[]{:S(2)}) %collective-permute-start.5) | collective-permute-done | bytes 65568 | tf_op jit(solution)/shard_map/ppermute | solution.py:24
  11.2 1.3 %collective-permute-start.6 = (bf16[2,1,32,1024]{3,2,0,1:T(8,128)(2,1)S(1)}, bf16[2,1,32,1024]{3,2,0,1:T(8,128)(2,1)S(1)}, u32[]{:S(2)}, u32[]{:S(2)}) collective-permute-start(bf16[2,1,32,1024]{3,2,0,1:T(8,128)(2,1)S(1)} %get-tuple-element.48), channel_id=1, source_target_pairs={{0,8},{4,12},{8,0},{12,4},{16,24},{20,28},{24,16},{28,20},{1,9},{5... | collective-permute-start | bytes 393224 | tf_op jit(solution)/shard_map/ppermute | solution.py:24
  12.5 0.7 %fusion.14 = s32[4,1]{0,1:T(1,128)S(1)} fusion(s32[1,4]{1,0:T(1,128)} %param.5, s32[]{:T(128)S(6)} %axis_index.29), kind=kLoop, calls=%fused_computation.68 | loop fusion | flops 48 | bytes 36 | tf_op jit(solution)/shard_map/concatenate | solution.py:89
  13.2 1.6 %collective-permute-start.2 = (bf16[4,1,16,1024]{3,2,0,1:T(8,128)(2,1)S(1)}, bf16[4,1,16,1024]{3,2,0,1:T(8,128)(2,1)S(1)}, u32[]{:S(2)}, u32[]{:S(2)}) collective-permute-start(bf16[4,1,16,1024]{3,2,0,1:T(8,128)(2,1)S(1)} %bitcast.161), channel_id=1, source_target_pairs={{0,4},{4,0},{8,12},{12,8},{16,20},{20,16},{24,28},{28,24},{1,5},{5... | collective-permute-start | bytes 393224 | tf_op jit(solution)/shard_map/ppermute | solution.py:24
  14.8 1.4 %collective-permute-done.6 = bf16[2,1,32,1024]{3,2,0,1:T(8,128)(2,1)S(1)} collective-permute-done((bf16[2,1,32,1024]{3,2,0,1:T(8,128)(2,1)S(1)}, bf16[2,1,32,1024]{3,2,0,1:T(8,128)(2,1)S(1)}, u32[]{:S(2)}, u32[]{:S(2)}) %collective-permute-start.6) | collective-permute-done | bytes 131104 | tf_op jit(solution)/shard_map/ppermute | solution.py:24
  16.3 1.6 %collective-permute-start.7 = (bf16[4,1,32,1024]{3,2,0,1:T(8,128)(2,1)S(1)}, bf16[4,1,32,1024]{3,2,0,1:T(8,128)(2,1)S(1)}, u32[]{:S(2)}, u32[]{:S(2)}) collective-permute-start(bf16[4,1,32,1024]{3,2,0,1:T(8,128)(2,1)S(1)} %bitcast.157), channel_id=1, source_target_pairs={{0,4},{4,0},{8,12},{12,8},{16,20},{20,16},{24,28},{28,24},{1,5},{5... | collective-permute-start | bytes 786440 | tf_op jit(solution)/shard_map/ppermute | solution.py:24
  17.9 0.7 %fusion.16 = s32[8]{0:T(128)S(1)} fusion(s32[4,1]{0,1:T(1,128)S(1)} %fusion.14, s32[4,1]{0,1:T(1,128)} %bitcast.169, s32[]{:T(128)S(6)} %axis_index.29), kind=kLoop, calls=%fused_computation.71 | loop fusion | flops 16 | bytes 68 | tf_op jit(solution)/shard_map/xor | solution.py:90
  18.6 1.0 %collective-permute-done.2 = bf16[4,1,16,1024]{3,2,0,1:T(8,128)(2,1)S(1)} collective-permute-done((bf16[4,1,16,1024]{3,2,0,1:T(8,128)(2,1)S(1)}, bf16[4,1,16,1024]{3,2,0,1:T(8,128)(2,1)S(1)}, u32[]{:S(2)}, u32[]{:S(2)}) %collective-permute-start.2) | collective-permute-done | bytes 131104 | tf_op jit(solution)/shard_map/ppermute | solution.py:24
  19.7 0.6 gather_fusion
  20.3 1.6 %collective-permute-start.3 = (bf16[1,8,16,1024]{3,2,1,0:T(8,128)(2,1)S(1)}, bf16[1,8,16,1024]{3,2,1,0:T(8,128)(2,1)S(1)}, u32[]{:S(2)}, u32[]{:S(2)}) collective-permute-start(bf16[1,8,16,1024]{3,2,1,0:T(8,128)(2,1)S(1)} %bitcast.152), channel_id=1, source_target_pairs={{0,2},{1,3},{2,0},{3,1},{4,6},{5,7},{6,4},{7,5},{8,10},{9,11},{10,... | collective-permute-start | bytes 786440 | tf_op jit(solution)/shard_map/ppermute | solution.py:24
  21.8 1.2 %collective-permute-done.7 = bf16[4,1,32,1024]{3,2,0,1:T(8,128)(2,1)S(1)} collective-permute-done((bf16[4,1,32,1024]{3,2,0,1:T(8,128)(2,1)S(1)}, bf16[4,1,32,1024]{3,2,0,1:T(8,128)(2,1)S(1)}, u32[]{:S(2)}, u32[]{:S(2)}) %collective-permute-start.7) | collective-permute-done | bytes 262176 | tf_op jit(solution)/shard_map/ppermute | solution.py:24
  23.1 0.6 gather_fusion.1
  23.9 2.9 %collective-permute-done.3 = bf16[1,8,16,1024]{3,2,1,0:T(8,128)(2,1)S(1)} collective-permute-done((bf16[1,8,16,1024]{3,2,1,0:T(8,128)(2,1)S(1)}, bf16[1,8,16,1024]{3,2,1,0:T(8,128)(2,1)S(1)}, u32[]{:S(2)}, u32[]{:S(2)}) %collective-permute-start.3) | collective-permute-done | bytes 262176 | tf_op jit(solution)/shard_map/ppermute | solution.py:24
  26.9 3.1 %multiply_convert_fusion.2 = (bf16[2,8,32,1024]{3,2,1,0:T(8,128)(2,1)S(1)}, bf16[2,8,32,1024]{3,2,1,0:T(8,128)(2,1)S(1)}, bf16[2,8,32,1024]{3,2,1,0:T(8,128)(2,1...) fusion(f32[2,8,1024]{2,1,0:T(8,128)S(1)} %get-tuple-element.35,, ...), kind=kLoop, calls=%fused_computation.6 | loop fusion | flops 8388608 | bytes 9437184 | tf_op jit(solution)/shard_map/convert_element_type | solution.py:108
  30.5 1.4 %multiply_convert_fusion.1 = bf16[4,2,16,16,1024]{4,3,2,1,0:T(8,128)(2,1)S(1)} fusion(f32[4,2,16,1024]{3,2,1,0:T(8,128)S(1)} %get-tuple-element.26, f32[4,2,16,1024]{3,2,1,0:T(8,128)S(1)} %get-tuple-element.23), kind=kLoop, calls=%fused_computation.3 | loop fusion | flops 4194304 | bytes 5242880 | tf_op jit(solution)/shard_map/convert_element_type | solution.py:69
  32.3 4.5 %bitcast_convert_fusion.1 = bf16[512,1024]{1,0:T(8,128)(2,1)S(1)} fusion(bf16[4,512,1024]{2,1,0:T(8,128)(2,1)S(1)} %bitcast.142, bf16[4,1024,1024]{2,1,0:T(8,128)(2,1)S(1)} %bitcast.172), kind=kOutput, calls=%fused_computation.5 | convolution fusion | flops 4295491584 | bytes 13631488 | tf_op jit(solution)/shard_map/dot_general | solution.py:72
  37.3 0.5 convolution_bitcast_fusion.3
  37.9 0.5 collective-permute-start.8
  38.4 1.4 %multiply_convert_fusion = bf16[4,2,16,16,1024]{4,3,2,1,0:T(8,128)(2,1)S(1)} fusion(f32[4,2,16,1024]{3,2,1,0:T(8,128)S(1)} %get-tuple-element.24, f32[4,2,16,1024]{3,2,1,0:T(8,128)S(1)} %get-tuple-element.25), kind=kLoop, calls=%fused_computation.2 | loop fusion | flops 4194304 | bytes 5242880 | tf_op jit(solution)/shard_map/convert_element_type | solution.py:69
  39.8 4.8 %bitcast_convert_fusion = bf16[512,1024]{1,0:T(8,128)(2,1)S(1)} fusion(bf16[4,512,1024]{2,1,0:T(8,128)(2,1)S(1)} %bitcast.143, bf16[4,1024,1024]{2,1,0:T(8,128)(2,1)S(1)} %bitcast.173), kind=kOutput, calls=%fused_computation.4 | convolution fusion | flops 4295491584 | bytes 13631488 | tf_op jit(solution)/shard_map/dot_general | solution.py:72
  46.2 0.5 fusion.8
  46.7 1.6 %collective-permute-start.9 = (bf16[1,2,256,256]{3,2,1,0:T(8,128)(2,1)S(1)}, bf16[1,2,256,256]{3,2,1,0:T(8,128)(2,1)S(1)}, u32[]{:S(2)}, u32[]{:S(2)}) collective-permute-start(bf16[1,2,256,256]{3,2,1,0:T(8,128)(2,1)S(1)} %fusion.8), channel_id=1, source_target_pairs={{0,2},{1,3},{2,0},{3,1},{4,6},{5,7},{6,4},{7,5},{8,10},{9,11},{10,... | collective-permute-start | bytes 786440 | tf_op jit(solution)/shard_map/ppermute | solution.py:24
  48.7 0.5 fusion.9
  49.2 1.2 %collective-permute-start.11 = (bf16[1,2,256,256]{3,2,1,0:T(8,128)(2,1)S(1)}, bf16[1,2,256,256]{3,2,1,0:T(8,128)(2,1)S(1)}, u32[]{:S(2)}, u32[]{:S(2)}) collective-permute-start(bf16[1,2,256,256]{3,2,1,0:T(8,128)(2,1)S(1)} %fusion.9), channel_id=1, source_target_pairs={{0,2},{1,3},{2,0},{3,1},{4,6},{5,7},{6,4},{7,5},{8,10},{9,11},{10,... | collective-permute-start | bytes 786440 | tf_op jit(solution)/shard_map/ppermute | solution.py:24
  50.4 5.5 %collective-permute-done.9 = bf16[1,2,256,256]{3,2,1,0:T(8,128)(2,1)S(1)} collective-permute-done((bf16[1,2,256,256]{3,2,1,0:T(8,128)(2,1)S(1)}, bf16[1,2,256,256]{3,2,1,0:T(8,128)(2,1)S(1)}, u32[]{:S(2)}, u32[]{:S(2)}) %collective-permute-start.9) | collective-permute-done | bytes 262176 | tf_op jit(solution)/shard_map/ppermute | solution.py:24
  56.0 5.1 %collective-permute-done.11 = bf16[1,2,256,256]{3,2,1,0:T(8,128)(2,1)S(1)} collective-permute-done((bf16[1,2,256,256]{3,2,1,0:T(8,128)(2,1)S(1)}, bf16[1,2,256,256]{3,2,1,0:T(8,128)(2,1)S(1)}, u32[]{:S(2)}, u32[]{:S(2)}) %collective-permute-start.11) | collective-permute-done | bytes 262176 | tf_op jit(solution)/shard_map/ppermute | solution.py:24
  61.2 1.0 %maximum_bitcast_fusion = f32[1,4,256,256]{3,2,1,0:T(8,128)} fusion(f32[2,256,256]{2,1,0:T(8,128)S(1)} %fusion.3, f32[2,256,256]{2,1,0:T(8,128)S(1)} %fusion.7), kind=kLoop, calls=%fused_computation.21 | loop fusion | flops 262144 | bytes 2097152 | tf_op jit(solution)/shard_map/broadcast_in_dim | solution.py:138
  (37 shorter events, 4.2 us)
Async XLA Ops:
  0.8 6.3 %collective-permute-start = (bf16[1,1,16,1024]{3,2,1,0:T(8,128)(2,1)S(1)}, bf16[1,1,16,1024]{3,2,1,0:T(8,128)(2,1)S(1)}, u32[]{:S(2)}, u32[]{:S(2)}) collective-permute-start(bf16[1,1,16,1024]{3,2,1,0:T(8,128)(2,1)S(1)} %get-tuple-element.52), channel_id=1, source_target_pairs={{0,16},{4,20},{8,24},{12,28},{16,0},{20,4},{24,8},{28,12},{1,17},{... | collective-permute-start | bytes 98312 | tf_op jit(solution)/shard_map/ppermute | solution.py:24
  5.7 5.5 %collective-permute-start.5 = (bf16[1,1,32,1024]{3,2,1,0:T(8,128)(2,1)S(1)}, bf16[1,1,32,1024]{3,2,1,0:T(8,128)(2,1)S(1)}, u32[]{:S(2)}, u32[]{:S(2)}) collective-permute-start(bf16[1,1,32,1024]{3,2,1,0:T(8,128)(2,1)S(1)} %get-tuple-element.50), channel_id=1, source_target_pairs={{0,16},{4,20},{8,24},{12,28},{16,0},{20,4},{24,8},{28,12},{1,17},{... | collective-permute-start | bytes 196616 | tf_op jit(solution)/shard_map/ppermute | solution.py:24
  7.1 6.2 %collective-permute-start.1 = (bf16[2,1,16,1024]{3,2,0,1:T(8,128)(2,1)S(1)}, bf16[2,1,16,1024]{3,2,0,1:T(8,128)(2,1)S(1)}, u32[]{:S(2)}, u32[]{:S(2)}) collective-permute-start(bf16[2,1,16,1024]{3,2,0,1:T(8,128)(2,1)S(1)} %get-tuple-element.54), channel_id=1, source_target_pairs={{0,8},{4,12},{8,0},{12,4},{16,24},{20,28},{24,16},{28,20},{1,9},{5... | collective-permute-start | bytes 196616 | tf_op jit(solution)/shard_map/ppermute | solution.py:24
  11.2 5.0 %collective-permute-start.6 = (bf16[2,1,32,1024]{3,2,0,1:T(8,128)(2,1)S(1)}, bf16[2,1,32,1024]{3,2,0,1:T(8,128)(2,1)S(1)}, u32[]{:S(2)}, u32[]{:S(2)}) collective-permute-start(bf16[2,1,32,1024]{3,2,0,1:T(8,128)(2,1)S(1)} %get-tuple-element.48), channel_id=1, source_target_pairs={{0,8},{4,12},{8,0},{12,4},{16,24},{20,28},{24,16},{28,20},{1,9},{5... | collective-permute-start | bytes 393224 | tf_op jit(solution)/shard_map/ppermute | solution.py:24
  13.2 6.4 %collective-permute-start.2 = (bf16[4,1,16,1024]{3,2,0,1:T(8,128)(2,1)S(1)}, bf16[4,1,16,1024]{3,2,0,1:T(8,128)(2,1)S(1)}, u32[]{:S(2)}, u32[]{:S(2)}) collective-permute-start(bf16[4,1,16,1024]{3,2,0,1:T(8,128)(2,1)S(1)} %bitcast.161), channel_id=1, source_target_pairs={{0,4},{4,0},{8,12},{12,8},{16,20},{20,16},{24,28},{28,24},{1,5},{5... | collective-permute-start | bytes 393224 | tf_op jit(solution)/shard_map/ppermute | solution.py:24
  16.3 6.7 %collective-permute-start.7 = (bf16[4,1,32,1024]{3,2,0,1:T(8,128)(2,1)S(1)}, bf16[4,1,32,1024]{3,2,0,1:T(8,128)(2,1)S(1)}, u32[]{:S(2)}, u32[]{:S(2)}) collective-permute-start(bf16[4,1,32,1024]{3,2,0,1:T(8,128)(2,1)S(1)} %bitcast.157), channel_id=1, source_target_pairs={{0,4},{4,0},{8,12},{12,8},{16,20},{20,16},{24,28},{28,24},{1,5},{5... | collective-permute-start | bytes 786440 | tf_op jit(solution)/shard_map/ppermute | solution.py:24
  20.3 6.4 %collective-permute-start.3 = (bf16[1,8,16,1024]{3,2,1,0:T(8,128)(2,1)S(1)}, bf16[1,8,16,1024]{3,2,1,0:T(8,128)(2,1)S(1)}, u32[]{:S(2)}, u32[]{:S(2)}) collective-permute-start(bf16[1,8,16,1024]{3,2,1,0:T(8,128)(2,1)S(1)} %bitcast.152), channel_id=1, source_target_pairs={{0,2},{1,3},{2,0},{3,1},{4,6},{5,7},{6,4},{7,5},{8,10},{9,11},{10,... | collective-permute-start | bytes 786440 | tf_op jit(solution)/shard_map/ppermute | solution.py:24
  26.8 3.3 %collective-permute-start.4 = (bf16[2,8,16,1024]{3,2,1,0:T(8,128)(2,1)S(1)}, bf16[2,8,16,1024]{3,2,1,0:T(8,128)(2,1)S(1)}, u32[]{:S(2)}, u32[]{:S(2)}) collective-permute-start(bf16[2,8,16,1024]{3,2,1,0:T(8,128)(2,1)S(1)} %maximum_select_fusion.2), channel_id=1, source_target_pairs={{0,1},{1,0},{2,3},{3,2},{4,5},{5,4},{6,7},{7,6},{8,9},{9,8},{10,11... | collective-permute-start | bytes 1572872 | tf_op jit(solution)/shard_map/ppermute | solution.py:24
  26.9 5.0 %slice-start = ((s8[8388608]{0:T(1024)(128)(4,1)}), s8[4194304]{0:T(1024)(128)(4,1)S(1)}, s32[]{:S(2)}) async-start(s8[8388608]{0:T(1024)(128)(4,1)} %bitcast.170), calls=%async_computation | async-start | bytes 8388608
  30.1 2.2 %slice-start.1 = ((s8[8388608]{0:T(1024)(128)(4,1)}), s8[4194304]{0:T(1024)(128)(4,1)S(1)}, s32[]{:S(2)}) async-start(s8[8388608]{0:T(1024)(128)(4,1)} %bitcast.170), calls=%async_computation.1 | async-start | bytes 8388608
  37.9 8.3 %collective-permute-start.8 = (f32[2,2,256,256]{3,2,1,0:T(8,128)S(1)}, f32[2,2,256,256]{3,2,1,0:T(8,128)S(1)}, u32[]{:S(2)}, u32[]{:S(2)}) collective-permute-start(f32[2,2,256,256]{3,2,1,0:T(8,128)S(1)} %pad_maximum_fusion), channel_id=1, source_target_pairs={{0,1},{1,0},{2,3},{3,2},{4,5},{5,4},{6,7},{7,6},{8,9},{9,8},{10,11... | collective-permute-start | bytes 3145736 | tf_op jit(solution)/shard_map/ppermute | solution.py:24
  45.6 3.1 %collective-permute-start.10 = (f32[2,2,256,256]{3,2,1,0:T(8,128)S(1)}, f32[2,2,256,256]{3,2,1,0:T(8,128)S(1)}, u32[]{:S(2)}, u32[]{:S(2)}) collective-permute-start(f32[2,2,256,256]{3,2,1,0:T(8,128)S(1)} %pad_maximum_fusion.1), channel_id=1, source_target_pairs={{0,1},{1,0},{2,3},{3,2},{4,5},{5,4},{6,7},{7,6},{8,9},{9,8},{10,11... | collective-permute-start | bytes 3145736 | tf_op jit(solution)/shard_map/ppermute | solution.py:24
  46.7 9.2 %collective-permute-start.9 = (bf16[1,2,256,256]{3,2,1,0:T(8,128)(2,1)S(1)}, bf16[1,2,256,256]{3,2,1,0:T(8,128)(2,1)S(1)}, u32[]{:S(2)}, u32[]{:S(2)}) collective-permute-start(bf16[1,2,256,256]{3,2,1,0:T(8,128)(2,1)S(1)} %fusion.8), channel_id=1, source_target_pairs={{0,2},{1,3},{2,0},{3,1},{4,6},{5,7},{6,4},{7,5},{8,10},{9,11},{10,... | collective-permute-start | bytes 786440 | tf_op jit(solution)/shard_map/ppermute | solution.py:24
  49.2 11.9 %collective-permute-start.11 = (bf16[1,2,256,256]{3,2,1,0:T(8,128)(2,1)S(1)}, bf16[1,2,256,256]{3,2,1,0:T(8,128)(2,1)S(1)}, u32[]{:S(2)}, u32[]{:S(2)}) collective-permute-start(bf16[1,2,256,256]{3,2,1,0:T(8,128)(2,1)S(1)} %fusion.9), channel_id=1, source_target_pairs={{0,2},{1,3},{2,0},{3,1},{4,6},{5,7},{6,4},{7,5},{8,10},{9,11},{10,... | collective-permute-start | bytes 786440 | tf_op jit(solution)/shard_map/ppermute | solution.py:24

commit v22 on v20

--- a/solution.py
+++ b/solution.py
@@ -53,9 +53,7 @@
 
 def screened_of(valence_a, valence_b, screening):
     col_count, chunk, _, mu_cols = valence_a.shape
-    valence_a = valence_a.astype(jnp.float32)
-    valence_b = valence_b.astype(jnp.float32)
-    val_pairs = (valence_a[:, :, :, None, :] * valence_b[:, :, None, :, :]).astype(jnp.bfloat16)
+    val_pairs = valence_a[:, :, :, None, :] * valence_b[:, :, None, :, :]
     val_pairs = val_pairs.reshape(col_count, chunk * NV * NV, mu_cols)
     screen = screening.reshape(col_count, mu_cols, screening.shape[1])
     screened = lax.dot_general(

time: 62 us -> 61 us (0.984)
  other arithmetic: 9.45 us -> 7.05 us
  local copies, waits for them, and re-layouts: 3.32 us -> 4.52 us
    convert_element_type x3 -> x0, other arithmetic: 3.03 us -> none  [the longest x2 2.78 us: screened_of(): (valence_a[:, :, :, None, :] * valence_b[:, :, None, :, :]).astype(jnp.bf...]
    unnamed x4, local copies, waits for them, and re-layouts: 0.36 us -> 1.49 us
    mul x0 -> x2, other arithmetic: none -> 0.68 us  [screened_of(): val_pairs = valence_a[:, :, :, None, :] * valence_b[:, :, None, :, :]]
  transfers between devices with their start and end apart: 12 -> 12, of which waited for: 8 -> 8; matrix products, arithmetic and copies ran while one was open for 26% -> 25% of each run, Pallas kernels for 0% -> 0%
where the time goes in v22:
time: 61 us; the launch traced here: 60.7 us
  waiting for transfers between devices  19.4 us (32%)
  starting transfers between devices  16.2 us (27%)
  matrix products  13.3 us (22%)
  other arithmetic  7.05 us (12%)
  local copies, waits for them, and re-layouts  4.52 us (7%)
    ppermute x12, waiting for transfers between devices, swap(): return lax.ppermute(x, axis, [(i, i ^ bit) for i in range(size)])  19.4 us
    ppermute x12, starting transfers between devices, swap(): return lax.ppermute(x, axis, [(i, i ^ bit) for i in range(size)])  16.2 us
    dot_general x2, matrix products, screened_of(): lax.dot_general(val_pairs, screen, (((0, 2), (0, 1)), ((), ())), preferre...  9.18 us
    dot_general x8, matrix products, own_block(): jnp.einsum('pan,pbn->pab', screened, cond_pairs, preferred_element_type=j...  4.09 us
    convert_element_type x1, other arithmetic, cond_block(): (rows[:, :, None, :] * cond_b[:, None, :, :]).astype(jnp.bfloat16)  3.06 us
    another operation x2, local copies, waits for them, and re-layouts, gather_axis(): cur = jnp.where(low, jnp.stack([cur, got], 1), jnp.stack([got, cur], 1))  1.61 us
    unnamed x4, local copies, waits for them, and re-layouts  1.49 us
  transfers between devices with their start and end apart: 12, of which 8 were waited for; matrix products, arithmetic and copies ran while one was open for 25% of the time, Pallas kernels for 0%

profile of v22, /device:TPU:0, one launch (start us, length us, event | category | flops | bytes accessed | tf_op | source)
XLA Modules:
  0.0 60.7 jit_solution(16605889569497436168)
XLA Ops:
  0.0 0.8 %slice_bitcast_fusion.7 = (bf16[1,1,1,16,1024]{4,3,2,1,0:T(8,128)(2,1)S(1)}, bf16[1,1,16,1024]{3,2,0,1:T(8,128)(2,1)S(1)}) fusion(bf16[1,48,1024]{2,1,0:T(8,128)(2,1)} %param.3), kind=kLoop, calls=%fused_computation.53 | loop fusion | bytes 98304 | tf_op jit(solution)/shard_map/stack | solution.py:24
  0.8 4.0 %collective-permute-start = (bf16[1,1,16,1024]{3,2,0,1:T(8,128)(2,1)S(1)}, bf16[1,1,16,1024]{3,2,0,1:T(8,128)(2,1)S(1)}, u32[]{:S(2)}, u32[]{:S(2)}) collective-permute-start(bf16[1,1,16,1024]{3,2,0,1:T(8,128)(2,1)S(1)} %get-tuple-element.50), channel_id=1, source_target_pairs={{0,16},{4,20},{8,24},{12,28},{16,0},{20,4},{24,8},{28,12},{1,17},{... | collective-permute-start | bytes 98312 | tf_op jit(solution)/shard_map/ppermute | solution.py:13
  4.8 0.8 %slice_bitcast_fusion.5 = (bf16[1,1,1,32,1024]{4,3,2,1,0:T(8,128)(2,1)S(1)}, bf16[1,1,32,1024]{3,2,0,1:T(8,128)(2,1)S(1)}) fusion(bf16[1,48,1024]{2,1,0:T(8,128)(2,1)} %param.3), kind=kLoop, calls=%fused_computation.51 | loop fusion | bytes 196608 | tf_op jit(solution)/shard_map/stack | solution.py:24
  5.7 0.7 %and_select_fusion = s32[4]{0:T(128)S(1)} fusion(s32[]{:T(128)S(6)} %axis_index.17, s32[1,4]{1,0:T(1,128)} %param.5), kind=kLoop, calls=%fused_computation.65 | loop fusion | flops 48 | bytes 36 | tf_op jit(solution)/shard_map/jit(remainder)/select_n | solution.py:73
  6.4 0.6 %collective-permute-done = bf16[1,1,16,1024]{3,2,0,1:T(8,128)(2,1)S(1)} collective-permute-done((bf16[1,1,16,1024]{3,2,0,1:T(8,128)(2,1)S(1)}, bf16[1,1,16,1024]{3,2,0,1:T(8,128)(2,1)S(1)}, u32[]{:S(2)}, u32[]{:S(2)}) %collective-permute-start) | collective-permute-done | bytes 32800 | tf_op jit(solution)/shard_map/ppermute | solution.py:13
  7.1 2.5 %collective-permute-start.1 = (bf16[2,1,16,1024]{3,2,0,1:T(8,128)(2,1)S(1)}, bf16[2,1,16,1024]{3,2,0,1:T(8,128)(2,1)S(1)}, u32[]{:S(2)}, u32[]{:S(2)}) collective-permute-start(bf16[2,1,16,1024]{3,2,0,1:T(8,128)(2,1)S(1)} %maximum_select_fusion.8), channel_id=1, source_target_pairs={{0,8},{4,12},{8,0},{12,4},{16,24},{20,28},{24,16},{28,20},{1,9},{5... | collective-permute-start | bytes 196616 | tf_op jit(solution)/shard_map/ppermute | solution.py:13
  9.5 1.6 %collective-permute-done.5 = bf16[1,1,32,1024]{3,2,0,1:T(8,128)(2,1)S(1)} collective-permute-done((bf16[1,1,32,1024]{3,2,0,1:T(8,128)(2,1)S(1)}, bf16[1,1,32,1024]{3,2,0,1:T(8,128)(2,1)S(1)}, u32[]{:S(2)}, u32[]{:S(2)}) %collective-permute-start.5) | collective-permute-done | bytes 65568 | tf_op jit(solution)/shard_map/ppermute | solution.py:13
  11.2 1.5 %collective-permute-start.6 = (bf16[2,1,32,1024]{3,2,0,1:T(8,128)(2,1)S(1)}, bf16[2,1,32,1024]{3,2,0,1:T(8,128)(2,1)S(1)}, u32[]{:S(2)}, u32[]{:S(2)}) collective-permute-start(bf16[2,1,32,1024]{3,2,0,1:T(8,128)(2,1)S(1)} %maximum_select_fusion.7), channel_id=1, source_target_pairs={{0,8},{4,12},{8,0},{12,4},{16,24},{20,28},{24,16},{28,20},{1,9},{5... | collective-permute-start | bytes 393224 | tf_op jit(solution)/shard_map/ppermute | solution.py:13
  12.8 1.6 %collective-permute-start.2 = (bf16[4,1,16,1024]{3,2,0,1:T(8,128)(2,1)S(1)}, bf16[4,1,16,1024]{3,2,0,1:T(8,128)(2,1)S(1)}, u32[]{:S(2)}, u32[]{:S(2)}) collective-permute-start(bf16[4,1,16,1024]{3,2,0,1:T(8,128)(2,1)S(1)} %bitcast.156), channel_id=1, source_target_pairs={{0,4},{4,0},{8,12},{12,8},{16,20},{20,16},{24,28},{28,24},{1,5},{5... | collective-permute-start | bytes 393224 | tf_op jit(solution)/shard_map/ppermute | solution.py:13
  14.4 1.9 %collective-permute-done.6 = bf16[2,1,32,1024]{3,2,0,1:T(8,128)(2,1)S(1)} collective-permute-done((bf16[2,1,32,1024]{3,2,0,1:T(8,128)(2,1)S(1)}, bf16[2,1,32,1024]{3,2,0,1:T(8,128)(2,1)S(1)}, u32[]{:S(2)}, u32[]{:S(2)}) %collective-permute-start.6) | collective-permute-done | bytes 131104 | tf_op jit(solution)/shard_map/ppermute | solution.py:13
  16.3 1.6 %collective-permute-start.7 = (bf16[4,1,32,1024]{3,2,0,1:T(8,128)(2,1)S(1)}, bf16[4,1,32,1024]{3,2,0,1:T(8,128)(2,1)S(1)}, u32[]{:S(2)}, u32[]{:S(2)}) collective-permute-start(bf16[4,1,32,1024]{3,2,0,1:T(8,128)(2,1)S(1)} %bitcast.152), channel_id=1, source_target_pairs={{0,4},{4,0},{8,12},{12,8},{16,20},{20,16},{24,28},{28,24},{1,5},{5... | collective-permute-start | bytes 786440 | tf_op jit(solution)/shard_map/ppermute | solution.py:13
  17.9 0.7 %pad_add_fusion = s32[8]{0:T(128)S(1)} fusion(s32[4]{0:T(128)S(1)} %and_select_fusion, s32[4]{0:T(128)} %bitcast.168), kind=kLoop, calls=%fused_computation.67 | loop fusion | flops 8 | bytes 64 | tf_op jit(solution)/shard_map/concatenate | solution.py:76
  18.6 0.5 collective-permute-done.2
  19.2 0.6 gather_fusion
  19.8 1.6 %collective-permute-start.3 = (bf16[1,8,16,1024]{3,2,1,0:T(8,128)(2,1)S(1)}, bf16[1,8,16,1024]{3,2,1,0:T(8,128)(2,1)S(1)}, u32[]{:S(2)}, u32[]{:S(2)}) collective-permute-start(bf16[1,8,16,1024]{3,2,1,0:T(8,128)(2,1)S(1)} %bitcast.147), channel_id=1, source_target_pairs={{0,2},{1,3},{2,0},{3,1},{4,6},{5,7},{6,4},{7,5},{8,10},{9,11},{10,... | collective-permute-start | bytes 786440 | tf_op jit(solution)/shard_map/ppermute | solution.py:13
  21.3 1.7 %collective-permute-done.7 = bf16[4,1,32,1024]{3,2,0,1:T(8,128)(2,1)S(1)} collective-permute-done((bf16[4,1,32,1024]{3,2,0,1:T(8,128)(2,1)S(1)}, bf16[4,1,32,1024]{3,2,0,1:T(8,128)(2,1)S(1)}, u32[]{:S(2)}, u32[]{:S(2)}) %collective-permute-start.7) | collective-permute-done | bytes 262176 | tf_op jit(solution)/shard_map/ppermute | solution.py:13
  23.1 0.6 gather_fusion.1
  23.9 2.3 %collective-permute-done.3 = bf16[1,8,16,1024]{3,2,1,0:T(8,128)(2,1)S(1)} collective-permute-done((bf16[1,8,16,1024]{3,2,1,0:T(8,128)(2,1)S(1)}, bf16[1,8,16,1024]{3,2,1,0:T(8,128)(2,1)S(1)}, u32[]{:S(2)}, u32[]{:S(2)}) %collective-permute-start.3) | collective-permute-done | bytes 262176 | tf_op jit(solution)/shard_map/ppermute | solution.py:13
  26.4 3.1 %multiply_convert_fusion = (bf16[2,8,32,1024]{3,2,1,0:T(8,128)(2,1)S(1)}, bf16[2,8,32,1024]{3,2,1,0:T(8,128)(2,1)S(1)}, bf16[2,8,32,1024]{3,2,1,0:T(8,128)(2,1)S...) fusion(f32[2,8,1024]{2,1,0:T(8,128)S(1)} %get-tuple-element.35,, ...), kind=kLoop, calls=%fused_computation.6 | loop fusion | flops 8388608 | bytes 9437184 | tf_op jit(solution)/shard_map/convert_element_type | solution.py:94
  30.2 1.5 %slice-done.1 = s8[4194304]{0:T(1024)(128)(4,1)S(1)} async-done(((s8[8388608]{0:T(1024)(128)(4,1)}), s8[4194304]{0:T(1024)(128)(4,1)S(1)}, s32[]{:S(2)}) %slice-start.1) | async-done | bytes 4194328
  31.7 4.5 %bitcast_convert_fusion.1 = bf16[512,1024]{1,0:T(8,128)(2,1)S(1)} fusion(bf16[4,512,1024]{2,1,0:T(8,128)(2,1)S(1)} %bitcast.142, bf16[4,1024,1024]{2,1,0:T(8,128)(2,1)S(1)} %bitcast.166), kind=kOutput, calls=%fused_computation.3 | convolution fusion | flops 4295491584 | bytes 13631488 | tf_op jit(solution)/shard_map/dot_general | solution.py:59
  36.2 0.6 convolution_bitcast_fusion.2
  36.7 0.6 convolution_bitcast_fusion.3
  37.4 0.5 collective-permute-start.8
  38.3 4.7 %bitcast_convert_fusion = bf16[512,1024]{1,0:T(8,128)(2,1)S(1)} fusion(bf16[4,512,1024]{2,1,0:T(8,128)(2,1)S(1)} %bitcast.143, bf16[4,1024,1024]{2,1,0:T(8,128)(2,1)S(1)} %bitcast.167), kind=kOutput, calls=%fused_computation.2 | convolution fusion | flops 4295491584 | bytes 13631488 | tf_op jit(solution)/shard_map/dot_general | solution.py:59
  44.1 0.6 fusion.15
  44.6 0.6 fusion.8
  45.2 1.6 %collective-permute-start.9 = (bf16[1,2,256,256]{3,2,1,0:T(8,128)(2,1)S(1)}, bf16[1,2,256,256]{3,2,1,0:T(8,128)(2,1)S(1)}, u32[]{:S(2)}, u32[]{:S(2)}) collective-permute-start(bf16[1,2,256,256]{3,2,1,0:T(8,128)(2,1)S(1)} %fusion.8), channel_id=1, source_target_pairs={{0,2},{1,3},{2,0},{3,1},{4,6},{5,7},{6,4},{7,5},{8,10},{9,11},{10,... | collective-permute-start | bytes 786440 | tf_op jit(solution)/shard_map/ppermute | solution.py:13
  47.7 1.0 %collective-permute-start.11 = (bf16[1,2,256,256]{3,2,1,0:T(8,128)(2,1)S(1)}, bf16[1,2,256,256]{3,2,1,0:T(8,128)(2,1)S(1)}, u32[]{:S(2)}, u32[]{:S(2)}) collective-permute-start(bf16[1,2,256,256]{3,2,1,0:T(8,128)(2,1)S(1)} %fusion.9), channel_id=1, source_target_pairs={{0,2},{1,3},{2,0},{3,1},{4,6},{5,7},{6,4},{7,5},{8,10},{9,11},{10,... | collective-permute-start | bytes 786440 | tf_op jit(solution)/shard_map/ppermute | solution.py:13
  48.7 5.6 %collective-permute-done.9 = bf16[1,2,256,256]{3,2,1,0:T(8,128)(2,1)S(1)} collective-permute-done((bf16[1,2,256,256]{3,2,1,0:T(8,128)(2,1)S(1)}, bf16[1,2,256,256]{3,2,1,0:T(8,128)(2,1)S(1)}, u32[]{:S(2)}, u32[]{:S(2)}) %collective-permute-start.9) | collective-permute-done | bytes 262176 | tf_op jit(solution)/shard_map/ppermute | solution.py:13
  54.5 5.1 %collective-permute-done.11 = bf16[1,2,256,256]{3,2,1,0:T(8,128)(2,1)S(1)} collective-permute-done((bf16[1,2,256,256]{3,2,1,0:T(8,128)(2,1)S(1)}, bf16[1,2,256,256]{3,2,1,0:T(8,128)(2,1)S(1)}, u32[]{:S(2)}, u32[]{:S(2)}) %collective-permute-start.11) | collective-permute-done | bytes 262176 | tf_op jit(solution)/shard_map/ppermute | solution.py:13
  59.7 1.0 %maximum_bitcast_fusion = f32[1,4,256,256]{3,2,1,0:T(8,128)} fusion(f32[2,256,256]{2,1,0:T(8,128)S(1)} %fusion.3, f32[2,256,256]{2,1,0:T(8,128)S(1)} %fusion.7), kind=kLoop, calls=%fused_computation.21 | loop fusion | flops 262144 | bytes 2097152 | tf_op jit(solution)/shard_map/broadcast_in_dim | solution.py:124
  (39 shorter events, 4.0 us)
Async XLA Ops:
  0.8 6.3 %collective-permute-start = (bf16[1,1,16,1024]{3,2,0,1:T(8,128)(2,1)S(1)}, bf16[1,1,16,1024]{3,2,0,1:T(8,128)(2,1)S(1)}, u32[]{:S(2)}, u32[]{:S(2)}) collective-permute-start(bf16[1,1,16,1024]{3,2,0,1:T(8,128)(2,1)S(1)} %get-tuple-element.50), channel_id=1, source_target_pairs={{0,16},{4,20},{8,24},{12,28},{16,0},{20,4},{24,8},{28,12},{1,17},{... | collective-permute-start | bytes 98312 | tf_op jit(solution)/shard_map/ppermute | solution.py:13
  5.7 5.5 %collective-permute-start.5 = (bf16[1,1,32,1024]{3,2,0,1:T(8,128)(2,1)S(1)}, bf16[1,1,32,1024]{3,2,0,1:T(8,128)(2,1)S(1)}, u32[]{:S(2)}, u32[]{:S(2)}) collective-permute-start(bf16[1,1,32,1024]{3,2,0,1:T(8,128)(2,1)S(1)} %get-tuple-element.48), channel_id=1, source_target_pairs={{0,16},{4,20},{8,24},{12,28},{16,0},{20,4},{24,8},{28,12},{1,17},{... | collective-permute-start | bytes 196616 | tf_op jit(solution)/shard_map/ppermute | solution.py:13
  7.1 5.7 %collective-permute-start.1 = (bf16[2,1,16,1024]{3,2,0,1:T(8,128)(2,1)S(1)}, bf16[2,1,16,1024]{3,2,0,1:T(8,128)(2,1)S(1)}, u32[]{:S(2)}, u32[]{:S(2)}) collective-permute-start(bf16[2,1,16,1024]{3,2,0,1:T(8,128)(2,1)S(1)} %maximum_select_fusion.8), channel_id=1, source_target_pairs={{0,8},{4,12},{8,0},{12,4},{16,24},{20,28},{24,16},{28,20},{1,9},{5... | collective-permute-start | bytes 196616 | tf_op jit(solution)/shard_map/ppermute | solution.py:13
  11.2 5.0 %collective-permute-start.6 = (bf16[2,1,32,1024]{3,2,0,1:T(8,128)(2,1)S(1)}, bf16[2,1,32,1024]{3,2,0,1:T(8,128)(2,1)S(1)}, u32[]{:S(2)}, u32[]{:S(2)}) collective-permute-start(bf16[2,1,32,1024]{3,2,0,1:T(8,128)(2,1)S(1)} %maximum_select_fusion.7), channel_id=1, source_target_pairs={{0,8},{4,12},{8,0},{12,4},{16,24},{20,28},{24,16},{28,20},{1,9},{5... | collective-permute-start | bytes 393224 | tf_op jit(solution)/shard_map/ppermute | solution.py:13
  12.8 6.4 %collective-permute-start.2 = (bf16[4,1,16,1024]{3,2,0,1:T(8,128)(2,1)S(1)}, bf16[4,1,16,1024]{3,2,0,1:T(8,128)(2,1)S(1)}, u32[]{:S(2)}, u32[]{:S(2)}) collective-permute-start(bf16[4,1,16,1024]{3,2,0,1:T(8,128)(2,1)S(1)} %bitcast.156), channel_id=1, source_target_pairs={{0,4},{4,0},{8,12},{12,8},{16,20},{20,16},{24,28},{28,24},{1,5},{5... | collective-permute-start | bytes 393224 | tf_op jit(solution)/shard_map/ppermute | solution.py:13
  16.3 6.7 %collective-permute-start.7 = (bf16[4,1,32,1024]{3,2,0,1:T(8,128)(2,1)S(1)}, bf16[4,1,32,1024]{3,2,0,1:T(8,128)(2,1)S(1)}, u32[]{:S(2)}, u32[]{:S(2)}) collective-permute-start(bf16[4,1,32,1024]{3,2,0,1:T(8,128)(2,1)S(1)} %bitcast.152), channel_id=1, source_target_pairs={{0,4},{4,0},{8,12},{12,8},{16,20},{20,16},{24,28},{28,24},{1,5},{5... | collective-permute-start | bytes 786440 | tf_op jit(solution)/shard_map/ppermute | solution.py:13
  19.8 6.4 %collective-permute-start.3 = (bf16[1,8,16,1024]{3,2,1,0:T(8,128)(2,1)S(1)}, bf16[1,8,16,1024]{3,2,1,0:T(8,128)(2,1)S(1)}, u32[]{:S(2)}, u32[]{:S(2)}) collective-permute-start(bf16[1,8,16,1024]{3,2,1,0:T(8,128)(2,1)S(1)} %bitcast.147), channel_id=1, source_target_pairs={{0,2},{1,3},{2,0},{3,1},{4,6},{5,7},{6,4},{7,5},{8,10},{9,11},{10,... | collective-permute-start | bytes 786440 | tf_op jit(solution)/shard_map/ppermute | solution.py:13
  26.3 3.3 %collective-permute-start.4 = (bf16[2,8,16,1024]{3,2,1,0:T(8,128)(2,1)S(1)}, bf16[2,8,16,1024]{3,2,1,0:T(8,128)(2,1)S(1)}, u32[]{:S(2)}, u32[]{:S(2)}) collective-permute-start(bf16[2,8,16,1024]{3,2,1,0:T(8,128)(2,1)S(1)} %maximum_select_fusion.2), channel_id=1, source_target_pairs={{0,1},{1,0},{2,3},{3,2},{4,5},{5,4},{6,7},{7,6},{8,9},{9,8},{10,11... | collective-permute-start | bytes 1572872 | tf_op jit(solution)/shard_map/ppermute | solution.py:13
  26.4 3.8 %slice-start = ((s8[8388608]{0:T(1024)(128)(4,1)}), s8[4194304]{0:T(1024)(128)(4,1)S(1)}, s32[]{:S(2)}) async-start(s8[8388608]{0:T(1024)(128)(4,1)} %bitcast.164), calls=%async_computation | async-start | bytes 8388608
  29.5 2.2 %slice-start.1 = ((s8[8388608]{0:T(1024)(128)(4,1)}), s8[4194304]{0:T(1024)(128)(4,1)S(1)}, s32[]{:S(2)}) async-start(s8[8388608]{0:T(1024)(128)(4,1)} %bitcast.164), calls=%async_computation.1 | async-start | bytes 8388608
  37.4 7.3 %collective-permute-start.8 = (f32[2,2,256,256]{3,2,1,0:T(8,128)S(1)}, f32[2,2,256,256]{3,2,1,0:T(8,128)S(1)}, u32[]{:S(2)}, u32[]{:S(2)}) collective-permute-start(f32[2,2,256,256]{3,2,1,0:T(8,128)S(1)} %pad_maximum_fusion), channel_id=1, source_target_pairs={{0,1},{1,0},{2,3},{3,2},{4,5},{5,4},{6,7},{7,6},{8,9},{9,8},{10,11... | collective-permute-start | bytes 3145736 | tf_op jit(solution)/shard_map/ppermute | solution.py:13
  44.0 3.3 %collective-permute-start.10 = (f32[2,2,256,256]{3,2,1,0:T(8,128)S(1)}, f32[2,2,256,256]{3,2,1,0:T(8,128)S(1)}, u32[]{:S(2)}, u32[]{:S(2)}) collective-permute-start(f32[2,2,256,256]{3,2,1,0:T(8,128)S(1)} %pad_maximum_fusion.1), channel_id=1, source_target_pairs={{0,1},{1,0},{2,3},{3,2},{4,5},{5,4},{6,7},{7,6},{8,9},{9,8},{10,11... | collective-permute-start | bytes 3145736 | tf_op jit(solution)/shard_map/ppermute | solution.py:13
  45.2 9.2 %collective-permute-start.9 = (bf16[1,2,256,256]{3,2,1,0:T(8,128)(2,1)S(1)}, bf16[1,2,256,256]{3,2,1,0:T(8,128)(2,1)S(1)}, u32[]{:S(2)}, u32[]{:S(2)}) collective-permute-start(bf16[1,2,256,256]{3,2,1,0:T(8,128)(2,1)S(1)} %fusion.8), channel_id=1, source_target_pairs={{0,2},{1,3},{2,0},{3,1},{4,6},{5,7},{6,4},{7,5},{8,10},{9,11},{10,... | collective-permute-start | bytes 786440 | tf_op jit(solution)/shard_map/ppermute | solution.py:13
  47.7 11.9 %collective-permute-start.11 = (bf16[1,2,256,256]{3,2,1,0:T(8,128)(2,1)S(1)}, bf16[1,2,256,256]{3,2,1,0:T(8,128)(2,1)S(1)}, u32[]{:S(2)}, u32[]{:S(2)}) collective-permute-start(bf16[1,2,256,256]{3,2,1,0:T(8,128)(2,1)S(1)} %fusion.9), channel_id=1, source_target_pairs={{0,2},{1,3},{2,0},{3,1},{4,6},{5,7},{6,4},{7,5},{8,10},{9,11},{10,... | collective-permute-start | bytes 786440 | tf_op jit(solution)/shard_map/ppermute | solution.py:13

commit v23 on v22

--- a/solution.py
+++ b/solution.py
@@ -80,7 +80,7 @@
     )
 
     valence = gather_axis(jnp.take(held_valence, wanted, axis=0, mode="clip"), "col")
-    conduction = jnp.take(held_conduction, wanted, axis=0, mode="clip").astype(jnp.float32)
+    conduction = jnp.take(held_conduction, wanted, axis=0, mode="clip")
     rows_per_block = NC // col_count
     chunk = pair_count // PAIR_CHUNKS
     starts = list(range(0, pair_count, chunk))
@@ -91,7 +91,7 @@
         rows = lax.dynamic_slice_in_dim(
             cond_a, (col_index ^ delta) * rows_per_block, rows_per_block, 1
         )
-        cond_pairs = (rows[:, :, None, :] * cond_b[:, None, :, :]).astype(jnp.bfloat16)
+        cond_pairs = rows[:, :, None, :] * cond_b[:, None, :, :]
         return cond_pairs.reshape(chunk, rows_per_block * NC, mu_cols)
 
     cond_blocks = [[cond_block(first, d) for d in range(col_count)] for first in starts]

time: 61 us -> 59 us (0.967)
  other arithmetic: 7.05 us -> 4.86 us
  waiting for transfers between devices: 19.4 us -> 20.2 us
    convert_element_type x1 -> x0, other arithmetic: 3.06 us -> none  [cond_block(): (rows[:, :, None, :] * cond_b[:, None, :, :]).astype(jnp.bfloat16)]
    mul x0 -> x1, other arithmetic: none -> 0.83 us  [cond_block(): cond_pairs = rows[:, :, None, :] * cond_b[:, None, :, :]]
    ppermute x12, waiting for transfers between devices: 19.4 us -> 20.2 us  [swap(): return lax.ppermute(x, axis, [(i, i ^ bit) for i in range(size)])]
  transfers between devices with their start and end apart: 12 -> 12, of which waited for: 8 -> 9; matrix products, arithmetic and copies ran while one was open for 25% -> 21% of each run, Pallas kernels for 0% -> 0%
where the time goes in v23:
time: 59 us; the launch traced here: 58.8 us
  waiting for transfers between devices  20.2 us (34%)
  starting transfers between devices  16.3 us (28%)
  matrix products  12.9 us (22%)
  other arithmetic  4.86 us (8%)
  local copies, waits for them, and re-layouts  4.18 us (7%)
    ppermute x12, waiting for transfers between devices, swap(): return lax.ppermute(x, axis, [(i, i ^ bit) for i in range(size)])  20.2 us
    ppermute x12, starting transfers between devices, swap(): return lax.ppermute(x, axis, [(i, i ^ bit) for i in range(size)])  16.3 us
    dot_general x2, matrix products, screened_of(): lax.dot_general(val_pairs, screen, (((0, 2), (0, 1)), ((), ())), preferre...  9.1 us
    dot_general x8, matrix products, own_block(): jnp.einsum('pan,pbn->pab', screened, cond_pairs, preferred_element_type=j...  3.76 us
    another operation x2, local copies, waits for them, and re-layouts, gather_axis(): cur = jnp.where(low, jnp.stack([cur, got], 1), jnp.stack([got, cur], 1))  1.61 us
    unnamed x4, local copies, waits for them, and re-layouts  1.2 us
  transfers between devices with their start and end apart: 12, of which 9 were waited for; matrix products, arithmetic and copies ran while one was open for 21% of the time, Pallas kernels for 0%

profile of v23, /device:TPU:0, one launch (start us, length us, event | category | flops | bytes accessed | tf_op | source)
XLA Modules:
  0.0 58.8 jit_solution(16025702240703920607)
XLA Ops:
  0.0 0.8 %slice_bitcast_fusion.7 = (bf16[1,1,1,16,1024]{4,3,2,1,0:T(8,128)(2,1)S(1)}, bf16[1,1,16,1024]{3,2,0,1:T(8,128)(2,1)S(1)}) fusion(bf16[1,48,1024]{2,1,0:T(8,128)(2,1)} %param.3), kind=kLoop, calls=%fused_computation.53 | loop fusion | bytes 98304 | tf_op jit(solution)/shard_map/stack | solution.py:24
  0.8 4.0 %collective-permute-start = (bf16[1,1,16,1024]{3,2,0,1:T(8,128)(2,1)S(1)}, bf16[1,1,16,1024]{3,2,0,1:T(8,128)(2,1)S(1)}, u32[]{:S(2)}, u32[]{:S(2)}) collective-permute-start(bf16[1,1,16,1024]{3,2,0,1:T(8,128)(2,1)S(1)} %get-tuple-element.50), channel_id=1, source_target_pairs={{0,16},{4,20},{8,24},{12,28},{16,0},{20,4},{24,8},{28,12},{1,17},{... | collective-permute-start | bytes 98312 | tf_op jit(solution)/shard_map/ppermute | solution.py:13
  4.8 0.8 %slice_bitcast_fusion.5 = (bf16[1,1,1,32,1024]{4,3,2,1,0:T(8,128)(2,1)S(1)}, bf16[1,1,32,1024]{3,2,0,1:T(8,128)(2,1)S(1)}) fusion(bf16[1,48,1024]{2,1,0:T(8,128)(2,1)} %param.3), kind=kLoop, calls=%fused_computation.51 | loop fusion | bytes 196608 | tf_op jit(solution)/shard_map/stack | solution.py:24
  5.7 0.7 %and_select_fusion = s32[4]{0:T(128)S(1)} fusion(s32[]{:T(128)S(6)} %axis_index.17, s32[1,4]{1,0:T(1,128)} %param.5), kind=kLoop, calls=%fused_computation.65 | loop fusion | flops 48 | bytes 36 | tf_op jit(solution)/shard_map/jit(remainder)/select_n | solution.py:73
  6.4 0.6 %collective-permute-done = bf16[1,1,16,1024]{3,2,0,1:T(8,128)(2,1)S(1)} collective-permute-done((bf16[1,1,16,1024]{3,2,0,1:T(8,128)(2,1)S(1)}, bf16[1,1,16,1024]{3,2,0,1:T(8,128)(2,1)S(1)}, u32[]{:S(2)}, u32[]{:S(2)}) %collective-permute-start) | collective-permute-done | bytes 32800 | tf_op jit(solution)/shard_map/ppermute | solution.py:13
  7.1 2.5 %collective-permute-start.1 = (bf16[2,1,16,1024]{3,2,0,1:T(8,128)(2,1)S(1)}, bf16[2,1,16,1024]{3,2,0,1:T(8,128)(2,1)S(1)}, u32[]{:S(2)}, u32[]{:S(2)}) collective-permute-start(bf16[2,1,16,1024]{3,2,0,1:T(8,128)(2,1)S(1)} %maximum_select_fusion.8), channel_id=1, source_target_pairs={{0,8},{4,12},{8,0},{12,4},{16,24},{20,28},{24,16},{28,20},{1,9},{5... | collective-permute-start | bytes 196616 | tf_op jit(solution)/shard_map/ppermute | solution.py:13
  9.5 1.6 %collective-permute-done.5 = bf16[1,1,32,1024]{3,2,0,1:T(8,128)(2,1)S(1)} collective-permute-done((bf16[1,1,32,1024]{3,2,0,1:T(8,128)(2,1)S(1)}, bf16[1,1,32,1024]{3,2,0,1:T(8,128)(2,1)S(1)}, u32[]{:S(2)}, u32[]{:S(2)}) %collective-permute-start.5) | collective-permute-done | bytes 65568 | tf_op jit(solution)/shard_map/ppermute | solution.py:13
  11.2 1.5 %collective-permute-start.6 = (bf16[2,1,32,1024]{3,2,0,1:T(8,128)(2,1)S(1)}, bf16[2,1,32,1024]{3,2,0,1:T(8,128)(2,1)S(1)}, u32[]{:S(2)}, u32[]{:S(2)}) collective-permute-start(bf16[2,1,32,1024]{3,2,0,1:T(8,128)(2,1)S(1)} %maximum_select_fusion.7), channel_id=1, source_target_pairs={{0,8},{4,12},{8,0},{12,4},{16,24},{20,28},{24,16},{28,20},{1,9},{5... | collective-permute-start | bytes 393224 | tf_op jit(solution)/shard_map/ppermute | solution.py:13
  12.8 1.6 %collective-permute-start.2 = (bf16[4,1,16,1024]{3,2,0,1:T(8,128)(2,1)S(1)}, bf16[4,1,16,1024]{3,2,0,1:T(8,128)(2,1)S(1)}, u32[]{:S(2)}, u32[]{:S(2)}) collective-permute-start(bf16[4,1,16,1024]{3,2,0,1:T(8,128)(2,1)S(1)} %bitcast.156), channel_id=1, source_target_pairs={{0,4},{4,0},{8,12},{12,8},{16,20},{20,16},{24,28},{28,24},{1,5},{5... | collective-permute-start | bytes 393224 | tf_op jit(solution)/shard_map/ppermute | solution.py:13
  14.4 1.9 %collective-permute-done.6 = bf16[2,1,32,1024]{3,2,0,1:T(8,128)(2,1)S(1)} collective-permute-done((bf16[2,1,32,1024]{3,2,0,1:T(8,128)(2,1)S(1)}, bf16[2,1,32,1024]{3,2,0,1:T(8,128)(2,1)S(1)}, u32[]{:S(2)}, u32[]{:S(2)}) %collective-permute-start.6) | collective-permute-done | bytes 131104 | tf_op jit(solution)/shard_map/ppermute | solution.py:13
  16.3 1.6 %collective-permute-start.7 = (bf16[4,1,32,1024]{3,2,0,1:T(8,128)(2,1)S(1)}, bf16[4,1,32,1024]{3,2,0,1:T(8,128)(2,1)S(1)}, u32[]{:S(2)}, u32[]{:S(2)}) collective-permute-start(bf16[4,1,32,1024]{3,2,0,1:T(8,128)(2,1)S(1)} %bitcast.152), channel_id=1, source_target_pairs={{0,4},{4,0},{8,12},{12,8},{16,20},{20,16},{24,28},{28,24},{1,5},{5... | collective-permute-start | bytes 786440 | tf_op jit(solution)/shard_map/ppermute | solution.py:13
  17.9 0.7 %pad_add_fusion = s32[8]{0:T(128)S(1)} fusion(s32[4]{0:T(128)S(1)} %and_select_fusion, s32[4]{0:T(128)} %bitcast.168), kind=kLoop, calls=%fused_computation.67 | loop fusion | flops 8 | bytes 64 | tf_op jit(solution)/shard_map/concatenate | solution.py:76
  18.6 0.5 collective-permute-done.2
  19.2 0.6 gather_fusion
  19.8 1.6 %collective-permute-start.3 = (bf16[1,8,16,1024]{3,2,1,0:T(8,128)(2,1)S(1)}, bf16[1,8,16,1024]{3,2,1,0:T(8,128)(2,1)S(1)}, u32[]{:S(2)}, u32[]{:S(2)}) collective-permute-start(bf16[1,8,16,1024]{3,2,1,0:T(8,128)(2,1)S(1)} %bitcast.147), channel_id=1, source_target_pairs={{0,2},{1,3},{2,0},{3,1},{4,6},{5,7},{6,4},{7,5},{8,10},{9,11},{10,... | collective-permute-start | bytes 786440 | tf_op jit(solution)/shard_map/ppermute | solution.py:13
  21.3 1.7 %collective-permute-done.7 = bf16[4,1,32,1024]{3,2,0,1:T(8,128)(2,1)S(1)} collective-permute-done((bf16[4,1,32,1024]{3,2,0,1:T(8,128)(2,1)S(1)}, bf16[4,1,32,1024]{3,2,0,1:T(8,128)(2,1)S(1)}, u32[]{:S(2)}, u32[]{:S(2)}) %collective-permute-start.7) | collective-permute-done | bytes 262176 | tf_op jit(solution)/shard_map/ppermute | solution.py:13
  23.1 0.6 gather_fusion.1
  23.8 2.4 %collective-permute-done.3 = bf16[1,8,16,1024]{3,2,1,0:T(8,128)(2,1)S(1)} collective-permute-done((bf16[1,8,16,1024]{3,2,1,0:T(8,128)(2,1)S(1)}, bf16[1,8,16,1024]{3,2,1,0:T(8,128)(2,1)S(1)}, u32[]{:S(2)}, u32[]{:S(2)}) %collective-permute-start.3) | collective-permute-done | bytes 262176 | tf_op jit(solution)/shard_map/ppermute | solution.py:13
  26.4 0.8 %broadcast_multiply_fusion.2 = (bf16[2,8,32,1024]{3,2,1,0:T(8,128)(2,1)S(1)}, bf16[2,8,32,1024]{3,2,1,0:T(8,128)(2,1)S(1)}, bf16[2,8,32,1024]{3,2,1,0:T(8,128)(2...) fusion(bf16[2,8,1024]{2,1,0:T(8,128)(2,1)S(1)} %get-tuple-eleme, ...), kind=kLoop, calls=%fused_computation.29 | loop fusion | flops 4194304 | bytes 8912896 | tf_op jit(solution)/shard_map/mul | solution.py:94
  27.3 0.9 %collective-permute-done.4 = bf16[2,8,16,1024]{3,2,1,0:T(8,128)(2,1)S(1)} collective-permute-done((bf16[2,8,16,1024]{3,2,1,0:T(8,128)(2,1)S(1)}, bf16[2,8,16,1024]{3,2,1,0:T(8,128)(2,1)S(1)}, u32[]{:S(2)}, u32[]{:S(2)}) %collective-permute-start.4) | collective-permute-done | bytes 524320 | tf_op jit(solution)/shard_map/ppermute | solution.py:13
  28.9 1.2 %slice-done.1 = s8[4194304]{0:T(1024)(128)(4,1)S(1)} async-done(((s8[8388608]{0:T(1024)(128)(4,1)}), s8[4194304]{0:T(1024)(128)(4,1)S(1)}, s32[]{:S(2)}) %slice-start.1) | async-done | bytes 4194328
  30.1 4.6 %bitcast_convert_fusion.1 = bf16[512,1024]{1,0:T(8,128)(2,1)S(1)} fusion(bf16[4,512,1024]{2,1,0:T(8,128)(2,1)S(1)} %bitcast.142, bf16[4,1024,1024]{2,1,0:T(8,128)(2,1)S(1)} %bitcast.166), kind=kOutput, calls=%fused_computation.3 | convolution fusion | flops 4295491584 | bytes 13631488 | tf_op jit(solution)/shard_map/dot_general | solution.py:59
  34.6 0.5 convolution_bitcast_fusion.2
  35.7 0.6 collective-permute-start.8
  36.6 4.6 %bitcast_convert_fusion = bf16[512,1024]{1,0:T(8,128)(2,1)S(1)} fusion(bf16[4,512,1024]{2,1,0:T(8,128)(2,1)S(1)} %bitcast.143, bf16[4,1024,1024]{2,1,0:T(8,128)(2,1)S(1)} %bitcast.167), kind=kOutput, calls=%fused_computation.2 | convolution fusion | flops 4295491584 | bytes 13631488 | tf_op jit(solution)/shard_map/dot_general | solution.py:59
  41.6 0.5 convolution_bitcast_fusion.1
  43.2 1.6 %collective-permute-start.9 = (bf16[1,2,256,256]{3,2,1,0:T(8,128)(2,1)S(1)}, bf16[1,2,256,256]{3,2,1,0:T(8,128)(2,1)S(1)}, u32[]{:S(2)}, u32[]{:S(2)}) collective-permute-start(bf16[1,2,256,256]{3,2,1,0:T(8,128)(2,1)S(1)} %fusion.8), channel_id=1, source_target_pairs={{0,2},{1,3},{2,0},{3,1},{4,6},{5,7},{6,4},{7,5},{8,10},{9,11},{10,... | collective-permute-start | bytes 786440 | tf_op jit(solution)/shard_map/ppermute | solution.py:13
  45.3 0.5 fusion.9
  45.8 1.2 %collective-permute-start.11 = (bf16[1,2,256,256]{3,2,1,0:T(8,128)(2,1)S(1)}, bf16[1,2,256,256]{3,2,1,0:T(8,128)(2,1)S(1)}, u32[]{:S(2)}, u32[]{:S(2)}) collective-permute-start(bf16[1,2,256,256]{3,2,1,0:T(8,128)(2,1)S(1)} %fusion.9), channel_id=1, source_target_pairs={{0,2},{1,3},{2,0},{3,1},{4,6},{5,7},{6,4},{7,5},{8,10},{9,11},{10,... | collective-permute-start | bytes 786440 | tf_op jit(solution)/shard_map/ppermute | solution.py:13
  47.0 5.4 %collective-permute-done.9 = bf16[1,2,256,256]{3,2,1,0:T(8,128)(2,1)S(1)} collective-permute-done((bf16[1,2,256,256]{3,2,1,0:T(8,128)(2,1)S(1)}, bf16[1,2,256,256]{3,2,1,0:T(8,128)(2,1)S(1)}, u32[]{:S(2)}, u32[]{:S(2)}) %collective-permute-start.9) | collective-permute-done | bytes 262176 | tf_op jit(solution)/shard_map/ppermute | solution.py:13
  52.5 5.1 %collective-permute-done.11 = bf16[1,2,256,256]{3,2,1,0:T(8,128)(2,1)S(1)} collective-permute-done((bf16[1,2,256,256]{3,2,1,0:T(8,128)(2,1)S(1)}, bf16[1,2,256,256]{3,2,1,0:T(8,128)(2,1)S(1)}, u32[]{:S(2)}, u32[]{:S(2)}) %collective-permute-start.11) | collective-permute-done | bytes 262176 | tf_op jit(solution)/shard_map/ppermute | solution.py:13
  57.7 1.0 %maximum_bitcast_fusion = f32[1,4,256,256]{3,2,1,0:T(8,128)} fusion(f32[2,256,256]{2,1,0:T(8,128)S(1)} %fusion.3, f32[2,256,256]{2,1,0:T(8,128)S(1)} %fusion.7), kind=kLoop, calls=%fused_computation.13 | loop fusion | flops 262144 | bytes 2097152 | tf_op jit(solution)/shard_map/broadcast_in_dim | solution.py:124
  (39 shorter events, 4.4 us)
Async XLA Ops:
  0.8 6.3 %collective-permute-start = (bf16[1,1,16,1024]{3,2,0,1:T(8,128)(2,1)S(1)}, bf16[1,1,16,1024]{3,2,0,1:T(8,128)(2,1)S(1)}, u32[]{:S(2)}, u32[]{:S(2)}) collective-permute-start(bf16[1,1,16,1024]{3,2,0,1:T(8,128)(2,1)S(1)} %get-tuple-element.50), channel_id=1, source_target_pairs={{0,16},{4,20},{8,24},{12,28},{16,0},{20,4},{24,8},{28,12},{1,17},{... | collective-permute-start | bytes 98312 | tf_op jit(solution)/shard_map/ppermute | solution.py:13
  5.7 5.5 %collective-permute-start.5 = (bf16[1,1,32,1024]{3,2,0,1:T(8,128)(2,1)S(1)}, bf16[1,1,32,1024]{3,2,0,1:T(8,128)(2,1)S(1)}, u32[]{:S(2)}, u32[]{:S(2)}) collective-permute-start(bf16[1,1,32,1024]{3,2,0,1:T(8,128)(2,1)S(1)} %get-tuple-element.48), channel_id=1, source_target_pairs={{0,16},{4,20},{8,24},{12,28},{16,0},{20,4},{24,8},{28,12},{1,17},{... | collective-permute-start | bytes 196616 | tf_op jit(solution)/shard_map/ppermute | solution.py:13
  7.1 5.7 %collective-permute-start.1 = (bf16[2,1,16,1024]{3,2,0,1:T(8,128)(2,1)S(1)}, bf16[2,1,16,1024]{3,2,0,1:T(8,128)(2,1)S(1)}, u32[]{:S(2)}, u32[]{:S(2)}) collective-permute-start(bf16[2,1,16,1024]{3,2,0,1:T(8,128)(2,1)S(1)} %maximum_select_fusion.8), channel_id=1, source_target_pairs={{0,8},{4,12},{8,0},{12,4},{16,24},{20,28},{24,16},{28,20},{1,9},{5... | collective-permute-start | bytes 196616 | tf_op jit(solution)/shard_map/ppermute | solution.py:13
  11.2 5.0 %collective-permute-start.6 = (bf16[2,1,32,1024]{3,2,0,1:T(8,128)(2,1)S(1)}, bf16[2,1,32,1024]{3,2,0,1:T(8,128)(2,1)S(1)}, u32[]{:S(2)}, u32[]{:S(2)}) collective-permute-start(bf16[2,1,32,1024]{3,2,0,1:T(8,128)(2,1)S(1)} %maximum_select_fusion.7), channel_id=1, source_target_pairs={{0,8},{4,12},{8,0},{12,4},{16,24},{20,28},{24,16},{28,20},{1,9},{5... | collective-permute-start | bytes 393224 | tf_op jit(solution)/shard_map/ppermute | solution.py:13
  12.8 6.4 %collective-permute-start.2 = (bf16[4,1,16,1024]{3,2,0,1:T(8,128)(2,1)S(1)}, bf16[4,1,16,1024]{3,2,0,1:T(8,128)(2,1)S(1)}, u32[]{:S(2)}, u32[]{:S(2)}) collective-permute-start(bf16[4,1,16,1024]{3,2,0,1:T(8,128)(2,1)S(1)} %bitcast.156), channel_id=1, source_target_pairs={{0,4},{4,0},{8,12},{12,8},{16,20},{20,16},{24,28},{28,24},{1,5},{5... | collective-permute-start | bytes 393224 | tf_op jit(solution)/shard_map/ppermute | solution.py:13
  16.3 6.7 %collective-permute-start.7 = (bf16[4,1,32,1024]{3,2,0,1:T(8,128)(2,1)S(1)}, bf16[4,1,32,1024]{3,2,0,1:T(8,128)(2,1)S(1)}, u32[]{:S(2)}, u32[]{:S(2)}) collective-permute-start(bf16[4,1,32,1024]{3,2,0,1:T(8,128)(2,1)S(1)} %bitcast.152), channel_id=1, source_target_pairs={{0,4},{4,0},{8,12},{12,8},{16,20},{20,16},{24,28},{28,24},{1,5},{5... | collective-permute-start | bytes 786440 | tf_op jit(solution)/shard_map/ppermute | solution.py:13
  19.8 6.4 %collective-permute-start.3 = (bf16[1,8,16,1024]{3,2,1,0:T(8,128)(2,1)S(1)}, bf16[1,8,16,1024]{3,2,1,0:T(8,128)(2,1)S(1)}, u32[]{:S(2)}, u32[]{:S(2)}) collective-permute-start(bf16[1,8,16,1024]{3,2,1,0:T(8,128)(2,1)S(1)} %bitcast.147), channel_id=1, source_target_pairs={{0,2},{1,3},{2,0},{3,1},{4,6},{5,7},{6,4},{7,5},{8,10},{9,11},{10,... | collective-permute-start | bytes 786440 | tf_op jit(solution)/shard_map/ppermute | solution.py:13
  26.3 2.0 %collective-permute-start.4 = (bf16[2,8,16,1024]{3,2,1,0:T(8,128)(2,1)S(1)}, bf16[2,8,16,1024]{3,2,1,0:T(8,128)(2,1)S(1)}, u32[]{:S(2)}, u32[]{:S(2)}) collective-permute-start(bf16[2,8,16,1024]{3,2,1,0:T(8,128)(2,1)S(1)} %maximum_select_fusion.2), channel_id=1, source_target_pairs={{0,1},{1,0},{2,3},{3,2},{4,5},{5,4},{6,7},{7,6},{8,9},{9,8},{10,11... | collective-permute-start | bytes 1572872 | tf_op jit(solution)/shard_map/ppermute | solution.py:13
  26.4 2.5 %slice-start = ((s8[8388608]{0:T(1024)(128)(4,1)}), s8[4194304]{0:T(1024)(128)(4,1)S(1)}, s32[]{:S(2)}) async-start(s8[8388608]{0:T(1024)(128)(4,1)} %bitcast.164), calls=%async_computation | async-start | bytes 8388608
  27.2 2.8 %slice-start.1 = ((s8[8388608]{0:T(1024)(128)(4,1)}), s8[4194304]{0:T(1024)(128)(4,1)S(1)}, s32[]{:S(2)}) async-start(s8[8388608]{0:T(1024)(128)(4,1)} %bitcast.164), calls=%async_computation.1 | async-start | bytes 8388608
  35.7 7.1 %collective-permute-start.8 = (f32[2,2,256,256]{3,2,1,0:T(8,128)S(1)}, f32[2,2,256,256]{3,2,1,0:T(8,128)S(1)}, u32[]{:S(2)}, u32[]{:S(2)}) collective-permute-start(f32[2,2,256,256]{3,2,1,0:T(8,128)S(1)} %pad_maximum_fusion), channel_id=1, source_target_pairs={{0,1},{1,0},{2,3},{3,2},{4,5},{5,4},{6,7},{7,6},{8,9},{9,8},{10,11... | collective-permute-start | bytes 3145736 | tf_op jit(solution)/shard_map/ppermute | solution.py:13
  42.2 3.1 %collective-permute-start.10 = (f32[2,2,256,256]{3,2,1,0:T(8,128)S(1)}, f32[2,2,256,256]{3,2,1,0:T(8,128)S(1)}, u32[]{:S(2)}, u32[]{:S(2)}) collective-permute-start(f32[2,2,256,256]{3,2,1,0:T(8,128)S(1)} %pad_maximum_fusion.1), channel_id=1, source_target_pairs={{0,1},{1,0},{2,3},{3,2},{4,5},{5,4},{6,7},{7,6},{8,9},{9,8},{10,11... | collective-permute-start | bytes 3145736 | tf_op jit(solution)/shard_map/ppermute | solution.py:13
  43.2 9.2 %collective-permute-start.9 = (bf16[1,2,256,256]{3,2,1,0:T(8,128)(2,1)S(1)}, bf16[1,2,256,256]{3,2,1,0:T(8,128)(2,1)S(1)}, u32[]{:S(2)}, u32[]{:S(2)}) collective-permute-start(bf16[1,2,256,256]{3,2,1,0:T(8,128)(2,1)S(1)} %fusion.8), channel_id=1, source_target_pairs={{0,2},{1,3},{2,0},{3,1},{4,6},{5,7},{6,4},{7,5},{8,10},{9,11},{10,... | collective-permute-start | bytes 786440 | tf_op jit(solution)/shard_map/ppermute | solution.py:13
  45.8 11.8 %collective-permute-start.11 = (bf16[1,2,256,256]{3,2,1,0:T(8,128)(2,1)S(1)}, bf16[1,2,256,256]{3,2,1,0:T(8,128)(2,1)S(1)}, u32[]{:S(2)}, u32[]{:S(2)}) collective-permute-start(bf16[1,2,256,256]{3,2,1,0:T(8,128)(2,1)S(1)} %fusion.9), channel_id=1, source_target_pairs={{0,2},{1,3},{2,0},{3,1},{4,6},{5,7},{6,4},{7,5},{8,10},{9,11},{10,... | collective-permute-start | bytes 786440 | tf_op jit(solution)/shard_map/ppermute | solution.py:13

commit v24 on v23

--- a/solution.py
+++ b/solution.py
@@ -5,7 +5,7 @@
 
 NV = 16
 NC = 32
-PAIR_CHUNKS = 2
+PAIR_CHUNKS = 1
 
 
 def swap(x, axis, bit):

time: 59 us -> 68.2 us (1.16)
  waiting for transfers between devices: 20.2 us -> 25.7 us
  matrix products: 12.9 us -> 16.6 us
  other arithmetic: 4.86 us -> 7.67 us
  starting transfers between devices: 16.3 us -> 14.7 us
  local copies, waits for them, and re-layouts: 4.18 us -> 2.99 us
    ppermute x12 -> x10, waiting for transfers between devices: 20.2 us -> 25.7 us  [swap(): return lax.ppermute(x, axis, [(i, i ^ bit) for i in range(size)])]
    dot_general x2 -> x1, matrix products: 9.1 us -> 13.6 us  [screened_of(): lax.dot_general(val_pairs, screen, (((0, 2), (0, 1)), ((), ())), preferre...]
    mul x2 -> x1, other arithmetic: 0.68 us -> 3.9 us  [screened_of(): val_pairs = valence_a[:, :, :, None, :] * valence_b[:, :, None, :, :]]
    ppermute x12 -> x10, starting transfers between devices: 16.3 us -> 14.7 us  [swap(): return lax.ppermute(x, axis, [(i, i ^ bit) for i in range(size)])]
    unnamed x4 -> x0, local copies, waits for them, and re-layouts: 1.2 us -> none
    dot_general x8 -> x4, matrix products: 3.76 us -> 2.98 us  [own_block(): jnp.einsum('pan,pbn->pab', screened, cond_pairs, preferred_element_type=j...]
  transfers between devices with their start and end apart: 12 -> 10, of which waited for: 9 -> 9; matrix products, arithmetic and copies ran while one was open for 21% -> 8% of each run, Pallas kernels for 0% -> 0%
where the time goes in v24:
time: 68.2 us; the launch traced here: 67.9 us
  waiting for transfers between devices  25.7 us (38%)
  matrix products  16.6 us (24%)
  starting transfers between devices  14.7 us (22%)
  other arithmetic  7.67 us (11%)
  local copies, waits for them, and re-layouts  2.99 us (4%)
    ppermute x10, waiting for transfers between devices, swap(): return lax.ppermute(x, axis, [(i, i ^ bit) for i in range(size)])  25.7 us
    ppermute x10, starting transfers between devices, swap(): return lax.ppermute(x, axis, [(i, i ^ bit) for i in range(size)])  14.7 us
    dot_general x1, matrix products, screened_of(): lax.dot_general(val_pairs, screen, (((0, 2), (0, 1)), ((), ())), preferre...  13.6 us
    mul x1, other arithmetic, screened_of(): val_pairs = valence_a[:, :, :, None, :] * valence_b[:, :, None, :, :]  3.9 us
    dot_general x4, matrix products, own_block(): jnp.einsum('pan,pbn->pab', screened, cond_pairs, preferred_element_type=j...  2.98 us
    another operation x2, local copies, waits for them, and re-layouts, gather_axis(): cur = jnp.where(low, jnp.stack([cur, got], 1), jnp.stack([got, cur], 1))  1.61 us
  transfers between devices with their start and end apart: 10, of which 9 were waited for; matrix products, arithmetic and copies ran while one was open for 8% of the time, Pallas kernels for 0%

profile of v24, /device:TPU:0, one launch (start us, length us, event | category | flops | bytes accessed | tf_op | source)
XLA Modules:
  0.0 67.9 jit_solution(11080796476295944849)
XLA Ops:
  0.0 0.8 %slice_bitcast_fusion.5 = (bf16[1,1,1,16,1024]{4,3,2,1,0:T(8,128)(2,1)S(1)}, bf16[1,1,16,1024]{3,2,0,1:T(8,128)(2,1)S(1)}) fusion(bf16[1,48,1024]{2,1,0:T(8,128)(2,1)} %param.3), kind=kLoop, calls=%fused_computation.37 | loop fusion | bytes 98304 | tf_op jit(solution)/shard_map/stack | solution.py:24
  0.8 4.0 %collective-permute-start = (bf16[1,1,16,1024]{3,2,0,1:T(8,128)(2,1)S(1)}, bf16[1,1,16,1024]{3,2,0,1:T(8,128)(2,1)S(1)}, u32[]{:S(2)}, u32[]{:S(2)}) collective-permute-start(bf16[1,1,16,1024]{3,2,0,1:T(8,128)(2,1)S(1)} %get-tuple-element.30), channel_id=1, source_target_pairs={{0,16},{4,20},{8,24},{12,28},{16,0},{20,4},{24,8},{28,12},{1,17},{... | collective-permute-start | bytes 98312 | tf_op jit(solution)/shard_map/ppermute | solution.py:13
  4.8 0.8 %slice_bitcast_fusion.3 = (bf16[1,1,1,32,1024]{4,3,2,1,0:T(8,128)(2,1)S(1)}, bf16[1,1,32,1024]{3,2,0,1:T(8,128)(2,1)S(1)}) fusion(bf16[1,48,1024]{2,1,0:T(8,128)(2,1)} %param.3), kind=kLoop, calls=%fused_computation.35 | loop fusion | bytes 196608 | tf_op jit(solution)/shard_map/stack | solution.py:24
  5.7 0.7 and_select_fusion
  6.4 0.6 collective-permute-done
  7.1 2.5 %collective-permute-start.1 = (bf16[2,1,16,1024]{3,2,0,1:T(8,128)(2,1)S(1)}, bf16[2,1,16,1024]{3,2,0,1:T(8,128)(2,1)S(1)}, u32[]{:S(2)}, u32[]{:S(2)}) collective-permute-start(bf16[2,1,16,1024]{3,2,0,1:T(8,128)(2,1)S(1)} %maximum_select_fusion.8), channel_id=1, source_target_pairs={{0,8},{4,12},{8,0},{12,4},{16,24},{20,28},{24,16},{28,20},{1,9},{5... | collective-permute-start | bytes 196616 | tf_op jit(solution)/shard_map/ppermute | solution.py:13
  9.5 1.6 %collective-permute-done.5 = bf16[1,1,32,1024]{3,2,0,1:T(8,128)(2,1)S(1)} collective-permute-done((bf16[1,1,32,1024]{3,2,0,1:T(8,128)(2,1)S(1)}, bf16[1,1,32,1024]{3,2,0,1:T(8,128)(2,1)S(1)}, u32[]{:S(2)}, u32[]{:S(2)}) %collective-permute-start.5) | collective-permute-done | bytes 65568 | tf_op jit(solution)/shard_map/ppermute | solution.py:13
  11.2 1.5 %collective-permute-start.6 = (bf16[2,1,32,1024]{3,2,0,1:T(8,128)(2,1)S(1)}, bf16[2,1,32,1024]{3,2,0,1:T(8,128)(2,1)S(1)}, u32[]{:S(2)}, u32[]{:S(2)}) collective-permute-start(bf16[2,1,32,1024]{3,2,0,1:T(8,128)(2,1)S(1)} %maximum_select_fusion.7), channel_id=1, source_target_pairs={{0,8},{4,12},{8,0},{12,4},{16,24},{20,28},{24,16},{28,20},{1,9},{5... | collective-permute-start | bytes 393224 | tf_op jit(solution)/shard_map/ppermute | solution.py:13
  12.8 1.6 %collective-permute-start.2 = (bf16[4,1,16,1024]{3,2,0,1:T(8,128)(2,1)S(1)}, bf16[4,1,16,1024]{3,2,0,1:T(8,128)(2,1)S(1)}, u32[]{:S(2)}, u32[]{:S(2)}) collective-permute-start(bf16[4,1,16,1024]{3,2,0,1:T(8,128)(2,1)S(1)} %bitcast.108), channel_id=1, source_target_pairs={{0,4},{4,0},{8,12},{12,8},{16,20},{20,16},{24,28},{28,24},{1,5},{5... | collective-permute-start | bytes 393224 | tf_op jit(solution)/shard_map/ppermute | solution.py:13
  14.4 1.9 %collective-permute-done.6 = bf16[2,1,32,1024]{3,2,0,1:T(8,128)(2,1)S(1)} collective-permute-done((bf16[2,1,32,1024]{3,2,0,1:T(8,128)(2,1)S(1)}, bf16[2,1,32,1024]{3,2,0,1:T(8,128)(2,1)S(1)}, u32[]{:S(2)}, u32[]{:S(2)}) %collective-permute-start.6) | collective-permute-done | bytes 131104 | tf_op jit(solution)/shard_map/ppermute | solution.py:13
  16.3 1.6 %collective-permute-start.7 = (bf16[4,1,32,1024]{3,2,0,1:T(8,128)(2,1)S(1)}, bf16[4,1,32,1024]{3,2,0,1:T(8,128)(2,1)S(1)}, u32[]{:S(2)}, u32[]{:S(2)}) collective-permute-start(bf16[4,1,32,1024]{3,2,0,1:T(8,128)(2,1)S(1)} %bitcast.104), channel_id=1, source_target_pairs={{0,4},{4,0},{8,12},{12,8},{16,20},{20,16},{24,28},{28,24},{1,5},{5... | collective-permute-start | bytes 786440 | tf_op jit(solution)/shard_map/ppermute | solution.py:13
  17.9 0.7 %pad_add_fusion = s32[8]{0:T(128)S(1)} fusion(s32[4]{0:T(128)S(1)} %and_select_fusion, s32[4]{0:T(128)} %bitcast.117), kind=kLoop, calls=%fused_computation.47 | loop fusion | flops 8 | bytes 64 | tf_op jit(solution)/shard_map/concatenate | solution.py:76
  18.6 0.5 collective-permute-done.2
  19.2 0.6 gather_fusion
  19.8 1.6 %collective-permute-start.3 = (bf16[1,8,16,1024]{3,2,1,0:T(8,128)(2,1)S(1)}, bf16[1,8,16,1024]{3,2,1,0:T(8,128)(2,1)S(1)}, u32[]{:S(2)}, u32[]{:S(2)}) collective-permute-start(bf16[1,8,16,1024]{3,2,1,0:T(8,128)(2,1)S(1)} %bitcast.99), channel_id=1, source_target_pairs={{0,2},{1,3},{2,0},{3,1},{4,6},{5,7},{6,4},{7,5},{8,10},{9,11},{10,... | collective-permute-start | bytes 786440 | tf_op jit(solution)/shard_map/ppermute | solution.py:13
  21.3 1.7 %collective-permute-done.7 = bf16[4,1,32,1024]{3,2,0,1:T(8,128)(2,1)S(1)} collective-permute-done((bf16[4,1,32,1024]{3,2,0,1:T(8,128)(2,1)S(1)}, bf16[4,1,32,1024]{3,2,0,1:T(8,128)(2,1)S(1)}, u32[]{:S(2)}, u32[]{:S(2)}) %collective-permute-start.7) | collective-permute-done | bytes 262176 | tf_op jit(solution)/shard_map/ppermute | solution.py:13
  23.1 0.6 gather_fusion.1
  23.8 2.4 %collective-permute-done.3 = bf16[1,8,16,1024]{3,2,1,0:T(8,128)(2,1)S(1)} collective-permute-done((bf16[1,8,16,1024]{3,2,1,0:T(8,128)(2,1)S(1)}, bf16[1,8,16,1024]{3,2,1,0:T(8,128)(2,1)S(1)}, u32[]{:S(2)}, u32[]{:S(2)}) %collective-permute-start.3) | collective-permute-done | bytes 262176 | tf_op jit(solution)/shard_map/ppermute | solution.py:13
  26.4 0.6 broadcast_multiply_fusion.1
  27.1 1.2 %collective-permute-done.4 = bf16[2,8,16,1024]{3,2,1,0:T(8,128)(2,1)S(1)} collective-permute-done((bf16[2,8,16,1024]{3,2,1,0:T(8,128)(2,1)S(1)}, bf16[2,8,16,1024]{3,2,1,0:T(8,128)(2,1)S(1)}, u32[]{:S(2)}, u32[]{:S(2)}) %collective-permute-start.4) | collective-permute-done | bytes 524320 | tf_op jit(solution)/shard_map/ppermute | solution.py:13
  28.3 0.2 maximum_select_fusion
  28.5 3.9 %broadcast_multiply_fusion = bf16[4,4,16,16,1024]{4,3,2,1,0:T(8,128)(2,1)} fusion(bf16[4,4,16,1024]{3,2,1,0:T(8,128)(2,1)S(1)} %get-tuple-element.16, bf16[4,4,16,1024]{3,2,1,0:T(8,128)(2,1)S(1)} %get-tuple-element.15), kind=kLoop, calls=%fused_computation.3 | loop fusion | flops 4194304 | bytes 9437184 | tf_op jit(solution)/shard_map/mul | solution.py:56
  32.4 13.6 %bitcast_convert_fusion = bf16[1024,1024]{1,0:T(8,128)(2,1)S(1)} fusion(bf16[4,1024,1024]{2,1,0:T(8,128)(2,1)} %bitcast.96, bf16[4,1024,1024]{2,1,0:T(8,128)(2,1)} %bitcast.116), kind=kOutput, calls=%fused_computation.2 | convolution fusion | flops 8590983168 | bytes 18874368 | tf_op jit(solution)/shard_map/dot_general | solution.py:59
  46.1 0.7 %convolution_bitcast_fusion = f32[1,4,256,256]{3,2,1,0:T(8,128)S(1)} fusion(bf16[4,256,1024]{2,1,0:T(8,128)(2,1)S(1)} %bitcast.89, bf16[4,256,1024]{2,1,0:T(8,128)(2,1)S(1)} %bitcast.95), kind=kOutput, calls=%fused_computation.5 | convolution fusion | flops 536870912 | bytes 5242880 | tf_op jit(solution)/shard_map/pan,pbn->pab/dot_general | solution.py:112
  46.8 0.7 %convolution_bitcast_fusion.1 = f32[1,4,256,256]{3,2,1,0:T(8,128)S(1)} fusion(bf16[4,256,1024]{2,1,0:T(8,128)(2,1)S(1)} %bitcast.90, bf16[4,256,1024]{2,1,0:T(8,128)(2,1)S(1)} %bitcast.94), kind=kOutput, calls=%fused_computation.6 | convolution fusion | flops 536870912 | bytes 5242880 | tf_op jit(solution)/shard_map/pan,pbn->pab/dot_general | solution.py:112
  47.7 0.2 collective-permute-start.8
  47.9 4.0 %collective-permute-done.8 = f32[2,4,256,256]{3,2,1,0:T(8,128)S(1)} collective-permute-done((f32[2,4,256,256]{3,2,1,0:T(8,128)S(1)}, f32[2,4,256,256]{3,2,1,0:T(8,128)S(1)}, u32[]{:S(2)}, u32[]{:S(2)}) %collective-permute-start.8) | collective-permute-done | bytes 2097184 | tf_op jit(solution)/shard_map/ppermute | solution.py:13
  52.0 0.8 %fusion.5 = bf16[1,4,256,256]{3,2,1,0:T(8,128)(2,1)S(1)} fusion(f32[2,4,256,256]{3,2,1,0:T(8,128)S(1)} %collective-permute-done.8, bf16[4,256,1024]{2,1,0:T(8,128)(2,1)S(1)} %bitcast.91, bf16[4,256,1024]{2,1,0:T(8,128)(2,1)S(1)} %bitcast.97), kind=kOutput, calls=%fused_computation.19 | convolution fusion | flops 537395200 | bytes 5767168 | tf_op jit(solution)/shard_map/pan,pbn->pab/dot_general | solution.py:112
  52.7 1.6 %collective-permute-start.9 = (bf16[1,4,256,256]{3,2,1,0:T(8,128)(2,1)S(1)}, bf16[1,4,256,256]{3,2,1,0:T(8,128)(2,1)S(1)}, u32[]{:S(2)}, u32[]{:S(2)}) collective-permute-start(bf16[1,4,256,256]{3,2,1,0:T(8,128)(2,1)S(1)} %fusion.5), channel_id=1, source_target_pairs={{0,2},{1,3},{2,0},{3,1},{4,6},{5,7},{6,4},{7,5},{8,10},{9,11},{10,... | collective-permute-start | bytes 1572872 | tf_op jit(solution)/shard_map/ppermute | solution.py:13
  54.3 0.7 %fusion.11 = f32[4,256,256]{2,1,0:T(8,128)S(1)} fusion(bf16[4,256,1024]{2,1,0:T(8,128)(2,1)S(1)} %bitcast.92, bf16[4,256,1024]{2,1,0:T(8,128)(2,1)S(1)} %bitcast.93), kind=kOutput, calls=%fused_computation.50 | convolution fusion | flops 536870912 | bytes 5242880 | tf_op jit(solution)/shard_map/pan,pbn->pab/dot_general | solution.py:112
  55.1 11.7 %collective-permute-done.9 = bf16[1,4,256,256]{3,2,1,0:T(8,128)(2,1)S(1)} collective-permute-done((bf16[1,4,256,256]{3,2,1,0:T(8,128)(2,1)S(1)}, bf16[1,4,256,256]{3,2,1,0:T(8,128)(2,1)S(1)}, u32[]{:S(2)}, u32[]{:S(2)}) %collective-permute-start.9) | collective-permute-done | bytes 524320 | tf_op jit(solution)/shard_map/ppermute | solution.py:13
  66.8 1.2 %fusion.4 = f32[1,4,256,256]{3,2,1,0:T(8,128)} fusion(f32[4,256,256]{2,1,0:T(8,128)S(1)} %fusion.11, f32[2,4,256,256]{3,2,1,0:T(8,128)S(1)} %collective-permute-done.8, bf16[1,4,256,256]{3,2,1,0:T(8,128)(2,1)S(1)} %collective-permute-done.9), kind=kLoop, calls=%fused_computation.13 | loop fusion | flops 786432 | bytes 3670016 | tf_op jit(solution)/shard_map/broadcast_in_dim | solution.py:124
  (20 shorter events, 0.9 us)
Async XLA Ops:
  0.8 6.3 %collective-permute-start = (bf16[1,1,16,1024]{3,2,0,1:T(8,128)(2,1)S(1)}, bf16[1,1,16,1024]{3,2,0,1:T(8,128)(2,1)S(1)}, u32[]{:S(2)}, u32[]{:S(2)}) collective-permute-start(bf16[1,1,16,1024]{3,2,0,1:T(8,128)(2,1)S(1)} %get-tuple-element.30), channel_id=1, source_target_pairs={{0,16},{4,20},{8,24},{12,28},{16,0},{20,4},{24,8},{28,12},{1,17},{... | collective-permute-start | bytes 98312 | tf_op jit(solution)/shard_map/ppermute | solution.py:13
  5.7 5.5 %collective-permute-start.5 = (bf16[1,1,32,1024]{3,2,0,1:T(8,128)(2,1)S(1)}, bf16[1,1,32,1024]{3,2,0,1:T(8,128)(2,1)S(1)}, u32[]{:S(2)}, u32[]{:S(2)}) collective-permute-start(bf16[1,1,32,1024]{3,2,0,1:T(8,128)(2,1)S(1)} %get-tuple-element.28), channel_id=1, source_target_pairs={{0,16},{4,20},{8,24},{12,28},{16,0},{20,4},{24,8},{28,12},{1,17},{... | collective-permute-start | bytes 196616 | tf_op jit(solution)/shard_map/ppermute | solution.py:13
  7.1 5.7 %collective-permute-start.1 = (bf16[2,1,16,1024]{3,2,0,1:T(8,128)(2,1)S(1)}, bf16[2,1,16,1024]{3,2,0,1:T(8,128)(2,1)S(1)}, u32[]{:S(2)}, u32[]{:S(2)}) collective-permute-start(bf16[2,1,16,1024]{3,2,0,1:T(8,128)(2,1)S(1)} %maximum_select_fusion.8), channel_id=1, source_target_pairs={{0,8},{4,12},{8,0},{12,4},{16,24},{20,28},{24,16},{28,20},{1,9},{5... | collective-permute-start | bytes 196616 | tf_op jit(solution)/shard_map/ppermute | solution.py:13
  11.2 5.0 %collective-permute-start.6 = (bf16[2,1,32,1024]{3,2,0,1:T(8,128)(2,1)S(1)}, bf16[2,1,32,1024]{3,2,0,1:T(8,128)(2,1)S(1)}, u32[]{:S(2)}, u32[]{:S(2)}) collective-permute-start(bf16[2,1,32,1024]{3,2,0,1:T(8,128)(2,1)S(1)} %maximum_select_fusion.7), channel_id=1, source_target_pairs={{0,8},{4,12},{8,0},{12,4},{16,24},{20,28},{24,16},{28,20},{1,9},{5... | collective-permute-start | bytes 393224 | tf_op jit(solution)/shard_map/ppermute | solution.py:13
  12.8 6.4 %collective-permute-start.2 = (bf16[4,1,16,1024]{3,2,0,1:T(8,128)(2,1)S(1)}, bf16[4,1,16,1024]{3,2,0,1:T(8,128)(2,1)S(1)}, u32[]{:S(2)}, u32[]{:S(2)}) collective-permute-start(bf16[4,1,16,1024]{3,2,0,1:T(8,128)(2,1)S(1)} %bitcast.108), channel_id=1, source_target_pairs={{0,4},{4,0},{8,12},{12,8},{16,20},{20,16},{24,28},{28,24},{1,5},{5... | collective-permute-start | bytes 393224 | tf_op jit(solution)/shard_map/ppermute | solution.py:13
  16.3 6.7 %collective-permute-start.7 = (bf16[4,1,32,1024]{3,2,0,1:T(8,128)(2,1)S(1)}, bf16[4,1,32,1024]{3,2,0,1:T(8,128)(2,1)S(1)}, u32[]{:S(2)}, u32[]{:S(2)}) collective-permute-start(bf16[4,1,32,1024]{3,2,0,1:T(8,128)(2,1)S(1)} %bitcast.104), channel_id=1, source_target_pairs={{0,4},{4,0},{8,12},{12,8},{16,20},{20,16},{24,28},{28,24},{1,5},{5... | collective-permute-start | bytes 786440 | tf_op jit(solution)/shard_map/ppermute | solution.py:13
  19.8 6.4 %collective-permute-start.3 = (bf16[1,8,16,1024]{3,2,1,0:T(8,128)(2,1)S(1)}, bf16[1,8,16,1024]{3,2,1,0:T(8,128)(2,1)S(1)}, u32[]{:S(2)}, u32[]{:S(2)}) collective-permute-start(bf16[1,8,16,1024]{3,2,1,0:T(8,128)(2,1)S(1)} %bitcast.99), channel_id=1, source_target_pairs={{0,2},{1,3},{2,0},{3,1},{4,6},{5,7},{6,4},{7,5},{8,10},{9,11},{10,... | collective-permute-start | bytes 786440 | tf_op jit(solution)/shard_map/ppermute | solution.py:13
  26.3 2.0 %collective-permute-start.4 = (bf16[2,8,16,1024]{3,2,1,0:T(8,128)(2,1)S(1)}, bf16[2,8,16,1024]{3,2,1,0:T(8,128)(2,1)S(1)}, u32[]{:S(2)}, u32[]{:S(2)}) collective-permute-start(bf16[2,8,16,1024]{3,2,1,0:T(8,128)(2,1)S(1)} %maximum_select_fusion.2), channel_id=1, source_target_pairs={{0,1},{1,0},{2,3},{3,2},{4,5},{5,4},{6,7},{7,6},{8,9},{9,8},{10,11... | collective-permute-start | bytes 1572872 | tf_op jit(solution)/shard_map/ppermute | solution.py:13
  47.7 4.2 %collective-permute-start.8 = (f32[2,4,256,256]{3,2,1,0:T(8,128)S(1)}, f32[2,4,256,256]{3,2,1,0:T(8,128)S(1)}, u32[]{:S(2)}, u32[]{:S(2)}) collective-permute-start(f32[2,4,256,256]{3,2,1,0:T(8,128)S(1)} %pad_maximum_fusion), channel_id=1, source_target_pairs={{0,1},{1,0},{2,3},{3,2},{4,5},{5,4},{6,7},{7,6},{8,9},{9,8},{10,11... | collective-permute-start | bytes 6291464 | tf_op jit(solution)/shard_map/ppermute | solution.py:13
  52.7 14.1 %collective-permute-start.9 = (bf16[1,4,256,256]{3,2,1,0:T(8,128)(2,1)S(1)}, bf16[1,4,256,256]{3,2,1,0:T(8,128)(2,1)S(1)}, u32[]{:S(2)}, u32[]{:S(2)}) collective-permute-start(bf16[1,4,256,256]{3,2,1,0:T(8,128)(2,1)S(1)} %fusion.5), channel_id=1, source_target_pairs={{0,2},{1,3},{2,0},{3,1},{4,6},{5,7},{6,4},{7,5},{8,10},{9,11},{10,... | collective-permute-start | bytes 1572872 | tf_op jit(solution)/shard_map/ppermute | solution.py:13

commit v25 on v21

--- a/solution.py
+++ b/solution.py
@@ -64,9 +64,7 @@
 
 def screened_of(valence_a, valence_b, screening):
     col_count, chunk, _, mu_cols = valence_a.shape
-    valence_a = valence_a.astype(jnp.float32)
-    valence_b = valence_b.astype(jnp.float32)
-    val_pairs = (valence_a[:, :, :, None, :] * valence_b[:, :, None, :, :]).astype(jnp.bfloat16)
+    val_pairs = valence_a[:, :, :, None, :] * valence_b[:, :, None, :, :]
     val_pairs = val_pairs.reshape(col_count, chunk * NV * NV, mu_cols)
     screen = screening.reshape(col_count, mu_cols, screening.shape[1])
     screened = lax.dot_general(
@@ -94,7 +92,7 @@
     )
 
     valence = gather_axis(jnp.take(held_valence, wanted, axis=0, mode="clip"), "col")
-    conduction = jnp.take(held_conduction, wanted, axis=0, mode="clip").astype(jnp.float32)
+    conduction = jnp.take(held_conduction, wanted, axis=0, mode="clip")
     rows_per_block = NC // col_count
     chunk = pair_count // PAIR_CHUNKS
     starts = list(range(0, pair_count, chunk))
@@ -105,7 +103,7 @@
         rows = lax.dynamic_slice_in_dim(
             cond_a, (col_index ^ delta) * rows_per_block, rows_per_block, 1
         )
-        cond_pairs = (rows[:, :, None, :] * cond_b[:, None, :, :]).astype(jnp.bfloat16)
+        cond_pairs = rows[:, :, None, :] * cond_b[:, None, :, :]
         return cond_pairs.reshape(chunk, rows_per_block * NC, mu_cols)
 
     cond_blocks = [[cond_block(first, d) for d in range(col_count)] for first in starts]

time: 62.5 us -> 59.5 us (0.952)
  other arithmetic: 9.4 us -> 4.82 us
  waiting for transfers between devices: 20 us -> 21 us
  local copies, waits for them, and re-layouts: 3.31 us -> 4.17 us
    convert_element_type x4 -> x0, other arithmetic: 6.12 us -> none  [the longest x1 3.09 us: cond_block(): (rows[:, :, None, :] * cond_b[:, None, :, :]).astype(jnp.bfloat16)]
    mul x0 -> x3, other arithmetic: none -> 1.51 us  [the longest x1 0.83 us: cond_block(): cond_pairs = rows[:, :, None, :] * cond_b[:, None, :, :]]
    ppermute x12, waiting for transfers between devices: 20 us -> 21 us  [swap(): return lax.ppermute(x, axis, [(i, i ^ bit) for i in range(size)])]
    unnamed x4, local copies, waits for them, and re-layouts: 0.36 us -> 1.2 us
  transfers between devices with their start and end apart: 12 -> 12, of which waited for: 8 -> 9; matrix products, arithmetic and copies ran while one was open for 26% -> 21% of each run, Pallas kernels for 0% -> 0%
where the time goes in v25:
time: 59.5 us; the launch traced here: 59.3 us
  waiting for transfers between devices  21 us (35%)
  starting transfers between devices  16.1 us (27%)
  matrix products  12.9 us (22%)
  other arithmetic  4.82 us (8%)
  local copies, waits for them, and re-layouts  4.17 us (7%)
    ppermute x12, waiting for transfers between devices, swap(): return lax.ppermute(x, axis, [(i, i ^ bit) for i in range(size)])  21 us
    ppermute x12, starting transfers between devices, swap(): return lax.ppermute(x, axis, [(i, i ^ bit) for i in range(size)])  16.1 us
    dot_general x2, matrix products, screened_of(): lax.dot_general(val_pairs, screen, (((0, 2), (0, 1)), ((), ())), preferre...  9.1 us
    dot_general x8, matrix products, own_block(): jnp.einsum('pan,pbn->pab', screened, cond_pairs, preferred_element_type=j...  3.76 us
    another operation x4, local copies, waits for them, and re-layouts, gather_axis_xor(): cur = jnp.stack([cur, got], 1).reshape((-1,) + mine.shape)  1.66 us
    unnamed x4, local copies, waits for them, and re-layouts  1.2 us
  transfers between devices with their start and end apart: 12, of which 9 were waited for; matrix products, arithmetic and copies ran while one was open for 21% of the time, Pallas kernels for 0%

profile of v25, /device:TPU:0, one launch (start us, length us, event | category | flops | bytes accessed | tf_op | source)
XLA Modules:
  0.0 59.3 jit_solution(14754785266587978862)
XLA Ops:
  0.0 0.8 %slice_bitcast_fusion.7 = (bf16[1,1,1,16,1024]{4,3,1,2,0:T(8,128)(2,1)S(1)}, bf16[1,1,16,1024]{3,2,1,0:T(8,128)(2,1)S(1)}) fusion(bf16[1,48,1024]{2,1,0:T(8,128)(2,1)} %param.3), kind=kLoop, calls=%fused_computation.51 | loop fusion | bytes 98304 | tf_op jit(solution)/shard_map/stack;broadcast_in_dim | solution.py:17
  0.8 4.0 %collective-permute-start = (bf16[1,1,16,1024]{3,2,1,0:T(8,128)(2,1)S(1)}, bf16[1,1,16,1024]{3,2,1,0:T(8,128)(2,1)S(1)}, u32[]{:S(2)}, u32[]{:S(2)}) collective-permute-start(bf16[1,1,16,1024]{3,2,1,0:T(8,128)(2,1)S(1)} %get-tuple-element.52), channel_id=1, source_target_pairs={{0,16},{4,20},{8,24},{12,28},{16,0},{20,4},{24,8},{28,12},{1,17},{... | collective-permute-start | bytes 98312 | tf_op jit(solution)/shard_map/ppermute | solution.py:24
  4.8 0.8 %slice_bitcast_fusion.5 = (bf16[1,1,1,32,1024]{4,3,1,2,0:T(8,128)(2,1)S(1)}, bf16[1,1,32,1024]{3,2,1,0:T(8,128)(2,1)S(1)}) fusion(bf16[1,48,1024]{2,1,0:T(8,128)(2,1)} %param.3), kind=kLoop, calls=%fused_computation.47 | loop fusion | bytes 196608 | tf_op jit(solution)/shard_map/stack;broadcast_in_dim | solution.py:17
  5.7 1.3 %collective-permute-done = bf16[1,1,16,1024]{3,2,1,0:T(8,128)(2,1)S(1)} collective-permute-done((bf16[1,1,16,1024]{3,2,1,0:T(8,128)(2,1)S(1)}, bf16[1,1,16,1024]{3,2,1,0:T(8,128)(2,1)S(1)}, u32[]{:S(2)}, u32[]{:S(2)}) %collective-permute-start) | collective-permute-done | bytes 32800 | tf_op jit(solution)/shard_map/ppermute | solution.py:24
  7.1 2.5 %collective-permute-start.1 = (bf16[2,1,16,1024]{3,2,0,1:T(8,128)(2,1)S(1)}, bf16[2,1,16,1024]{3,2,0,1:T(8,128)(2,1)S(1)}, u32[]{:S(2)}, u32[]{:S(2)}) collective-permute-start(bf16[2,1,16,1024]{3,2,0,1:T(8,128)(2,1)S(1)} %get-tuple-element.54), channel_id=1, source_target_pairs={{0,8},{4,12},{8,0},{12,4},{16,24},{20,28},{24,16},{28,20},{1,9},{5... | collective-permute-start | bytes 196616 | tf_op jit(solution)/shard_map/ppermute | solution.py:24
  9.5 1.7 %collective-permute-done.5 = bf16[1,1,32,1024]{3,2,1,0:T(8,128)(2,1)S(1)} collective-permute-done((bf16[1,1,32,1024]{3,2,1,0:T(8,128)(2,1)S(1)}, bf16[1,1,32,1024]{3,2,1,0:T(8,128)(2,1)S(1)}, u32[]{:S(2)}, u32[]{:S(2)}) %collective-permute-start.5) | collective-permute-done | bytes 65568 | tf_op jit(solution)/shard_map/ppermute | solution.py:24
  11.2 1.3 %collective-permute-start.6 = (bf16[2,1,32,1024]{3,2,0,1:T(8,128)(2,1)S(1)}, bf16[2,1,32,1024]{3,2,0,1:T(8,128)(2,1)S(1)}, u32[]{:S(2)}, u32[]{:S(2)}) collective-permute-start(bf16[2,1,32,1024]{3,2,0,1:T(8,128)(2,1)S(1)} %get-tuple-element.48), channel_id=1, source_target_pairs={{0,8},{4,12},{8,0},{12,4},{16,24},{20,28},{24,16},{28,20},{1,9},{5... | collective-permute-start | bytes 393224 | tf_op jit(solution)/shard_map/ppermute | solution.py:24
  12.5 0.7 %fusion.14 = s32[4,1]{0,1:T(1,128)S(1)} fusion(s32[1,4]{1,0:T(1,128)} %param.5, s32[]{:T(128)S(6)} %axis_index.29), kind=kLoop, calls=%fused_computation.64 | loop fusion | flops 48 | bytes 36 | tf_op jit(solution)/shard_map/concatenate | solution.py:87
  13.2 1.6 %collective-permute-start.2 = (bf16[4,1,16,1024]{3,2,0,1:T(8,128)(2,1)S(1)}, bf16[4,1,16,1024]{3,2,0,1:T(8,128)(2,1)S(1)}, u32[]{:S(2)}, u32[]{:S(2)}) collective-permute-start(bf16[4,1,16,1024]{3,2,0,1:T(8,128)(2,1)S(1)} %bitcast.161), channel_id=1, source_target_pairs={{0,4},{4,0},{8,12},{12,8},{16,20},{20,16},{24,28},{28,24},{1,5},{5... | collective-permute-start | bytes 393224 | tf_op jit(solution)/shard_map/ppermute | solution.py:24
  14.8 1.4 %collective-permute-done.6 = bf16[2,1,32,1024]{3,2,0,1:T(8,128)(2,1)S(1)} collective-permute-done((bf16[2,1,32,1024]{3,2,0,1:T(8,128)(2,1)S(1)}, bf16[2,1,32,1024]{3,2,0,1:T(8,128)(2,1)S(1)}, u32[]{:S(2)}, u32[]{:S(2)}) %collective-permute-start.6) | collective-permute-done | bytes 131104 | tf_op jit(solution)/shard_map/ppermute | solution.py:24
  16.3 1.6 %collective-permute-start.7 = (bf16[4,1,32,1024]{3,2,0,1:T(8,128)(2,1)S(1)}, bf16[4,1,32,1024]{3,2,0,1:T(8,128)(2,1)S(1)}, u32[]{:S(2)}, u32[]{:S(2)}) collective-permute-start(bf16[4,1,32,1024]{3,2,0,1:T(8,128)(2,1)S(1)} %bitcast.157), channel_id=1, source_target_pairs={{0,4},{4,0},{8,12},{12,8},{16,20},{20,16},{24,28},{28,24},{1,5},{5... | collective-permute-start | bytes 786440 | tf_op jit(solution)/shard_map/ppermute | solution.py:24
  17.9 0.7 %fusion.16 = s32[8]{0:T(128)S(1)} fusion(s32[4,1]{0,1:T(1,128)S(1)} %fusion.14, s32[4,1]{0,1:T(1,128)} %bitcast.169, s32[]{:T(128)S(6)} %axis_index.29), kind=kLoop, calls=%fused_computation.67 | loop fusion | flops 16 | bytes 68 | tf_op jit(solution)/shard_map/xor | solution.py:88
  18.6 1.0 %collective-permute-done.2 = bf16[4,1,16,1024]{3,2,0,1:T(8,128)(2,1)S(1)} collective-permute-done((bf16[4,1,16,1024]{3,2,0,1:T(8,128)(2,1)S(1)}, bf16[4,1,16,1024]{3,2,0,1:T(8,128)(2,1)S(1)}, u32[]{:S(2)}, u32[]{:S(2)}) %collective-permute-start.2) | collective-permute-done | bytes 131104 | tf_op jit(solution)/shard_map/ppermute | solution.py:24
  19.7 0.6 gather_fusion
  20.3 1.6 %collective-permute-start.3 = (bf16[1,8,16,1024]{3,2,1,0:T(8,128)(2,1)S(1)}, bf16[1,8,16,1024]{3,2,1,0:T(8,128)(2,1)S(1)}, u32[]{:S(2)}, u32[]{:S(2)}) collective-permute-start(bf16[1,8,16,1024]{3,2,1,0:T(8,128)(2,1)S(1)} %bitcast.152), channel_id=1, source_target_pairs={{0,2},{1,3},{2,0},{3,1},{4,6},{5,7},{6,4},{7,5},{8,10},{9,11},{10,... | collective-permute-start | bytes 786440 | tf_op jit(solution)/shard_map/ppermute | solution.py:24
  21.8 1.2 %collective-permute-done.7 = bf16[4,1,32,1024]{3,2,0,1:T(8,128)(2,1)S(1)} collective-permute-done((bf16[4,1,32,1024]{3,2,0,1:T(8,128)(2,1)S(1)}, bf16[4,1,32,1024]{3,2,0,1:T(8,128)(2,1)S(1)}, u32[]{:S(2)}, u32[]{:S(2)}) %collective-permute-start.7) | collective-permute-done | bytes 262176 | tf_op jit(solution)/shard_map/ppermute | solution.py:24
  23.1 0.6 gather_fusion.1
  23.8 2.9 %collective-permute-done.3 = bf16[1,8,16,1024]{3,2,1,0:T(8,128)(2,1)S(1)} collective-permute-done((bf16[1,8,16,1024]{3,2,1,0:T(8,128)(2,1)S(1)}, bf16[1,8,16,1024]{3,2,1,0:T(8,128)(2,1)S(1)}, u32[]{:S(2)}, u32[]{:S(2)}) %collective-permute-start.3) | collective-permute-done | bytes 262176 | tf_op jit(solution)/shard_map/ppermute | solution.py:24
  26.9 0.8 %broadcast_multiply_fusion.2 = (bf16[2,8,32,1024]{3,2,1,0:T(8,128)(2,1)S(1)}, bf16[2,8,32,1024]{3,2,1,0:T(8,128)(2,1)S(1)}, bf16[2,8,32,1024]{3,2,1,0:T(8,128)(2...) fusion(bf16[2,8,1024]{2,1,0:T(8,128)(2,1)S(1)} %get-tuple-eleme, ...), kind=kLoop, calls=%fused_computation.29 | loop fusion | flops 4194304 | bytes 8912896 | tf_op jit(solution)/shard_map/mul | solution.py:106
  27.8 0.9 %collective-permute-done.4 = bf16[2,8,16,1024]{3,2,1,0:T(8,128)(2,1)S(1)} collective-permute-done((bf16[2,8,16,1024]{3,2,1,0:T(8,128)(2,1)S(1)}, bf16[2,8,16,1024]{3,2,1,0:T(8,128)(2,1)S(1)}, u32[]{:S(2)}, u32[]{:S(2)}) %collective-permute-start.4) | collective-permute-done | bytes 524320 | tf_op jit(solution)/shard_map/ppermute | solution.py:24
  29.4 1.2 %slice-done.1 = s8[4194304]{0:T(1024)(128)(4,1)S(1)} async-done(((s8[8388608]{0:T(1024)(128)(4,1)}), s8[4194304]{0:T(1024)(128)(4,1)S(1)}, s32[]{:S(2)}) %slice-start.1) | async-done | bytes 4194328
  30.6 4.6 %bitcast_convert_fusion.1 = bf16[512,1024]{1,0:T(8,128)(2,1)S(1)} fusion(bf16[4,512,1024]{2,1,0:T(8,128)(2,1)S(1)} %bitcast.147, bf16[4,1024,1024]{2,1,0:T(8,128)(2,1)S(1)} %bitcast.172), kind=kOutput, calls=%fused_computation.3 | convolution fusion | flops 4295491584 | bytes 13631488 | tf_op jit(solution)/shard_map/dot_general | solution.py:70
  36.2 0.6 collective-permute-start.8
  37.1 4.6 %bitcast_convert_fusion = bf16[512,1024]{1,0:T(8,128)(2,1)S(1)} fusion(bf16[4,512,1024]{2,1,0:T(8,128)(2,1)S(1)} %bitcast.148, bf16[4,1024,1024]{2,1,0:T(8,128)(2,1)S(1)} %bitcast.173), kind=kOutput, calls=%fused_computation.2 | convolution fusion | flops 4295491584 | bytes 13631488 | tf_op jit(solution)/shard_map/dot_general | solution.py:70
  41.6 0.5 convolution_bitcast_fusion
  43.3 0.5 fusion.8
  43.7 1.6 %collective-permute-start.9 = (bf16[1,2,256,256]{3,2,1,0:T(8,128)(2,1)S(1)}, bf16[1,2,256,256]{3,2,1,0:T(8,128)(2,1)S(1)}, u32[]{:S(2)}, u32[]{:S(2)}) collective-permute-start(bf16[1,2,256,256]{3,2,1,0:T(8,128)(2,1)S(1)} %fusion.8), channel_id=1, source_target_pairs={{0,2},{1,3},{2,0},{3,1},{4,6},{5,7},{6,4},{7,5},{8,10},{9,11},{10,... | collective-permute-start | bytes 786440 | tf_op jit(solution)/shard_map/ppermute | solution.py:24
  45.8 0.5 fusion.9
  46.3 1.2 %collective-permute-start.11 = (bf16[1,2,256,256]{3,2,1,0:T(8,128)(2,1)S(1)}, bf16[1,2,256,256]{3,2,1,0:T(8,128)(2,1)S(1)}, u32[]{:S(2)}, u32[]{:S(2)}) collective-permute-start(bf16[1,2,256,256]{3,2,1,0:T(8,128)(2,1)S(1)} %fusion.9), channel_id=1, source_target_pairs={{0,2},{1,3},{2,0},{3,1},{4,6},{5,7},{6,4},{7,5},{8,10},{9,11},{10,... | collective-permute-start | bytes 786440 | tf_op jit(solution)/shard_map/ppermute | solution.py:24
  47.5 5.5 %collective-permute-done.9 = bf16[1,2,256,256]{3,2,1,0:T(8,128)(2,1)S(1)} collective-permute-done((bf16[1,2,256,256]{3,2,1,0:T(8,128)(2,1)S(1)}, bf16[1,2,256,256]{3,2,1,0:T(8,128)(2,1)S(1)}, u32[]{:S(2)}, u32[]{:S(2)}) %collective-permute-start.9) | collective-permute-done | bytes 262176 | tf_op jit(solution)/shard_map/ppermute | solution.py:24
  53.0 5.1 %collective-permute-done.11 = bf16[1,2,256,256]{3,2,1,0:T(8,128)(2,1)S(1)} collective-permute-done((bf16[1,2,256,256]{3,2,1,0:T(8,128)(2,1)S(1)}, bf16[1,2,256,256]{3,2,1,0:T(8,128)(2,1)S(1)}, u32[]{:S(2)}, u32[]{:S(2)}) %collective-permute-start.11) | collective-permute-done | bytes 262176 | tf_op jit(solution)/shard_map/ppermute | solution.py:24
  58.2 1.0 %maximum_bitcast_fusion = f32[1,4,256,256]{3,2,1,0:T(8,128)} fusion(f32[2,256,256]{2,1,0:T(8,128)S(1)} %fusion.3, f32[2,256,256]{2,1,0:T(8,128)S(1)} %fusion.7), kind=kLoop, calls=%fused_computation.13 | loop fusion | flops 262144 | bytes 2097152 | tf_op jit(solution)/shard_map/broadcast_in_dim | solution.py:136
  (37 shorter events, 4.4 us)
Async XLA Ops:
  0.8 6.3 %collective-permute-start = (bf16[1,1,16,1024]{3,2,1,0:T(8,128)(2,1)S(1)}, bf16[1,1,16,1024]{3,2,1,0:T(8,128)(2,1)S(1)}, u32[]{:S(2)}, u32[]{:S(2)}) collective-permute-start(bf16[1,1,16,1024]{3,2,1,0:T(8,128)(2,1)S(1)} %get-tuple-element.52), channel_id=1, source_target_pairs={{0,16},{4,20},{8,24},{12,28},{16,0},{20,4},{24,8},{28,12},{1,17},{... | collective-permute-start | bytes 98312 | tf_op jit(solution)/shard_map/ppermute | solution.py:24
  5.7 5.5 %collective-permute-start.5 = (bf16[1,1,32,1024]{3,2,1,0:T(8,128)(2,1)S(1)}, bf16[1,1,32,1024]{3,2,1,0:T(8,128)(2,1)S(1)}, u32[]{:S(2)}, u32[]{:S(2)}) collective-permute-start(bf16[1,1,32,1024]{3,2,1,0:T(8,128)(2,1)S(1)} %get-tuple-element.50), channel_id=1, source_target_pairs={{0,16},{4,20},{8,24},{12,28},{16,0},{20,4},{24,8},{28,12},{1,17},{... | collective-permute-start | bytes 196616 | tf_op jit(solution)/shard_map/ppermute | solution.py:24
  7.1 6.2 %collective-permute-start.1 = (bf16[2,1,16,1024]{3,2,0,1:T(8,128)(2,1)S(1)}, bf16[2,1,16,1024]{3,2,0,1:T(8,128)(2,1)S(1)}, u32[]{:S(2)}, u32[]{:S(2)}) collective-permute-start(bf16[2,1,16,1024]{3,2,0,1:T(8,128)(2,1)S(1)} %get-tuple-element.54), channel_id=1, source_target_pairs={{0,8},{4,12},{8,0},{12,4},{16,24},{20,28},{24,16},{28,20},{1,9},{5... | collective-permute-start | bytes 196616 | tf_op jit(solution)/shard_map/ppermute | solution.py:24
  11.2 5.0 %collective-permute-start.6 = (bf16[2,1,32,1024]{3,2,0,1:T(8,128)(2,1)S(1)}, bf16[2,1,32,1024]{3,2,0,1:T(8,128)(2,1)S(1)}, u32[]{:S(2)}, u32[]{:S(2)}) collective-permute-start(bf16[2,1,32,1024]{3,2,0,1:T(8,128)(2,1)S(1)} %get-tuple-element.48), channel_id=1, source_target_pairs={{0,8},{4,12},{8,0},{12,4},{16,24},{20,28},{24,16},{28,20},{1,9},{5... | collective-permute-start | bytes 393224 | tf_op jit(solution)/shard_map/ppermute | solution.py:24
  13.2 6.4 %collective-permute-start.2 = (bf16[4,1,16,1024]{3,2,0,1:T(8,128)(2,1)S(1)}, bf16[4,1,16,1024]{3,2,0,1:T(8,128)(2,1)S(1)}, u32[]{:S(2)}, u32[]{:S(2)}) collective-permute-start(bf16[4,1,16,1024]{3,2,0,1:T(8,128)(2,1)S(1)} %bitcast.161), channel_id=1, source_target_pairs={{0,4},{4,0},{8,12},{12,8},{16,20},{20,16},{24,28},{28,24},{1,5},{5... | collective-permute-start | bytes 393224 | tf_op jit(solution)/shard_map/ppermute | solution.py:24
  16.3 6.7 %collective-permute-start.7 = (bf16[4,1,32,1024]{3,2,0,1:T(8,128)(2,1)S(1)}, bf16[4,1,32,1024]{3,2,0,1:T(8,128)(2,1)S(1)}, u32[]{:S(2)}, u32[]{:S(2)}) collective-permute-start(bf16[4,1,32,1024]{3,2,0,1:T(8,128)(2,1)S(1)} %bitcast.157), channel_id=1, source_target_pairs={{0,4},{4,0},{8,12},{12,8},{16,20},{20,16},{24,28},{28,24},{1,5},{5... | collective-permute-start | bytes 786440 | tf_op jit(solution)/shard_map/ppermute | solution.py:24
  20.3 6.4 %collective-permute-start.3 = (bf16[1,8,16,1024]{3,2,1,0:T(8,128)(2,1)S(1)}, bf16[1,8,16,1024]{3,2,1,0:T(8,128)(2,1)S(1)}, u32[]{:S(2)}, u32[]{:S(2)}) collective-permute-start(bf16[1,8,16,1024]{3,2,1,0:T(8,128)(2,1)S(1)} %bitcast.152), channel_id=1, source_target_pairs={{0,2},{1,3},{2,0},{3,1},{4,6},{5,7},{6,4},{7,5},{8,10},{9,11},{10,... | collective-permute-start | bytes 786440 | tf_op jit(solution)/shard_map/ppermute | solution.py:24
  26.8 2.0 %collective-permute-start.4 = (bf16[2,8,16,1024]{3,2,1,0:T(8,128)(2,1)S(1)}, bf16[2,8,16,1024]{3,2,1,0:T(8,128)(2,1)S(1)}, u32[]{:S(2)}, u32[]{:S(2)}) collective-permute-start(bf16[2,8,16,1024]{3,2,1,0:T(8,128)(2,1)S(1)} %maximum_select_fusion.2), channel_id=1, source_target_pairs={{0,1},{1,0},{2,3},{3,2},{4,5},{5,4},{6,7},{7,6},{8,9},{9,8},{10,11... | collective-permute-start | bytes 1572872 | tf_op jit(solution)/shard_map/ppermute | solution.py:24
  26.9 2.5 %slice-start = ((s8[8388608]{0:T(1024)(128)(4,1)}), s8[4194304]{0:T(1024)(128)(4,1)S(1)}, s32[]{:S(2)}) async-start(s8[8388608]{0:T(1024)(128)(4,1)} %bitcast.170), calls=%async_computation | async-start | bytes 8388608
  27.7 2.8 %slice-start.1 = ((s8[8388608]{0:T(1024)(128)(4,1)}), s8[4194304]{0:T(1024)(128)(4,1)S(1)}, s32[]{:S(2)}) async-start(s8[8388608]{0:T(1024)(128)(4,1)} %bitcast.170), calls=%async_computation.1 | async-start | bytes 8388608
  36.2 7.1 %collective-permute-start.8 = (f32[2,2,256,256]{3,2,1,0:T(8,128)S(1)}, f32[2,2,256,256]{3,2,1,0:T(8,128)S(1)}, u32[]{:S(2)}, u32[]{:S(2)}) collective-permute-start(f32[2,2,256,256]{3,2,1,0:T(8,128)S(1)} %pad_maximum_fusion), channel_id=1, source_target_pairs={{0,1},{1,0},{2,3},{3,2},{4,5},{5,4},{6,7},{7,6},{8,9},{9,8},{10,11... | collective-permute-start | bytes 3145736 | tf_op jit(solution)/shard_map/ppermute | solution.py:24
  42.7 3.1 %collective-permute-start.10 = (f32[2,2,256,256]{3,2,1,0:T(8,128)S(1)}, f32[2,2,256,256]{3,2,1,0:T(8,128)S(1)}, u32[]{:S(2)}, u32[]{:S(2)}) collective-permute-start(f32[2,2,256,256]{3,2,1,0:T(8,128)S(1)} %pad_maximum_fusion.1), channel_id=1, source_target_pairs={{0,1},{1,0},{2,3},{3,2},{4,5},{5,4},{6,7},{7,6},{8,9},{9,8},{10,11... | collective-permute-start | bytes 3145736 | tf_op jit(solution)/shard_map/ppermute | solution.py:24
  43.7 9.2 %collective-permute-start.9 = (bf16[1,2,256,256]{3,2,1,0:T(8,128)(2,1)S(1)}, bf16[1,2,256,256]{3,2,1,0:T(8,128)(2,1)S(1)}, u32[]{:S(2)}, u32[]{:S(2)}) collective-permute-start(bf16[1,2,256,256]{3,2,1,0:T(8,128)(2,1)S(1)} %fusion.8), channel_id=1, source_target_pairs={{0,2},{1,3},{2,0},{3,1},{4,6},{5,7},{6,4},{7,5},{8,10},{9,11},{10,... | collective-permute-start | bytes 786440 | tf_op jit(solution)/shard_map/ppermute | solution.py:24
  46.3 11.9 %collective-permute-start.11 = (bf16[1,2,256,256]{3,2,1,0:T(8,128)(2,1)S(1)}, bf16[1,2,256,256]{3,2,1,0:T(8,128)(2,1)S(1)}, u32[]{:S(2)}, u32[]{:S(2)}) collective-permute-start(bf16[1,2,256,256]{3,2,1,0:T(8,128)(2,1)S(1)} %fusion.9), channel_id=1, source_target_pairs={{0,2},{1,3},{2,0},{3,1},{4,6},{5,7},{6,4},{7,5},{8,10},{9,11},{10,... | collective-permute-start | bytes 786440 | tf_op jit(solution)/shard_map/ppermute | solution.py:24

commit v26 on v24

--- a/solution.py
+++ b/solution.py
@@ -5,7 +5,7 @@
 
 NV = 16
 NC = 32
-PAIR_CHUNKS = 1
+PAIR_CHUNKS = 4
 
 
 def swap(x, axis, bit):

time: 68.2 us -> 60.5 us (0.89)
  waiting for transfers between devices: 25.7 us -> 18.4 us
  starting transfers between devices: 14.7 us -> 18.5 us
  other arithmetic: 7.67 us -> 4.78 us
  matrix products: 16.6 us -> 15.2 us
    ppermute x10 -> x16, waiting for transfers between devices: 25.7 us -> 18.4 us  [swap(): return lax.ppermute(x, axis, [(i, i ^ bit) for i in range(size)])]
    dot_general x1 -> x4, matrix products: 13.6 us -> 9.73 us  [screened_of(): lax.dot_general(val_pairs, screen, (((0, 2), (0, 1)), ((), ())), preferre...]
    ppermute x10 -> x16, starting transfers between devices: 14.7 us -> 18.5 us  [swap(): return lax.ppermute(x, axis, [(i, i ^ bit) for i in range(size)])]
    mul x1 -> x4, other arithmetic: 3.9 us -> 0.69 us  [screened_of(): val_pairs = valence_a[:, :, :, None, :] * valence_b[:, :, None, :, :]]
    dot_general x4 -> x16, matrix products: 2.98 us -> 5.43 us  [own_block(): jnp.einsum('pan,pbn->pab', screened, cond_pairs, preferred_element_type=j...]
  transfers between devices with their start and end apart: 10 -> 16, of which waited for: 9 -> 11; matrix products, arithmetic and copies ran while one was open for 8% -> 29% of each run, Pallas kernels for 0% -> 0%
where the time goes in v26:
time: 60.5 us; the launch traced here: 60.3 us
  starting transfers between devices  18.5 us (31%)
  waiting for transfers between devices  18.4 us (30%)
  matrix products  15.2 us (25%)
  other arithmetic  4.78 us (8%)
  local copies, waits for them, and re-layouts  3.02 us (5%)
    ppermute x16, starting transfers between devices, swap(): return lax.ppermute(x, axis, [(i, i ^ bit) for i in range(size)])  18.5 us
    ppermute x16, waiting for transfers between devices, swap(): return lax.ppermute(x, axis, [(i, i ^ bit) for i in range(size)])  18.4 us
    dot_general x4, matrix products, screened_of(): lax.dot_general(val_pairs, screen, (((0, 2), (0, 1)), ((), ())), preferre...  9.73 us
    dot_general x16, matrix products, own_block(): jnp.einsum('pan,pbn->pab', screened, cond_pairs, preferred_element_type=j...  5.43 us
    another operation x2, local copies, waits for them, and re-layouts, gather_axis(): cur = jnp.where(low, jnp.stack([cur, got], 1), jnp.stack([got, cur], 1))  1.61 us
  transfers between devices with their start and end apart: 16, of which 11 were waited for; matrix products, arithmetic and copies ran while one was open for 29% of the time, Pallas kernels for 0%

profile of v26, /device:TPU:0, one launch (start us, length us, event | category | flops | bytes accessed | tf_op | source)
XLA Modules:
  0.0 60.3 jit_solution(1377821450403453794)
XLA Ops:
  0.0 0.8 %slice_bitcast_fusion.23 = (bf16[1,1,1,16,1024]{4,3,2,1,0:T(8,128)(2,1)S(1)}, bf16[1,1,16,1024]{3,2,0,1:T(8,128)(2,1)S(1)}) fusion(bf16[1,48,1024]{2,1,0:T(8,128)(2,1)} %param.3), kind=kLoop, calls=%fused_computation.129 | loop fusion | bytes 98304 | tf_op jit(solution)/shard_map/stack | solution.py:24
  0.8 4.0 %collective-permute-start = (bf16[1,1,16,1024]{3,2,0,1:T(8,128)(2,1)S(1)}, bf16[1,1,16,1024]{3,2,0,1:T(8,128)(2,1)S(1)}, u32[]{:S(2)}, u32[]{:S(2)}) collective-permute-start(bf16[1,1,16,1024]{3,2,0,1:T(8,128)(2,1)S(1)} %get-tuple-element.58), channel_id=1, source_target_pairs={{0,16},{4,20},{8,24},{12,28},{16,0},{20,4},{24,8},{28,12},{1,17},{... | collective-permute-start | bytes 98312 | tf_op jit(solution)/shard_map/ppermute | solution.py:13
  4.8 0.8 %slice_bitcast_fusion.21 = (bf16[1,1,1,32,1024]{4,3,2,1,0:T(8,128)(2,1)S(1)}, bf16[1,1,32,1024]{3,2,0,1:T(8,128)(2,1)S(1)}) fusion(bf16[1,48,1024]{2,1,0:T(8,128)(2,1)} %param.3), kind=kLoop, calls=%fused_computation.127 | loop fusion | bytes 196608 | tf_op jit(solution)/shard_map/stack | solution.py:24
  5.7 0.7 %and_select_fusion = s32[4]{0:T(128)S(1)} fusion(s32[]{:T(128)S(6)} %axis_index.17, s32[1,4]{1,0:T(1,128)} %param.5), kind=kLoop, calls=%fused_computation.149 | loop fusion | flops 48 | bytes 36 | tf_op jit(solution)/shard_map/jit(remainder)/select_n | solution.py:73
  6.4 0.6 %collective-permute-done = bf16[1,1,16,1024]{3,2,0,1:T(8,128)(2,1)S(1)} collective-permute-done((bf16[1,1,16,1024]{3,2,0,1:T(8,128)(2,1)S(1)}, bf16[1,1,16,1024]{3,2,0,1:T(8,128)(2,1)S(1)}, u32[]{:S(2)}, u32[]{:S(2)}) %collective-permute-start) | collective-permute-done | bytes 32800 | tf_op jit(solution)/shard_map/ppermute | solution.py:13
  7.1 2.5 %collective-permute-start.1 = (bf16[2,1,16,1024]{3,2,0,1:T(8,128)(2,1)S(1)}, bf16[2,1,16,1024]{3,2,0,1:T(8,128)(2,1)S(1)}, u32[]{:S(2)}, u32[]{:S(2)}) collective-permute-start(bf16[2,1,16,1024]{3,2,0,1:T(8,128)(2,1)S(1)} %maximum_select_fusion.8), channel_id=1, source_target_pairs={{0,8},{4,12},{8,0},{12,4},{16,24},{20,28},{24,16},{28,20},{1,9},{5... | collective-permute-start | bytes 196616 | tf_op jit(solution)/shard_map/ppermute | solution.py:13
  9.5 1.6 %collective-permute-done.5 = bf16[1,1,32,1024]{3,2,0,1:T(8,128)(2,1)S(1)} collective-permute-done((bf16[1,1,32,1024]{3,2,0,1:T(8,128)(2,1)S(1)}, bf16[1,1,32,1024]{3,2,0,1:T(8,128)(2,1)S(1)}, u32[]{:S(2)}, u32[]{:S(2)}) %collective-permute-start.5) | collective-permute-done | bytes 65568 | tf_op jit(solution)/shard_map/ppermute | solution.py:13
  11.2 1.5 %collective-permute-start.6 = (bf16[2,1,32,1024]{3,2,0,1:T(8,128)(2,1)S(1)}, bf16[2,1,32,1024]{3,2,0,1:T(8,128)(2,1)S(1)}, u32[]{:S(2)}, u32[]{:S(2)}) collective-permute-start(bf16[2,1,32,1024]{3,2,0,1:T(8,128)(2,1)S(1)} %maximum_select_fusion.7), channel_id=1, source_target_pairs={{0,8},{4,12},{8,0},{12,4},{16,24},{20,28},{24,16},{28,20},{1,9},{5... | collective-permute-start | bytes 393224 | tf_op jit(solution)/shard_map/ppermute | solution.py:13
  12.8 1.6 %collective-permute-start.2 = (bf16[4,1,16,1024]{3,2,0,1:T(8,128)(2,1)S(1)}, bf16[4,1,16,1024]{3,2,0,1:T(8,128)(2,1)S(1)}, u32[]{:S(2)}, u32[]{:S(2)}) collective-permute-start(bf16[4,1,16,1024]{3,2,0,1:T(8,128)(2,1)S(1)} %bitcast.356), channel_id=1, source_target_pairs={{0,4},{4,0},{8,12},{12,8},{16,20},{20,16},{24,28},{28,24},{1,5},{5... | collective-permute-start | bytes 393224 | tf_op jit(solution)/shard_map/ppermute | solution.py:13
  14.4 1.9 %collective-permute-done.6 = bf16[2,1,32,1024]{3,2,0,1:T(8,128)(2,1)S(1)} collective-permute-done((bf16[2,1,32,1024]{3,2,0,1:T(8,128)(2,1)S(1)}, bf16[2,1,32,1024]{3,2,0,1:T(8,128)(2,1)S(1)}, u32[]{:S(2)}, u32[]{:S(2)}) %collective-permute-start.6) | collective-permute-done | bytes 131104 | tf_op jit(solution)/shard_map/ppermute | solution.py:13
  16.3 1.6 %collective-permute-start.7 = (bf16[4,1,32,1024]{3,2,0,1:T(8,128)(2,1)S(1)}, bf16[4,1,32,1024]{3,2,0,1:T(8,128)(2,1)S(1)}, u32[]{:S(2)}, u32[]{:S(2)}) collective-permute-start(bf16[4,1,32,1024]{3,2,0,1:T(8,128)(2,1)S(1)} %bitcast.352), channel_id=1, source_target_pairs={{0,4},{4,0},{8,12},{12,8},{16,20},{20,16},{24,28},{28,24},{1,5},{5... | collective-permute-start | bytes 786440 | tf_op jit(solution)/shard_map/ppermute | solution.py:13
  17.9 0.7 %pad_add_fusion = s32[8]{0:T(128)S(1)} fusion(s32[4]{0:T(128)S(1)} %and_select_fusion, s32[4]{0:T(128)} %bitcast.370), kind=kLoop, calls=%fused_computation.151 | loop fusion | flops 8 | bytes 64 | tf_op jit(solution)/shard_map/concatenate | solution.py:76
  18.6 0.5 collective-permute-done.2
  19.2 0.6 gather_fusion
  19.8 1.6 %collective-permute-start.3 = (bf16[1,8,16,1024]{3,2,1,0:T(8,128)(2,1)S(1)}, bf16[1,8,16,1024]{3,2,1,0:T(8,128)(2,1)S(1)}, u32[]{:S(2)}, u32[]{:S(2)}) collective-permute-start(bf16[1,8,16,1024]{3,2,1,0:T(8,128)(2,1)S(1)} %bitcast.327), channel_id=1, source_target_pairs={{0,2},{1,3},{2,0},{3,1},{4,6},{5,7},{6,4},{7,5},{8,10},{9,11},{10,... | collective-permute-start | bytes 786440 | tf_op jit(solution)/shard_map/ppermute | solution.py:13
  21.3 1.7 %collective-permute-done.7 = bf16[4,1,32,1024]{3,2,0,1:T(8,128)(2,1)S(1)} collective-permute-done((bf16[4,1,32,1024]{3,2,0,1:T(8,128)(2,1)S(1)}, bf16[4,1,32,1024]{3,2,0,1:T(8,128)(2,1)S(1)}, u32[]{:S(2)}, u32[]{:S(2)}) %collective-permute-start.7) | collective-permute-done | bytes 262176 | tf_op jit(solution)/shard_map/ppermute | solution.py:13
  23.1 0.6 gather_fusion.1
  24.3 1.9 %collective-permute-done.3 = bf16[1,8,16,1024]{3,2,1,0:T(8,128)(2,1)S(1)} collective-permute-done((bf16[1,8,16,1024]{3,2,1,0:T(8,128)(2,1)S(1)}, bf16[1,8,16,1024]{3,2,1,0:T(8,128)(2,1)S(1)}, u32[]{:S(2)}, u32[]{:S(2)}) %collective-permute-start.3) | collective-permute-done | bytes 262176 | tf_op jit(solution)/shard_map/ppermute | solution.py:13
  26.9 1.3 %collective-permute-done.4 = bf16[2,8,16,1024]{3,2,1,0:T(8,128)(2,1)S(1)} collective-permute-done((bf16[2,8,16,1024]{3,2,1,0:T(8,128)(2,1)S(1)}, bf16[2,8,16,1024]{3,2,1,0:T(8,128)(2,1)S(1)}, u32[]{:S(2)}, u32[]{:S(2)}) %collective-permute-start.4) | collective-permute-done | bytes 524320 | tf_op jit(solution)/shard_map/ppermute | solution.py:13
  28.7 2.4 %fusion = bf16[256,1024]{1,0:T(8,128)(2,1)S(1)} fusion(bf16[4,256,1024]{2,1,0:T(8,128)(2,1)S(1)} %bitcast.342, bf16[4,1024,1024]{2,1,0:T(8,128)(2,1)S(1)} %bitcast.366), kind=kOutput, calls=%fused_computation.6 | convolution fusion | flops 2147745792 | bytes 11010048 | tf_op jit(solution)/shard_map/dot_general | solution.py:59
  32.8 2.4 %fusion.3 = bf16[256,1024]{1,0:T(8,128)(2,1)S(1)} fusion(bf16[4,256,1024]{2,1,0:T(8,128)(2,1)S(1)} %bitcast.343, bf16[4,1024,1024]{2,1,0:T(8,128)(2,1)S(1)} %bitcast.367), kind=kOutput, calls=%fused_computation.9 | convolution fusion | flops 2147745792 | bytes 11010048 | tf_op jit(solution)/shard_map/dot_general | solution.py:59
  36.7 2.4 %fusion.2 = bf16[256,1024]{1,0:T(8,128)(2,1)S(1)} fusion(bf16[4,256,1024]{2,1,0:T(8,128)(2,1)S(1)} %bitcast.344, bf16[4,1024,1024]{2,1,0:T(8,128)(2,1)S(1)} %bitcast.368), kind=kOutput, calls=%fused_computation.8 | convolution fusion | flops 2147745792 | bytes 11010048 | tf_op jit(solution)/shard_map/dot_general | solution.py:59
  40.7 2.6 %fusion.1 = bf16[256,1024]{1,0:T(8,128)(2,1)S(1)} fusion(bf16[4,256,1024]{2,1,0:T(8,128)(2,1)S(1)} %bitcast.345, bf16[4,1024,1024]{2,1,0:T(8,128)(2,1)S(1)} %bitcast.369), kind=kOutput, calls=%fused_computation.7 | convolution fusion | flops 2147745792 | bytes 11010048 | tf_op jit(solution)/shard_map/dot_general | solution.py:59
  45.0 1.6 %collective-permute-start.9 = (bf16[1,1,256,256]{3,2,1,0:T(8,128)(2,1)S(1)}, bf16[1,1,256,256]{3,2,1,0:T(8,128)(2,1)S(1)}, u32[]{:S(2)}, u32[]{:S(2)}) collective-permute-start(bf16[1,1,256,256]{3,2,1,0:T(8,128)(2,1)S(1)} %fusion.48), channel_id=1, source_target_pairs={{0,2},{1,3},{2,0},{3,1},{4,6},{5,7},{6,4},{7,5},{8,10},{9,11},{10,... | collective-permute-start | bytes 393224 | tf_op jit(solution)/shard_map/ppermute | solution.py:13
  46.9 0.6 collective-permute-start.15
  47.8 1.6 %collective-permute-start.13 = (bf16[1,1,256,256]{3,2,1,0:T(8,128)(2,1)S(1)}, bf16[1,1,256,256]{3,2,1,0:T(8,128)(2,1)S(1)}, u32[]{:S(2)}, u32[]{:S(2)}) collective-permute-start(bf16[1,1,256,256]{3,2,1,0:T(8,128)(2,1)S(1)} %fusion.50), channel_id=1, source_target_pairs={{0,2},{1,3},{2,0},{3,1},{4,6},{5,7},{6,4},{7,5},{8,10},{9,11},{10,... | collective-permute-start | bytes 393224 | tf_op jit(solution)/shard_map/ppermute | solution.py:13
  49.8 0.6 collective-permute-start.11
  50.3 1.0 %collective-permute-done.9 = bf16[1,1,256,256]{3,2,1,0:T(8,128)(2,1)S(1)} collective-permute-done((bf16[1,1,256,256]{3,2,1,0:T(8,128)(2,1)S(1)}, bf16[1,1,256,256]{3,2,1,0:T(8,128)(2,1)S(1)}, u32[]{:S(2)}, u32[]{:S(2)}) %collective-permute-start.9) | collective-permute-done | bytes 131104 | tf_op jit(solution)/shard_map/ppermute | solution.py:13
  51.4 2.8 %collective-permute-done.15 = bf16[1,1,256,256]{3,2,1,0:T(8,128)(2,1)S(1)} collective-permute-done((bf16[1,1,256,256]{3,2,1,0:T(8,128)(2,1)S(1)}, bf16[1,1,256,256]{3,2,1,0:T(8,128)(2,1)S(1)}, u32[]{:S(2)}, u32[]{:S(2)}) %collective-permute-start.15) | collective-permute-done | bytes 131104 | tf_op jit(solution)/shard_map/ppermute | solution.py:13
  54.2 2.8 %collective-permute-done.13 = bf16[1,1,256,256]{3,2,1,0:T(8,128)(2,1)S(1)} collective-permute-done((bf16[1,1,256,256]{3,2,1,0:T(8,128)(2,1)S(1)}, bf16[1,1,256,256]{3,2,1,0:T(8,128)(2,1)S(1)}, u32[]{:S(2)}, u32[]{:S(2)}) %collective-permute-start.13) | collective-permute-done | bytes 131104 | tf_op jit(solution)/shard_map/ppermute | solution.py:13
  57.0 2.2 %collective-permute-done.11 = bf16[1,1,256,256]{3,2,1,0:T(8,128)(2,1)S(1)} collective-permute-done((bf16[1,1,256,256]{3,2,1,0:T(8,128)(2,1)S(1)}, bf16[1,1,256,256]{3,2,1,0:T(8,128)(2,1)S(1)}, u32[]{:S(2)}, u32[]{:S(2)}) %collective-permute-start.11) | collective-permute-done | bytes 131104 | tf_op jit(solution)/shard_map/ppermute | solution.py:13
  59.3 1.0 %maximum_bitcast_fusion = f32[1,4,256,256]{3,2,1,0:T(8,128)} fusion(f32[1,256,256]{2,1,0:T(8,128)S(1)} %fusion.32, f32[1,256,256]{2,1,0:T(8,128)S(1)} %fusion.37, f32[1,256,256]{2,1,0:T(8,128)S(1)} %fusion.42, f32[1,256,256]{2,1,0:T(8,128)S(1)} %fusion.47), kind=kLoop, calls=%fused_computation.19 | loop fusion | flops 786432 | bytes 2097152 | tf_op jit(solution)/shard_map/broadcast_in_dim | solution.py:124
  (66 shorter events, 9.5 us)
Async XLA Ops:
  0.8 6.3 %collective-permute-start = (bf16[1,1,16,1024]{3,2,0,1:T(8,128)(2,1)S(1)}, bf16[1,1,16,1024]{3,2,0,1:T(8,128)(2,1)S(1)}, u32[]{:S(2)}, u32[]{:S(2)}) collective-permute-start(bf16[1,1,16,1024]{3,2,0,1:T(8,128)(2,1)S(1)} %get-tuple-element.58), channel_id=1, source_target_pairs={{0,16},{4,20},{8,24},{12,28},{16,0},{20,4},{24,8},{28,12},{1,17},{... | collective-permute-start | bytes 98312 | tf_op jit(solution)/shard_map/ppermute | solution.py:13
  5.7 5.5 %collective-permute-start.5 = (bf16[1,1,32,1024]{3,2,0,1:T(8,128)(2,1)S(1)}, bf16[1,1,32,1024]{3,2,0,1:T(8,128)(2,1)S(1)}, u32[]{:S(2)}, u32[]{:S(2)}) collective-permute-start(bf16[1,1,32,1024]{3,2,0,1:T(8,128)(2,1)S(1)} %get-tuple-element.56), channel_id=1, source_target_pairs={{0,16},{4,20},{8,24},{12,28},{16,0},{20,4},{24,8},{28,12},{1,17},{... | collective-permute-start | bytes 196616 | tf_op jit(solution)/shard_map/ppermute | solution.py:13
  7.1 5.7 %collective-permute-start.1 = (bf16[2,1,16,1024]{3,2,0,1:T(8,128)(2,1)S(1)}, bf16[2,1,16,1024]{3,2,0,1:T(8,128)(2,1)S(1)}, u32[]{:S(2)}, u32[]{:S(2)}) collective-permute-start(bf16[2,1,16,1024]{3,2,0,1:T(8,128)(2,1)S(1)} %maximum_select_fusion.8), channel_id=1, source_target_pairs={{0,8},{4,12},{8,0},{12,4},{16,24},{20,28},{24,16},{28,20},{1,9},{5... | collective-permute-start | bytes 196616 | tf_op jit(solution)/shard_map/ppermute | solution.py:13
  11.2 5.0 %collective-permute-start.6 = (bf16[2,1,32,1024]{3,2,0,1:T(8,128)(2,1)S(1)}, bf16[2,1,32,1024]{3,2,0,1:T(8,128)(2,1)S(1)}, u32[]{:S(2)}, u32[]{:S(2)}) collective-permute-start(bf16[2,1,32,1024]{3,2,0,1:T(8,128)(2,1)S(1)} %maximum_select_fusion.7), channel_id=1, source_target_pairs={{0,8},{4,12},{8,0},{12,4},{16,24},{20,28},{24,16},{28,20},{1,9},{5... | collective-permute-start | bytes 393224 | tf_op jit(solution)/shard_map/ppermute | solution.py:13
  12.8 6.4 %collective-permute-start.2 = (bf16[4,1,16,1024]{3,2,0,1:T(8,128)(2,1)S(1)}, bf16[4,1,16,1024]{3,2,0,1:T(8,128)(2,1)S(1)}, u32[]{:S(2)}, u32[]{:S(2)}) collective-permute-start(bf16[4,1,16,1024]{3,2,0,1:T(8,128)(2,1)S(1)} %bitcast.356), channel_id=1, source_target_pairs={{0,4},{4,0},{8,12},{12,8},{16,20},{20,16},{24,28},{28,24},{1,5},{5... | collective-permute-start | bytes 393224 | tf_op jit(solution)/shard_map/ppermute | solution.py:13
  16.3 6.7 %collective-permute-start.7 = (bf16[4,1,32,1024]{3,2,0,1:T(8,128)(2,1)S(1)}, bf16[4,1,32,1024]{3,2,0,1:T(8,128)(2,1)S(1)}, u32[]{:S(2)}, u32[]{:S(2)}) collective-permute-start(bf16[4,1,32,1024]{3,2,0,1:T(8,128)(2,1)S(1)} %bitcast.352), channel_id=1, source_target_pairs={{0,4},{4,0},{8,12},{12,8},{16,20},{20,16},{24,28},{28,24},{1,5},{5... | collective-permute-start | bytes 786440 | tf_op jit(solution)/shard_map/ppermute | solution.py:13
  19.8 6.4 %collective-permute-start.3 = (bf16[1,8,16,1024]{3,2,1,0:T(8,128)(2,1)S(1)}, bf16[1,8,16,1024]{3,2,1,0:T(8,128)(2,1)S(1)}, u32[]{:S(2)}, u32[]{:S(2)}) collective-permute-start(bf16[1,8,16,1024]{3,2,1,0:T(8,128)(2,1)S(1)} %bitcast.327), channel_id=1, source_target_pairs={{0,2},{1,3},{2,0},{3,1},{4,6},{5,7},{6,4},{7,5},{8,10},{9,11},{10,... | collective-permute-start | bytes 786440 | tf_op jit(solution)/shard_map/ppermute | solution.py:13
  23.9 4.8 %slice-start = ((s8[8388608]{0:T(1024)(128)(4,1)}), s8[4194304]{0:T(1024)(128)(4,1)S(1)}, s32[]{:S(2)}) async-start(s8[8388608]{0:T(1024)(128)(4,1)} %bitcast.364), calls=%async_computation | async-start | bytes 8388608
  26.3 2.0 %collective-permute-start.4 = (bf16[2,8,16,1024]{3,2,1,0:T(8,128)(2,1)S(1)}, bf16[2,8,16,1024]{3,2,1,0:T(8,128)(2,1)S(1)}, u32[]{:S(2)}, u32[]{:S(2)}) collective-permute-start(bf16[2,8,16,1024]{3,2,1,0:T(8,128)(2,1)S(1)} %maximum_select_fusion.2), channel_id=1, source_target_pairs={{0,1},{1,0},{2,3},{3,2},{4,5},{5,4},{6,7},{7,6},{8,9},{9,8},{10,11... | collective-permute-start | bytes 1572872 | tf_op jit(solution)/shard_map/ppermute | solution.py:13
  26.4 2.3 %slice-start.1 = ((s8[8388608]{0:T(1024)(128)(4,1)}), s8[4194304]{0:T(1024)(128)(4,1)S(1)}, s32[]{:S(2)}) async-start(s8[8388608]{0:T(1024)(128)(4,1)} %bitcast.364), calls=%async_computation.1 | async-start | bytes 8388608
  32.2 12.4 %collective-permute-start.8 = (f32[2,1,256,256]{3,2,1,0:T(8,128)S(1)}, f32[2,1,256,256]{3,2,1,0:T(8,128)S(1)}, u32[]{:S(2)}, u32[]{:S(2)}) collective-permute-start(f32[2,1,256,256]{3,2,1,0:T(8,128)S(1)} %pad_maximum_fusion), channel_id=1, source_target_pairs={{0,1},{1,0},{2,3},{3,2},{4,5},{5,4},{6,7},{7,6},{8,9},{9,8},{10,11... | collective-permute-start | bytes 1572872 | tf_op jit(solution)/shard_map/ppermute | solution.py:13
  36.3 10.3 %collective-permute-start.14 = (f32[2,1,256,256]{3,2,1,0:T(8,128)S(1)}, f32[2,1,256,256]{3,2,1,0:T(8,128)S(1)}, u32[]{:S(2)}, u32[]{:S(2)}) collective-permute-start(f32[2,1,256,256]{3,2,1,0:T(8,128)S(1)} %pad_maximum_fusion.3), channel_id=1, source_target_pairs={{0,1},{1,0},{2,3},{3,2},{4,5},{5,4},{6,7},{7,6},{8,9},{9,8},{10,11... | collective-permute-start | bytes 1572872 | tf_op jit(solution)/shard_map/ppermute | solution.py:13
  40.1 7.4 %collective-permute-start.12 = (f32[2,1,256,256]{3,2,1,0:T(8,128)S(1)}, f32[2,1,256,256]{3,2,1,0:T(8,128)S(1)}, u32[]{:S(2)}, u32[]{:S(2)}) collective-permute-start(f32[2,1,256,256]{3,2,1,0:T(8,128)S(1)} %pad_maximum_fusion.2), channel_id=1, source_target_pairs={{0,1},{1,0},{2,3},{3,2},{4,5},{5,4},{6,7},{7,6},{8,9},{9,8},{10,11... | collective-permute-start | bytes 1572872 | tf_op jit(solution)/shard_map/ppermute | solution.py:13
  44.0 5.4 %collective-permute-start.10 = (f32[2,1,256,256]{3,2,1,0:T(8,128)S(1)}, f32[2,1,256,256]{3,2,1,0:T(8,128)S(1)}, u32[]{:S(2)}, u32[]{:S(2)}) collective-permute-start(f32[2,1,256,256]{3,2,1,0:T(8,128)S(1)} %pad_maximum_fusion.1), channel_id=1, source_target_pairs={{0,1},{1,0},{2,3},{3,2},{4,5},{5,4},{6,7},{7,6},{8,9},{9,8},{10,11... | collective-permute-start | bytes 1572872 | tf_op jit(solution)/shard_map/ppermute | solution.py:13
  45.0 6.4 %collective-permute-start.9 = (bf16[1,1,256,256]{3,2,1,0:T(8,128)(2,1)S(1)}, bf16[1,1,256,256]{3,2,1,0:T(8,128)(2,1)S(1)}, u32[]{:S(2)}, u32[]{:S(2)}) collective-permute-start(bf16[1,1,256,256]{3,2,1,0:T(8,128)(2,1)S(1)} %fusion.48), channel_id=1, source_target_pairs={{0,2},{1,3},{2,0},{3,1},{4,6},{5,7},{6,4},{7,5},{8,10},{9,11},{10,... | collective-permute-start | bytes 393224 | tf_op jit(solution)/shard_map/ppermute | solution.py:13
  46.9 7.3 %collective-permute-start.15 = (bf16[1,1,256,256]{3,2,1,0:T(8,128)(2,1)S(1)}, bf16[1,1,256,256]{3,2,1,0:T(8,128)(2,1)S(1)}, u32[]{:S(2)}, u32[]{:S(2)}) collective-permute-start(bf16[1,1,256,256]{3,2,1,0:T(8,128)(2,1)S(1)} %fusion.51), channel_id=1, source_target_pairs={{0,2},{1,3},{2,0},{3,1},{4,6},{5,7},{6,4},{7,5},{8,10},{9,11},{10,... | collective-permute-start | bytes 393224 | tf_op jit(solution)/shard_map/ppermute | solution.py:13
  47.8 9.1 %collective-permute-start.13 = (bf16[1,1,256,256]{3,2,1,0:T(8,128)(2,1)S(1)}, bf16[1,1,256,256]{3,2,1,0:T(8,128)(2,1)S(1)}, u32[]{:S(2)}, u32[]{:S(2)}) collective-permute-start(bf16[1,1,256,256]{3,2,1,0:T(8,128)(2,1)S(1)} %fusion.50), channel_id=1, source_target_pairs={{0,2},{1,3},{2,0},{3,1},{4,6},{5,7},{6,4},{7,5},{8,10},{9,11},{10,... | collective-permute-start | bytes 393224 | tf_op jit(solution)/shard_map/ppermute | solution.py:13
  49.8 9.5 %collective-permute-start.11 = (bf16[1,1,256,256]{3,2,1,0:T(8,128)(2,1)S(1)}, bf16[1,1,256,256]{3,2,1,0:T(8,128)(2,1)S(1)}, u32[]{:S(2)}, u32[]{:S(2)}) collective-permute-start(bf16[1,1,256,256]{3,2,1,0:T(8,128)(2,1)S(1)} %fusion.49), channel_id=1, source_target_pairs={{0,2},{1,3},{2,0},{3,1},{4,6},{5,7},{6,4},{7,5},{8,10},{9,11},{10,... | collective-permute-start | bytes 393224 | tf_op jit(solution)/shard_map/ppermute | solution.py:13

commit v27 on v23

--- a/solution.py
+++ b/solution.py
@@ -89,8 +89,8 @@
         cond_a = conduction[first : first + chunk]
         cond_b = conduction[pair_count + first : pair_count + first + chunk]
         rows = lax.dynamic_slice_in_dim(
-            cond_a, (col_index ^ delta) * rows_per_block, rows_per_block, 1
-        )
+            cond_a.astype(jnp.float32), (col_index ^ delta) * rows_per_block, rows_per_block, 1
+        ).astype(jnp.bfloat16)
         cond_pairs = rows[:, :, None, :] * cond_b[:, None, :, :]
         return cond_pairs.reshape(chunk, rows_per_block * NC, mu_cols)
 

time: 59 us -> 59 us (level)
  no operation moved by 1% of the time
where the time goes in v27:
time: 59 us; the launch traced here: 58.8 us
  waiting for transfers between devices  20.2 us (34%)
  starting transfers between devices  16.3 us (28%)
  matrix products  12.9 us (22%)
  other arithmetic  4.86 us (8%)
  local copies, waits for them, and re-layouts  4.18 us (7%)
    ppermute x12, waiting for transfers between devices, swap(): return lax.ppermute(x, axis, [(i, i ^ bit) for i in range(size)])  20.2 us
    ppermute x12, starting transfers between devices, swap(): return lax.ppermute(x, axis, [(i, i ^ bit) for i in range(size)])  16.3 us
    dot_general x2, matrix products, screened_of(): lax.dot_general(val_pairs, screen, (((0, 2), (0, 1)), ((), ())), preferre...  9.1 us
    dot_general x8, matrix products, own_block(): jnp.einsum('pan,pbn->pab', screened, cond_pairs, preferred_element_type=j...  3.76 us
    another operation x2, local copies, waits for them, and re-layouts, gather_axis(): cur = jnp.where(low, jnp.stack([cur, got], 1), jnp.stack([got, cur], 1))  1.61 us
    unnamed x4, local copies, waits for them, and re-layouts  1.2 us
  transfers between devices with their start and end apart: 12, of which 9 were waited for; matrix products, arithmetic and copies ran while one was open for 21% of the time, Pallas kernels for 0%

profile of v27, /device:TPU:0, one launch (start us, length us, event | category | flops | bytes accessed | tf_op | source)
XLA Modules:
  0.0 58.8 jit_solution(16025702240703920607)
XLA Ops:
  0.0 0.8 %slice_bitcast_fusion.7 = (bf16[1,1,1,16,1024]{4,3,2,1,0:T(8,128)(2,1)S(1)}, bf16[1,1,16,1024]{3,2,0,1:T(8,128)(2,1)S(1)}) fusion(bf16[1,48,1024]{2,1,0:T(8,128)(2,1)} %param.3), kind=kLoop, calls=%fused_computation.63 | loop fusion | bytes 98304 | tf_op jit(solution)/shard_map/stack | solution.py:24
  0.8 4.0 %collective-permute-start = (bf16[1,1,16,1024]{3,2,0,1:T(8,128)(2,1)S(1)}, bf16[1,1,16,1024]{3,2,0,1:T(8,128)(2,1)S(1)}, u32[]{:S(2)}, u32[]{:S(2)}) collective-permute-start(bf16[1,1,16,1024]{3,2,0,1:T(8,128)(2,1)S(1)} %get-tuple-element.50), channel_id=1, source_target_pairs={{0,16},{4,20},{8,24},{12,28},{16,0},{20,4},{24,8},{28,12},{1,17},{... | collective-permute-start | bytes 98312 | tf_op jit(solution)/shard_map/ppermute | solution.py:13
  4.8 0.8 %slice_bitcast_fusion.5 = (bf16[1,1,1,32,1024]{4,3,2,1,0:T(8,128)(2,1)S(1)}, bf16[1,1,32,1024]{3,2,0,1:T(8,128)(2,1)S(1)}) fusion(bf16[1,48,1024]{2,1,0:T(8,128)(2,1)} %param.3), kind=kLoop, calls=%fused_computation.61 | loop fusion | bytes 196608 | tf_op jit(solution)/shard_map/stack | solution.py:24
  5.7 0.7 %and_select_fusion = s32[4]{0:T(128)S(1)} fusion(s32[]{:T(128)S(6)} %axis_index.17, s32[1,4]{1,0:T(1,128)} %param.5), kind=kLoop, calls=%fused_computation.67 | loop fusion | flops 48 | bytes 36 | tf_op jit(solution)/shard_map/jit(remainder)/select_n | solution.py:73
  6.4 0.6 %collective-permute-done = bf16[1,1,16,1024]{3,2,0,1:T(8,128)(2,1)S(1)} collective-permute-done((bf16[1,1,16,1024]{3,2,0,1:T(8,128)(2,1)S(1)}, bf16[1,1,16,1024]{3,2,0,1:T(8,128)(2,1)S(1)}, u32[]{:S(2)}, u32[]{:S(2)}) %collective-permute-start) | collective-permute-done | bytes 32800 | tf_op jit(solution)/shard_map/ppermute | solution.py:13
  7.1 2.5 %collective-permute-start.1 = (bf16[2,1,16,1024]{3,2,0,1:T(8,128)(2,1)S(1)}, bf16[2,1,16,1024]{3,2,0,1:T(8,128)(2,1)S(1)}, u32[]{:S(2)}, u32[]{:S(2)}) collective-permute-start(bf16[2,1,16,1024]{3,2,0,1:T(8,128)(2,1)S(1)} %maximum_select_fusion.8), channel_id=1, source_target_pairs={{0,8},{4,12},{8,0},{12,4},{16,24},{20,28},{24,16},{28,20},{1,9},{5... | collective-permute-start | bytes 196616 | tf_op jit(solution)/shard_map/ppermute | solution.py:13
  9.5 1.6 %collective-permute-done.5 = bf16[1,1,32,1024]{3,2,0,1:T(8,128)(2,1)S(1)} collective-permute-done((bf16[1,1,32,1024]{3,2,0,1:T(8,128)(2,1)S(1)}, bf16[1,1,32,1024]{3,2,0,1:T(8,128)(2,1)S(1)}, u32[]{:S(2)}, u32[]{:S(2)}) %collective-permute-start.5) | collective-permute-done | bytes 65568 | tf_op jit(solution)/shard_map/ppermute | solution.py:13
  11.2 1.5 %collective-permute-start.6 = (bf16[2,1,32,1024]{3,2,0,1:T(8,128)(2,1)S(1)}, bf16[2,1,32,1024]{3,2,0,1:T(8,128)(2,1)S(1)}, u32[]{:S(2)}, u32[]{:S(2)}) collective-permute-start(bf16[2,1,32,1024]{3,2,0,1:T(8,128)(2,1)S(1)} %maximum_select_fusion.7), channel_id=1, source_target_pairs={{0,8},{4,12},{8,0},{12,4},{16,24},{20,28},{24,16},{28,20},{1,9},{5... | collective-permute-start | bytes 393224 | tf_op jit(solution)/shard_map/ppermute | solution.py:13
  12.8 1.6 %collective-permute-start.2 = (bf16[4,1,16,1024]{3,2,0,1:T(8,128)(2,1)S(1)}, bf16[4,1,16,1024]{3,2,0,1:T(8,128)(2,1)S(1)}, u32[]{:S(2)}, u32[]{:S(2)}) collective-permute-start(bf16[4,1,16,1024]{3,2,0,1:T(8,128)(2,1)S(1)} %bitcast.156), channel_id=1, source_target_pairs={{0,4},{4,0},{8,12},{12,8},{16,20},{20,16},{24,28},{28,24},{1,5},{5... | collective-permute-start | bytes 393224 | tf_op jit(solution)/shard_map/ppermute | solution.py:13
  14.4 1.9 %collective-permute-done.6 = bf16[2,1,32,1024]{3,2,0,1:T(8,128)(2,1)S(1)} collective-permute-done((bf16[2,1,32,1024]{3,2,0,1:T(8,128)(2,1)S(1)}, bf16[2,1,32,1024]{3,2,0,1:T(8,128)(2,1)S(1)}, u32[]{:S(2)}, u32[]{:S(2)}) %collective-permute-start.6) | collective-permute-done | bytes 131104 | tf_op jit(solution)/shard_map/ppermute | solution.py:13
  16.3 1.6 %collective-permute-start.7 = (bf16[4,1,32,1024]{3,2,0,1:T(8,128)(2,1)S(1)}, bf16[4,1,32,1024]{3,2,0,1:T(8,128)(2,1)S(1)}, u32[]{:S(2)}, u32[]{:S(2)}) collective-permute-start(bf16[4,1,32,1024]{3,2,0,1:T(8,128)(2,1)S(1)} %bitcast.152), channel_id=1, source_target_pairs={{0,4},{4,0},{8,12},{12,8},{16,20},{20,16},{24,28},{28,24},{1,5},{5... | collective-permute-start | bytes 786440 | tf_op jit(solution)/shard_map/ppermute | solution.py:13
  17.9 0.7 %pad_add_fusion = s32[8]{0:T(128)S(1)} fusion(s32[4]{0:T(128)S(1)} %and_select_fusion, s32[4]{0:T(128)} %bitcast.168), kind=kLoop, calls=%fused_computation.69 | loop fusion | flops 8 | bytes 64 | tf_op jit(solution)/shard_map/concatenate | solution.py:76
  18.6 0.5 collective-permute-done.2
  19.2 0.6 gather_fusion
  19.8 1.6 %collective-permute-start.3 = (bf16[1,8,16,1024]{3,2,1,0:T(8,128)(2,1)S(1)}, bf16[1,8,16,1024]{3,2,1,0:T(8,128)(2,1)S(1)}, u32[]{:S(2)}, u32[]{:S(2)}) collective-permute-start(bf16[1,8,16,1024]{3,2,1,0:T(8,128)(2,1)S(1)} %bitcast.147), channel_id=1, source_target_pairs={{0,2},{1,3},{2,0},{3,1},{4,6},{5,7},{6,4},{7,5},{8,10},{9,11},{10,... | collective-permute-start | bytes 786440 | tf_op jit(solution)/shard_map/ppermute | solution.py:13
  21.3 1.7 %collective-permute-done.7 = bf16[4,1,32,1024]{3,2,0,1:T(8,128)(2,1)S(1)} collective-permute-done((bf16[4,1,32,1024]{3,2,0,1:T(8,128)(2,1)S(1)}, bf16[4,1,32,1024]{3,2,0,1:T(8,128)(2,1)S(1)}, u32[]{:S(2)}, u32[]{:S(2)}) %collective-permute-start.7) | collective-permute-done | bytes 262176 | tf_op jit(solution)/shard_map/ppermute | solution.py:13
  23.1 0.6 gather_fusion.1
  23.8 2.4 %collective-permute-done.3 = bf16[1,8,16,1024]{3,2,1,0:T(8,128)(2,1)S(1)} collective-permute-done((bf16[1,8,16,1024]{3,2,1,0:T(8,128)(2,1)S(1)}, bf16[1,8,16,1024]{3,2,1,0:T(8,128)(2,1)S(1)}, u32[]{:S(2)}, u32[]{:S(2)}) %collective-permute-start.3) | collective-permute-done | bytes 262176 | tf_op jit(solution)/shard_map/ppermute | solution.py:13
  26.4 0.8 %broadcast_multiply_fusion.2 = (bf16[2,8,32,1024]{3,2,1,0:T(8,128)(2,1)S(1)}, bf16[2,8,32,1024]{3,2,1,0:T(8,128)(2,1)S(1)}, bf16[2,8,32,1024]{3,2,1,0:T(8,128)(2...) fusion(bf16[2,8,1024]{2,1,0:T(8,128)(2,1)S(1)} %get-tuple-eleme, ...), kind=kLoop, calls=%fused_computation.29 | loop fusion | flops 4194304 | bytes 8912896 | tf_op jit(solution)/shard_map/mul | solution.py:94
  27.3 0.9 %collective-permute-done.4 = bf16[2,8,16,1024]{3,2,1,0:T(8,128)(2,1)S(1)} collective-permute-done((bf16[2,8,16,1024]{3,2,1,0:T(8,128)(2,1)S(1)}, bf16[2,8,16,1024]{3,2,1,0:T(8,128)(2,1)S(1)}, u32[]{:S(2)}, u32[]{:S(2)}) %collective-permute-start.4) | collective-permute-done | bytes 524320 | tf_op jit(solution)/shard_map/ppermute | solution.py:13
  28.9 1.2 %slice-done.1 = s8[4194304]{0:T(1024)(128)(4,1)S(1)} async-done(((s8[8388608]{0:T(1024)(128)(4,1)}), s8[4194304]{0:T(1024)(128)(4,1)S(1)}, s32[]{:S(2)}) %slice-start.1) | async-done | bytes 4194328
  30.1 4.6 %bitcast_convert_fusion.1 = bf16[512,1024]{1,0:T(8,128)(2,1)S(1)} fusion(bf16[4,512,1024]{2,1,0:T(8,128)(2,1)S(1)} %bitcast.142, bf16[4,1024,1024]{2,1,0:T(8,128)(2,1)S(1)} %bitcast.166), kind=kOutput, calls=%fused_computation.3 | convolution fusion | flops 4295491584 | bytes 13631488 | tf_op jit(solution)/shard_map/dot_general | solution.py:59
  34.6 0.5 convolution_bitcast_fusion.2
  35.7 0.6 collective-permute-start.8
  36.6 4.6 %bitcast_convert_fusion = bf16[512,1024]{1,0:T(8,128)(2,1)S(1)} fusion(bf16[4,512,1024]{2,1,0:T(8,128)(2,1)S(1)} %bitcast.143, bf16[4,1024,1024]{2,1,0:T(8,128)(2,1)S(1)} %bitcast.167), kind=kOutput, calls=%fused_computation.2 | convolution fusion | flops 4295491584 | bytes 13631488 | tf_op jit(solution)/shard_map/dot_general | solution.py:59
  41.6 0.5 convolution_bitcast_fusion.1
  43.2 1.6 %collective-permute-start.9 = (bf16[1,2,256,256]{3,2,1,0:T(8,128)(2,1)S(1)}, bf16[1,2,256,256]{3,2,1,0:T(8,128)(2,1)S(1)}, u32[]{:S(2)}, u32[]{:S(2)}) collective-permute-start(bf16[1,2,256,256]{3,2,1,0:T(8,128)(2,1)S(1)} %fusion.8), channel_id=1, source_target_pairs={{0,2},{1,3},{2,0},{3,1},{4,6},{5,7},{6,4},{7,5},{8,10},{9,11},{10,... | collective-permute-start | bytes 786440 | tf_op jit(solution)/shard_map/ppermute | solution.py:13
  45.3 0.5 fusion.9
  45.8 1.2 %collective-permute-start.11 = (bf16[1,2,256,256]{3,2,1,0:T(8,128)(2,1)S(1)}, bf16[1,2,256,256]{3,2,1,0:T(8,128)(2,1)S(1)}, u32[]{:S(2)}, u32[]{:S(2)}) collective-permute-start(bf16[1,2,256,256]{3,2,1,0:T(8,128)(2,1)S(1)} %fusion.9), channel_id=1, source_target_pairs={{0,2},{1,3},{2,0},{3,1},{4,6},{5,7},{6,4},{7,5},{8,10},{9,11},{10,... | collective-permute-start | bytes 786440 | tf_op jit(solution)/shard_map/ppermute | solution.py:13
  47.0 5.4 %collective-permute-done.9 = bf16[1,2,256,256]{3,2,1,0:T(8,128)(2,1)S(1)} collective-permute-done((bf16[1,2,256,256]{3,2,1,0:T(8,128)(2,1)S(1)}, bf16[1,2,256,256]{3,2,1,0:T(8,128)(2,1)S(1)}, u32[]{:S(2)}, u32[]{:S(2)}) %collective-permute-start.9) | collective-permute-done | bytes 262176 | tf_op jit(solution)/shard_map/ppermute | solution.py:13
  52.5 5.1 %collective-permute-done.11 = bf16[1,2,256,256]{3,2,1,0:T(8,128)(2,1)S(1)} collective-permute-done((bf16[1,2,256,256]{3,2,1,0:T(8,128)(2,1)S(1)}, bf16[1,2,256,256]{3,2,1,0:T(8,128)(2,1)S(1)}, u32[]{:S(2)}, u32[]{:S(2)}) %collective-permute-start.11) | collective-permute-done | bytes 262176 | tf_op jit(solution)/shard_map/ppermute | solution.py:13
  57.7 1.0 %maximum_bitcast_fusion = f32[1,4,256,256]{3,2,1,0:T(8,128)} fusion(f32[2,256,256]{2,1,0:T(8,128)S(1)} %fusion.3, f32[2,256,256]{2,1,0:T(8,128)S(1)} %fusion.7), kind=kLoop, calls=%fused_computation.13 | loop fusion | flops 262144 | bytes 2097152 | tf_op jit(solution)/shard_map/broadcast_in_dim | solution.py:124
  (39 shorter events, 4.4 us)
Async XLA Ops:
  0.8 6.3 %collective-permute-start = (bf16[1,1,16,1024]{3,2,0,1:T(8,128)(2,1)S(1)}, bf16[1,1,16,1024]{3,2,0,1:T(8,128)(2,1)S(1)}, u32[]{:S(2)}, u32[]{:S(2)}) collective-permute-start(bf16[1,1,16,1024]{3,2,0,1:T(8,128)(2,1)S(1)} %get-tuple-element.50), channel_id=1, source_target_pairs={{0,16},{4,20},{8,24},{12,28},{16,0},{20,4},{24,8},{28,12},{1,17},{... | collective-permute-start | bytes 98312 | tf_op jit(solution)/shard_map/ppermute | solution.py:13
  5.7 5.5 %collective-permute-start.5 = (bf16[1,1,32,1024]{3,2,0,1:T(8,128)(2,1)S(1)}, bf16[1,1,32,1024]{3,2,0,1:T(8,128)(2,1)S(1)}, u32[]{:S(2)}, u32[]{:S(2)}) collective-permute-start(bf16[1,1,32,1024]{3,2,0,1:T(8,128)(2,1)S(1)} %get-tuple-element.48), channel_id=1, source_target_pairs={{0,16},{4,20},{8,24},{12,28},{16,0},{20,4},{24,8},{28,12},{1,17},{... | collective-permute-start | bytes 196616 | tf_op jit(solution)/shard_map/ppermute | solution.py:13
  7.1 5.7 %collective-permute-start.1 = (bf16[2,1,16,1024]{3,2,0,1:T(8,128)(2,1)S(1)}, bf16[2,1,16,1024]{3,2,0,1:T(8,128)(2,1)S(1)}, u32[]{:S(2)}, u32[]{:S(2)}) collective-permute-start(bf16[2,1,16,1024]{3,2,0,1:T(8,128)(2,1)S(1)} %maximum_select_fusion.8), channel_id=1, source_target_pairs={{0,8},{4,12},{8,0},{12,4},{16,24},{20,28},{24,16},{28,20},{1,9},{5... | collective-permute-start | bytes 196616 | tf_op jit(solution)/shard_map/ppermute | solution.py:13
  11.2 5.0 %collective-permute-start.6 = (bf16[2,1,32,1024]{3,2,0,1:T(8,128)(2,1)S(1)}, bf16[2,1,32,1024]{3,2,0,1:T(8,128)(2,1)S(1)}, u32[]{:S(2)}, u32[]{:S(2)}) collective-permute-start(bf16[2,1,32,1024]{3,2,0,1:T(8,128)(2,1)S(1)} %maximum_select_fusion.7), channel_id=1, source_target_pairs={{0,8},{4,12},{8,0},{12,4},{16,24},{20,28},{24,16},{28,20},{1,9},{5... | collective-permute-start | bytes 393224 | tf_op jit(solution)/shard_map/ppermute | solution.py:13
  12.8 6.4 %collective-permute-start.2 = (bf16[4,1,16,1024]{3,2,0,1:T(8,128)(2,1)S(1)}, bf16[4,1,16,1024]{3,2,0,1:T(8,128)(2,1)S(1)}, u32[]{:S(2)}, u32[]{:S(2)}) collective-permute-start(bf16[4,1,16,1024]{3,2,0,1:T(8,128)(2,1)S(1)} %bitcast.156), channel_id=1, source_target_pairs={{0,4},{4,0},{8,12},{12,8},{16,20},{20,16},{24,28},{28,24},{1,5},{5... | collective-permute-start | bytes 393224 | tf_op jit(solution)/shard_map/ppermute | solution.py:13
  16.3 6.7 %collective-permute-start.7 = (bf16[4,1,32,1024]{3,2,0,1:T(8,128)(2,1)S(1)}, bf16[4,1,32,1024]{3,2,0,1:T(8,128)(2,1)S(1)}, u32[]{:S(2)}, u32[]{:S(2)}) collective-permute-start(bf16[4,1,32,1024]{3,2,0,1:T(8,128)(2,1)S(1)} %bitcast.152), channel_id=1, source_target_pairs={{0,4},{4,0},{8,12},{12,8},{16,20},{20,16},{24,28},{28,24},{1,5},{5... | collective-permute-start | bytes 786440 | tf_op jit(solution)/shard_map/ppermute | solution.py:13
  19.8 6.4 %collective-permute-start.3 = (bf16[1,8,16,1024]{3,2,1,0:T(8,128)(2,1)S(1)}, bf16[1,8,16,1024]{3,2,1,0:T(8,128)(2,1)S(1)}, u32[]{:S(2)}, u32[]{:S(2)}) collective-permute-start(bf16[1,8,16,1024]{3,2,1,0:T(8,128)(2,1)S(1)} %bitcast.147), channel_id=1, source_target_pairs={{0,2},{1,3},{2,0},{3,1},{4,6},{5,7},{6,4},{7,5},{8,10},{9,11},{10,... | collective-permute-start | bytes 786440 | tf_op jit(solution)/shard_map/ppermute | solution.py:13
  26.3 2.0 %collective-permute-start.4 = (bf16[2,8,16,1024]{3,2,1,0:T(8,128)(2,1)S(1)}, bf16[2,8,16,1024]{3,2,1,0:T(8,128)(2,1)S(1)}, u32[]{:S(2)}, u32[]{:S(2)}) collective-permute-start(bf16[2,8,16,1024]{3,2,1,0:T(8,128)(2,1)S(1)} %maximum_select_fusion.2), channel_id=1, source_target_pairs={{0,1},{1,0},{2,3},{3,2},{4,5},{5,4},{6,7},{7,6},{8,9},{9,8},{10,11... | collective-permute-start | bytes 1572872 | tf_op jit(solution)/shard_map/ppermute | solution.py:13
  26.4 2.5 %slice-start = ((s8[8388608]{0:T(1024)(128)(4,1)}), s8[4194304]{0:T(1024)(128)(4,1)S(1)}, s32[]{:S(2)}) async-start(s8[8388608]{0:T(1024)(128)(4,1)} %bitcast.164), calls=%async_computation | async-start | bytes 8388608
  27.2 2.8 %slice-start.1 = ((s8[8388608]{0:T(1024)(128)(4,1)}), s8[4194304]{0:T(1024)(128)(4,1)S(1)}, s32[]{:S(2)}) async-start(s8[8388608]{0:T(1024)(128)(4,1)} %bitcast.164), calls=%async_computation.1 | async-start | bytes 8388608
  35.7 7.1 %collective-permute-start.8 = (f32[2,2,256,256]{3,2,1,0:T(8,128)S(1)}, f32[2,2,256,256]{3,2,1,0:T(8,128)S(1)}, u32[]{:S(2)}, u32[]{:S(2)}) collective-permute-start(f32[2,2,256,256]{3,2,1,0:T(8,128)S(1)} %pad_maximum_fusion), channel_id=1, source_target_pairs={{0,1},{1,0},{2,3},{3,2},{4,5},{5,4},{6,7},{7,6},{8,9},{9,8},{10,11... | collective-permute-start | bytes 3145736 | tf_op jit(solution)/shard_map/ppermute | solution.py:13
  42.2 3.1 %collective-permute-start.10 = (f32[2,2,256,256]{3,2,1,0:T(8,128)S(1)}, f32[2,2,256,256]{3,2,1,0:T(8,128)S(1)}, u32[]{:S(2)}, u32[]{:S(2)}) collective-permute-start(f32[2,2,256,256]{3,2,1,0:T(8,128)S(1)} %pad_maximum_fusion.1), channel_id=1, source_target_pairs={{0,1},{1,0},{2,3},{3,2},{4,5},{5,4},{6,7},{7,6},{8,9},{9,8},{10,11... | collective-permute-start | bytes 3145736 | tf_op jit(solution)/shard_map/ppermute | solution.py:13
  43.2 9.2 %collective-permute-start.9 = (bf16[1,2,256,256]{3,2,1,0:T(8,128)(2,1)S(1)}, bf16[1,2,256,256]{3,2,1,0:T(8,128)(2,1)S(1)}, u32[]{:S(2)}, u32[]{:S(2)}) collective-permute-start(bf16[1,2,256,256]{3,2,1,0:T(8,128)(2,1)S(1)} %fusion.8), channel_id=1, source_target_pairs={{0,2},{1,3},{2,0},{3,1},{4,6},{5,7},{6,4},{7,5},{8,10},{9,11},{10,... | collective-permute-start | bytes 786440 | tf_op jit(solution)/shard_map/ppermute | solution.py:13
  45.8 11.8 %collective-permute-start.11 = (bf16[1,2,256,256]{3,2,1,0:T(8,128)(2,1)S(1)}, bf16[1,2,256,256]{3,2,1,0:T(8,128)(2,1)S(1)}, u32[]{:S(2)}, u32[]{:S(2)}) collective-permute-start(bf16[1,2,256,256]{3,2,1,0:T(8,128)(2,1)S(1)} %fusion.9), channel_id=1, source_target_pairs={{0,2},{1,3},{2,0},{3,1},{4,6},{5,7},{6,4},{7,5},{8,10},{9,11},{10,... | collective-permute-start | bytes 786440 | tf_op jit(solution)/shard_map/ppermute | solution.py:13
